TPU v7x, 512 devices: a whole 4x4x16 slice. The times are simulated.
512 devices in a mesh: tm: 16 (over z), row: 4 (over x), col: 8 (over y, core).
Axes of the slice: x: 4, y: 4, z: 16, core: 2. Of those that a mesh axis runs over, the one named last changes fastest.
Arguments:
- latents: bfloat16 [32, 32, 256, 192], P('tm', 'row', 'col'), may hold values from -6 to 6
- first_gain: float32 [192], replicated, may hold values from 0.1 to 1.9
- first_weight: bfloat16 [3, 3, 3, 192, 192], replicated, may hold values from -0.078125 to 0.078125
- first_bias: float32 [192], replicated, may hold values from -3 to 3
- second_gain: float32 [192], replicated, may hold values from 0.1 to 1.9
- second_weight: bfloat16 [3, 3, 3, 192, 192], replicated, may hold values from -0.078125 to 0.078125
- second_bias: float32 [192], replicated, may hold values from -3 to 3
Outputs:
- decoded: bfloat16 [32, 32, 256, 192], P('tm', 'row', 'col')
All inputs are finite; a program needn't handle non-finite values.
Results may differ from a plain program's by a relative error of at most 0.011.
Values may be sent and summed in bfloat16 or wider, within the bound.
No kernel may reach another device: no remote copies, remote signals or barrier semaphores. Data moves between devices by JAX's collectives and lax.ppermute only.
A program may use at most 64 MiB of HBM per device.

v0:
```python
import jax
import jax.numpy as jnp
from jax import lax
from jax.sharding import PartitionSpec as P


def with_halo(cells, sides, width):
    for axis, dim in sides:
        count = lax.axis_size(axis)
        ends = count - 1
        head = lax.slice_in_dim(cells, 0, width, axis=dim)
        tail = lax.slice_in_dim(cells, cells.shape[dim] - width, cells.shape[dim], axis=dim)
        cells = jnp.concatenate(
            [
                lax.ppermute(tail, axis, [(i, (i + 1) % count) for i in range(ends)]),
                cells,
                lax.ppermute(head, axis, [((i + 1) % count, i) for i in range(ends)]),
            ],
            axis=dim,
        )
    return cells


def shifted(value, axis, steps):
    count = lax.axis_size(axis)
    initial, last = (max(0, -steps), min(count, count - steps))
    return lax.ppermute(value, axis, [(source, source + steps) for source in range(initial, last)])


def rms_norm(values, gain):
    return values * lax.rsqrt(jnp.mean(values * values, axis=-1, keepdims=True) + 1e-06) * gain


def causal_local(extended, kernel, out_rows, out_cols):
    chans = extended.shape[-1]
    widened = jnp.concatenate(
        [
            extended[:, :, 0:out_cols, :],
            extended[:, :, 1 : out_cols + 1, :],
            extended[:, :, 2 : out_cols + 2, :],
        ],
        axis=-1,
    )
    folded = kernel.reshape(3, 3, 3 * chans, kernel.shape[-1])
    results = []
    for frame_idx in range(extended.shape[0] - 2):
        accum = None
        for before in range(3):
            for upward in range(3):
                window = widened[frame_idx + before, upward : upward + out_rows].reshape(
                    out_rows * out_cols, 3 * chans
                )
                term = jnp.dot(window, folded[before, upward], preferred_element_type=jnp.float32)
                accum = term if accum is None else accum + term
        results.append(accum)
    return jnp.stack(results, axis=0).reshape(
        extended.shape[0] - 2, out_rows, out_cols, kernel.shape[-1]
    )


def local(latents, first_gain, first_weight, first_bias, second_gain, second_weight, second_bias):
    frames, rows, cols, chans = latents.shape
    values = latents.astype(jnp.float32)
    first_act = jax.nn.silu(rms_norm(values, first_gain)).astype(jnp.bfloat16)
    first_ext = with_halo(first_act, (("row", 1), ("col", 2)), 1)
    margin = 0
    first_cache = shifted(first_ext, "tm", 1)
    first_conv = causal_local(
        jnp.concatenate([first_cache, first_ext], axis=0),
        first_weight,
        rows + 2 * margin,
        cols + 2 * margin,
    )
    hidden = (first_conv + first_bias).astype(jnp.bfloat16)
    second_act = jax.nn.silu(rms_norm(hidden.astype(jnp.float32), second_gain))
    second_ext = with_halo(second_act.astype(jnp.bfloat16), (("row", 1), ("col", 2)), 1)
    second_cache = shifted(second_ext, "tm", 1)
    second_conv = causal_local(
        jnp.concatenate([second_cache, second_ext], axis=0), second_weight, rows, cols
    )
    decoded = values + second_conv + second_bias
    return decoded.astype(jnp.bfloat16)


def solution(mesh):
    in_specs = (P("tm", "row", "col", None), P(), P(), P(), P(), P(), P())
    out_specs = P("tm", "row", "col", None)
    return jax.shard_map(local, mesh=mesh, in_specs=in_specs, out_specs=out_specs, check_vma=False)
```

profile of v0, /device:TPU:393, one launch (start us, length us, event | category | flops | bytes accessed | tf_op | source)
XLA Modules:
  0.0 85.8 jit_solution(8132527059777860640)
XLA Ops:
  0.0 1.1 %fusion.8 = f32[2,8,32]{2,1,0:T(8,128)S(1)} fusion(bf16[2,8,32,192]{3,2,1,0:T(8,128)(2,1)} %param.7), kind=kLoop, calls=%fused_computation.49 | loop fusion | flops 294400 | bytes 198656 | tf_op jit(solution)/shard_map/reduce_sum | solution.py:31
  1.1 1.2 %fusion.15 = bf16[2,8,32,192]{3,2,1,0:T(8,128)(2,1)S(1)} fusion(bf16[2,8,32,192]{3,2,1,0:T(8,128)(2,1)} %param.7, f32[192]{0:T(256)} %param.8, f32[2,8,32]{2,1,0:T(8,128)S(1)} %add_rsqrt_fusion.1), kind=kLoop, calls=%fused_computation.56 | loop fusion | flops 786432 | bytes 396032 | tf_op jit(solution)/shard_map/convert_element_type | solution.py:64
  2.3 3.1 %collective-permute-start = (bf16[2,1,32,192]{3,2,1,0:T(8,128)(2,1)S(1)}, bf16[2,1,32,192]{3,2,1,0:T(8,128)(2,1)S(1)}, u32[]{:S(2)}, u32[]{:S(2)}) collective-permute-start(bf16[2,1,32,192]{3,2,1,0:T(8,128)(2,1)S(1)} %get-tuple-element.41), channel_id=1, source_target_pairs={{0,8},{8,16},{16,24},{1,9},{9,17},{17,25},{2,10},{10,18},{18,26},{... | collective-permute-start | bytes 73736 | tf_op jit(solution)/shard_map/ppermute | solution.py:15
  5.4 1.3 %collective-permute-start.1 = (bf16[2,1,32,192]{3,2,1,0:T(8,128)(2,1)S(1)}, bf16[2,1,32,192]{3,2,1,0:T(8,128)(2,1)S(1)}, u32[]{:S(2)}, u32[]{:S(2)}) collective-permute-start(bf16[2,1,32,192]{3,2,1,0:T(8,128)(2,1)S(1)} %get-tuple-element.42), channel_id=1, source_target_pairs={{8,0},{16,8},{24,16},{9,1},{17,9},{25,17},{10,2},{18,10},{26,18},{... | collective-permute-start | bytes 73736 | tf_op jit(solution)/shard_map/ppermute | solution.py:17
  6.8 3.3 %collective-permute-done.1 = bf16[2,1,32,192]{3,2,1,0:T(8,128)(2,1)S(1)} collective-permute-done((bf16[2,1,32,192]{3,2,1,0:T(8,128)(2,1)S(1)}, bf16[2,1,32,192]{3,2,1,0:T(8,128)(2,1)S(1)}, u32[]{:S(2)}, u32[]{:S(2)}) %collective-permute-start.1) | collective-permute-done | bytes 24608 | tf_op jit(solution)/shard_map/ppermute | solution.py:17
  10.1 5.2 %collective-permute-start.2 = (bf16[2,10,1,192]{3,2,1,0:T(2,128)(2,1)S(1)}, bf16[2,10,1,192]{3,2,1,0:T(2,128)(2,1)S(1)}, u32[]{:S(2)}, u32[]{:S(2)}) collective-permute-start(bf16[2,10,1,192]{3,2,1,0:T(2,128)(2,1)S(1)} %get-tuple-element.37), channel_id=1, source_target_pairs={{0,1},{1,2},{2,3},{3,4},{4,5},{5,6},{6,7},{8,9},{9,10},{10,11},{11... | collective-permute-start | bytes 23048 | tf_op jit(solution)/shard_map/ppermute | solution.py:15
  15.3 1.9 %collective-permute-start.3 = (bf16[2,10,1,192]{3,2,1,0:T(2,128)(2,1)S(1)}, bf16[2,10,1,192]{3,2,1,0:T(2,128)(2,1)S(1)}, u32[]{:S(2)}, u32[]{:S(2)}) collective-permute-start(bf16[2,10,1,192]{3,2,1,0:T(2,128)(2,1)S(1)} %get-tuple-element.38), channel_id=1, source_target_pairs={{1,0},{2,1},{3,2},{4,3},{5,4},{6,5},{7,6},{9,8},{10,9},{11,10},{12... | collective-permute-start | bytes 23048 | tf_op jit(solution)/shard_map/ppermute | solution.py:17
  17.3 3.2 %collective-permute-done.3 = bf16[2,10,1,192]{3,2,1,0:T(2,128)(2,1)S(1)} collective-permute-done((bf16[2,10,1,192]{3,2,1,0:T(2,128)(2,1)S(1)}, bf16[2,10,1,192]{3,2,1,0:T(2,128)(2,1)S(1)}, u32[]{:S(2)}, u32[]{:S(2)}) %collective-permute-start.3) | collective-permute-done | bytes 7712 | tf_op jit(solution)/shard_map/ppermute | solution.py:17
  20.6 2.6 %collective-permute-start.4 = (bf16[2,10,34,192]{3,2,1,0:T(8,128)(2,1)S(1)}, bf16[2,10,34,192]{3,2,1,0:T(8,128)(2,1)S(1)}, u32[]{:S(2)}, u32[]{:S(2)}) collective-permute-start(bf16[2,10,34,192]{3,2,1,0:T(8,128)(2,1)S(1)} %pad_maximum_fusion.2), channel_id=1, source_target_pairs={{0,32},{32,64},{64,96},{96,128},{128,160},{160,192},{192,224},{224... | collective-permute-start | bytes 783368 | tf_op jit(solution)/shard_map/ppermute | solution.py:27
  23.3 10.9 %collective-permute-done.4 = bf16[2,10,34,192]{3,2,1,0:T(8,128)(2,1)S(1)} collective-permute-done((bf16[2,10,34,192]{3,2,1,0:T(8,128)(2,1)S(1)}, bf16[2,10,34,192]{3,2,1,0:T(8,128)(2,1)S(1)}, u32[]{:S(2)}, u32[]{:S(2)}) %collective-permute-start.4) | collective-permute-done | bytes 261152 | tf_op jit(solution)/shard_map/ppermute | solution.py:27
  34.2 0.3 maximum_maximum_fusion
  34.5 0.5 fusion.26
  35.0 0.7 pad_maximum_fusion
  35.7 0.4 fusion.24
  36.1 1.3 %copy-done = bf16[3,3,3,192,192]{4,3,2,1,0:T(8,128)(2,1)S(1)} copy-done((bf16[3,3,3,192,192]{4,3,2,1,0:T(8,128)(2,1)S(1)}, bf16[3,3,3,192,192]{4,3,2,1,0:T(8,128)(2,1)}, u32[]{:S(2)}) %copy-start) | copy-done | bytes 1990680
  37.5 0.3 fusion.19
  37.8 0.3 fusion.20
  38.1 0.3 convolution_add_fusion.31
  38.5 0.3 convolution_add_fusion.30
  38.8 0.3 convolution_add_fusion.29
  39.1 0.3 convolution_add_fusion.28
  39.5 0.3 convolution_add_fusion.23
  39.8 0.3 convolution_add_fusion.22
  40.1 0.3 convolution_add_fusion.27
  40.5 0.3 convolution_add_fusion.26
  40.8 0.3 convolution_add_fusion.21
  41.1 0.3 convolution_add_fusion.20
  41.5 0.3 convolution_add_fusion.25
  41.8 0.3 convolution_add_fusion.24
  42.2 0.3 convolution_add_fusion.19
  42.5 0.3 convolution_add_fusion.18
  42.9 0.3 convolution_add_fusion.17
  43.2 0.3 convolution_add_fusion.16
  44.2 3.1 %collective-permute-start.5 = (bf16[2,1,32,192]{3,2,1,0:T(8,128)(2,1)S(1)}, bf16[2,1,32,192]{3,2,1,0:T(8,128)(2,1)S(1)}, u32[]{:S(2)}, u32[]{:S(2)}) collective-permute-start(bf16[2,1,32,192]{3,2,1,0:T(8,128)(2,1)S(1)} %get-tuple-element.39), channel_id=1, source_target_pairs={{0,8},{8,16},{16,24},{1,9},{9,17},{17,25},{2,10},{10,18},{18,26},{... | collective-permute-start | bytes 73736 | tf_op jit(solution)/shard_map/ppermute | solution.py:15
  47.4 1.3 %collective-permute-start.6 = (bf16[2,1,32,192]{3,2,1,0:T(8,128)(2,1)S(1)}, bf16[2,1,32,192]{3,2,1,0:T(8,128)(2,1)S(1)}, u32[]{:S(2)}, u32[]{:S(2)}) collective-permute-start(bf16[2,1,32,192]{3,2,1,0:T(8,128)(2,1)S(1)} %get-tuple-element.40), channel_id=1, source_target_pairs={{8,0},{16,8},{24,16},{9,1},{17,9},{25,17},{10,2},{18,10},{26,18},{... | collective-permute-start | bytes 73736 | tf_op jit(solution)/shard_map/ppermute | solution.py:17
  48.7 3.3 %collective-permute-done.6 = bf16[2,1,32,192]{3,2,1,0:T(8,128)(2,1)S(1)} collective-permute-done((bf16[2,1,32,192]{3,2,1,0:T(8,128)(2,1)S(1)}, bf16[2,1,32,192]{3,2,1,0:T(8,128)(2,1)S(1)}, u32[]{:S(2)}, u32[]{:S(2)}) %collective-permute-start.6) | collective-permute-done | bytes 24608 | tf_op jit(solution)/shard_map/ppermute | solution.py:17
  52.1 4.8 %collective-permute-start.7 = (bf16[2,10,1,192]{3,2,1,0:T(2,128)(2,1)S(1)}, bf16[2,10,1,192]{3,2,1,0:T(2,128)(2,1)S(1)}, u32[]{:S(2)}, u32[]{:S(2)}) collective-permute-start(bf16[2,10,1,192]{3,2,1,0:T(2,128)(2,1)S(1)} %get-tuple-element.35), channel_id=1, source_target_pairs={{0,1},{1,2},{2,3},{3,4},{4,5},{5,6},{6,7},{8,9},{9,10},{10,11},{11... | collective-permute-start | bytes 23048 | tf_op jit(solution)/shard_map/ppermute | solution.py:15
  56.9 1.9 %collective-permute-start.8 = (bf16[2,10,1,192]{3,2,1,0:T(2,128)(2,1)S(1)}, bf16[2,10,1,192]{3,2,1,0:T(2,128)(2,1)S(1)}, u32[]{:S(2)}, u32[]{:S(2)}) collective-permute-start(bf16[2,10,1,192]{3,2,1,0:T(2,128)(2,1)S(1)} %get-tuple-element.36), channel_id=1, source_target_pairs={{1,0},{2,1},{3,2},{4,3},{5,4},{6,5},{7,6},{9,8},{10,9},{11,10},{12... | collective-permute-start | bytes 23048 | tf_op jit(solution)/shard_map/ppermute | solution.py:17
  58.8 3.2 %collective-permute-done.8 = bf16[2,10,1,192]{3,2,1,0:T(2,128)(2,1)S(1)} collective-permute-done((bf16[2,10,1,192]{3,2,1,0:T(2,128)(2,1)S(1)}, bf16[2,10,1,192]{3,2,1,0:T(2,128)(2,1)S(1)}, u32[]{:S(2)}, u32[]{:S(2)}) %collective-permute-start.8) | collective-permute-done | bytes 7712 | tf_op jit(solution)/shard_map/ppermute | solution.py:17
  62.2 2.1 %collective-permute-start.9 = (bf16[2,10,34,192]{3,2,1,0:T(8,128)(2,1)S(1)}, bf16[2,10,34,192]{3,2,1,0:T(8,128)(2,1)S(1)}, u32[]{:S(2)}, u32[]{:S(2)}) collective-permute-start(bf16[2,10,34,192]{3,2,1,0:T(8,128)(2,1)S(1)} %pad_maximum_fusion.3), channel_id=1, source_target_pairs={{0,32},{32,64},{64,96},{96,128},{128,160},{160,192},{192,224},{224... | collective-permute-start | bytes 783368 | tf_op jit(solution)/shard_map/ppermute | solution.py:27
  64.3 11.2 %collective-permute-done.9 = bf16[2,10,34,192]{3,2,1,0:T(8,128)(2,1)S(1)} collective-permute-done((bf16[2,10,34,192]{3,2,1,0:T(8,128)(2,1)S(1)}, bf16[2,10,34,192]{3,2,1,0:T(8,128)(2,1)S(1)}, u32[]{:S(2)}, u32[]{:S(2)}) %collective-permute-start.9) | collective-permute-done | bytes 261152 | tf_op jit(solution)/shard_map/ppermute | solution.py:27
  75.8 0.5 fusion.25
  76.2 0.7 pad_maximum_fusion.1
  76.9 0.4 fusion.23
  77.4 1.3 %copy-done.1 = bf16[3,3,3,192,192]{4,3,2,1,0:T(8,128)(2,1)S(1)} copy-done((bf16[3,3,3,192,192]{4,3,2,1,0:T(8,128)(2,1)S(1)}, bf16[3,3,3,192,192]{4,3,2,1,0:T(8,128)(2,1)}, u32[]{:S(2)}) %copy-start.1) | copy-done | bytes 1990680
  78.7 0.3 fusion.21
  79.0 0.3 fusion.22
  79.4 0.3 convolution_add_fusion.15
  79.7 0.3 convolution_add_fusion.14
  80.0 0.3 convolution_add_fusion.13
  80.4 0.3 convolution_add_fusion.12
  80.7 0.3 convolution_add_fusion.7
  81.0 0.3 convolution_add_fusion.6
  81.4 0.3 convolution_add_fusion.11
  81.7 0.3 convolution_add_fusion.10
  82.0 0.3 convolution_add_fusion.5
  82.4 0.3 convolution_add_fusion.4
  82.7 0.3 convolution_add_fusion.9
  83.1 0.3 convolution_add_fusion.8
  83.4 0.3 convolution_add_fusion.3
  83.7 0.3 convolution_add_fusion.2
  84.1 0.3 convolution_add_fusion.1
  84.4 0.3 convolution_add_fusion
  85.0 0.8 fusion.17
  (29 shorter events, 1.7 us)
Async XLA Ops:
  2.3 4.4 %collective-permute-start = (bf16[2,1,32,192]{3,2,1,0:T(8,128)(2,1)S(1)}, bf16[2,1,32,192]{3,2,1,0:T(8,128)(2,1)S(1)}, u32[]{:S(2)}, u32[]{:S(2)}) collective-permute-start(bf16[2,1,32,192]{3,2,1,0:T(8,128)(2,1)S(1)} %get-tuple-element.41), channel_id=1, source_target_pairs={{0,8},{8,16},{16,24},{1,9},{9,17},{17,25},{2,10},{10,18},{18,26},{... | collective-permute-start | bytes 73736 | tf_op jit(solution)/shard_map/ppermute | solution.py:15
  5.4 4.7 %collective-permute-start.1 = (bf16[2,1,32,192]{3,2,1,0:T(8,128)(2,1)S(1)}, bf16[2,1,32,192]{3,2,1,0:T(8,128)(2,1)S(1)}, u32[]{:S(2)}, u32[]{:S(2)}) collective-permute-start(bf16[2,1,32,192]{3,2,1,0:T(8,128)(2,1)S(1)} %get-tuple-element.42), channel_id=1, source_target_pairs={{8,0},{16,8},{24,16},{9,1},{17,9},{25,17},{10,2},{18,10},{26,18},{... | collective-permute-start | bytes 73736 | tf_op jit(solution)/shard_map/ppermute | solution.py:17
  10.1 7.1 %collective-permute-start.2 = (bf16[2,10,1,192]{3,2,1,0:T(2,128)(2,1)S(1)}, bf16[2,10,1,192]{3,2,1,0:T(2,128)(2,1)S(1)}, u32[]{:S(2)}, u32[]{:S(2)}) collective-permute-start(bf16[2,10,1,192]{3,2,1,0:T(2,128)(2,1)S(1)} %get-tuple-element.37), channel_id=1, source_target_pairs={{0,1},{1,2},{2,3},{3,4},{4,5},{5,6},{6,7},{8,9},{9,10},{10,11},{11... | collective-permute-start | bytes 23048 | tf_op jit(solution)/shard_map/ppermute | solution.py:15
  15.3 5.1 %collective-permute-start.3 = (bf16[2,10,1,192]{3,2,1,0:T(2,128)(2,1)S(1)}, bf16[2,10,1,192]{3,2,1,0:T(2,128)(2,1)S(1)}, u32[]{:S(2)}, u32[]{:S(2)}) collective-permute-start(bf16[2,10,1,192]{3,2,1,0:T(2,128)(2,1)S(1)} %get-tuple-element.38), channel_id=1, source_target_pairs={{1,0},{2,1},{3,2},{4,3},{5,4},{6,5},{7,6},{9,8},{10,9},{11,10},{12... | collective-permute-start | bytes 23048 | tf_op jit(solution)/shard_map/ppermute | solution.py:17
  20.6 13.6 %collective-permute-start.4 = (bf16[2,10,34,192]{3,2,1,0:T(8,128)(2,1)S(1)}, bf16[2,10,34,192]{3,2,1,0:T(8,128)(2,1)S(1)}, u32[]{:S(2)}, u32[]{:S(2)}) collective-permute-start(bf16[2,10,34,192]{3,2,1,0:T(8,128)(2,1)S(1)} %pad_maximum_fusion.2), channel_id=1, source_target_pairs={{0,32},{32,64},{64,96},{96,128},{128,160},{160,192},{192,224},{224... | collective-permute-start | bytes 783368 | tf_op jit(solution)/shard_map/ppermute | solution.py:27
  35.7 1.8 %copy-start = (bf16[3,3,3,192,192]{4,3,2,1,0:T(8,128)(2,1)S(1)}, bf16[3,3,3,192,192]{4,3,2,1,0:T(8,128)(2,1)}, u32[]{:S(2)}) copy-start(bf16[3,3,3,192,192]{4,3,2,1,0:T(8,128)(2,1)} %param.9) | copy-start | bytes 5971972
  42.2 1.6 %copy-start.3 = (f32[192]{0:T(256)S(1)}, f32[192]{0:T(256)}, u32[]{:S(2)}) copy-start(f32[192]{0:T(256)} %param.10) | copy-start | bytes 2308
  42.2 1.8 %copy-start.4 = (f32[192]{0:T(256)S(1)}, f32[192]{0:T(256)}, u32[]{:S(2)}) copy-start(f32[192]{0:T(256)} %param.11) | copy-start | bytes 2308
  44.2 4.4 %collective-permute-start.5 = (bf16[2,1,32,192]{3,2,1,0:T(8,128)(2,1)S(1)}, bf16[2,1,32,192]{3,2,1,0:T(8,128)(2,1)S(1)}, u32[]{:S(2)}, u32[]{:S(2)}) collective-permute-start(bf16[2,1,32,192]{3,2,1,0:T(8,128)(2,1)S(1)} %get-tuple-element.39), channel_id=1, source_target_pairs={{0,8},{8,16},{16,24},{1,9},{9,17},{17,25},{2,10},{10,18},{18,26},{... | collective-permute-start | bytes 73736 | tf_op jit(solution)/shard_map/ppermute | solution.py:15
  47.4 4.7 %collective-permute-start.6 = (bf16[2,1,32,192]{3,2,1,0:T(8,128)(2,1)S(1)}, bf16[2,1,32,192]{3,2,1,0:T(8,128)(2,1)S(1)}, u32[]{:S(2)}, u32[]{:S(2)}) collective-permute-start(bf16[2,1,32,192]{3,2,1,0:T(8,128)(2,1)S(1)} %get-tuple-element.40), channel_id=1, source_target_pairs={{8,0},{16,8},{24,16},{9,1},{17,9},{25,17},{10,2},{18,10},{26,18},{... | collective-permute-start | bytes 73736 | tf_op jit(solution)/shard_map/ppermute | solution.py:17
  52.1 6.7 %collective-permute-start.7 = (bf16[2,10,1,192]{3,2,1,0:T(2,128)(2,1)S(1)}, bf16[2,10,1,192]{3,2,1,0:T(2,128)(2,1)S(1)}, u32[]{:S(2)}, u32[]{:S(2)}) collective-permute-start(bf16[2,10,1,192]{3,2,1,0:T(2,128)(2,1)S(1)} %get-tuple-element.35), channel_id=1, source_target_pairs={{0,1},{1,2},{2,3},{3,4},{4,5},{5,6},{6,7},{8,9},{9,10},{10,11},{11... | collective-permute-start | bytes 23048 | tf_op jit(solution)/shard_map/ppermute | solution.py:15
  56.9 5.1 %collective-permute-start.8 = (bf16[2,10,1,192]{3,2,1,0:T(2,128)(2,1)S(1)}, bf16[2,10,1,192]{3,2,1,0:T(2,128)(2,1)S(1)}, u32[]{:S(2)}, u32[]{:S(2)}) collective-permute-start(bf16[2,10,1,192]{3,2,1,0:T(2,128)(2,1)S(1)} %get-tuple-element.36), channel_id=1, source_target_pairs={{1,0},{2,1},{3,2},{4,3},{5,4},{6,5},{7,6},{9,8},{10,9},{11,10},{12... | collective-permute-start | bytes 23048 | tf_op jit(solution)/shard_map/ppermute | solution.py:17
  62.2 13.3 %collective-permute-start.9 = (bf16[2,10,34,192]{3,2,1,0:T(8,128)(2,1)S(1)}, bf16[2,10,34,192]{3,2,1,0:T(8,128)(2,1)S(1)}, u32[]{:S(2)}, u32[]{:S(2)}) collective-permute-start(bf16[2,10,34,192]{3,2,1,0:T(8,128)(2,1)S(1)} %pad_maximum_fusion.3), channel_id=1, source_target_pairs={{0,32},{32,64},{64,96},{96,128},{128,160},{160,192},{192,224},{224... | collective-permute-start | bytes 783368 | tf_op jit(solution)/shard_map/ppermute | solution.py:27
  76.9 1.8 %copy-start.1 = (bf16[3,3,3,192,192]{4,3,2,1,0:T(8,128)(2,1)S(1)}, bf16[3,3,3,192,192]{4,3,2,1,0:T(8,128)(2,1)}, u32[]{:S(2)}) copy-start(bf16[3,3,3,192,192]{4,3,2,1,0:T(8,128)(2,1)} %param.12) | copy-start | bytes 5971972
  83.4 1.6 %copy-start.2 = (bf16[2,8,32,192]{3,2,1,0:T(8,128)(2,1)S(1)}, bf16[2,8,32,192]{3,2,1,0:T(8,128)(2,1)}, u32[]{:S(2)}) copy-start(bf16[2,8,32,192]{3,2,1,0:T(8,128)(2,1)} %param.7) | copy-start | bytes 589828
  83.4 1.6 %copy-start.5 = (f32[192]{0:T(256)S(1)}, f32[192]{0:T(256)}, u32[]{:S(2)}) copy-start(f32[192]{0:T(256)} %param.13) | copy-start | bytes 2308
where the time goes:
time: 86.3 us; the launch traced here: 85.8 us
  waiting for transfers between devices  35.2 us (41%)
  starting transfers between devices  27.4 us (32%)
  matrix products  12.1 us (14%)
  other arithmetic  5.86 us (7%)
  local copies, waits for them, and re-layouts  4.97 us (6%)
    ppermute x2, waiting for transfers between devices, shifted(): lax.ppermute(value, axis, [(source, source + steps) for source in range(i...  22.1 us
    ppermute x4, starting transfers between devices, with_halo(): lax.ppermute(tail, axis, [(i, (i + 1) % count) for i in range(ends)])  16.2 us
    ppermute x4, waiting for transfers between devices, with_halo(): lax.ppermute(head, axis, [((i + 1) % count, i) for i in range(ends)])  13 us
    dot_general x36, matrix products, causal_local(): jnp.dot(window, folded[before, upward], preferred_element_type=jnp.float32)  12.1 us
    ppermute x4, starting transfers between devices, with_halo(): lax.ppermute(head, axis, [((i + 1) % count, i) for i in range(ends)])  6.43 us
    ppermute x2, starting transfers between devices, shifted(): lax.ppermute(value, axis, [(source, source + steps) for source in range(i...  4.75 us
    unnamed x12, local copies, waits for them, and re-layouts  2.69 us
  transfers between devices with their start and end apart: 10, of which 6 were waited for; matrix products, arithmetic and copies ran while one was open for 0% of the time, Pallas kernels for 0%

commit v1 on v0

v1 whole, which is shorter than its diff:
```python
import jax
import jax.numpy as jnp
from jax import lax
from jax.sharding import PartitionSpec as P


def with_halo(cells, sides, width):
    for axis, dim in sides:
        count = lax.axis_size(axis)
        ends = count - 1
        head = lax.slice_in_dim(cells, 0, width, axis=dim)
        tail = lax.slice_in_dim(cells, cells.shape[dim] - width, cells.shape[dim], axis=dim)
        cells = jnp.concatenate(
            [
                lax.ppermute(tail, axis, [(i, i + 1) for i in range(ends)]),
                cells,
                lax.ppermute(head, axis, [(i + 1, i) for i in range(ends)]),
            ],
            axis=dim,
        )
    return cells


def shifted(value, axis, steps):
    count = lax.axis_size(axis)
    initial, last = (max(0, -steps), min(count, count - steps))
    return lax.ppermute(value, axis, [(source, source + steps) for source in range(initial, last)])


def rms_norm(values, gain):
    return values * lax.rsqrt(jnp.mean(values * values, axis=-1, keepdims=True) + 1e-06) * gain


def conv_valid(stack, kernel):
    out = lax.conv_general_dilated(
        stack[None],
        kernel,
        window_strides=(1, 1, 1),
        padding="VALID",
        dimension_numbers=("NDHWC", "DHWIO", "NDHWC"),
        preferred_element_type=jnp.float32,
    )
    return out[0]


def inside(axis, size, width):
    total = size * lax.axis_size(axis)
    start = lax.axis_index(axis) * size - width
    index = start + jnp.arange(size + 2 * width)
    return (index >= 0) & (index < total)


def local(latents, first_gain, first_weight, first_bias, second_gain, second_weight, second_bias):
    frames, rows, cols, chans = latents.shape
    values = latents.astype(jnp.float32)
    first_act = jax.nn.silu(rms_norm(values, first_gain)).astype(jnp.bfloat16)
    first_ext = with_halo(first_act, (("row", 1), ("col", 2)), 2)
    first_cache = shifted(first_ext, "tm", 1)
    first_conv = conv_valid(jnp.concatenate([first_cache, first_ext], axis=0), first_weight)
    hidden = (first_conv + first_bias).astype(jnp.bfloat16)
    second_act = jax.nn.silu(rms_norm(hidden.astype(jnp.float32), second_gain))
    keep = inside("row", rows, 1)[:, None] & inside("col", cols, 1)[None, :]
    second_act = jnp.where(keep[None, :, :, None], second_act, 0.0).astype(jnp.bfloat16)
    second_cache = shifted(second_act, "tm", 1)
    second_conv = conv_valid(jnp.concatenate([second_cache, second_act], axis=0), second_weight)
    decoded = values + second_conv + second_bias
    return decoded.astype(jnp.bfloat16)


def solution(mesh):
    in_specs = (P("tm", "row", "col", None), P(), P(), P(), P(), P(), P())
    out_specs = P("tm", "row", "col", None)
    return jax.shard_map(local, mesh=mesh, in_specs=in_specs, out_specs=out_specs, check_vma=False)
```

time: 86.3 us -> 62.8 us (0.73)
  the two profiles are of different devices: /device:TPU:393 before, /device:TPU:274 now
where the time goes in v1:
time: 62.8 us; the launch traced here: 62.5 us
  waiting for transfers between devices  29.4 us (47%)
  starting transfers between devices  16.3 us (26%)
  other arithmetic  6.41 us (10%)
  local copies, waits for them, and re-layouts  5.62 us (9%)
  matrix products  4.47 us (7%)
    ppermute x2, waiting for transfers between devices, shifted(): lax.ppermute(value, axis, [(source, source + steps) for source in range(i...  24.2 us
    ppermute x2, starting transfers between devices, with_halo(): lax.ppermute(head, axis, [(i + 1, i) for i in range(ends)])  6.08 us
    ppermute x2, starting transfers between devices, with_halo(): lax.ppermute(tail, axis, [(i, i + 1) for i in range(ends)])  5.32 us
    ppermute x2, waiting for transfers between devices, with_halo(): lax.ppermute(head, axis, [(i + 1, i) for i in range(ends)])  4.95 us
    ppermute x2, starting transfers between devices, shifted(): lax.ppermute(value, axis, [(source, source + steps) for source in range(i...  4.85 us
    conv_general_dilated x2, matrix products, conv_valid(): lax.conv_general_dilated(stack[None], kernel, window_strides=(1, 1, 1), p...  4.47 us
    unnamed x16, local copies, waits for them, and re-layouts  2.14 us
    reduce_sum x2, other arithmetic, rms_norm(): jnp.mean(values * values, axis=-1, keepdims=True) + 1e-06  1.81 us
  transfers between devices with their start and end apart: 6, of which 5 were waited for; matrix products, arithmetic and copies ran while one was open for 0% of the time, Pallas kernels for 0%

profile of v1, /device:TPU:274, one launch (start us, length us, event | category | flops | bytes accessed | tf_op | source)
XLA Modules:
  0.0 62.5 jit_solution(7192701564367103165)
XLA Ops:
  0.0 0.0 copy-start
  0.0 1.3 %fusion.24 = f32[2,8,32]{1,2,0:T(8,128)S(1)} fusion(bf16[2,8,32,192]{3,2,1,0:T(8,128)(2,1)} %param.7), kind=kLoop, calls=%fused_computation.34 | loop fusion | flops 294400 | bytes 198656 | tf_op jit(solution)/shard_map/reduce_sum | solution.py:31
  1.4 1.2 %fusion.31 = bf16[2,8,32,192]{3,1,2,0:T(8,128)(2,1)S(1)} fusion(f32[192]{0:T(256)} %param.8, f32[2,8,32]{1,2,0:T(8,128)S(1)} %add_rsqrt_fusion.1, bf16[2,8,32,192]{3,2,1,0:T(8,128)(2,1)} %param.7), kind=kLoop, calls=%fused_computation.41 | loop fusion | flops 786432 | bytes 396032 | tf_op jit(solution)/shard_map/convert_element_type | solution.py:56
  2.6 0.1 fusion.40
  2.7 3.4 %collective-permute-start = (bf16[2,2,32,192]{3,1,2,0:T(2,128)(2,1)S(1)}, bf16[2,2,32,192]{3,1,2,0:T(2,128)(2,1)S(1)}, u32[]{:S(2)}, u32[]{:S(2)}) collective-permute-start(bf16[2,2,32,192]{3,1,2,0:T(2,128)(2,1)S(1)} %get-tuple-element.7), channel_id=1, source_target_pairs={{0,8},{8,16},{16,24},{1,9},{9,17},{17,25},{2,10},{10,18},{18,26},{... | collective-permute-start | bytes 147464 | tf_op jit(solution)/shard_map/ppermute | solution.py:15
  6.1 2.4 %collective-permute-start.1 = (bf16[2,2,32,192]{3,1,2,0:T(2,128)(2,1)S(1)}, bf16[2,2,32,192]{3,1,2,0:T(2,128)(2,1)S(1)}, u32[]{:S(2)}, u32[]{:S(2)}) collective-permute-start(bf16[2,2,32,192]{3,1,2,0:T(2,128)(2,1)S(1)} %get-tuple-element.8), channel_id=1, source_target_pairs={{8,0},{16,8},{24,16},{9,1},{17,9},{25,17},{10,2},{18,10},{26,18},{... | collective-permute-start | bytes 147464 | tf_op jit(solution)/shard_map/ppermute | solution.py:17
  8.6 0.3 collective-permute-done
  8.8 3.4 %collective-permute-done.1 = bf16[2,2,32,192]{3,1,2,0:T(2,128)(2,1)S(1)} collective-permute-done((bf16[2,2,32,192]{3,1,2,0:T(2,128)(2,1)S(1)}, bf16[2,2,32,192]{3,1,2,0:T(2,128)(2,1)S(1)}, u32[]{:S(2)}, u32[]{:S(2)}) %collective-permute-start.1) | collective-permute-done | bytes 49184 | tf_op jit(solution)/shard_map/ppermute | solution.py:17
  12.3 1.9 %collective-permute-start.2 = (bf16[2,12,2,192]{3,1,2,0:T(8,128)(2,1)S(1)}, bf16[2,12,2,192]{3,1,2,0:T(8,128)(2,1)S(1)}, u32[]{:S(2)}, u32[]{:S(2)}) collective-permute-start(bf16[2,12,2,192]{3,1,2,0:T(8,128)(2,1)S(1)} %get-tuple-element.5), channel_id=1, source_target_pairs={{0,1},{1,2},{2,3},{3,4},{4,5},{5,6},{6,7},{8,9},{9,10},{10,11},{11... | collective-permute-start | bytes 55304 | tf_op jit(solution)/shard_map/ppermute | solution.py:15
  14.2 3.6 %collective-permute-start.3 = (bf16[2,12,2,192]{3,1,2,0:T(8,128)(2,1)S(1)}, bf16[2,12,2,192]{3,1,2,0:T(8,128)(2,1)S(1)}, u32[]{:S(2)}, u32[]{:S(2)}) collective-permute-start(bf16[2,12,2,192]{3,1,2,0:T(8,128)(2,1)S(1)} %get-tuple-element.6), channel_id=1, source_target_pairs={{1,0},{2,1},{3,2},{4,3},{5,4},{6,5},{7,6},{9,8},{10,9},{11,10},{12... | collective-permute-start | bytes 55304 | tf_op jit(solution)/shard_map/ppermute | solution.py:17
  17.9 0.0 collective-permute-done.2
  17.9 1.5 %collective-permute-done.3 = bf16[2,12,2,192]{3,1,2,0:T(8,128)(2,1)S(1)} collective-permute-done((bf16[2,12,2,192]{3,1,2,0:T(8,128)(2,1)S(1)}, bf16[2,12,2,192]{3,1,2,0:T(8,128)(2,1)S(1)}, u32[]{:S(2)}, u32[]{:S(2)}) %collective-permute-start.3) | collective-permute-done | bytes 18464 | tf_op jit(solution)/shard_map/ppermute | solution.py:17
  19.5 0.3 pad_maximum_fusion
  19.8 0.5 copy.18
  20.3 2.9 %collective-permute-start.4 = (bf16[2,12,36,192]{3,0,2,1:T(2,128)(2,1)S(1)}, bf16[2,12,36,192]{3,0,2,1:T(2,128)(2,1)S(1)}, u32[]{:S(2)}, u32[]{:S(2)}) collective-permute-start(bf16[2,12,36,192]{3,0,2,1:T(2,128)(2,1)S(1)} %copy.18), channel_id=1, source_target_pairs={{0,32},{32,64},{64,96},{96,128},{128,160},{160,192},{192,224},{224... | collective-permute-start | bytes 995336 | tf_op jit(solution)/shard_map/ppermute | solution.py:27
  23.2 0.1 broadcast_and_fusion
  23.3 12.7 %collective-permute-done.4 = bf16[2,12,36,192]{3,0,2,1:T(2,128)(2,1)S(1)} collective-permute-done((bf16[2,12,36,192]{3,0,2,1:T(2,128)(2,1)S(1)}, bf16[2,12,36,192]{3,0,2,1:T(2,128)(2,1)S(1)}, u32[]{:S(2)}, u32[]{:S(2)}) %collective-permute-start.4) | collective-permute-done | bytes 331808 | tf_op jit(solution)/shard_map/ppermute | solution.py:27
  36.0 0.1 copy.19
  36.1 0.4 maximum_bitcast_fusion
  36.5 0.2 pad
  36.8 0.0 copy-start.7
  36.8 0.4 copy.22
  37.1 0.1 slice.22
  37.2 0.0 copy-done
  37.3 0.2 copy-done.7
  37.5 2.5 %fusion.9 = f32[2,10,8,5,192]{4,2,3,1,0:T(8,128)S(1)} fusion(bf16[3,3,3,192,192]{4,3,2,1,0:T(8,128)(2,1)S(1)} %copy-done, bf16[4,12,1,7,2,192]{5,3,4,1,0,2:T(8,128)(2,1)S(1)} %slice.22, bf16[4,12,1,8,5,192]{5,3,4,1,0,2:T(8,128)(2,1)S(1)} %copy.22, pred[8,5]{0,1:T(8,128)(4,1)S(1)} %copy-done.7), kind=kOutput, calls=%fused_computation.10 | convolution fusion | flops 1595774976 | bytes 3600424 | tf_op jit(solution)/shard_map/conv_general_dilated | solution.py:35
  39.9 0.0 copy-start.2
  39.9 0.0 copy-start.3
  40.0 0.6 %copy.23 = f32[2,10,8,5,192]{4,0,3,2,1:T(2,128)S(1)} copy(f32[2,10,8,5,192]{4,2,3,1,0:T(8,128)S(1)} %fusion.9) | data formatting | bytes 1228800 | tf_op jit(solution)/shard_map/conv_general_dilated | solution.py:35
  40.6 0.0 copy-done.2
  40.6 0.5 fusion.18
  41.1 0.0 copy-done.3
  41.1 1.4 %select_convert_fusion = bf16[2,10,34,192]{3,0,2,1:T(2,128)(2,1)S(1)} fusion(pred[10,34]{1,0:T(8,128)(4,1)S(1)} %broadcast_and_fusion, f32[192]{0:T(256)S(1)} %copy-done.3, f32[2,10,34]{0,2,1:T(8,128)S(1)} %add_rsqrt_fusion, f32[192]{0:T(256)S(1)} %copy-done.2, f32[2,10,1,40,192]{4,0,3,1,2:T(2,128)S(1)} %bitcast.33), kind=kLoop, calls=%fused_computation.30 | loop fusion | flops 1436160 | bytes 787956 | tf_op jit(solution)/shard_map/convert_element_type | solution.py:63
  42.6 1.9 %collective-permute-start.5 = (bf16[2,10,34,192]{3,0,2,1:T(2,128)(2,1)S(1)}, bf16[2,10,34,192]{3,0,2,1:T(2,128)(2,1)S(1)}, u32[]{:S(2)}, u32[]{:S(2)}) collective-permute-start(bf16[2,10,34,192]{3,0,2,1:T(2,128)(2,1)S(1)} %select_convert_fusion), channel_id=1, source_target_pairs={{0,32},{32,64},{64,96},{96,128},{128,160},{160,192},{192,224},{224... | collective-permute-start | bytes 783368 | tf_op jit(solution)/shard_map/ppermute | solution.py:27
  44.5 11.5 %collective-permute-done.5 = bf16[2,10,34,192]{3,0,2,1:T(2,128)(2,1)S(1)} collective-permute-done((bf16[2,10,34,192]{3,0,2,1:T(2,128)(2,1)S(1)}, bf16[2,10,34,192]{3,0,2,1:T(2,128)(2,1)S(1)}, u32[]{:S(2)}, u32[]{:S(2)}) %collective-permute-start.5) | collective-permute-done | bytes 261152 | tf_op jit(solution)/shard_map/ppermute | solution.py:27
  56.0 0.8 %maximum_bitcast_fusion.1 = bf16[4,10,1,34,192]{4,0,3,1,2:T(4,128)(2,1)S(1)} fusion(bf16[2,10,34,192]{3,0,2,1:T(2,128)(2,1)S(1)} %select_convert_fusion, bf16[2,10,34,192]{3,0,2,1:T(2,128)(2,1)S(1)} %collective-permute-done.5), kind=kLoop, calls=%fused_computation.29 | loop fusion | flops 1044480 | bytes 1044480 | tf_op jit(solution)/shard_map/broadcast_in_dim | solution.py:36
  56.8 0.0 copy-start.5
  56.8 0.4 pad.2
  57.2 0.0 copy-start.6
  57.2 0.1 copy.25
  57.3 0.1 slice.24
  57.4 1.2 %copy-done.5 = bf16[3,3,3,192,192]{4,3,2,1,0:T(8,128)(2,1)S(1)} copy-done((bf16[3,3,3,192,192]{4,3,2,1,0:T(8,128)(2,1)S(1)}, bf16[3,3,3,192,192]{4,3,2,1,0:T(8,128)(2,1)}, u32[]{:S(2)}) %copy-start.5) | copy-done | bytes 1990680
  58.5 0.0 copy-done.6
  58.5 0.0 copy-start.4
  58.5 2.0 %convolution_select_fusion = f32[2,8,8,5,192]{4,2,3,1,0:T(8,128)S(1)} fusion(bf16[3,3,3,192,192]{4,3,2,1,0:T(8,128)(2,1)S(1)} %copy-done.5, bf16[4,10,1,7,2,192]{5,3,4,1,0,2:T(8,128)(2,1)S(1)} %slice.24, bf16[4,10,1,8,5,192]{5,3,4,1,0,2:T(8,128)(2,1)S(1)} %copy.25, pred[8,5]{0,1:T(8,128)(4,1)S(1)} %copy-done.6), kind=kOutput, calls=%fused_computation.11 | convolution fusion | flops 1276723200 | bytes 3311656 | tf_op jit(solution)/shard_map/conv_general_dilated | solution.py:35
  60.6 0.0 copy-start.1
  60.6 0.2 copy.26
  60.8 0.0 copy-done.4
  60.8 0.7 %copy-done.1 = bf16[2,8,32,192]{3,2,1,0:T(8,128)(2,1)S(1)} copy-done((bf16[2,8,32,192]{3,2,1,0:T(8,128)(2,1)S(1)}, bf16[2,8,32,192]{3,2,1,0:T(8,128)(2,1)}, u32[]{:S(2)}) %copy-start.1) | copy-done | bytes 196632
  61.5 0.2 fusion.33
  61.7 0.8 %copy.27 = bf16[2,8,32,192]{3,2,1,0:T(8,128)(2,1)} copy(bf16[2,8,32,192]{3,1,2,0:T(8,128)(2,1)S(1)} %fusion.33) | data formatting | bytes 393216 | tf_op jit(solution)/shard_map/convert_element_type | solution.py:67
  (5 shorter events, 0.1 us)
Async XLA Ops:
  0.0 37.2 %copy-start = (bf16[3,3,3,192,192]{4,3,2,1,0:T(8,128)(2,1)S(1)}, bf16[3,3,3,192,192]{4,3,2,1,0:T(8,128)(2,1)}, u32[]{:S(2)}) copy-start(bf16[3,3,3,192,192]{4,3,2,1,0:T(8,128)(2,1)} %param.9) | copy-start | bytes 5971972
  2.7 6.2 %collective-permute-start = (bf16[2,2,32,192]{3,1,2,0:T(2,128)(2,1)S(1)}, bf16[2,2,32,192]{3,1,2,0:T(2,128)(2,1)S(1)}, u32[]{:S(2)}, u32[]{:S(2)}) collective-permute-start(bf16[2,2,32,192]{3,1,2,0:T(2,128)(2,1)S(1)} %get-tuple-element.7), channel_id=1, source_target_pairs={{0,8},{8,16},{16,24},{1,9},{9,17},{17,25},{2,10},{10,18},{18,26},{... | collective-permute-start | bytes 147464 | tf_op jit(solution)/shard_map/ppermute | solution.py:15
  6.1 6.2 %collective-permute-start.1 = (bf16[2,2,32,192]{3,1,2,0:T(2,128)(2,1)S(1)}, bf16[2,2,32,192]{3,1,2,0:T(2,128)(2,1)S(1)}, u32[]{:S(2)}, u32[]{:S(2)}) collective-permute-start(bf16[2,2,32,192]{3,1,2,0:T(2,128)(2,1)S(1)} %get-tuple-element.8), channel_id=1, source_target_pairs={{8,0},{16,8},{24,16},{9,1},{17,9},{25,17},{10,2},{18,10},{26,18},{... | collective-permute-start | bytes 147464 | tf_op jit(solution)/shard_map/ppermute | solution.py:17
  12.3 5.6 %collective-permute-start.2 = (bf16[2,12,2,192]{3,1,2,0:T(8,128)(2,1)S(1)}, bf16[2,12,2,192]{3,1,2,0:T(8,128)(2,1)S(1)}, u32[]{:S(2)}, u32[]{:S(2)}) collective-permute-start(bf16[2,12,2,192]{3,1,2,0:T(8,128)(2,1)S(1)} %get-tuple-element.5), channel_id=1, source_target_pairs={{0,1},{1,2},{2,3},{3,4},{4,5},{5,6},{6,7},{8,9},{9,10},{10,11},{11... | collective-permute-start | bytes 55304 | tf_op jit(solution)/shard_map/ppermute | solution.py:15
  14.2 5.2 %collective-permute-start.3 = (bf16[2,12,2,192]{3,1,2,0:T(8,128)(2,1)S(1)}, bf16[2,12,2,192]{3,1,2,0:T(8,128)(2,1)S(1)}, u32[]{:S(2)}, u32[]{:S(2)}) collective-permute-start(bf16[2,12,2,192]{3,1,2,0:T(8,128)(2,1)S(1)} %get-tuple-element.6), channel_id=1, source_target_pairs={{1,0},{2,1},{3,2},{4,3},{5,4},{6,5},{7,6},{9,8},{10,9},{11,10},{12... | collective-permute-start | bytes 55304 | tf_op jit(solution)/shard_map/ppermute | solution.py:17
  20.3 15.7 %collective-permute-start.4 = (bf16[2,12,36,192]{3,0,2,1:T(2,128)(2,1)S(1)}, bf16[2,12,36,192]{3,0,2,1:T(2,128)(2,1)S(1)}, u32[]{:S(2)}, u32[]{:S(2)}) collective-permute-start(bf16[2,12,36,192]{3,0,2,1:T(2,128)(2,1)S(1)} %copy.18), channel_id=1, source_target_pairs={{0,32},{32,64},{64,96},{96,128},{128,160},{160,192},{192,224},{224... | collective-permute-start | bytes 995336 | tf_op jit(solution)/shard_map/ppermute | solution.py:27
  36.8 0.7 %copy-start.7 = (pred[8,5]{0,1:T(8,128)(4,1)S(1)}, pred[8,5]{0,1:T(8,128)(4,1)}, u32[]{:S(2)}) copy-start(pred[8,5]{0,1:T(8,128)(4,1)} %constant.47) | copy-start | bytes 124
  39.9 0.7 %copy-start.2 = (f32[192]{0:T(256)S(1)}, f32[192]{0:T(256)}, u32[]{:S(2)}) copy-start(f32[192]{0:T(256)} %param.10) | copy-start | bytes 2308
  39.9 1.2 %copy-start.3 = (f32[192]{0:T(256)S(1)}, f32[192]{0:T(256)}, u32[]{:S(2)}) copy-start(f32[192]{0:T(256)} %param.11) | copy-start | bytes 2308
  42.6 13.4 %collective-permute-start.5 = (bf16[2,10,34,192]{3,0,2,1:T(2,128)(2,1)S(1)}, bf16[2,10,34,192]{3,0,2,1:T(2,128)(2,1)S(1)}, u32[]{:S(2)}, u32[]{:S(2)}) collective-permute-start(bf16[2,10,34,192]{3,0,2,1:T(2,128)(2,1)S(1)} %select_convert_fusion), channel_id=1, source_target_pairs={{0,32},{32,64},{64,96},{96,128},{128,160},{160,192},{192,224},{224... | collective-permute-start | bytes 783368 | tf_op jit(solution)/shard_map/ppermute | solution.py:27
  56.8 1.8 %copy-start.5 = (bf16[3,3,3,192,192]{4,3,2,1,0:T(8,128)(2,1)S(1)}, bf16[3,3,3,192,192]{4,3,2,1,0:T(8,128)(2,1)}, u32[]{:S(2)}) copy-start(bf16[3,3,3,192,192]{4,3,2,1,0:T(8,128)(2,1)} %param.12) | copy-start | bytes 5971972
  57.2 1.4 %copy-start.6 = (pred[8,5]{0,1:T(8,128)(4,1)S(1)}, pred[8,5]{0,1:T(8,128)(4,1)}, u32[]{:S(2)}) copy-start(pred[8,5]{0,1:T(8,128)(4,1)} %constant.46) | copy-start | bytes 124
  58.5 2.2 %copy-start.4 = (f32[192]{0:T(256)S(1)}, f32[192]{0:T(256)}, u32[]{:S(2)}) copy-start(f32[192]{0:T(256)} %param.13) | copy-start | bytes 2308
  60.6 1.0 %copy-start.1 = (bf16[2,8,32,192]{3,2,1,0:T(8,128)(2,1)S(1)}, bf16[2,8,32,192]{3,2,1,0:T(8,128)(2,1)}, u32[]{:S(2)}) copy-start(bf16[2,8,32,192]{3,2,1,0:T(8,128)(2,1)} %param.7) | copy-start | bytes 589828

commit v2 on v1

--- a/solution.py
+++ b/solution.py
@@ -54,15 +54,18 @@
     frames, rows, cols, chans = latents.shape
     values = latents.astype(jnp.float32)
     first_act = jax.nn.silu(rms_norm(values, first_gain)).astype(jnp.bfloat16)
-    first_ext = with_halo(first_act, (("row", 1), ("col", 2)), 2)
-    first_cache = shifted(first_ext, "tm", 1)
-    first_conv = conv_valid(jnp.concatenate([first_cache, first_ext], axis=0), first_weight)
+    stack = jnp.concatenate(
+        [shifted(first_act, "tm", 2), shifted(first_act, "tm", 1), first_act], axis=0
+    )
+    first_ext = with_halo(stack, (("row", 1), ("col", 2)), 2)
+    first_conv = conv_valid(first_ext, first_weight)
     hidden = (first_conv + first_bias).astype(jnp.bfloat16)
     second_act = jax.nn.silu(rms_norm(hidden.astype(jnp.float32), second_gain))
+    early = lax.axis_index("tm") * frames - 2 + jnp.arange(2 * frames) >= 0
     keep = inside("row", rows, 1)[:, None] & inside("col", cols, 1)[None, :]
-    second_act = jnp.where(keep[None, :, :, None], second_act, 0.0).astype(jnp.bfloat16)
-    second_cache = shifted(second_act, "tm", 1)
-    second_conv = conv_valid(jnp.concatenate([second_cache, second_act], axis=0), second_weight)
+    keep = early[:, None, None] & keep[None]
+    second_act = jnp.where(keep[..., None], second_act, 0.0).astype(jnp.bfloat16)
+    second_conv = conv_valid(second_act, second_weight)
     decoded = values + second_conv + second_bias
     return decoded.astype(jnp.bfloat16)
 

time: 62.8 us -> 68.3 us (1.088)
  the two profiles are of different devices: /device:TPU:274 before, /device:TPU:129 now
where the time goes in v2:
time: 68.3 us; the launch traced here: 67.9 us
  waiting for transfers between devices  25.4 us (37%)
  starting transfers between devices  20.2 us (30%)
  other arithmetic  9.06 us (13%)
  matrix products  7.16 us (10%)
  local copies, waits for them, and re-layouts  5.88 us (9%)
    ppermute x2, waiting for transfers between devices, shifted(): lax.ppermute(value, axis, [(source, source + steps) for source in range(i...  15 us
    ppermute x2, starting transfers between devices, with_halo(): lax.ppermute(tail, axis, [(i, i + 1) for i in range(ends)])  8.5 us
    ppermute x2, starting transfers between devices, shifted(): lax.ppermute(value, axis, [(source, source + steps) for source in range(i...  8.45 us
    ppermute x2, waiting for transfers between devices, with_halo(): lax.ppermute(head, axis, [(i + 1, i) for i in range(ends)])  8.37 us
    conv_general_dilated x2, matrix products, conv_valid(): lax.conv_general_dilated(stack[None], kernel, window_strides=(1, 1, 1), p...  7.16 us
    ppermute x2, starting transfers between devices, with_halo(): lax.ppermute(head, axis, [(i + 1, i) for i in range(ends)])  3.2 us
    broadcast_in_dim x1, other arithmetic, conv_valid(): stack[None]  2.14 us
    conv_general_dilated x6, local copies, waits for them, and re-layouts, conv_valid(): lax.conv_general_dilated(stack[None], kernel, window_strides=(1, 1, 1), p...  2.14 us
  transfers between devices with their start and end apart: 6, of which 5 were waited for; matrix products, arithmetic and copies ran while one was open for 0% of the time, Pallas kernels for 0%

profile of v2, /device:TPU:129, one launch (start us, length us, event | category | flops | bytes accessed | tf_op | source)
XLA Modules:
  0.0 67.9 jit_solution(9347921872124405180)
XLA Ops:
  0.0 0.0 copy-start
  0.0 1.3 %fusion.26 = f32[2,8,32]{1,2,0:T(8,128)S(1)} fusion(bf16[2,8,32,192]{3,2,1,0:T(8,128)(2,1)} %param.7), kind=kLoop, calls=%fused_computation.35 | loop fusion | flops 294400 | bytes 198656 | tf_op jit(solution)/shard_map/reduce_sum | solution.py:31
  1.4 1.2 %fusion.33 = bf16[2,8,32,192]{3,1,2,0:T(8,128)(2,1)S(1)} fusion(f32[192]{0:T(256)} %param.8, f32[2,8,32]{1,2,0:T(8,128)S(1)} %add_rsqrt_fusion.1, bf16[2,8,32,192]{3,2,1,0:T(8,128)(2,1)} %param.7), kind=kLoop, calls=%fused_computation.42 | loop fusion | flops 786432 | bytes 396032 | tf_op jit(solution)/shard_map/convert_element_type | solution.py:56
  2.6 4.9 %collective-permute-start = (bf16[2,8,32,192]{3,1,2,0:T(8,128)(2,1)S(1)}, bf16[2,8,32,192]{3,1,2,0:T(8,128)(2,1)S(1)}, u32[]{:S(2)}, u32[]{:S(2)}) collective-permute-start(bf16[2,8,32,192]{3,1,2,0:T(8,128)(2,1)S(1)} %fusion.33), channel_id=1, source_target_pairs={{0,64},{32,96},{64,128},{96,160},{128,192},{160,224},{192,256},{22... | collective-permute-start | bytes 589832 | tf_op jit(solution)/shard_map/ppermute | solution.py:27
  7.5 3.5 %collective-permute-start.1 = (bf16[2,8,32,192]{3,1,2,0:T(8,128)(2,1)S(1)}, bf16[2,8,32,192]{3,1,2,0:T(8,128)(2,1)S(1)}, u32[]{:S(2)}, u32[]{:S(2)}) collective-permute-start(bf16[2,8,32,192]{3,1,2,0:T(8,128)(2,1)S(1)} %fusion.33), channel_id=1, source_target_pairs={{0,32},{32,64},{64,96},{96,128},{128,160},{160,192},{192,224},{224... | collective-permute-start | bytes 589832 | tf_op jit(solution)/shard_map/ppermute | solution.py:27
  11.1 8.2 %collective-permute-done = bf16[2,8,32,192]{3,1,2,0:T(8,128)(2,1)S(1)} collective-permute-done((bf16[2,8,32,192]{3,1,2,0:T(8,128)(2,1)S(1)}, bf16[2,8,32,192]{3,1,2,0:T(8,128)(2,1)S(1)}, u32[]{:S(2)}, u32[]{:S(2)}) %collective-permute-start) | collective-permute-done | bytes 196640 | tf_op jit(solution)/shard_map/ppermute | solution.py:27
  19.3 6.8 %collective-permute-done.1 = bf16[2,8,32,192]{3,1,2,0:T(8,128)(2,1)S(1)} collective-permute-done((bf16[2,8,32,192]{3,1,2,0:T(8,128)(2,1)S(1)}, bf16[2,8,32,192]{3,1,2,0:T(8,128)(2,1)S(1)}, u32[]{:S(2)}, u32[]{:S(2)}) %collective-permute-start.1) | collective-permute-done | bytes 196640 | tf_op jit(solution)/shard_map/ppermute | solution.py:27
  26.1 1.1 %pad_maximum_fusion.2 = (bf16[6,2,32,192]{3,1,2,0:T(2,128)(2,1)}, bf16[6,2,32,192]{3,1,2,0:T(2,128)(2,1)}) fusion(bf16[2,8,32,192]{3,1,2,0:T(8,128)(2,1)S(1)} %fusion.33, bf16[2,8,32,192]{3,1,2,0:T(8,128)(2,1)S(1)} %collective-permute-done.1, bf16[2,8,32,192]{3,1,2,0:T(8,128)(2,1)S(1)} %collective-permute-done), kind=kLoop, calls=%fused_computation.49 | loop fusion | flops 884736 | bytes 884736 | tf_op jit(solution)/shard_map/slice | solution.py:12
  27.1 3.8 %collective-permute-start.2 = (bf16[6,2,32,192]{3,1,2,0:T(2,128)(2,1)}, bf16[6,2,32,192]{3,1,2,0:T(2,128)(2,1)}, u32[]{:S(2)}, u32[]{:S(2)}) collective-permute-start(bf16[6,2,32,192]{3,1,2,0:T(2,128)(2,1)} %get-tuple-element.7), channel_id=1, source_target_pairs={{0,8},{8,16},{16,24},{1,9},{9,17},{17,25},{2,10},{10,18},{18,26},{... | collective-permute-start | bytes 442376 | tf_op jit(solution)/shard_map/ppermute | solution.py:15
  30.9 1.3 %collective-permute-start.3 = (bf16[6,2,32,192]{3,1,2,0:T(2,128)(2,1)}, bf16[6,2,32,192]{3,1,2,0:T(2,128)(2,1)}, u32[]{:S(2)}, u32[]{:S(2)}) collective-permute-start(bf16[6,2,32,192]{3,1,2,0:T(2,128)(2,1)} %get-tuple-element.8), channel_id=1, source_target_pairs={{8,0},{16,8},{24,16},{9,1},{17,9},{25,17},{10,2},{18,10},{26,18},{... | collective-permute-start | bytes 442376 | tf_op jit(solution)/shard_map/ppermute | solution.py:17
  32.2 0.1 broadcast_and_fusion.1
  32.3 2.0 %collective-permute-done.2 = bf16[6,2,32,192]{3,1,2,0:T(2,128)(2,1)} collective-permute-done((bf16[6,2,32,192]{3,1,2,0:T(2,128)(2,1)}, bf16[6,2,32,192]{3,1,2,0:T(2,128)(2,1)}, u32[]{:S(2)}, u32[]{:S(2)}) %collective-permute-start.2) | collective-permute-done | bytes 147488 | tf_op jit(solution)/shard_map/ppermute | solution.py:15
  34.3 4.5 %collective-permute-done.3 = bf16[6,2,32,192]{3,1,2,0:T(2,128)(2,1)} collective-permute-done((bf16[6,2,32,192]{3,1,2,0:T(2,128)(2,1)}, bf16[6,2,32,192]{3,1,2,0:T(2,128)(2,1)}, u32[]{:S(2)}, u32[]{:S(2)}) %collective-permute-start.3) | collective-permute-done | bytes 147488 | tf_op jit(solution)/shard_map/ppermute | solution.py:17
  38.8 0.9 %pad_maximum_fusion.7 = (bf16[6,12,2,192]{3,1,2,0:T(8,128)(2,1)S(1)}, bf16[6,12,2,192]{3,1,2,0:T(8,128)(2,1)S(1)}) fusion(bf16[6,2,32,192]{3,1,2,0:T(2,128)(2,1)} %collective-permute-done.3, bf16[6,2,32,192]{3,1,2,0:T(2,128)(2,1)} %collective-permute-done.2, bf16[2,8,32,192]{3,1,2,0:T(8,128)(2,1)S(1)} %fusion.33, ...), kind=kLoop, calls=%fused_computation.55 | loop fusion | flops 552960 | bytes 995328 | tf_op jit(solution)/shard_map/slice | solution.py:12
  39.7 4.7 %collective-permute-start.4 = (bf16[6,12,2,192]{3,1,2,0:T(8,128)(2,1)S(1)}, bf16[6,12,2,192]{3,1,2,0:T(8,128)(2,1)S(1)}, u32[]{:S(2)}, u32[]{:S(2)}) collective-permute-start(bf16[6,12,2,192]{3,1,2,0:T(8,128)(2,1)S(1)} %get-tuple-element.5), channel_id=1, source_target_pairs={{0,1},{1,2},{2,3},{3,4},{4,5},{5,6},{6,7},{8,9},{9,10},{10,11},{11... | collective-permute-start | bytes 165896 | tf_op jit(solution)/shard_map/ppermute | solution.py:15
  44.4 1.9 %collective-permute-start.5 = (bf16[6,12,2,192]{3,1,2,0:T(8,128)(2,1)S(1)}, bf16[6,12,2,192]{3,1,2,0:T(8,128)(2,1)S(1)}, u32[]{:S(2)}, u32[]{:S(2)}) collective-permute-start(bf16[6,12,2,192]{3,1,2,0:T(8,128)(2,1)S(1)} %get-tuple-element.6), channel_id=1, source_target_pairs={{1,0},{2,1},{3,2},{4,3},{5,4},{6,5},{7,6},{9,8},{10,9},{11,10},{12... | collective-permute-start | bytes 165896 | tf_op jit(solution)/shard_map/ppermute | solution.py:17
  46.3 0.1 broadcast_and_fusion
  46.5 0.0 collective-permute-done.4
  46.5 3.9 %collective-permute-done.5 = bf16[6,12,2,192]{3,1,2,0:T(8,128)(2,1)S(1)} collective-permute-done((bf16[6,12,2,192]{3,1,2,0:T(8,128)(2,1)S(1)}, bf16[6,12,2,192]{3,1,2,0:T(8,128)(2,1)S(1)}, u32[]{:S(2)}, u32[]{:S(2)}) %collective-permute-start.5) | collective-permute-done | bytes 55328 | tf_op jit(solution)/shard_map/ppermute | solution.py:17
  50.4 2.1 %maximum_bitcast_fusion = bf16[6,12,1,36,192]{4,1,3,0,2:T(8,128)(2,1)S(1)} fusion(bf16[6,12,2,192]{3,1,2,0:T(8,128)(2,1)S(1)} %collective-permute-done.5, bf16[6,2,32,192]{3,1,2,0:T(2,128)(2,1)} %collective-permute-done.3, bf16[2,8,32,192]{3,1,2,0:T(8,128)(2,1)S(1)} %fusion.33, bf16[2,8,32,192]{3,1,2,0:T(8,128)(2,1)S(1)} %collective-permute-done.1, ...), kind=kLoop, calls=%fused_computation.10 | loop fusion | flops 6967296 | bytes 1990656 | tf_op jit(solution)/shard_map/broadcast_in_dim | solution.py:36
  52.5 0.4 pad
  52.9 0.0 copy-start.4
  52.9 0.0 copy-start.7
  52.9 0.5 copy.10
  53.5 0.1 slice.21
  53.6 0.0 copy-done
  53.6 0.0 copy-done.4
  53.6 0.0 copy-done.7
  53.6 5.2 %fusion.23 = (f32[4,10,8,5,192]{4,2,3,1,0:T(8,128)S(1)}, f32[4,10,8,5,192]{4,2,3,1,0:T(8,128)S(1)}) fusion(f32[192]{0:T(256)S(1)} %copy-done.4, bf16[3,3,3,192,192]{4,3,2,1,0:T(8,128)(2,1)S(1)} %copy-done, bf16[6,12,1,7,2,192]{5,3,4,1,0,2:T(8,128)(2,1)S(1)} %slice.21, bf16[6,12,1,8,5,192]{5,3,4,1,0,2:T(8,128)(2,1)S(1)} %copy.10, pred[8,5]{0,1:T(8,128)(4,1)S(1)} %copy-done.7), kind=kOutput, calls=%fused_computation.29 | convolution fusion | flops 3190923264 | bytes 5942056 | tf_op jit(solution)/shard_map/conv_general_dilated | solution.py:35
  58.8 1.1 %copy.12 = f32[4,10,8,5,192]{4,0,3,2,1:T(4,128)S(1)} copy(f32[4,10,8,5,192]{4,2,3,1,0:T(8,128)S(1)} %get-tuple-element.10) | data formatting | bytes 2457600 | tf_op jit(solution)/shard_map/conv_general_dilated | solution.py:35
  59.9 0.5 multiply_reduce_fusion
  60.3 0.0 copy-start.2
  60.4 1.1 %copy.11 = f32[4,10,8,5,192]{4,0,3,2,1:T(4,128)S(1)} copy(f32[4,10,8,5,192]{4,2,3,1,0:T(8,128)S(1)} %get-tuple-element.9) | data formatting | bytes 2457600 | tf_op jit(solution)/shard_map/convert_element_type | solution.py:63
  61.5 0.0 copy-done.2
  61.5 1.4 %fusion.24 = bf16[4,10,1,34,192]{4,0,3,1,2:T(4,128)(2,1)S(1)} fusion(f32[192]{0:T(256)S(1)} %copy-done.2, f32[4,10,34]{0,2,1:T(8,128)S(1)} %add_rsqrt_fusion, f32[4,10,1,40,192]{4,0,3,1,2:T(4,128)S(1)} %bitcast.44, pred[4,10,34]{0,2,1:T(8,128)(4,1)S(1)} %broadcast_and_fusion), kind=kLoop, calls=%fused_computation.33 | loop fusion | flops 2088960 | bytes 1574288 | tf_op jit(solution)/shard_map/convert_element_type | solution.py:67
  62.9 0.0 copy-start.5
  62.9 0.0 copy-start.6
  63.0 0.4 pad.2
  63.3 0.1 copy.14
  63.4 0.1 slice.24
  63.5 1.2 %copy-done.5 = bf16[3,3,3,192,192]{4,3,2,1,0:T(8,128)(2,1)S(1)} copy-done((bf16[3,3,3,192,192]{4,3,2,1,0:T(8,128)(2,1)S(1)}, bf16[3,3,3,192,192]{4,3,2,1,0:T(8,128)(2,1)}, u32[]{:S(2)}) %copy-start.5) | copy-done | bytes 1990680
  64.7 0.0 copy-done.6
  64.7 0.0 copy-start.1
  64.7 0.0 copy-start.3
  64.7 2.0 %convolution_select_fusion = f32[2,8,8,5,192]{4,2,3,1,0:T(8,128)S(1)} fusion(bf16[3,3,3,192,192]{4,3,2,1,0:T(8,128)(2,1)S(1)} %copy-done.5, bf16[4,10,1,7,2,192]{5,3,4,1,0,2:T(8,128)(2,1)S(1)} %slice.24, bf16[4,10,1,8,5,192]{5,3,4,1,0,2:T(8,128)(2,1)S(1)} %copy.14, pred[8,5]{0,1:T(8,128)(4,1)S(1)} %copy-done.6), kind=kOutput, calls=%fused_computation.22 | convolution fusion | flops 1276723200 | bytes 3311656 | tf_op jit(solution)/shard_map/conv_general_dilated | solution.py:35
  66.7 0.2 copy.15
  66.9 0.0 copy-done.1
  66.9 0.0 copy-done.3
  66.9 0.2 fusion.35
  67.1 0.8 %copy.16 = bf16[2,8,32,192]{3,2,1,0:T(8,128)(2,1)} copy(bf16[2,8,32,192]{3,1,2,0:T(8,128)(2,1)S(1)} %fusion.35) | data formatting | bytes 393216 | tf_op jit(solution)/shard_map/convert_element_type | solution.py:70
  (5 shorter events, 0.1 us)
Async XLA Ops:
  0.0 53.6 %copy-start = (bf16[3,3,3,192,192]{4,3,2,1,0:T(8,128)(2,1)S(1)}, bf16[3,3,3,192,192]{4,3,2,1,0:T(8,128)(2,1)}, u32[]{:S(2)}) copy-start(bf16[3,3,3,192,192]{4,3,2,1,0:T(8,128)(2,1)} %param.9) | copy-start | bytes 5971972
  2.6 16.7 %collective-permute-start = (bf16[2,8,32,192]{3,1,2,0:T(8,128)(2,1)S(1)}, bf16[2,8,32,192]{3,1,2,0:T(8,128)(2,1)S(1)}, u32[]{:S(2)}, u32[]{:S(2)}) collective-permute-start(bf16[2,8,32,192]{3,1,2,0:T(8,128)(2,1)S(1)} %fusion.33), channel_id=1, source_target_pairs={{0,64},{32,96},{64,128},{96,160},{128,192},{160,224},{192,256},{22... | collective-permute-start | bytes 589832 | tf_op jit(solution)/shard_map/ppermute | solution.py:27
  7.5 18.6 %collective-permute-start.1 = (bf16[2,8,32,192]{3,1,2,0:T(8,128)(2,1)S(1)}, bf16[2,8,32,192]{3,1,2,0:T(8,128)(2,1)S(1)}, u32[]{:S(2)}, u32[]{:S(2)}) collective-permute-start(bf16[2,8,32,192]{3,1,2,0:T(8,128)(2,1)S(1)} %fusion.33), channel_id=1, source_target_pairs={{0,32},{32,64},{64,96},{96,128},{128,160},{160,192},{192,224},{224... | collective-permute-start | bytes 589832 | tf_op jit(solution)/shard_map/ppermute | solution.py:27
  27.1 7.2 %collective-permute-start.2 = (bf16[6,2,32,192]{3,1,2,0:T(2,128)(2,1)}, bf16[6,2,32,192]{3,1,2,0:T(2,128)(2,1)}, u32[]{:S(2)}, u32[]{:S(2)}) collective-permute-start(bf16[6,2,32,192]{3,1,2,0:T(2,128)(2,1)} %get-tuple-element.7), channel_id=1, source_target_pairs={{0,8},{8,16},{16,24},{1,9},{9,17},{17,25},{2,10},{10,18},{18,26},{... | collective-permute-start | bytes 442376 | tf_op jit(solution)/shard_map/ppermute | solution.py:15
  30.9 7.9 %collective-permute-start.3 = (bf16[6,2,32,192]{3,1,2,0:T(2,128)(2,1)}, bf16[6,2,32,192]{3,1,2,0:T(2,128)(2,1)}, u32[]{:S(2)}, u32[]{:S(2)}) collective-permute-start(bf16[6,2,32,192]{3,1,2,0:T(2,128)(2,1)} %get-tuple-element.8), channel_id=1, source_target_pairs={{8,0},{16,8},{24,16},{9,1},{17,9},{25,17},{10,2},{18,10},{26,18},{... | collective-permute-start | bytes 442376 | tf_op jit(solution)/shard_map/ppermute | solution.py:17
  39.7 6.8 %collective-permute-start.4 = (bf16[6,12,2,192]{3,1,2,0:T(8,128)(2,1)S(1)}, bf16[6,12,2,192]{3,1,2,0:T(8,128)(2,1)S(1)}, u32[]{:S(2)}, u32[]{:S(2)}) collective-permute-start(bf16[6,12,2,192]{3,1,2,0:T(8,128)(2,1)S(1)} %get-tuple-element.5), channel_id=1, source_target_pairs={{0,1},{1,2},{2,3},{3,4},{4,5},{5,6},{6,7},{8,9},{9,10},{10,11},{11... | collective-permute-start | bytes 165896 | tf_op jit(solution)/shard_map/ppermute | solution.py:15
  44.4 5.9 %collective-permute-start.5 = (bf16[6,12,2,192]{3,1,2,0:T(8,128)(2,1)S(1)}, bf16[6,12,2,192]{3,1,2,0:T(8,128)(2,1)S(1)}, u32[]{:S(2)}, u32[]{:S(2)}) collective-permute-start(bf16[6,12,2,192]{3,1,2,0:T(8,128)(2,1)S(1)} %get-tuple-element.6), channel_id=1, source_target_pairs={{1,0},{2,1},{3,2},{4,3},{5,4},{6,5},{7,6},{9,8},{10,9},{11,10},{12... | collective-permute-start | bytes 165896 | tf_op jit(solution)/shard_map/ppermute | solution.py:17
  52.9 0.7 %copy-start.4 = (f32[192]{0:T(256)S(1)}, f32[192]{0:T(256)}, u32[]{:S(2)}) copy-start(f32[192]{0:T(256)} %param.10) | copy-start | bytes 2308
  52.9 0.7 %copy-start.7 = (pred[8,5]{0,1:T(8,128)(4,1)S(1)}, pred[8,5]{0,1:T(8,128)(4,1)}, u32[]{:S(2)}) copy-start(pred[8,5]{0,1:T(8,128)(4,1)} %constant.58) | copy-start | bytes 124
  60.3 1.1 %copy-start.2 = (f32[192]{0:T(256)S(1)}, f32[192]{0:T(256)}, u32[]{:S(2)}) copy-start(f32[192]{0:T(256)} %param.11) | copy-start | bytes 2308
  62.9 1.8 %copy-start.5 = (bf16[3,3,3,192,192]{4,3,2,1,0:T(8,128)(2,1)S(1)}, bf16[3,3,3,192,192]{4,3,2,1,0:T(8,128)(2,1)}, u32[]{:S(2)}) copy-start(bf16[3,3,3,192,192]{4,3,2,1,0:T(8,128)(2,1)} %param.12) | copy-start | bytes 5971972
  62.9 1.7 %copy-start.6 = (pred[8,5]{0,1:T(8,128)(4,1)S(1)}, pred[8,5]{0,1:T(8,128)(4,1)}, u32[]{:S(2)}) copy-start(pred[8,5]{0,1:T(8,128)(4,1)} %constant.57) | copy-start | bytes 124
  64.7 2.2 %copy-start.1 = (bf16[2,8,32,192]{3,2,1,0:T(8,128)(2,1)S(1)}, bf16[2,8,32,192]{3,2,1,0:T(8,128)(2,1)}, u32[]{:S(2)}) copy-start(bf16[2,8,32,192]{3,2,1,0:T(8,128)(2,1)} %param.7) | copy-start | bytes 589828
  64.7 2.2 %copy-start.3 = (f32[192]{0:T(256)S(1)}, f32[192]{0:T(256)}, u32[]{:S(2)}) copy-start(f32[192]{0:T(256)} %param.13) | copy-start | bytes 2308

commit v3 on v1

--- a/solution.py
+++ b/solution.py
@@ -54,9 +54,9 @@
     frames, rows, cols, chans = latents.shape
     values = latents.astype(jnp.float32)
     first_act = jax.nn.silu(rms_norm(values, first_gain)).astype(jnp.bfloat16)
-    first_ext = with_halo(first_act, (("row", 1), ("col", 2)), 2)
-    first_cache = shifted(first_ext, "tm", 1)
-    first_conv = conv_valid(jnp.concatenate([first_cache, first_ext], axis=0), first_weight)
+    stack = jnp.concatenate([shifted(first_act, "tm", 1), first_act], axis=0)
+    first_ext = with_halo(stack, (("row", 1), ("col", 2)), 2)
+    first_conv = conv_valid(first_ext, first_weight)
     hidden = (first_conv + first_bias).astype(jnp.bfloat16)
     second_act = jax.nn.silu(rms_norm(hidden.astype(jnp.float32), second_gain))
     keep = inside("row", rows, 1)[:, None] & inside("col", cols, 1)[None, :]

time: 62.8 us -> 57.6 us (0.917)
  the two profiles are of different devices: /device:TPU:274 before, /device:TPU:273 now
where the time goes in v3:
time: 57.6 us; the launch traced here: 57.4 us
  waiting for transfers between devices  26.2 us (45%)
  starting transfers between devices  16.9 us (29%)
  other arithmetic  6.56 us (11%)
  matrix products  4.48 us (8%)
  local copies, waits for them, and re-layouts  2.91 us (5%)
    ppermute x2, waiting for transfers between devices, shifted(): lax.ppermute(value, axis, [(source, source + steps) for source in range(i...  18.2 us
    ppermute x2, starting transfers between devices, with_halo(): lax.ppermute(tail, axis, [(i, i + 1) for i in range(ends)])  8.88 us
    ppermute x2, waiting for transfers between devices, with_halo(): lax.ppermute(head, axis, [(i + 1, i) for i in range(ends)])  7.37 us
    ppermute x2, starting transfers between devices, shifted(): lax.ppermute(value, axis, [(source, source + steps) for source in range(i...  4.83 us
    conv_general_dilated x2, matrix products, conv_valid(): lax.conv_general_dilated(stack[None], kernel, window_strides=(1, 1, 1), p...  4.48 us
    ppermute x2, starting transfers between devices, with_halo(): lax.ppermute(head, axis, [(i + 1, i) for i in range(ends)])  3.21 us
    reduce_sum x2, other arithmetic, rms_norm(): jnp.mean(values * values, axis=-1, keepdims=True) + 1e-06  1.81 us
    broadcast_in_dim x2, other arithmetic, conv_valid(): stack[None]  1.5 us
  transfers between devices with their start and end apart: 6, of which 5 were waited for; matrix products, arithmetic and copies ran while one was open for 0% of the time, Pallas kernels for 0%

profile of v3, /device:TPU:273, one launch (start us, length us, event | category | flops | bytes accessed | tf_op | source)
XLA Modules:
  0.0 57.4 jit_solution(9118155143301291876)
XLA Ops:
  0.0 0.0 copy-start
  0.0 1.3 %fusion.24 = f32[2,8,32]{1,2,0:T(8,128)S(1)} fusion(bf16[2,8,32,192]{3,2,1,0:T(8,128)(2,1)} %param.7), kind=kLoop, calls=%fused_computation.33 | loop fusion | flops 294400 | bytes 198656 | tf_op jit(solution)/shard_map/reduce_sum | solution.py:31
  1.4 1.2 %fusion.31 = bf16[2,8,32,192]{3,1,2,0:T(8,128)(2,1)S(1)} fusion(f32[192]{0:T(256)} %param.8, f32[2,8,32]{1,2,0:T(8,128)S(1)} %add_rsqrt_fusion.1, bf16[2,8,32,192]{3,2,1,0:T(8,128)(2,1)} %param.7), kind=kLoop, calls=%fused_computation.40 | loop fusion | flops 786432 | bytes 396032 | tf_op jit(solution)/shard_map/convert_element_type | solution.py:56
  2.6 2.6 %collective-permute-start = (bf16[2,8,32,192]{3,1,2,0:T(8,128)(2,1)S(1)}, bf16[2,8,32,192]{3,1,2,0:T(8,128)(2,1)S(1)}, u32[]{:S(2)}, u32[]{:S(2)}) collective-permute-start(bf16[2,8,32,192]{3,1,2,0:T(8,128)(2,1)S(1)} %fusion.31), channel_id=1, source_target_pairs={{0,32},{32,64},{64,96},{96,128},{128,160},{160,192},{192,224},{224... | collective-permute-start | bytes 589832 | tf_op jit(solution)/shard_map/ppermute | solution.py:27
  5.3 7.6 %collective-permute-done = bf16[2,8,32,192]{3,1,2,0:T(8,128)(2,1)S(1)} collective-permute-done((bf16[2,8,32,192]{3,1,2,0:T(8,128)(2,1)S(1)}, bf16[2,8,32,192]{3,1,2,0:T(8,128)(2,1)S(1)}, u32[]{:S(2)}, u32[]{:S(2)}) %collective-permute-start) | collective-permute-done | bytes 196640 | tf_op jit(solution)/shard_map/ppermute | solution.py:27
  12.9 0.2 pad_maximum_fusion.1
  13.1 3.1 %collective-permute-start.1 = (bf16[4,2,32,192]{3,1,2,0:T(2,128)(2,1)S(1)}, bf16[4,2,32,192]{3,1,2,0:T(2,128)(2,1)S(1)}, u32[]{:S(2)}, u32[]{:S(2)}) collective-permute-start(bf16[4,2,32,192]{3,1,2,0:T(2,128)(2,1)S(1)} %get-tuple-element.7), channel_id=1, source_target_pairs={{0,8},{8,16},{16,24},{1,9},{9,17},{17,25},{2,10},{10,18},{18,26},{... | collective-permute-start | bytes 294920 | tf_op jit(solution)/shard_map/ppermute | solution.py:15
  16.2 1.3 %collective-permute-start.2 = (bf16[4,2,32,192]{3,1,2,0:T(2,128)(2,1)S(1)}, bf16[4,2,32,192]{3,1,2,0:T(2,128)(2,1)S(1)}, u32[]{:S(2)}, u32[]{:S(2)}) collective-permute-start(bf16[4,2,32,192]{3,1,2,0:T(2,128)(2,1)S(1)} %get-tuple-element.8), channel_id=1, source_target_pairs={{8,0},{16,8},{24,16},{9,1},{17,9},{25,17},{10,2},{18,10},{26,18},{... | collective-permute-start | bytes 294920 | tf_op jit(solution)/shard_map/ppermute | solution.py:17
  17.5 0.6 %collective-permute-done.1 = bf16[4,2,32,192]{3,1,2,0:T(2,128)(2,1)S(1)} collective-permute-done((bf16[4,2,32,192]{3,1,2,0:T(2,128)(2,1)S(1)}, bf16[4,2,32,192]{3,1,2,0:T(2,128)(2,1)S(1)}, u32[]{:S(2)}, u32[]{:S(2)}) %collective-permute-start.1) | collective-permute-done | bytes 98336 | tf_op jit(solution)/shard_map/ppermute | solution.py:15
  18.1 3.8 %collective-permute-done.2 = bf16[4,2,32,192]{3,1,2,0:T(2,128)(2,1)S(1)} collective-permute-done((bf16[4,2,32,192]{3,1,2,0:T(2,128)(2,1)S(1)}, bf16[4,2,32,192]{3,1,2,0:T(2,128)(2,1)S(1)}, u32[]{:S(2)}, u32[]{:S(2)}) %collective-permute-start.2) | collective-permute-done | bytes 98336 | tf_op jit(solution)/shard_map/ppermute | solution.py:17
  21.9 0.1 pad_maximum_fusion.5
  22.0 5.8 %collective-permute-start.3 = (bf16[4,12,2,192]{3,1,2,0:T(8,128)(2,1)S(1)}, bf16[4,12,2,192]{3,1,2,0:T(8,128)(2,1)S(1)}, u32[]{:S(2)}, u32[]{:S(2)}) collective-permute-start(bf16[4,12,2,192]{3,1,2,0:T(8,128)(2,1)S(1)} %get-tuple-element.5), channel_id=1, source_target_pairs={{0,1},{1,2},{2,3},{3,4},{4,5},{5,6},{6,7},{8,9},{9,10},{10,11},{11... | collective-permute-start | bytes 110600 | tf_op jit(solution)/shard_map/ppermute | solution.py:15
  27.8 1.9 %collective-permute-start.4 = (bf16[4,12,2,192]{3,1,2,0:T(8,128)(2,1)S(1)}, bf16[4,12,2,192]{3,1,2,0:T(8,128)(2,1)S(1)}, u32[]{:S(2)}, u32[]{:S(2)}) collective-permute-start(bf16[4,12,2,192]{3,1,2,0:T(8,128)(2,1)S(1)} %get-tuple-element.6), channel_id=1, source_target_pairs={{1,0},{2,1},{3,2},{4,3},{5,4},{6,5},{7,6},{9,8},{10,9},{11,10},{12... | collective-permute-start | bytes 110600 | tf_op jit(solution)/shard_map/ppermute | solution.py:17
  29.7 0.1 broadcast_and_fusion
  29.8 0.0 collective-permute-done.3
  29.8 3.6 %collective-permute-done.4 = bf16[4,12,2,192]{3,1,2,0:T(8,128)(2,1)S(1)} collective-permute-done((bf16[4,12,2,192]{3,1,2,0:T(8,128)(2,1)S(1)}, bf16[4,12,2,192]{3,1,2,0:T(8,128)(2,1)S(1)}, u32[]{:S(2)}, u32[]{:S(2)}) %collective-permute-start.4) | collective-permute-done | bytes 36896 | tf_op jit(solution)/shard_map/ppermute | solution.py:17
  33.4 0.7 %maximum_bitcast_fusion = bf16[4,12,1,36,192]{4,1,3,0,2:T(8,128)(2,1)S(1)} fusion(bf16[4,12,2,192]{3,1,2,0:T(8,128)(2,1)S(1)} %collective-permute-done.4, bf16[4,2,32,192]{3,1,2,0:T(2,128)(2,1)S(1)} %collective-permute-done.2, bf16[2,8,32,192]{3,1,2,0:T(8,128)(2,1)S(1)} %fusion.31, bf16[2,8,32,192]{3,1,2,0:T(8,128)(2,1)S(1)} %collective-permute-done, ...), kind=kLoop, calls=%fused_computation.12 | loop fusion | flops 3981312 | bytes 1327104 | tf_op jit(solution)/shard_map/broadcast_in_dim | solution.py:36
  34.0 0.0 copy-start.7
  34.1 0.3 pad
  34.3 0.4 copy.11
  34.7 0.1 slice.20
  34.8 0.0 copy-done
  34.8 0.0 copy-done.7
  34.8 0.0 copy-start.2
  34.8 2.5 %fusion.9 = f32[2,10,8,5,192]{4,2,3,1,0:T(8,128)S(1)} fusion(bf16[3,3,3,192,192]{4,3,2,1,0:T(8,128)(2,1)S(1)} %copy-done, bf16[4,12,1,7,2,192]{5,3,4,1,0,2:T(8,128)(2,1)S(1)} %slice.20, bf16[4,12,1,8,5,192]{5,3,4,1,0,2:T(8,128)(2,1)S(1)} %copy.11, pred[8,5]{0,1:T(8,128)(4,1)S(1)} %copy-done.7), kind=kOutput, calls=%fused_computation.10 | convolution fusion | flops 1595774976 | bytes 3600424 | tf_op jit(solution)/shard_map/conv_general_dilated | solution.py:35
  37.3 0.0 copy-start.3
  37.3 0.6 %copy.12 = f32[2,10,8,5,192]{4,0,3,2,1:T(2,128)S(1)} copy(f32[2,10,8,5,192]{4,2,3,1,0:T(8,128)S(1)} %fusion.9) | data formatting | bytes 1228800 | tf_op jit(solution)/shard_map/conv_general_dilated | solution.py:35
  37.9 0.0 copy-done.2
  38.0 0.5 fusion.18
  38.5 0.0 copy-done.3
  38.5 1.4 %select_convert_fusion = bf16[2,10,34,192]{3,0,2,1:T(2,128)(2,1)S(1)} fusion(pred[10,34]{1,0:T(8,128)(4,1)S(1)} %broadcast_and_fusion, f32[192]{0:T(256)S(1)} %copy-done.3, f32[2,10,34]{0,2,1:T(8,128)S(1)} %add_rsqrt_fusion, f32[192]{0:T(256)S(1)} %copy-done.2, f32[2,10,1,40,192]{4,0,3,1,2:T(2,128)S(1)} %bitcast.33), kind=kLoop, calls=%fused_computation.30 | loop fusion | flops 1436160 | bytes 787956 | tf_op jit(solution)/shard_map/convert_element_type | solution.py:63
  39.9 0.0 copy-start.5
  39.9 0.0 copy-start.6
  39.9 2.2 %collective-permute-start.5 = (bf16[2,10,34,192]{3,0,2,1:T(2,128)(2,1)S(1)}, bf16[2,10,34,192]{3,0,2,1:T(2,128)(2,1)S(1)}, u32[]{:S(2)}, u32[]{:S(2)}) collective-permute-start(bf16[2,10,34,192]{3,0,2,1:T(2,128)(2,1)S(1)} %select_convert_fusion), channel_id=1, source_target_pairs={{0,32},{32,64},{64,96},{96,128},{128,160},{160,192},{192,224},{224... | collective-permute-start | bytes 783368 | tf_op jit(solution)/shard_map/ppermute | solution.py:27
  42.1 10.6 %collective-permute-done.5 = bf16[2,10,34,192]{3,0,2,1:T(2,128)(2,1)S(1)} collective-permute-done((bf16[2,10,34,192]{3,0,2,1:T(2,128)(2,1)S(1)}, bf16[2,10,34,192]{3,0,2,1:T(2,128)(2,1)S(1)}, u32[]{:S(2)}, u32[]{:S(2)}) %collective-permute-start.5) | collective-permute-done | bytes 261152 | tf_op jit(solution)/shard_map/ppermute | solution.py:27
  52.7 0.8 %maximum_bitcast_fusion.1 = bf16[4,10,1,34,192]{4,0,3,1,2:T(4,128)(2,1)S(1)} fusion(bf16[2,10,34,192]{3,0,2,1:T(2,128)(2,1)S(1)} %select_convert_fusion, bf16[2,10,34,192]{3,0,2,1:T(2,128)(2,1)S(1)} %collective-permute-done.5), kind=kLoop, calls=%fused_computation.29 | loop fusion | flops 1044480 | bytes 1044480 | tf_op jit(solution)/shard_map/broadcast_in_dim | solution.py:36
  53.5 0.4 pad.2
  53.9 0.1 copy.14
  54.0 0.1 slice.22
  54.1 0.0 copy-done.5
  54.1 0.0 copy-done.6
  54.1 0.0 copy-start.1
  54.1 0.0 copy-start.4
  54.1 2.0 %convolution_select_fusion = f32[2,8,8,5,192]{4,2,3,1,0:T(8,128)S(1)} fusion(bf16[3,3,3,192,192]{4,3,2,1,0:T(8,128)(2,1)S(1)} %copy-done.5, bf16[4,10,1,7,2,192]{5,3,4,1,0,2:T(8,128)(2,1)S(1)} %slice.22, bf16[4,10,1,8,5,192]{5,3,4,1,0,2:T(8,128)(2,1)S(1)} %copy.14, pred[8,5]{0,1:T(8,128)(4,1)S(1)} %copy-done.6), kind=kOutput, calls=%fused_computation.11 | convolution fusion | flops 1276723200 | bytes 3311656 | tf_op jit(solution)/shard_map/conv_general_dilated | solution.py:35
  56.2 0.2 copy.15
  56.4 0.0 copy-done.1
  56.4 0.0 copy-done.4
  56.4 0.2 fusion.33
  56.6 0.8 %copy.16 = bf16[2,8,32,192]{3,2,1,0:T(8,128)(2,1)} copy(bf16[2,8,32,192]{3,1,2,0:T(8,128)(2,1)S(1)} %fusion.33) | data formatting | bytes 393216 | tf_op jit(solution)/shard_map/convert_element_type | solution.py:67
  (4 shorter events, 0.1 us)
Async XLA Ops:
  0.0 34.8 %copy-start = (bf16[3,3,3,192,192]{4,3,2,1,0:T(8,128)(2,1)S(1)}, bf16[3,3,3,192,192]{4,3,2,1,0:T(8,128)(2,1)}, u32[]{:S(2)}) copy-start(bf16[3,3,3,192,192]{4,3,2,1,0:T(8,128)(2,1)} %param.9) | copy-start | bytes 5971972
  2.6 10.3 %collective-permute-start = (bf16[2,8,32,192]{3,1,2,0:T(8,128)(2,1)S(1)}, bf16[2,8,32,192]{3,1,2,0:T(8,128)(2,1)S(1)}, u32[]{:S(2)}, u32[]{:S(2)}) collective-permute-start(bf16[2,8,32,192]{3,1,2,0:T(8,128)(2,1)S(1)} %fusion.31), channel_id=1, source_target_pairs={{0,32},{32,64},{64,96},{96,128},{128,160},{160,192},{192,224},{224... | collective-permute-start | bytes 589832 | tf_op jit(solution)/shard_map/ppermute | solution.py:27
  13.1 5.1 %collective-permute-start.1 = (bf16[4,2,32,192]{3,1,2,0:T(2,128)(2,1)S(1)}, bf16[4,2,32,192]{3,1,2,0:T(2,128)(2,1)S(1)}, u32[]{:S(2)}, u32[]{:S(2)}) collective-permute-start(bf16[4,2,32,192]{3,1,2,0:T(2,128)(2,1)S(1)} %get-tuple-element.7), channel_id=1, source_target_pairs={{0,8},{8,16},{16,24},{1,9},{9,17},{17,25},{2,10},{10,18},{18,26},{... | collective-permute-start | bytes 294920 | tf_op jit(solution)/shard_map/ppermute | solution.py:15
  16.2 5.7 %collective-permute-start.2 = (bf16[4,2,32,192]{3,1,2,0:T(2,128)(2,1)S(1)}, bf16[4,2,32,192]{3,1,2,0:T(2,128)(2,1)S(1)}, u32[]{:S(2)}, u32[]{:S(2)}) collective-permute-start(bf16[4,2,32,192]{3,1,2,0:T(2,128)(2,1)S(1)} %get-tuple-element.8), channel_id=1, source_target_pairs={{8,0},{16,8},{24,16},{9,1},{17,9},{25,17},{10,2},{18,10},{26,18},{... | collective-permute-start | bytes 294920 | tf_op jit(solution)/shard_map/ppermute | solution.py:17
  22.0 7.8 %collective-permute-start.3 = (bf16[4,12,2,192]{3,1,2,0:T(8,128)(2,1)S(1)}, bf16[4,12,2,192]{3,1,2,0:T(8,128)(2,1)S(1)}, u32[]{:S(2)}, u32[]{:S(2)}) collective-permute-start(bf16[4,12,2,192]{3,1,2,0:T(8,128)(2,1)S(1)} %get-tuple-element.5), channel_id=1, source_target_pairs={{0,1},{1,2},{2,3},{3,4},{4,5},{5,6},{6,7},{8,9},{9,10},{10,11},{11... | collective-permute-start | bytes 110600 | tf_op jit(solution)/shard_map/ppermute | solution.py:15
  27.8 5.6 %collective-permute-start.4 = (bf16[4,12,2,192]{3,1,2,0:T(8,128)(2,1)S(1)}, bf16[4,12,2,192]{3,1,2,0:T(8,128)(2,1)S(1)}, u32[]{:S(2)}, u32[]{:S(2)}) collective-permute-start(bf16[4,12,2,192]{3,1,2,0:T(8,128)(2,1)S(1)} %get-tuple-element.6), channel_id=1, source_target_pairs={{1,0},{2,1},{3,2},{4,3},{5,4},{6,5},{7,6},{9,8},{10,9},{11,10},{12... | collective-permute-start | bytes 110600 | tf_op jit(solution)/shard_map/ppermute | solution.py:17
  34.0 0.8 %copy-start.7 = (pred[8,5]{0,1:T(8,128)(4,1)S(1)}, pred[8,5]{0,1:T(8,128)(4,1)}, u32[]{:S(2)}) copy-start(pred[8,5]{0,1:T(8,128)(4,1)} %constant.47) | copy-start | bytes 124
  34.8 3.1 %copy-start.2 = (f32[192]{0:T(256)S(1)}, f32[192]{0:T(256)}, u32[]{:S(2)}) copy-start(f32[192]{0:T(256)} %param.10) | copy-start | bytes 2308
  37.3 1.2 %copy-start.3 = (f32[192]{0:T(256)S(1)}, f32[192]{0:T(256)}, u32[]{:S(2)}) copy-start(f32[192]{0:T(256)} %param.11) | copy-start | bytes 2308
  39.9 14.2 %copy-start.5 = (bf16[3,3,3,192,192]{4,3,2,1,0:T(8,128)(2,1)S(1)}, bf16[3,3,3,192,192]{4,3,2,1,0:T(8,128)(2,1)}, u32[]{:S(2)}) copy-start(bf16[3,3,3,192,192]{4,3,2,1,0:T(8,128)(2,1)} %param.12) | copy-start | bytes 5971972
  39.9 14.2 %copy-start.6 = (pred[8,5]{0,1:T(8,128)(4,1)S(1)}, pred[8,5]{0,1:T(8,128)(4,1)}, u32[]{:S(2)}) copy-start(pred[8,5]{0,1:T(8,128)(4,1)} %constant.46) | copy-start | bytes 124
  39.9 12.8 %collective-permute-start.5 = (bf16[2,10,34,192]{3,0,2,1:T(2,128)(2,1)S(1)}, bf16[2,10,34,192]{3,0,2,1:T(2,128)(2,1)S(1)}, u32[]{:S(2)}, u32[]{:S(2)}) collective-permute-start(bf16[2,10,34,192]{3,0,2,1:T(2,128)(2,1)S(1)} %select_convert_fusion), channel_id=1, source_target_pairs={{0,32},{32,64},{64,96},{96,128},{128,160},{160,192},{192,224},{224... | collective-permute-start | bytes 783368 | tf_op jit(solution)/shard_map/ppermute | solution.py:27
  54.1 2.2 %copy-start.1 = (bf16[2,8,32,192]{3,2,1,0:T(8,128)(2,1)S(1)}, bf16[2,8,32,192]{3,2,1,0:T(8,128)(2,1)}, u32[]{:S(2)}) copy-start(bf16[2,8,32,192]{3,2,1,0:T(8,128)(2,1)} %param.7) | copy-start | bytes 589828
  54.1 2.2 %copy-start.4 = (f32[192]{0:T(256)S(1)}, f32[192]{0:T(256)}, u32[]{:S(2)}) copy-start(f32[192]{0:T(256)} %param.13) | copy-start | bytes 2308

commit v4 on v3

--- a/solution.py
+++ b/solution.py
@@ -1,6 +1,7 @@
 import jax
 import jax.numpy as jnp
 from jax import lax
+from jax.experimental import pallas as pl
 from jax.sharding import PartitionSpec as P
 
 
@@ -31,6 +32,39 @@
     return values * lax.rsqrt(jnp.mean(values * values, axis=-1, keepdims=True) + 1e-06) * gain
 
 
+def _act_kernel(x_ref, gain_ref, bias_ref, keep_ref, out_ref, *, rounded):
+    values = x_ref[...].astype(jnp.float32) + bias_ref[...]
+    if rounded:
+        values = values.astype(jnp.bfloat16).astype(jnp.float32)
+    scale = lax.rsqrt(jnp.mean(values * values, axis=-1, keepdims=True) + 1e-06)
+    normed = values * scale * gain_ref[...]
+    act = normed / (1.0 + jnp.exp(-normed))
+    out_ref[...] = (act * keep_ref[...]).astype(out_ref.dtype)
+
+
+def activation(cells, gain, bias, keep, rounded):
+    shape = cells.shape
+    flat = cells.reshape(-1, shape[-1])
+    out = pl.pallas_call(
+        lambda *refs: _act_kernel(*refs, rounded=rounded),
+        out_shape=jax.ShapeDtypeStruct(flat.shape, jnp.bfloat16),
+    )(flat, gain.reshape(1, -1), bias.reshape(1, -1), keep.reshape(-1, 1).astype(jnp.float32))
+    return out.reshape(shape)
+
+
+def _residual_kernel(x_ref, conv_ref, bias_ref, out_ref):
+    out_ref[...] = (x_ref[...].astype(jnp.float32) + conv_ref[...] + bias_ref[...]).astype(out_ref.dtype)
+
+
+def residual(latents, conv, bias):
+    shape = latents.shape
+    out = pl.pallas_call(
+        _residual_kernel,
+        out_shape=jax.ShapeDtypeStruct((shape[0] * shape[1] * shape[2], shape[3]), latents.dtype),
+    )(latents.reshape(-1, shape[-1]), conv.reshape(-1, shape[-1]), bias.reshape(1, -1))
+    return out.reshape(shape)
+
+
 def conv_valid(stack, kernel):
     out = lax.conv_general_dilated(
         stack[None],
@@ -52,19 +86,17 @@
 
 def local(latents, first_gain, first_weight, first_bias, second_gain, second_weight, second_bias):
     frames, rows, cols, chans = latents.shape
-    values = latents.astype(jnp.float32)
-    first_act = jax.nn.silu(rms_norm(values, first_gain)).astype(jnp.bfloat16)
+    ones = jnp.ones((frames, rows, cols), jnp.float32)
+    first_act = activation(latents, first_gain, jnp.zeros_like(first_bias), ones, False)
     stack = jnp.concatenate([shifted(first_act, "tm", 1), first_act], axis=0)
     first_ext = with_halo(stack, (("row", 1), ("col", 2)), 2)
     first_conv = conv_valid(first_ext, first_weight)
-    hidden = (first_conv + first_bias).astype(jnp.bfloat16)
-    second_act = jax.nn.silu(rms_norm(hidden.astype(jnp.float32), second_gain))
     keep = inside("row", rows, 1)[:, None] & inside("col", cols, 1)[None, :]
-    second_act = jnp.where(keep[None, :, :, None], second_act, 0.0).astype(jnp.bfloat16)
+    keep = jnp.broadcast_to(keep[None], first_conv.shape[:3])
+    second_act = activation(first_conv, second_gain, first_bias, keep, True)
     second_cache = shifted(second_act, "tm", 1)
     second_conv = conv_valid(jnp.concatenate([second_cache, second_act], axis=0), second_weight)
-    decoded = values + second_conv + second_bias
-    return decoded.astype(jnp.bfloat16)
+    return residual(latents, second_conv, second_bias)
 
 
 def solution(mesh):

time: 57.6 us -> 82 us (1.42)
  matrix products: 4.48 us -> 23.3 us
  Pallas kernels: 0 us -> 6.31 us
  other arithmetic: 6.56 us -> 2.19 us
  local copies, waits for them, and re-layouts: 2.91 us -> 6.28 us
    conv_general_dilated x2, matrix products: 4.48 us -> 23.3 us  [conv_valid(): lax.conv_general_dilated(stack[None], kernel, window_strides=(1, 1, 1), p...]
    pallas_call x0 -> x3, Pallas kernels: none -> 6.31 us  [the longest x2 4.44 us: activation(): pl.pallas_call(lambda *refs: _act_kernel(*refs, rounded=rounded), out_sha...]
    reshape x0 -> x4, local copies, waits for them, and re-layouts: none -> 3.58 us  [the longest x2 2.32 us: activation(): return out.reshape(shape)]
    convert_element_type x3 -> x1, other arithmetic: 2.84 us -> 0.07 us  [activation(): keep.reshape(-1, 1).astype(jnp.float32)]
    reduce_sum x2 -> x0, other arithmetic: 1.81 us -> none  [rms_norm(): jnp.mean(values * values, axis=-1, keepdims=True) + 1e-06]
    conv_general_dilated x6 -> x0, local copies, waits for them, and re-layouts: 1.47 us -> none  [conv_valid(): lax.conv_general_dilated(stack[None], kernel, window_strides=(1, 1, 1), p...]
    ppermute x2, waiting for transfers between devices: 18.2 us -> 19.5 us  [shifted(): lax.ppermute(value, axis, [(source, source + steps) for source in range(i...]
    another operation x0 -> x1, local copies, waits for them, and re-layouts: none -> 0.94 us  [activation(): flat = cells.reshape(-1, shape[-1])]
  transfers between devices with their start and end apart: 6 -> 6, of which waited for: 5 -> 5; matrix products, arithmetic and copies ran while one was open for 0% -> 1% of each run, Pallas kernels for 0% -> 0%
where the time goes in v4:
time: 82 us; the launch traced here: 81.6 us
  waiting for transfers between devices  26.6 us (32%)
  matrix products  23.3 us (28%)
  starting transfers between devices  16.8 us (20%)
  Pallas kernels  6.31 us (8%)
  local copies, waits for them, and re-layouts  6.28 us (8%)
  other arithmetic  2.19 us (3%)
    conv_general_dilated x2, matrix products, conv_valid(): lax.conv_general_dilated(stack[None], kernel, window_strides=(1, 1, 1), p...  23.3 us
    ppermute x2, waiting for transfers between devices, shifted(): lax.ppermute(value, axis, [(source, source + steps) for source in range(i...  19.5 us
    ppermute x2, starting transfers between devices, with_halo(): lax.ppermute(tail, axis, [(i, i + 1) for i in range(ends)])  8.87 us
    ppermute x2, waiting for transfers between devices, with_halo(): lax.ppermute(head, axis, [(i + 1, i) for i in range(ends)])  6.48 us
    ppermute x2, starting transfers between devices, shifted(): lax.ppermute(value, axis, [(source, source + steps) for source in range(i...  4.75 us
    pallas_call x2, Pallas kernels, activation(): pl.pallas_call(lambda *refs: _act_kernel(*refs, rounded=rounded), out_sha...  4.44 us
    ppermute x2, starting transfers between devices, with_halo(): lax.ppermute(head, axis, [(i + 1, i) for i in range(ends)])  3.21 us
    reshape x2, local copies, waits for them, and re-layouts, activation(): return out.reshape(shape)  2.32 us
  transfers between devices with their start and end apart: 6, of which 5 were waited for; matrix products, arithmetic and copies ran while one was open for 1% of the time, Pallas kernels for 0%

profile of v4, /device:TPU:273, one launch (start us, length us, event | category | flops | bytes accessed | tf_op | source)
XLA Modules:
  0.0 81.6 jit_solution(6341691560574690691)
XLA Ops:
  0.0 0.0 copy-start
  0.0 0.7 reshape.89.refs_3_
  0.7 0.5 reshape.88.refs_2_
  1.3 2.1 %shard_map.73 = bf16[512,192]{1,0:T(8,128)(2,1)} custom-call(bf16[512,192]{1,0:T(8,128)(2,1)} %bitcast.15, f32[1,192]{1,0:T(1,128)} %bitcast.18, f32[1,192]{1,0:T(1,128)} %reshape.88.refs_2_, f32[512,1]{1,0:T(8,128)} %reshape.89.refs_3_), custom_call_target="tpu_custom_call" | custom-call | tf_op jit(solution)/shard_map/pallas_call | solution.py:48
  3.3 1.2 %copy.8 = bf16[2,8,32,192]{3,0,2,1:T(2,128)(2,1)S(1)} copy(bf16[2,8,32,192]{3,2,1,0:T(8,128)(2,1)} %bitcast.17) | data formatting | bytes 393216 | tf_op jit(solution)/shard_map/reshape | solution.py:52
  4.6 2.6 %collective-permute-start = (bf16[2,8,32,192]{3,0,2,1:T(2,128)(2,1)S(1)}, bf16[2,8,32,192]{3,0,2,1:T(2,128)(2,1)S(1)}, u32[]{:S(2)}, u32[]{:S(2)}) collective-permute-start(bf16[2,8,32,192]{3,0,2,1:T(2,128)(2,1)S(1)} %copy.8), channel_id=1, source_target_pairs={{0,32},{32,64},{64,96},{96,128},{128,160},{160,192},{192,224},{224... | collective-permute-start | bytes 589832 | tf_op jit(solution)/shard_map/ppermute | solution.py:28
  7.2 7.6 %collective-permute-done = bf16[2,8,32,192]{3,0,2,1:T(2,128)(2,1)S(1)} collective-permute-done((bf16[2,8,32,192]{3,0,2,1:T(2,128)(2,1)S(1)}, bf16[2,8,32,192]{3,0,2,1:T(2,128)(2,1)S(1)}, u32[]{:S(2)}, u32[]{:S(2)}) %collective-permute-start) | collective-permute-done | bytes 196640 | tf_op jit(solution)/shard_map/ppermute | solution.py:28
  14.9 0.3 pad_maximum_fusion.1
  15.2 3.1 %collective-permute-start.1 = (bf16[4,2,32,192]{3,0,2,1:T(4,128)(2,1)S(1)}, bf16[4,2,32,192]{3,0,2,1:T(4,128)(2,1)S(1)}, u32[]{:S(2)}, u32[]{:S(2)}) collective-permute-start(bf16[4,2,32,192]{3,0,2,1:T(4,128)(2,1)S(1)} %get-tuple-element.7), channel_id=1, source_target_pairs={{0,8},{8,16},{16,24},{1,9},{9,17},{17,25},{2,10},{10,18},{18,26},{... | collective-permute-start | bytes 294920 | tf_op jit(solution)/shard_map/ppermute | solution.py:16
  18.3 1.3 %collective-permute-start.2 = (bf16[4,2,32,192]{3,0,2,1:T(4,128)(2,1)S(1)}, bf16[4,2,32,192]{3,0,2,1:T(4,128)(2,1)S(1)}, u32[]{:S(2)}, u32[]{:S(2)}) collective-permute-start(bf16[4,2,32,192]{3,0,2,1:T(4,128)(2,1)S(1)} %get-tuple-element.8), channel_id=1, source_target_pairs={{8,0},{16,8},{24,16},{9,1},{17,9},{25,17},{10,2},{18,10},{26,18},{... | collective-permute-start | bytes 294920 | tf_op jit(solution)/shard_map/ppermute | solution.py:18
  19.6 0.6 collective-permute-done.1
  20.2 3.8 %collective-permute-done.2 = bf16[4,2,32,192]{3,0,2,1:T(4,128)(2,1)S(1)} collective-permute-done((bf16[4,2,32,192]{3,0,2,1:T(4,128)(2,1)S(1)}, bf16[4,2,32,192]{3,0,2,1:T(4,128)(2,1)S(1)}, u32[]{:S(2)}, u32[]{:S(2)}) %collective-permute-start.2) | collective-permute-done | bytes 98336 | tf_op jit(solution)/shard_map/ppermute | solution.py:18
  24.0 0.7 pad_maximum_fusion.5
  24.7 5.7 %collective-permute-start.3 = (bf16[4,12,2,192]{3,0,2,1:T(4,128)(2,1)}, bf16[4,12,2,192]{3,0,2,1:T(4,128)(2,1)S(1)}, u32[]{:S(2)}, u32[]{:S(2)}) collective-permute-start(bf16[4,12,2,192]{3,0,2,1:T(4,128)(2,1)} %get-tuple-element.5), channel_id=1, source_target_pairs={{0,1},{1,2},{2,3},{3,4},{4,5},{5,6},{6,7},{8,9},{9,10},{10,11},{11... | collective-permute-start | bytes 110600 | tf_op jit(solution)/shard_map/ppermute | solution.py:16
  30.5 1.9 %collective-permute-start.4 = (bf16[4,12,2,192]{3,0,2,1:T(4,128)(2,1)}, bf16[4,12,2,192]{3,0,2,1:T(4,128)(2,1)S(1)}, u32[]{:S(2)}, u32[]{:S(2)}) collective-permute-start(bf16[4,12,2,192]{3,0,2,1:T(4,128)(2,1)} %get-tuple-element.6), channel_id=1, source_target_pairs={{1,0},{2,1},{3,2},{4,3},{5,4},{6,5},{7,6},{9,8},{10,9},{11,10},{12... | collective-permute-start | bytes 110600 | tf_op jit(solution)/shard_map/ppermute | solution.py:18
  32.4 0.1 and_convert_fusion
  32.5 0.9 %convert_element_type.7.refs_3_ = f32[680,1]{1,0:T(8,128)} reshape(f32[2,10,34]{2,1,0:T(8,128)S(1)} %broadcast_in_dim.7) | data formatting | bytes 5440 | tf_op jit(solution)/shard_map/convert_element_type | solution.py:51
  33.4 0.0 collective-permute-done.3
  33.4 2.7 %collective-permute-done.4 = bf16[4,12,2,192]{3,0,2,1:T(4,128)(2,1)S(1)} collective-permute-done((bf16[4,12,2,192]{3,0,2,1:T(4,128)(2,1)}, bf16[4,12,2,192]{3,0,2,1:T(4,128)(2,1)S(1)}, u32[]{:S(2)}, u32[]{:S(2)}) %collective-permute-start.4) | collective-permute-done | bytes 36896 | tf_op jit(solution)/shard_map/ppermute | solution.py:18
  36.1 0.9 %maximum_bitcast_fusion = bf16[1,4,12,36,192]{4,1,3,2,0:T(4,128)(2,1)S(1)} fusion(bf16[4,12,2,192]{3,0,2,1:T(4,128)(2,1)S(1)} %collective-permute-done.4, bf16[4,2,32,192]{3,0,2,1:T(4,128)(2,1)S(1)} %collective-permute-done.2, bf16[2,8,32,192]{3,0,2,1:T(2,128)(2,1)S(1)} %copy.8, bf16[2,8,32,192]{3,0,2,1:T(2,128)(2,1)S(1)} %collective-permute-done, ...), kind=kLoop, calls=%fused_computation.5 | loop fusion | flops 3981312 | bytes 1327104 | tf_op jit(solution)/shard_map/broadcast_in_dim | solution.py:70
  37.0 0.0 copy-done
  37.0 13.3 %fusion.4 = f32[2,10,34,192]{3,2,1,0:T(8,128)S(1)} fusion(bf16[3,3,3,192,192]{4,3,2,1,0:T(8,128)(2,1)S(1)} %copy-done, bf16[1,4,12,36,192]{4,1,3,2,0:T(4,128)(2,1)S(1)} %maximum_bitcast_fusion), kind=kOutput, calls=%fused_computation.4 | convolution fusion | flops 1353646080 | bytes 3176448 | tf_op jit(solution)/shard_map/conv_general_dilated | solution.py:69
  50.4 0.9 %reshape_squeeze.6.refs_0_ = f32[680,192]{1,0:T(8,128)} reshape(f32[2,10,34,192]{3,2,1,0:T(8,128)S(1)} %fusion.4) | data formatting | bytes 1044480 | tf_op jit(solution)/shard_map/reshape;squeeze | solution.py:47
  51.3 2.4 %shard_map.74 = bf16[680,192]{1,0:T(8,128)(2,1)} custom-call(f32[680,192]{1,0:T(8,128)} %reshape_squeeze.6.refs_0_, f32[1,192]{1,0:T(1,128)} %bitcast.20, f32[1,192]{1,0:T(1,128)} %bitcast.21, f32[680,1]{1,0:T(8,128)} %convert_element_type.7.refs_3_), custom_call_target="tpu_custom_call" | custom-call | tf_op jit(solution)/shard_map/pallas_call | solution.py:48
  53.7 1.1 %reshape.93 = bf16[2,10,34,192]{3,2,1,0:T(8,128)(2,1)S(1)} reshape(bf16[680,192]{1,0:T(8,128)(2,1)} %shard_map.74) | data formatting | bytes 522240 | tf_op jit(solution)/shard_map/reshape | solution.py:52
  54.8 2.1 %collective-permute-start.5 = (bf16[2,10,34,192]{3,2,1,0:T(8,128)(2,1)S(1)}, bf16[2,10,34,192]{3,2,1,0:T(8,128)(2,1)S(1)}, u32[]{:S(2)}, u32[]{:S(2)}) collective-permute-start(bf16[2,10,34,192]{3,2,1,0:T(8,128)(2,1)S(1)} %reshape.93), channel_id=1, source_target_pairs={{0,32},{32,64},{64,96},{96,128},{128,160},{160,192},{192,224},{224... | collective-permute-start | bytes 783368 | tf_op jit(solution)/shard_map/ppermute | solution.py:28
  56.9 11.8 %collective-permute-done.5 = bf16[2,10,34,192]{3,2,1,0:T(8,128)(2,1)S(1)} collective-permute-done((bf16[2,10,34,192]{3,2,1,0:T(8,128)(2,1)S(1)}, bf16[2,10,34,192]{3,2,1,0:T(8,128)(2,1)S(1)}, u32[]{:S(2)}, u32[]{:S(2)}) %collective-permute-start.5) | collective-permute-done | bytes 261152 | tf_op jit(solution)/shard_map/ppermute | solution.py:28
  68.8 0.1 maximum_bitcast_fusion.1
  68.9 9.9 %fusion.2 = f32[1,2,8,32,192]{4,0,3,2,1:T(1,128)S(1)} fusion(bf16[3,3,3,192,192]{4,3,2,1,0:T(8,128)(2,1)} %param.12, bf16[1,4,10,34,192]{4,3,2,1,0:T(8,128)(2,1)S(1)} %maximum_bitcast_fusion.1), kind=kOutput, calls=%fused_computation.2 | convolution fusion | flops 1019215872 | bytes 2906112 | tf_op jit(solution)/shard_map/conv_general_dilated | solution.py:69
  78.9 0.8 %copy.17 = f32[1,2,8,32,192]{4,3,0,2,1:T(8,128)} copy(f32[1,2,8,32,192]{4,0,3,2,1:T(1,128)S(1)} %fusion.2) | data formatting | bytes 786432
  79.7 1.9 %shard_map.75 = bf16[512,192]{1,0:T(8,128)(2,1)} custom-call(bf16[512,192]{1,0:T(8,128)(2,1)} %bitcast.16, f32[512,192]{1,0:T(8,128)} %bitcast.14, f32[1,192]{1,0:T(1,128)} %bitcast.19), custom_call_target="tpu_custom_call" | custom-call | tf_op jit(solution)/shard_map/pallas_call | solution.py:61
  (3 shorter events, 0.0 us)
Async XLA Ops:
  0.0 37.0 %copy-start = (bf16[3,3,3,192,192]{4,3,2,1,0:T(8,128)(2,1)S(1)}, bf16[3,3,3,192,192]{4,3,2,1,0:T(8,128)(2,1)}, u32[]{:S(2)}) copy-start(bf16[3,3,3,192,192]{4,3,2,1,0:T(8,128)(2,1)} %param.9) | copy-start | bytes 5971972
  4.6 10.3 %collective-permute-start = (bf16[2,8,32,192]{3,0,2,1:T(2,128)(2,1)S(1)}, bf16[2,8,32,192]{3,0,2,1:T(2,128)(2,1)S(1)}, u32[]{:S(2)}, u32[]{:S(2)}) collective-permute-start(bf16[2,8,32,192]{3,0,2,1:T(2,128)(2,1)S(1)} %copy.8), channel_id=1, source_target_pairs={{0,32},{32,64},{64,96},{96,128},{128,160},{160,192},{192,224},{224... | collective-permute-start | bytes 589832 | tf_op jit(solution)/shard_map/ppermute | solution.py:28
  15.2 5.1 %collective-permute-start.1 = (bf16[4,2,32,192]{3,0,2,1:T(4,128)(2,1)S(1)}, bf16[4,2,32,192]{3,0,2,1:T(4,128)(2,1)S(1)}, u32[]{:S(2)}, u32[]{:S(2)}) collective-permute-start(bf16[4,2,32,192]{3,0,2,1:T(4,128)(2,1)S(1)} %get-tuple-element.7), channel_id=1, source_target_pairs={{0,8},{8,16},{16,24},{1,9},{9,17},{17,25},{2,10},{10,18},{18,26},{... | collective-permute-start | bytes 294920 | tf_op jit(solution)/shard_map/ppermute | solution.py:16
  18.3 5.7 %collective-permute-start.2 = (bf16[4,2,32,192]{3,0,2,1:T(4,128)(2,1)S(1)}, bf16[4,2,32,192]{3,0,2,1:T(4,128)(2,1)S(1)}, u32[]{:S(2)}, u32[]{:S(2)}) collective-permute-start(bf16[4,2,32,192]{3,0,2,1:T(4,128)(2,1)S(1)} %get-tuple-element.8), channel_id=1, source_target_pairs={{8,0},{16,8},{24,16},{9,1},{17,9},{25,17},{10,2},{18,10},{26,18},{... | collective-permute-start | bytes 294920 | tf_op jit(solution)/shard_map/ppermute | solution.py:18
  24.7 8.7 %collective-permute-start.3 = (bf16[4,12,2,192]{3,0,2,1:T(4,128)(2,1)}, bf16[4,12,2,192]{3,0,2,1:T(4,128)(2,1)S(1)}, u32[]{:S(2)}, u32[]{:S(2)}) collective-permute-start(bf16[4,12,2,192]{3,0,2,1:T(4,128)(2,1)} %get-tuple-element.5), channel_id=1, source_target_pairs={{0,1},{1,2},{2,3},{3,4},{4,5},{5,6},{6,7},{8,9},{9,10},{10,11},{11... | collective-permute-start | bytes 110600 | tf_op jit(solution)/shard_map/ppermute | solution.py:16
  30.5 5.6 %collective-permute-start.4 = (bf16[4,12,2,192]{3,0,2,1:T(4,128)(2,1)}, bf16[4,12,2,192]{3,0,2,1:T(4,128)(2,1)S(1)}, u32[]{:S(2)}, u32[]{:S(2)}) collective-permute-start(bf16[4,12,2,192]{3,0,2,1:T(4,128)(2,1)} %get-tuple-element.6), channel_id=1, source_target_pairs={{1,0},{2,1},{3,2},{4,3},{5,4},{6,5},{7,6},{9,8},{10,9},{11,10},{12... | collective-permute-start | bytes 110600 | tf_op jit(solution)/shard_map/ppermute | solution.py:18
  54.8 14.0 %collective-permute-start.5 = (bf16[2,10,34,192]{3,2,1,0:T(8,128)(2,1)S(1)}, bf16[2,10,34,192]{3,2,1,0:T(8,128)(2,1)S(1)}, u32[]{:S(2)}, u32[]{:S(2)}) collective-permute-start(bf16[2,10,34,192]{3,2,1,0:T(8,128)(2,1)S(1)} %reshape.93), channel_id=1, source_target_pairs={{0,32},{32,64},{64,96},{96,128},{128,160},{160,192},{192,224},{224... | collective-permute-start | bytes 783368 | tf_op jit(solution)/shard_map/ppermute | solution.py:28

commit v5 on v3

--- a/solution.py
+++ b/solution.py
@@ -27,6 +27,38 @@
     return lax.ppermute(value, axis, [(source, source + steps) for source in range(initial, last)])
 
 
+def own_wide(cells, width):
+    count = lax.axis_size("col")
+    head = cells[:, :, :width]
+    tail = cells[:, :, cells.shape[2] - width :]
+    from_left = lax.ppermute(tail, "col", [(i, i + 1) for i in range(count - 1)])
+    from_right = lax.ppermute(head, "col", [(i + 1, i) for i in range(count - 1)])
+    return jnp.concatenate([from_left, cells, from_right], axis=2)
+
+
+def previous_wide(cells, width):
+    groups = lax.axis_size("tm")
+    count = lax.axis_size("col")
+    head = cells[:, :, :width]
+    tail = cells[:, :, cells.shape[2] - width :]
+
+    def place(group, column):
+        return group * count + column
+
+    middle = lax.ppermute(cells, "tm", [(g, g + 1) for g in range(groups - 1)])
+    from_left = lax.ppermute(
+        tail,
+        ("tm", "col"),
+        [(place(g, c), place(g + 1, c + 1)) for g in range(groups - 1) for c in range(count - 1)],
+    )
+    from_right = lax.ppermute(
+        head,
+        ("tm", "col"),
+        [(place(g, c + 1), place(g + 1, c)) for g in range(groups - 1) for c in range(count - 1)],
+    )
+    return jnp.concatenate([from_left, middle, from_right], axis=2)
+
+
 def rms_norm(values, gain):
     return values * lax.rsqrt(jnp.mean(values * values, axis=-1, keepdims=True) + 1e-06) * gain
 
@@ -54,8 +86,8 @@
     frames, rows, cols, chans = latents.shape
     values = latents.astype(jnp.float32)
     first_act = jax.nn.silu(rms_norm(values, first_gain)).astype(jnp.bfloat16)
-    stack = jnp.concatenate([shifted(first_act, "tm", 1), first_act], axis=0)
-    first_ext = with_halo(stack, (("row", 1), ("col", 2)), 2)
+    stack = jnp.concatenate([previous_wide(first_act, 2), own_wide(first_act, 2)], axis=0)
+    first_ext = with_halo(stack, (("row", 1),), 2)
     first_conv = conv_valid(first_ext, first_weight)
     hidden = (first_conv + first_bias).astype(jnp.bfloat16)
     second_act = jax.nn.silu(rms_norm(hidden.astype(jnp.float32), second_gain))

time: 57.6 us -> 60 us (1.042)
  the two profiles are of different devices: /device:TPU:273 before, /device:TPU:136 now
where the time goes in v5:
time: 60 us; the launch traced here: 59.7 us
  starting transfers between devices  24.8 us (41%)
  waiting for transfers between devices  20.6 us (34%)
  other arithmetic  6.55 us (11%)
  matrix products  4.48 us (7%)
  local copies, waits for them, and re-layouts  2.92 us (5%)
    ppermute x1, waiting for transfers between devices, shifted(): lax.ppermute(value, axis, [(source, source + steps) for source in range(i...  7.57 us
    ppermute x1, waiting for transfers between devices, previous_wide(): middle = lax.ppermute(cells, 'tm', [(g, g + 1) for g in range(groups - 1)])  7.37 us
    conv_general_dilated x2, matrix products, conv_valid(): lax.conv_general_dilated(stack[None], kernel, window_strides=(1, 1, 1), p...  4.48 us
    ppermute x1, waiting for transfers between devices, with_halo(): lax.ppermute(head, axis, [(i + 1, i) for i in range(ends)])  4.39 us
    ppermute x1, starting transfers between devices, previous_wide(): middle = lax.ppermute(cells, 'tm', [(g, g + 1) for g in range(groups - 1)])  3.83 us
    ppermute x1, starting transfers between devices, own_wide(): lax.ppermute(tail, 'col', [(i, i + 1) for i in range(count - 1)])  3.6 us
    ppermute x1, starting transfers between devices, shifted(): lax.ppermute(value, axis, [(source, source + steps) for source in range(i...  3.52 us
    ppermute x1, starting transfers between devices, with_halo(): lax.ppermute(tail, axis, [(i, i + 1) for i in range(ends)])  3.4 us
  transfers between devices with their start and end apart: 8, of which 4 were waited for; matrix products, arithmetic and copies ran while one was open for 0% of the time, Pallas kernels for 0%

profile of v5, /device:TPU:136, one launch (start us, length us, event | category | flops | bytes accessed | tf_op | source)
XLA Modules:
  0.0 59.7 jit_solution(10045878591816257894)
XLA Ops:
  0.0 0.0 copy-start
  0.0 1.3 %fusion.24 = f32[2,8,32]{1,2,0:T(8,128)S(1)} fusion(bf16[2,8,32,192]{3,2,1,0:T(8,128)(2,1)} %param.7), kind=kLoop, calls=%fused_computation.33 | loop fusion | flops 294400 | bytes 198656 | tf_op jit(solution)/shard_map/reduce_sum | solution.py:63
  1.4 1.2 %fusion.31 = bf16[2,8,32,192]{3,1,2,0:T(8,128)(2,1)S(1)} fusion(f32[192]{0:T(256)} %param.8, f32[2,8,32]{1,2,0:T(8,128)S(1)} %add_rsqrt_fusion.1, bf16[2,8,32,192]{3,2,1,0:T(8,128)(2,1)} %param.7), kind=kLoop, calls=%fused_computation.40 | loop fusion | flops 786432 | bytes 396032 | tf_op jit(solution)/shard_map/convert_element_type | solution.py:88
  2.6 3.3 %collective-permute-start = (bf16[2,8,2,192]{3,1,2,0:T(8,128)(2,1)S(1)}, bf16[2,8,2,192]{3,1,2,0:T(8,128)(2,1)S(1)}, u32[]{:S(2)}, u32[]{:S(2)}) collective-permute-start(bf16[2,8,2,192]{3,1,2,0:T(8,128)(2,1)S(1)} %get-tuple-element.7), channel_id=1, source_target_pairs={{0,33},{1,34},{2,35},{3,36},{4,37},{5,38},{6,39},{32,65},{33,66},{... | collective-permute-start | bytes 36872 | tf_op jit(solution)/shard_map/ppermute | solution.py:49
  5.9 3.6 %collective-permute-start.3 = (bf16[2,8,2,192]{3,1,2,0:T(8,128)(2,1)S(1)}, bf16[2,8,2,192]{3,1,2,0:T(8,128)(2,1)S(1)}, u32[]{:S(2)}, u32[]{:S(2)}) collective-permute-start(bf16[2,8,2,192]{3,1,2,0:T(8,128)(2,1)S(1)} %get-tuple-element.7), channel_id=1, source_target_pairs={{0,1},{1,2},{2,3},{3,4},{4,5},{5,6},{6,7},{8,9},{9,10},{10,11},{11... | collective-permute-start | bytes 36872 | tf_op jit(solution)/shard_map/ppermute | solution.py:34
  9.5 3.3 %collective-permute-start.2 = (bf16[2,8,2,192]{3,1,2,0:T(8,128)(2,1)S(1)}, bf16[2,8,2,192]{3,1,2,0:T(8,128)(2,1)S(1)}, u32[]{:S(2)}, u32[]{:S(2)}) collective-permute-start(bf16[2,8,2,192]{3,1,2,0:T(8,128)(2,1)S(1)} %get-tuple-element.8), channel_id=1, source_target_pairs={{1,32},{2,33},{3,34},{4,35},{5,36},{6,37},{7,38},{33,64},{34,65},{... | collective-permute-start | bytes 36872 | tf_op jit(solution)/shard_map/ppermute | solution.py:54
  12.8 2.6 %collective-permute-start.4 = (bf16[2,8,2,192]{3,1,2,0:T(8,128)(2,1)S(1)}, bf16[2,8,2,192]{3,1,2,0:T(8,128)(2,1)S(1)}, u32[]{:S(2)}, u32[]{:S(2)}) collective-permute-start(bf16[2,8,2,192]{3,1,2,0:T(8,128)(2,1)S(1)} %get-tuple-element.8), channel_id=1, source_target_pairs={{1,0},{2,1},{3,2},{4,3},{5,4},{6,5},{7,6},{9,8},{10,9},{11,10},{12... | collective-permute-start | bytes 36872 | tf_op jit(solution)/shard_map/ppermute | solution.py:35
  15.4 3.8 %collective-permute-start.1 = (bf16[2,8,32,192]{3,1,2,0:T(8,128)(2,1)S(1)}, bf16[2,8,32,192]{3,1,2,0:T(8,128)(2,1)S(1)}, u32[]{:S(2)}, u32[]{:S(2)}) collective-permute-start(bf16[2,8,32,192]{3,1,2,0:T(8,128)(2,1)S(1)} %fusion.31), channel_id=1, source_target_pairs={{0,32},{32,64},{64,96},{96,128},{128,160},{160,192},{192,224},{224... | collective-permute-start | bytes 589832 | tf_op jit(solution)/shard_map/ppermute | solution.py:48
  19.3 0.0 collective-permute-done
  19.3 0.0 collective-permute-done.2
  19.3 0.0 collective-permute-done.3
  19.3 0.0 collective-permute-done.4
  19.3 7.4 %collective-permute-done.1 = bf16[2,8,32,192]{3,1,2,0:T(8,128)(2,1)S(1)} collective-permute-done((bf16[2,8,32,192]{3,1,2,0:T(8,128)(2,1)S(1)}, bf16[2,8,32,192]{3,1,2,0:T(8,128)(2,1)S(1)}, u32[]{:S(2)}, u32[]{:S(2)}) %collective-permute-start.1) | collective-permute-done | bytes 196640 | tf_op jit(solution)/shard_map/ppermute | solution.py:48
  26.7 0.2 maximum_maximum_fusion
  26.9 3.4 %collective-permute-start.5 = (bf16[4,2,36,192]{3,1,2,0:T(2,128)(2,1)S(1)}, bf16[4,2,36,192]{3,1,2,0:T(2,128)(2,1)S(1)}, u32[]{:S(2)}, u32[]{:S(2)}) collective-permute-start(bf16[4,2,36,192]{3,1,2,0:T(2,128)(2,1)S(1)} %get-tuple-element.5), channel_id=1, source_target_pairs={{0,8},{8,16},{16,24},{1,9},{9,17},{17,25},{2,10},{10,18},{18,26},{... | collective-permute-start | bytes 331784 | tf_op jit(solution)/shard_map/ppermute | solution.py:15
  30.3 1.3 %collective-permute-start.6 = (bf16[4,2,36,192]{3,1,2,0:T(2,128)(2,1)S(1)}, bf16[4,2,36,192]{3,1,2,0:T(2,128)(2,1)S(1)}, u32[]{:S(2)}, u32[]{:S(2)}) collective-permute-start(bf16[4,2,36,192]{3,1,2,0:T(2,128)(2,1)S(1)} %get-tuple-element.6), channel_id=1, source_target_pairs={{8,0},{16,8},{24,16},{9,1},{17,9},{25,17},{10,2},{18,10},{26,18},{... | collective-permute-start | bytes 331784 | tf_op jit(solution)/shard_map/ppermute | solution.py:17
  31.6 0.1 broadcast_and_fusion
  31.7 1.3 %collective-permute-done.5 = bf16[4,2,36,192]{3,1,2,0:T(2,128)(2,1)S(1)} collective-permute-done((bf16[4,2,36,192]{3,1,2,0:T(2,128)(2,1)S(1)}, bf16[4,2,36,192]{3,1,2,0:T(2,128)(2,1)S(1)}, u32[]{:S(2)}, u32[]{:S(2)}) %collective-permute-start.5) | collective-permute-done | bytes 110624 | tf_op jit(solution)/shard_map/ppermute | solution.py:15
  33.0 4.4 %collective-permute-done.6 = bf16[4,2,36,192]{3,1,2,0:T(2,128)(2,1)S(1)} collective-permute-done((bf16[4,2,36,192]{3,1,2,0:T(2,128)(2,1)S(1)}, bf16[4,2,36,192]{3,1,2,0:T(2,128)(2,1)S(1)}, u32[]{:S(2)}, u32[]{:S(2)}) %collective-permute-start.6) | collective-permute-done | bytes 110624 | tf_op jit(solution)/shard_map/ppermute | solution.py:17
  37.3 0.7 %maximum_bitcast_fusion = bf16[4,12,1,36,192]{4,1,3,0,2:T(8,128)(2,1)S(1)} fusion(bf16[4,2,36,192]{3,1,2,0:T(2,128)(2,1)S(1)} %collective-permute-done.6, bf16[2,8,2,192]{3,1,2,0:T(8,128)(2,1)S(1)} %collective-permute-done.4, bf16[2,8,32,192]{3,1,2,0:T(8,128)(2,1)S(1)} %fusion.31, bf16[2,8,2,192]{3,1,2,0:T(8,128)(2,1)S(1)} %collective-permute-done.3, ...), kind=kLoop, calls=%fused_computation.12 | loop fusion | flops 5308416 | bytes 1327104 | tf_op jit(solution)/shard_map/broadcast_in_dim | solution.py:68
  38.1 0.0 copy-start.7
  38.1 0.3 pad
  38.4 0.4 copy.11
  38.7 0.1 slice.24
  38.8 0.0 copy-done
  38.8 0.0 copy-done.7
  38.8 0.0 copy-start.2
  38.8 2.5 %fusion.9 = f32[2,10,8,5,192]{4,2,3,1,0:T(8,128)S(1)} fusion(bf16[3,3,3,192,192]{4,3,2,1,0:T(8,128)(2,1)S(1)} %copy-done, bf16[4,12,1,7,2,192]{5,3,4,1,0,2:T(8,128)(2,1)S(1)} %slice.24, bf16[4,12,1,8,5,192]{5,3,4,1,0,2:T(8,128)(2,1)S(1)} %copy.11, pred[8,5]{0,1:T(8,128)(4,1)S(1)} %copy-done.7), kind=kOutput, calls=%fused_computation.10 | convolution fusion | flops 1595774976 | bytes 3600424 | tf_op jit(solution)/shard_map/conv_general_dilated | solution.py:67
  41.3 0.0 copy-start.3
  41.3 0.6 %copy.12 = f32[2,10,8,5,192]{4,0,3,2,1:T(2,128)S(1)} copy(f32[2,10,8,5,192]{4,2,3,1,0:T(8,128)S(1)} %fusion.9) | data formatting | bytes 1228800 | tf_op jit(solution)/shard_map/conv_general_dilated | solution.py:67
  42.0 0.0 copy-done.2
  42.0 0.5 fusion.18
  42.5 0.0 copy-done.3
  42.5 1.4 %select_convert_fusion = bf16[2,10,34,192]{3,0,2,1:T(2,128)(2,1)S(1)} fusion(pred[10,34]{1,0:T(8,128)(4,1)S(1)} %broadcast_and_fusion, f32[192]{0:T(256)S(1)} %copy-done.3, f32[2,10,34]{0,2,1:T(8,128)S(1)} %add_rsqrt_fusion, f32[192]{0:T(256)S(1)} %copy-done.2, f32[2,10,1,40,192]{4,0,3,1,2:T(2,128)S(1)} %bitcast.33), kind=kLoop, calls=%fused_computation.30 | loop fusion | flops 1436160 | bytes 787956 | tf_op jit(solution)/shard_map/convert_element_type | solution.py:95
  43.9 0.0 copy-start.5
  43.9 0.0 copy-start.6
  44.0 3.5 %collective-permute-start.7 = (bf16[2,10,34,192]{3,0,2,1:T(2,128)(2,1)S(1)}, bf16[2,10,34,192]{3,0,2,1:T(2,128)(2,1)S(1)}, u32[]{:S(2)}, u32[]{:S(2)}) collective-permute-start(bf16[2,10,34,192]{3,0,2,1:T(2,128)(2,1)S(1)} %select_convert_fusion), channel_id=1, source_target_pairs={{0,32},{32,64},{64,96},{96,128},{128,160},{160,192},{192,224},{224... | collective-permute-start | bytes 783368 | tf_op jit(solution)/shard_map/ppermute | solution.py:27
  47.5 7.6 %collective-permute-done.7 = bf16[2,10,34,192]{3,0,2,1:T(2,128)(2,1)S(1)} collective-permute-done((bf16[2,10,34,192]{3,0,2,1:T(2,128)(2,1)S(1)}, bf16[2,10,34,192]{3,0,2,1:T(2,128)(2,1)S(1)}, u32[]{:S(2)}, u32[]{:S(2)}) %collective-permute-start.7) | collective-permute-done | bytes 261152 | tf_op jit(solution)/shard_map/ppermute | solution.py:27
  55.1 0.8 %maximum_bitcast_fusion.1 = bf16[4,10,1,34,192]{4,0,3,1,2:T(4,128)(2,1)S(1)} fusion(bf16[2,10,34,192]{3,0,2,1:T(2,128)(2,1)S(1)} %select_convert_fusion, bf16[2,10,34,192]{3,0,2,1:T(2,128)(2,1)S(1)} %collective-permute-done.7), kind=kLoop, calls=%fused_computation.29 | loop fusion | flops 1044480 | bytes 1044480 | tf_op jit(solution)/shard_map/broadcast_in_dim | solution.py:68
  55.9 0.4 pad.2
  56.2 0.1 copy.14
  56.4 0.1 slice.26
  56.5 0.0 copy-done.5
  56.5 0.0 copy-done.6
  56.5 0.0 copy-start.1
  56.5 0.0 copy-start.4
  56.5 2.0 %convolution_select_fusion = f32[2,8,8,5,192]{4,2,3,1,0:T(8,128)S(1)} fusion(bf16[3,3,3,192,192]{4,3,2,1,0:T(8,128)(2,1)S(1)} %copy-done.5, bf16[4,10,1,7,2,192]{5,3,4,1,0,2:T(8,128)(2,1)S(1)} %slice.26, bf16[4,10,1,8,5,192]{5,3,4,1,0,2:T(8,128)(2,1)S(1)} %copy.14, pred[8,5]{0,1:T(8,128)(4,1)S(1)} %copy-done.6), kind=kOutput, calls=%fused_computation.11 | convolution fusion | flops 1276723200 | bytes 3311656 | tf_op jit(solution)/shard_map/conv_general_dilated | solution.py:67
  58.5 0.2 copy.15
  58.7 0.0 copy-done.1
  58.7 0.0 copy-done.4
  58.7 0.2 fusion.33
  58.9 0.8 %copy.16 = bf16[2,8,32,192]{3,2,1,0:T(8,128)(2,1)} copy(bf16[2,8,32,192]{3,1,2,0:T(8,128)(2,1)S(1)} %fusion.33) | data formatting | bytes 393216 | tf_op jit(solution)/shard_map/convert_element_type | solution.py:99
  (5 shorter events, 0.1 us)
Async XLA Ops:
  0.0 38.8 %copy-start = (bf16[3,3,3,192,192]{4,3,2,1,0:T(8,128)(2,1)S(1)}, bf16[3,3,3,192,192]{4,3,2,1,0:T(8,128)(2,1)}, u32[]{:S(2)}) copy-start(bf16[3,3,3,192,192]{4,3,2,1,0:T(8,128)(2,1)} %param.9) | copy-start | bytes 5971972
  2.6 16.7 %collective-permute-start = (bf16[2,8,2,192]{3,1,2,0:T(8,128)(2,1)S(1)}, bf16[2,8,2,192]{3,1,2,0:T(8,128)(2,1)S(1)}, u32[]{:S(2)}, u32[]{:S(2)}) collective-permute-start(bf16[2,8,2,192]{3,1,2,0:T(8,128)(2,1)S(1)} %get-tuple-element.7), channel_id=1, source_target_pairs={{0,33},{1,34},{2,35},{3,36},{4,37},{5,38},{6,39},{32,65},{33,66},{... | collective-permute-start | bytes 36872 | tf_op jit(solution)/shard_map/ppermute | solution.py:49
  5.9 13.4 %collective-permute-start.3 = (bf16[2,8,2,192]{3,1,2,0:T(8,128)(2,1)S(1)}, bf16[2,8,2,192]{3,1,2,0:T(8,128)(2,1)S(1)}, u32[]{:S(2)}, u32[]{:S(2)}) collective-permute-start(bf16[2,8,2,192]{3,1,2,0:T(8,128)(2,1)S(1)} %get-tuple-element.7), channel_id=1, source_target_pairs={{0,1},{1,2},{2,3},{3,4},{4,5},{5,6},{6,7},{8,9},{9,10},{10,11},{11... | collective-permute-start | bytes 36872 | tf_op jit(solution)/shard_map/ppermute | solution.py:34
  9.5 9.8 %collective-permute-start.2 = (bf16[2,8,2,192]{3,1,2,0:T(8,128)(2,1)S(1)}, bf16[2,8,2,192]{3,1,2,0:T(8,128)(2,1)S(1)}, u32[]{:S(2)}, u32[]{:S(2)}) collective-permute-start(bf16[2,8,2,192]{3,1,2,0:T(8,128)(2,1)S(1)} %get-tuple-element.8), channel_id=1, source_target_pairs={{1,32},{2,33},{3,34},{4,35},{5,36},{6,37},{7,38},{33,64},{34,65},{... | collective-permute-start | bytes 36872 | tf_op jit(solution)/shard_map/ppermute | solution.py:54
  12.8 6.5 %collective-permute-start.4 = (bf16[2,8,2,192]{3,1,2,0:T(8,128)(2,1)S(1)}, bf16[2,8,2,192]{3,1,2,0:T(8,128)(2,1)S(1)}, u32[]{:S(2)}, u32[]{:S(2)}) collective-permute-start(bf16[2,8,2,192]{3,1,2,0:T(8,128)(2,1)S(1)} %get-tuple-element.8), channel_id=1, source_target_pairs={{1,0},{2,1},{3,2},{4,3},{5,4},{6,5},{7,6},{9,8},{10,9},{11,10},{12... | collective-permute-start | bytes 36872 | tf_op jit(solution)/shard_map/ppermute | solution.py:35
  15.4 11.3 %collective-permute-start.1 = (bf16[2,8,32,192]{3,1,2,0:T(8,128)(2,1)S(1)}, bf16[2,8,32,192]{3,1,2,0:T(8,128)(2,1)S(1)}, u32[]{:S(2)}, u32[]{:S(2)}) collective-permute-start(bf16[2,8,32,192]{3,1,2,0:T(8,128)(2,1)S(1)} %fusion.31), channel_id=1, source_target_pairs={{0,32},{32,64},{64,96},{96,128},{128,160},{160,192},{192,224},{224... | collective-permute-start | bytes 589832 | tf_op jit(solution)/shard_map/ppermute | solution.py:48
  26.9 6.1 %collective-permute-start.5 = (bf16[4,2,36,192]{3,1,2,0:T(2,128)(2,1)S(1)}, bf16[4,2,36,192]{3,1,2,0:T(2,128)(2,1)S(1)}, u32[]{:S(2)}, u32[]{:S(2)}) collective-permute-start(bf16[4,2,36,192]{3,1,2,0:T(2,128)(2,1)S(1)} %get-tuple-element.5), channel_id=1, source_target_pairs={{0,8},{8,16},{16,24},{1,9},{9,17},{17,25},{2,10},{10,18},{18,26},{... | collective-permute-start | bytes 331784 | tf_op jit(solution)/shard_map/ppermute | solution.py:15
  30.3 7.0 %collective-permute-start.6 = (bf16[4,2,36,192]{3,1,2,0:T(2,128)(2,1)S(1)}, bf16[4,2,36,192]{3,1,2,0:T(2,128)(2,1)S(1)}, u32[]{:S(2)}, u32[]{:S(2)}) collective-permute-start(bf16[4,2,36,192]{3,1,2,0:T(2,128)(2,1)S(1)} %get-tuple-element.6), channel_id=1, source_target_pairs={{8,0},{16,8},{24,16},{9,1},{17,9},{25,17},{10,2},{18,10},{26,18},{... | collective-permute-start | bytes 331784 | tf_op jit(solution)/shard_map/ppermute | solution.py:17
  38.1 0.8 %copy-start.7 = (pred[8,5]{0,1:T(8,128)(4,1)S(1)}, pred[8,5]{0,1:T(8,128)(4,1)}, u32[]{:S(2)}) copy-start(pred[8,5]{0,1:T(8,128)(4,1)} %constant.47) | copy-start | bytes 124
  38.8 3.1 %copy-start.2 = (f32[192]{0:T(256)S(1)}, f32[192]{0:T(256)}, u32[]{:S(2)}) copy-start(f32[192]{0:T(256)} %param.10) | copy-start | bytes 2308
  41.3 1.2 %copy-start.3 = (f32[192]{0:T(256)S(1)}, f32[192]{0:T(256)}, u32[]{:S(2)}) copy-start(f32[192]{0:T(256)} %param.11) | copy-start | bytes 2308
  43.9 12.5 %copy-start.5 = (bf16[3,3,3,192,192]{4,3,2,1,0:T(8,128)(2,1)S(1)}, bf16[3,3,3,192,192]{4,3,2,1,0:T(8,128)(2,1)}, u32[]{:S(2)}) copy-start(bf16[3,3,3,192,192]{4,3,2,1,0:T(8,128)(2,1)} %param.12) | copy-start | bytes 5971972
  43.9 12.5 %copy-start.6 = (pred[8,5]{0,1:T(8,128)(4,1)S(1)}, pred[8,5]{0,1:T(8,128)(4,1)}, u32[]{:S(2)}) copy-start(pred[8,5]{0,1:T(8,128)(4,1)} %constant.46) | copy-start | bytes 124
  44.0 11.1 %collective-permute-start.7 = (bf16[2,10,34,192]{3,0,2,1:T(2,128)(2,1)S(1)}, bf16[2,10,34,192]{3,0,2,1:T(2,128)(2,1)S(1)}, u32[]{:S(2)}, u32[]{:S(2)}) collective-permute-start(bf16[2,10,34,192]{3,0,2,1:T(2,128)(2,1)S(1)} %select_convert_fusion), channel_id=1, source_target_pairs={{0,32},{32,64},{64,96},{96,128},{128,160},{160,192},{192,224},{224... | collective-permute-start | bytes 783368 | tf_op jit(solution)/shard_map/ppermute | solution.py:27
  56.5 2.2 %copy-start.1 = (bf16[2,8,32,192]{3,2,1,0:T(8,128)(2,1)S(1)}, bf16[2,8,32,192]{3,2,1,0:T(8,128)(2,1)}, u32[]{:S(2)}) copy-start(bf16[2,8,32,192]{3,2,1,0:T(8,128)(2,1)} %param.7) | copy-start | bytes 589828
  56.5 2.2 %copy-start.4 = (f32[192]{0:T(256)S(1)}, f32[192]{0:T(256)}, u32[]{:S(2)}) copy-start(f32[192]{0:T(256)} %param.13) | copy-start | bytes 2308

commit v6 on v3

--- a/solution.py
+++ b/solution.py
@@ -19,6 +19,21 @@
             axis=dim,
         )
     return cells
+
+
+def rows_exchanged(cells, width):
+    count = lax.axis_size("row")
+    here = lax.axis_index("row")
+    head = lax.slice_in_dim(cells, 0, width, axis=1)
+    tail = lax.slice_in_dim(cells, cells.shape[1] - width, cells.shape[1], axis=1)
+    target = jnp.arange(count)[:, None, None, None, None]
+    chunks = jnp.where(target == here - 1, head[None], jnp.where(target == here + 1, tail[None], 0))
+    got = lax.all_to_all(chunks.astype(cells.dtype), "row", 0, 0)
+    above = jnp.where(here > 0, lax.dynamic_index_in_dim(got, jnp.maximum(here - 1, 0), 0, False), 0)
+    below = jnp.where(
+        here < count - 1, lax.dynamic_index_in_dim(got, jnp.minimum(here + 1, count - 1), 0, False), 0
+    )
+    return jnp.concatenate([above.astype(cells.dtype), cells, below.astype(cells.dtype)], axis=1)
 
 
 def shifted(value, axis, steps):
@@ -55,7 +70,7 @@
     values = latents.astype(jnp.float32)
     first_act = jax.nn.silu(rms_norm(values, first_gain)).astype(jnp.bfloat16)
     stack = jnp.concatenate([shifted(first_act, "tm", 1), first_act], axis=0)
-    first_ext = with_halo(stack, (("row", 1), ("col", 2)), 2)
+    first_ext = with_halo(rows_exchanged(stack, 2), (("col", 2),), 2)
     first_conv = conv_valid(first_ext, first_weight)
     hidden = (first_conv + first_bias).astype(jnp.bfloat16)
     second_act = jax.nn.silu(rms_norm(hidden.astype(jnp.float32), second_gain))

time: 57.6 us -> 63.1 us (1.095)
  the two profiles are of different devices: /device:TPU:273 before, /device:TPU:401 now
where the time goes in v6:
time: 63.1 us; the launch traced here: 62.8 us
  waiting for transfers between devices  29.3 us (46%)
  starting transfers between devices  16.6 us (26%)
  other arithmetic  9.15 us (15%)
  matrix products  4.47 us (7%)
  local copies, waits for them, and re-layouts  2.91 us (5%)
    ppermute x2, waiting for transfers between devices, shifted(): lax.ppermute(value, axis, [(source, source + steps) for source in range(i...  18.2 us
    all_to_all x1, waiting for transfers between devices, rows_exchanged(): got = lax.all_to_all(chunks.astype(cells.dtype), 'row', 0, 0)  7.56 us
    ppermute x1, starting transfers between devices, with_halo(): lax.ppermute(tail, axis, [(i, i + 1) for i in range(ends)])  5.67 us
    ppermute x2, starting transfers between devices, shifted(): lax.ppermute(value, axis, [(source, source + steps) for source in range(i...  4.83 us
    conv_general_dilated x2, matrix products, conv_valid(): lax.conv_general_dilated(stack[None], kernel, window_strides=(1, 1, 1), p...  4.47 us
    all_to_all x1, starting transfers between devices, rows_exchanged(): got = lax.all_to_all(chunks.astype(cells.dtype), 'row', 0, 0)  4.14 us
    ppermute x1, waiting for transfers between devices, with_halo(): lax.ppermute(head, axis, [(i + 1, i) for i in range(ends)])  3.58 us
    ppermute x1, starting transfers between devices, with_halo(): lax.ppermute(head, axis, [(i + 1, i) for i in range(ends)])  1.92 us
  transfers between devices with their start and end apart: 5, of which 4 were waited for; matrix products, arithmetic and copies ran while one was open for 0% of the time, Pallas kernels for 0%

profile of v6, /device:TPU:401, one launch (start us, length us, event | category | flops | bytes accessed | tf_op | source)
XLA Modules:
  0.0 62.8 jit_solution(1904061764915819893)
XLA Ops:
  0.0 0.0 copy-start
  0.0 1.3 %fusion.24 = f32[2,8,32]{1,2,0:T(8,128)S(1)} fusion(bf16[2,8,32,192]{3,2,1,0:T(8,128)(2,1)} %param.7), kind=kLoop, calls=%fused_computation.35 | loop fusion | flops 294400 | bytes 198656 | tf_op jit(solution)/shard_map/reduce_sum | solution.py:46
  1.4 1.2 %fusion.31 = bf16[2,8,32,192]{3,1,2,0:T(8,128)(2,1)S(1)} fusion(f32[192]{0:T(256)} %param.8, f32[2,8,32]{1,2,0:T(8,128)S(1)} %add_rsqrt_fusion.1, bf16[2,8,32,192]{3,2,1,0:T(8,128)(2,1)} %param.7), kind=kLoop, calls=%fused_computation.42 | loop fusion | flops 786432 | bytes 396032 | tf_op jit(solution)/shard_map/convert_element_type | solution.py:71
  2.6 2.6 %collective-permute-start = (bf16[2,8,32,192]{3,1,2,0:T(8,128)(2,1)S(1)}, bf16[2,8,32,192]{3,1,2,0:T(8,128)(2,1)S(1)}, u32[]{:S(2)}, u32[]{:S(2)}) collective-permute-start(bf16[2,8,32,192]{3,1,2,0:T(8,128)(2,1)S(1)} %fusion.31), channel_id=1, source_target_pairs={{0,32},{32,64},{64,96},{96,128},{128,160},{160,192},{192,224},{224... | collective-permute-start | bytes 589832 | tf_op jit(solution)/shard_map/ppermute | solution.py:42
  5.3 7.6 %collective-permute-done = bf16[2,8,32,192]{3,1,2,0:T(8,128)(2,1)S(1)} collective-permute-done((bf16[2,8,32,192]{3,1,2,0:T(8,128)(2,1)S(1)}, bf16[2,8,32,192]{3,1,2,0:T(8,128)(2,1)S(1)}, u32[]{:S(2)}, u32[]{:S(2)}) %collective-permute-start) | collective-permute-done | bytes 196640 | tf_op jit(solution)/shard_map/ppermute | solution.py:42
  12.9 0.2 pad_maximum_fusion.1
  13.1 1.4 %broadcast_select_fusion = bf16[4,4,2,32,192]{4,2,3,1,0:T(2,128)(2,1)} fusion(pred[4]{0:T(512)(128)(4,1)S(1)} %get-tuple-element.12, pred[4]{0:T(512)(128)(4,1)S(1)} %get-tuple-element.11, bf16[4,2,32,192]{3,1,2,0:T(2,128)(2,1)S(1)} %get-tuple-element.10, bf16[4,2,32,192]{3,1,2,0:T(2,128)(2,1)S(1)} %get-tuple-element.9), kind=kLoop, calls=%fused_computation.18 | loop fusion | flops 393216 | bytes 589832 | tf_op jit(solution)/shard_map/jit(_where)/select_n | solution.py:30
  14.5 4.1 %all-to-all-start = ((bf16[4,4,2,32,192]{4,2,3,1,0:T(2,128)(2,1)}), bf16[4,4,2,32,192]{4,2,3,1,0:T(2,128)(2,1)}, u32[]{:S(2)}, u32[]{:S(2)}) async-start(bf16[4,4,2,32,192]{4,2,3,1,0:T(2,128)(2,1)} %broadcast_select_fusion), calls=%async_computation | async-start | bytes 1048576 | tf_op jit(solution)/shard_map/all_to_all | solution.py:31
  18.7 7.6 %all-to-all-done = bf16[4,4,2,32,192]{4,2,3,1,0:T(2,128)(2,1)} async-done(((bf16[4,4,2,32,192]{4,2,3,1,0:T(2,128)(2,1)}), bf16[4,4,2,32,192]{4,2,3,1,0:T(2,128)(2,1)}, u32[]{:S(2)}, u32[]{:S(2)}) %all-to-all-start) | async-done | bytes 393248 | tf_op jit(solution)/shard_map/all_to_all | solution.py:31
  26.2 1.2 %fusion.34 = (bf16[4,2,32,192]{3,1,2,0:T(2,128)(2,1)S(1)}, bf16[4,2,32,192]{3,1,2,0:T(2,128)(2,1)S(1)}) fusion(pred[]{:T(512)S(6)} %gt.3, bf16[4,4,2,32,192]{4,2,3,1,0:T(2,128)(2,1)} %all-to-all-done, s32[]{:T(128)S(6)} %max.3, s32[]{:T(128)S(6)} %select_n.43, pred[]{:T(512)S(6)} %lt.28), kind=kLoop, calls=%fused_computation.49 | loop fusion | flops 98304 | bytes 393226 | tf_op jit(solution)/shard_map/jit(_where)/select_n | solution.py:32
  27.4 0.1 pad_maximum_fusion.5
  27.5 5.7 %collective-permute-start.1 = (bf16[4,12,2,192]{3,1,2,0:T(8,128)(2,1)S(1)}, bf16[4,12,2,192]{3,1,2,0:T(8,128)(2,1)S(1)}, u32[]{:S(2)}, u32[]{:S(2)}) collective-permute-start(bf16[4,12,2,192]{3,1,2,0:T(8,128)(2,1)S(1)} %get-tuple-element.5), channel_id=1, source_target_pairs={{0,1},{1,2},{2,3},{3,4},{4,5},{5,6},{6,7},{8,9},{9,10},{10,11},{11... | collective-permute-start | bytes 110600 | tf_op jit(solution)/shard_map/ppermute | solution.py:15
  33.2 1.9 %collective-permute-start.2 = (bf16[4,12,2,192]{3,1,2,0:T(8,128)(2,1)S(1)}, bf16[4,12,2,192]{3,1,2,0:T(8,128)(2,1)S(1)}, u32[]{:S(2)}, u32[]{:S(2)}) collective-permute-start(bf16[4,12,2,192]{3,1,2,0:T(8,128)(2,1)S(1)} %get-tuple-element.6), channel_id=1, source_target_pairs={{1,0},{2,1},{3,2},{4,3},{5,4},{6,5},{7,6},{9,8},{10,9},{11,10},{12... | collective-permute-start | bytes 110600 | tf_op jit(solution)/shard_map/ppermute | solution.py:17
  35.1 0.1 broadcast_and_fusion
  35.2 0.0 collective-permute-done.1
  35.2 3.6 %collective-permute-done.2 = bf16[4,12,2,192]{3,1,2,0:T(8,128)(2,1)S(1)} collective-permute-done((bf16[4,12,2,192]{3,1,2,0:T(8,128)(2,1)S(1)}, bf16[4,12,2,192]{3,1,2,0:T(8,128)(2,1)S(1)}, u32[]{:S(2)}, u32[]{:S(2)}) %collective-permute-start.2) | collective-permute-done | bytes 36896 | tf_op jit(solution)/shard_map/ppermute | solution.py:17
  38.8 0.7 %maximum_bitcast_fusion = bf16[4,12,1,36,192]{4,1,3,0,2:T(8,128)(2,1)S(1)} fusion(bf16[4,12,2,192]{3,1,2,0:T(8,128)(2,1)S(1)} %collective-permute-done.2, bf16[4,2,32,192]{3,1,2,0:T(2,128)(2,1)S(1)} %get-tuple-element.8, bf16[2,8,32,192]{3,1,2,0:T(8,128)(2,1)S(1)} %fusion.31, bf16[2,8,32,192]{3,1,2,0:T(8,128)(2,1)S(1)} %collective-permute-done, ...), kind=kLoop, calls=%fused_computation.12 | loop fusion | flops 3981312 | bytes 1327104 | tf_op jit(solution)/shard_map/broadcast_in_dim | solution.py:51
  39.5 0.0 copy-start.7
  39.5 0.3 pad
  39.7 0.4 copy.11
  40.1 0.1 slice.20
  40.2 0.0 copy-done
  40.2 0.0 copy-done.7
  40.2 0.0 copy-start.2
  40.2 2.5 %fusion.9 = f32[2,10,8,5,192]{4,2,3,1,0:T(8,128)S(1)} fusion(bf16[3,3,3,192,192]{4,3,2,1,0:T(8,128)(2,1)S(1)} %copy-done, bf16[4,12,1,7,2,192]{5,3,4,1,0,2:T(8,128)(2,1)S(1)} %slice.20, bf16[4,12,1,8,5,192]{5,3,4,1,0,2:T(8,128)(2,1)S(1)} %copy.11, pred[8,5]{0,1:T(8,128)(4,1)S(1)} %copy-done.7), kind=kOutput, calls=%fused_computation.10 | convolution fusion | flops 1595774976 | bytes 3600424 | tf_op jit(solution)/shard_map/conv_general_dilated | solution.py:50
  42.7 0.0 copy-start.3
  42.7 0.6 %copy.12 = f32[2,10,8,5,192]{4,0,3,2,1:T(2,128)S(1)} copy(f32[2,10,8,5,192]{4,2,3,1,0:T(8,128)S(1)} %fusion.9) | data formatting | bytes 1228800 | tf_op jit(solution)/shard_map/conv_general_dilated | solution.py:50
  43.3 0.0 copy-done.2
  43.4 0.5 fusion.18
  43.9 0.0 copy-done.3
  43.9 1.4 %select_convert_fusion = bf16[2,10,34,192]{3,0,2,1:T(2,128)(2,1)S(1)} fusion(pred[10,34]{1,0:T(8,128)(4,1)S(1)} %broadcast_and_fusion, f32[192]{0:T(256)S(1)} %copy-done.3, f32[2,10,34]{0,2,1:T(8,128)S(1)} %add_rsqrt_fusion, f32[192]{0:T(256)S(1)} %copy-done.2, f32[2,10,1,40,192]{4,0,3,1,2:T(2,128)S(1)} %bitcast.37), kind=kLoop, calls=%fused_computation.32 | loop fusion | flops 1436160 | bytes 787956 | tf_op jit(solution)/shard_map/convert_element_type | solution.py:78
  45.3 0.0 copy-start.5
  45.3 0.0 copy-start.6
  45.3 2.2 %collective-permute-start.3 = (bf16[2,10,34,192]{3,0,2,1:T(2,128)(2,1)S(1)}, bf16[2,10,34,192]{3,0,2,1:T(2,128)(2,1)S(1)}, u32[]{:S(2)}, u32[]{:S(2)}) collective-permute-start(bf16[2,10,34,192]{3,0,2,1:T(2,128)(2,1)S(1)} %select_convert_fusion), channel_id=1, source_target_pairs={{0,32},{32,64},{64,96},{96,128},{128,160},{160,192},{192,224},{224... | collective-permute-start | bytes 783368 | tf_op jit(solution)/shard_map/ppermute | solution.py:42
  47.5 10.6 %collective-permute-done.3 = bf16[2,10,34,192]{3,0,2,1:T(2,128)(2,1)S(1)} collective-permute-done((bf16[2,10,34,192]{3,0,2,1:T(2,128)(2,1)S(1)}, bf16[2,10,34,192]{3,0,2,1:T(2,128)(2,1)S(1)}, u32[]{:S(2)}, u32[]{:S(2)}) %collective-permute-start.3) | collective-permute-done | bytes 261152 | tf_op jit(solution)/shard_map/ppermute | solution.py:42
  58.1 0.8 %maximum_bitcast_fusion.1 = bf16[4,10,1,34,192]{4,0,3,1,2:T(4,128)(2,1)S(1)} fusion(bf16[2,10,34,192]{3,0,2,1:T(2,128)(2,1)S(1)} %select_convert_fusion, bf16[2,10,34,192]{3,0,2,1:T(2,128)(2,1)S(1)} %collective-permute-done.3), kind=kLoop, calls=%fused_computation.31 | loop fusion | flops 1044480 | bytes 1044480 | tf_op jit(solution)/shard_map/broadcast_in_dim | solution.py:51
  58.9 0.4 pad.2
  59.3 0.1 copy.14
  59.4 0.1 slice.22
  59.5 0.0 copy-done.5
  59.5 0.0 copy-done.6
  59.5 0.0 copy-start.1
  59.5 0.0 copy-start.4
  59.5 2.0 %convolution_select_fusion = f32[2,8,8,5,192]{4,2,3,1,0:T(8,128)S(1)} fusion(bf16[3,3,3,192,192]{4,3,2,1,0:T(8,128)(2,1)S(1)} %copy-done.5, bf16[4,10,1,7,2,192]{5,3,4,1,0,2:T(8,128)(2,1)S(1)} %slice.22, bf16[4,10,1,8,5,192]{5,3,4,1,0,2:T(8,128)(2,1)S(1)} %copy.14, pred[8,5]{0,1:T(8,128)(4,1)S(1)} %copy-done.6), kind=kOutput, calls=%fused_computation.11 | convolution fusion | flops 1276723200 | bytes 3311656 | tf_op jit(solution)/shard_map/conv_general_dilated | solution.py:50
  61.6 0.2 copy.15
  61.8 0.0 copy-done.1
  61.8 0.0 copy-done.4
  61.8 0.2 fusion.33
  62.0 0.8 %copy.16 = bf16[2,8,32,192]{3,2,1,0:T(8,128)(2,1)} copy(bf16[2,8,32,192]{3,1,2,0:T(8,128)(2,1)S(1)} %fusion.33) | data formatting | bytes 393216 | tf_op jit(solution)/shard_map/convert_element_type | solution.py:82
  (5 shorter events, 0.1 us)
Async XLA Ops:
  0.0 40.2 %copy-start = (bf16[3,3,3,192,192]{4,3,2,1,0:T(8,128)(2,1)S(1)}, bf16[3,3,3,192,192]{4,3,2,1,0:T(8,128)(2,1)}, u32[]{:S(2)}) copy-start(bf16[3,3,3,192,192]{4,3,2,1,0:T(8,128)(2,1)} %param.9) | copy-start | bytes 5971972
  2.6 10.3 %collective-permute-start = (bf16[2,8,32,192]{3,1,2,0:T(8,128)(2,1)S(1)}, bf16[2,8,32,192]{3,1,2,0:T(8,128)(2,1)S(1)}, u32[]{:S(2)}, u32[]{:S(2)}) collective-permute-start(bf16[2,8,32,192]{3,1,2,0:T(8,128)(2,1)S(1)} %fusion.31), channel_id=1, source_target_pairs={{0,32},{32,64},{64,96},{96,128},{128,160},{160,192},{192,224},{224... | collective-permute-start | bytes 589832 | tf_op jit(solution)/shard_map/ppermute | solution.py:42
  14.5 11.8 %all-to-all-start = ((bf16[4,4,2,32,192]{4,2,3,1,0:T(2,128)(2,1)}), bf16[4,4,2,32,192]{4,2,3,1,0:T(2,128)(2,1)}, u32[]{:S(2)}, u32[]{:S(2)}) async-start(bf16[4,4,2,32,192]{4,2,3,1,0:T(2,128)(2,1)} %broadcast_select_fusion), calls=%async_computation | async-start | bytes 1048576 | tf_op jit(solution)/shard_map/all_to_all | solution.py:31
  27.5 7.7 %collective-permute-start.1 = (bf16[4,12,2,192]{3,1,2,0:T(8,128)(2,1)S(1)}, bf16[4,12,2,192]{3,1,2,0:T(8,128)(2,1)S(1)}, u32[]{:S(2)}, u32[]{:S(2)}) collective-permute-start(bf16[4,12,2,192]{3,1,2,0:T(8,128)(2,1)S(1)} %get-tuple-element.5), channel_id=1, source_target_pairs={{0,1},{1,2},{2,3},{3,4},{4,5},{5,6},{6,7},{8,9},{9,10},{10,11},{11... | collective-permute-start | bytes 110600 | tf_op jit(solution)/shard_map/ppermute | solution.py:15
  33.2 5.6 %collective-permute-start.2 = (bf16[4,12,2,192]{3,1,2,0:T(8,128)(2,1)S(1)}, bf16[4,12,2,192]{3,1,2,0:T(8,128)(2,1)S(1)}, u32[]{:S(2)}, u32[]{:S(2)}) collective-permute-start(bf16[4,12,2,192]{3,1,2,0:T(8,128)(2,1)S(1)} %get-tuple-element.6), channel_id=1, source_target_pairs={{1,0},{2,1},{3,2},{4,3},{5,4},{6,5},{7,6},{9,8},{10,9},{11,10},{12... | collective-permute-start | bytes 110600 | tf_op jit(solution)/shard_map/ppermute | solution.py:17
  39.5 0.8 %copy-start.7 = (pred[8,5]{0,1:T(8,128)(4,1)S(1)}, pred[8,5]{0,1:T(8,128)(4,1)}, u32[]{:S(2)}) copy-start(pred[8,5]{0,1:T(8,128)(4,1)} %constant.62) | copy-start | bytes 124
  40.2 3.1 %copy-start.2 = (f32[192]{0:T(256)S(1)}, f32[192]{0:T(256)}, u32[]{:S(2)}) copy-start(f32[192]{0:T(256)} %param.10) | copy-start | bytes 2308
  42.7 1.2 %copy-start.3 = (f32[192]{0:T(256)S(1)}, f32[192]{0:T(256)}, u32[]{:S(2)}) copy-start(f32[192]{0:T(256)} %param.11) | copy-start | bytes 2308
  45.3 14.2 %copy-start.5 = (bf16[3,3,3,192,192]{4,3,2,1,0:T(8,128)(2,1)S(1)}, bf16[3,3,3,192,192]{4,3,2,1,0:T(8,128)(2,1)}, u32[]{:S(2)}) copy-start(bf16[3,3,3,192,192]{4,3,2,1,0:T(8,128)(2,1)} %param.12) | copy-start | bytes 5971972
  45.3 14.2 %copy-start.6 = (pred[8,5]{0,1:T(8,128)(4,1)S(1)}, pred[8,5]{0,1:T(8,128)(4,1)}, u32[]{:S(2)}) copy-start(pred[8,5]{0,1:T(8,128)(4,1)} %constant.61) | copy-start | bytes 124
  45.3 12.8 %collective-permute-start.3 = (bf16[2,10,34,192]{3,0,2,1:T(2,128)(2,1)S(1)}, bf16[2,10,34,192]{3,0,2,1:T(2,128)(2,1)S(1)}, u32[]{:S(2)}, u32[]{:S(2)}) collective-permute-start(bf16[2,10,34,192]{3,0,2,1:T(2,128)(2,1)S(1)} %select_convert_fusion), channel_id=1, source_target_pairs={{0,32},{32,64},{64,96},{96,128},{128,160},{160,192},{192,224},{224... | collective-permute-start | bytes 783368 | tf_op jit(solution)/shard_map/ppermute | solution.py:42
  59.5 2.2 %copy-start.1 = (bf16[2,8,32,192]{3,2,1,0:T(8,128)(2,1)S(1)}, bf16[2,8,32,192]{3,2,1,0:T(8,128)(2,1)}, u32[]{:S(2)}) copy-start(bf16[2,8,32,192]{3,2,1,0:T(8,128)(2,1)} %param.7) | copy-start | bytes 589828
  59.5 2.2 %copy-start.4 = (f32[192]{0:T(256)S(1)}, f32[192]{0:T(256)}, u32[]{:S(2)}) copy-start(f32[192]{0:T(256)} %param.13) | copy-start | bytes 2308

commit v7 on v3

--- a/solution.py
+++ b/solution.py
@@ -28,7 +28,13 @@
 
 
 def rms_norm(values, gain):
-    return values * lax.rsqrt(jnp.mean(values * values, axis=-1, keepdims=True) + 1e-06) * gain
+    chans = values.shape[-1]
+    total = jnp.dot(values * values, jnp.ones((chans, 1), jnp.float32), precision=lax.Precision.HIGHEST)
+    return values * lax.rsqrt(total / chans + 1e-06) * gain
+
+
+def silu(values):
+    return values * (0.5 * jnp.tanh(0.5 * values) + 0.5)
 
 
 def conv_valid(stack, kernel):
@@ -53,12 +59,12 @@
 def local(latents, first_gain, first_weight, first_bias, second_gain, second_weight, second_bias):
     frames, rows, cols, chans = latents.shape
     values = latents.astype(jnp.float32)
-    first_act = jax.nn.silu(rms_norm(values, first_gain)).astype(jnp.bfloat16)
+    first_act = silu(rms_norm(values, first_gain)).astype(jnp.bfloat16)
     stack = jnp.concatenate([shifted(first_act, "tm", 1), first_act], axis=0)
     first_ext = with_halo(stack, (("row", 1), ("col", 2)), 2)
     first_conv = conv_valid(first_ext, first_weight)
     hidden = (first_conv + first_bias).astype(jnp.bfloat16)
-    second_act = jax.nn.silu(rms_norm(hidden.astype(jnp.float32), second_gain))
+    second_act = silu(rms_norm(hidden.astype(jnp.float32), second_gain))
     keep = inside("row", rows, 1)[:, None] & inside("col", cols, 1)[None, :]
     second_act = jnp.where(keep[None, :, :, None], second_act, 0.0).astype(jnp.bfloat16)
     second_cache = shifted(second_act, "tm", 1)

time: 57.6 us -> 63.2 us (1.097)
  the two profiles are of different devices: /device:TPU:273 before, /device:TPU:401 now
where the time goes in v7:
time: 63.2 us; the launch traced here: 62.9 us
  waiting for transfers between devices  26 us (41%)
  starting transfers between devices  17.1 us (27%)
  matrix products  7.12 us (11%)
  other arithmetic  6.95 us (11%)
  local copies, waits for them, and re-layouts  5.37 us (8%)
    ppermute x2, waiting for transfers between devices, shifted(): lax.ppermute(value, axis, [(source, source + steps) for source in range(i...  18 us
    ppermute x2, starting transfers between devices, with_halo(): lax.ppermute(tail, axis, [(i, i + 1) for i in range(ends)])  8.88 us
    ppermute x2, waiting for transfers between devices, with_halo(): lax.ppermute(head, axis, [(i + 1, i) for i in range(ends)])  7.37 us
    ppermute x2, starting transfers between devices, shifted(): lax.ppermute(value, axis, [(source, source + steps) for source in range(i...  5.01 us
    conv_general_dilated x2, matrix products, conv_valid(): lax.conv_general_dilated(stack[None], kernel, window_strides=(1, 1, 1), p...  4.48 us
    ppermute x2, starting transfers between devices, with_halo(): lax.ppermute(head, axis, [(i + 1, i) for i in range(ends)])  3.21 us
    dot_general x2, matrix products, rms_norm(): jnp.dot(values * values, jnp.ones((chans, 1), jnp.float32), precision=lax...  2.64 us
    broadcast_in_dim x2, other arithmetic, conv_valid(): stack[None]  1.5 us
  transfers between devices with their start and end apart: 6, of which 5 were waited for; matrix products, arithmetic and copies ran while one was open for 0% of the time, Pallas kernels for 0%

profile of v7, /device:TPU:401, one launch (start us, length us, event | category | flops | bytes accessed | tf_op | source)
XLA Modules:
  0.0 62.9 jit_solution(15867414400728364297)
XLA Ops:
  0.0 0.0 copy-start
  0.0 1.3 %convert_multiply_fusion.2 = f32[2,8,32,192]{3,1,2,0:T(8,128)S(1)} fusion(bf16[2,8,32,192]{3,2,1,0:T(8,128)(2,1)} %param.7), kind=kLoop, calls=%fused_computation.24 | loop fusion | flops 196608 | bytes 589824 | tf_op jit(solution)/shard_map/mul | solution.py:32
  1.3 1.2 %fusion.33 = f32[1,2,8,32]{3,0,2,1:T(1,128)S(1)} fusion(f32[2,8,32,192]{3,1,2,0:T(8,128)S(1)} %convert_multiply_fusion.2), kind=kOutput, calls=%fused_computation.43 | convolution fusion | flops 1179648 | bytes 395264 | tf_op jit(solution)/shard_map/dot_general | solution.py:32
  2.5 0.1 copy.20
  2.6 1.2 %fusion.30 = bf16[2,8,32,192]{3,1,2,0:T(8,128)(2,1)S(1)} fusion(f32[192]{0:T(256)} %param.8, f32[2,8,32]{1,2,0:T(8,128)S(1)} %fusion.38, bf16[2,8,32,192]{3,2,1,0:T(8,128)(2,1)} %param.7), kind=kLoop, calls=%fused_computation.39 | loop fusion | flops 786432 | bytes 396032 | tf_op jit(solution)/shard_map/convert_element_type | solution.py:62
  3.8 2.6 %collective-permute-start = (bf16[2,8,32,192]{3,1,2,0:T(8,128)(2,1)S(1)}, bf16[2,8,32,192]{3,1,2,0:T(8,128)(2,1)S(1)}, u32[]{:S(2)}, u32[]{:S(2)}) collective-permute-start(bf16[2,8,32,192]{3,1,2,0:T(8,128)(2,1)S(1)} %fusion.30), channel_id=1, source_target_pairs={{0,32},{32,64},{64,96},{96,128},{128,160},{160,192},{192,224},{224... | collective-permute-start | bytes 589832 | tf_op jit(solution)/shard_map/ppermute | solution.py:27
  6.5 7.6 %collective-permute-done = bf16[2,8,32,192]{3,1,2,0:T(8,128)(2,1)S(1)} collective-permute-done((bf16[2,8,32,192]{3,1,2,0:T(8,128)(2,1)S(1)}, bf16[2,8,32,192]{3,1,2,0:T(8,128)(2,1)S(1)}, u32[]{:S(2)}, u32[]{:S(2)}) %collective-permute-start) | collective-permute-done | bytes 196640 | tf_op jit(solution)/shard_map/ppermute | solution.py:27
  14.1 0.2 pad_maximum_fusion.1
  14.3 3.1 %collective-permute-start.1 = (bf16[4,2,32,192]{3,1,2,0:T(2,128)(2,1)S(1)}, bf16[4,2,32,192]{3,1,2,0:T(2,128)(2,1)S(1)}, u32[]{:S(2)}, u32[]{:S(2)}) collective-permute-start(bf16[4,2,32,192]{3,1,2,0:T(2,128)(2,1)S(1)} %get-tuple-element.7), channel_id=1, source_target_pairs={{0,8},{8,16},{16,24},{1,9},{9,17},{17,25},{2,10},{10,18},{18,26},{... | collective-permute-start | bytes 294920 | tf_op jit(solution)/shard_map/ppermute | solution.py:15
  17.4 1.3 %collective-permute-start.2 = (bf16[4,2,32,192]{3,1,2,0:T(2,128)(2,1)S(1)}, bf16[4,2,32,192]{3,1,2,0:T(2,128)(2,1)S(1)}, u32[]{:S(2)}, u32[]{:S(2)}) collective-permute-start(bf16[4,2,32,192]{3,1,2,0:T(2,128)(2,1)S(1)} %get-tuple-element.8), channel_id=1, source_target_pairs={{8,0},{16,8},{24,16},{9,1},{17,9},{25,17},{10,2},{18,10},{26,18},{... | collective-permute-start | bytes 294920 | tf_op jit(solution)/shard_map/ppermute | solution.py:17
  18.7 0.6 collective-permute-done.1
  19.3 3.8 %collective-permute-done.2 = bf16[4,2,32,192]{3,1,2,0:T(2,128)(2,1)S(1)} collective-permute-done((bf16[4,2,32,192]{3,1,2,0:T(2,128)(2,1)S(1)}, bf16[4,2,32,192]{3,1,2,0:T(2,128)(2,1)S(1)}, u32[]{:S(2)}, u32[]{:S(2)}) %collective-permute-start.2) | collective-permute-done | bytes 98336 | tf_op jit(solution)/shard_map/ppermute | solution.py:17
  23.1 0.1 pad_maximum_fusion.5
  23.2 5.8 %collective-permute-start.3 = (bf16[4,12,2,192]{3,1,2,0:T(8,128)(2,1)S(1)}, bf16[4,12,2,192]{3,1,2,0:T(8,128)(2,1)S(1)}, u32[]{:S(2)}, u32[]{:S(2)}) collective-permute-start(bf16[4,12,2,192]{3,1,2,0:T(8,128)(2,1)S(1)} %get-tuple-element.5), channel_id=1, source_target_pairs={{0,1},{1,2},{2,3},{3,4},{4,5},{5,6},{6,7},{8,9},{9,10},{10,11},{11... | collective-permute-start | bytes 110600 | tf_op jit(solution)/shard_map/ppermute | solution.py:15
  29.0 1.9 %collective-permute-start.4 = (bf16[4,12,2,192]{3,1,2,0:T(8,128)(2,1)S(1)}, bf16[4,12,2,192]{3,1,2,0:T(8,128)(2,1)S(1)}, u32[]{:S(2)}, u32[]{:S(2)}) collective-permute-start(bf16[4,12,2,192]{3,1,2,0:T(8,128)(2,1)S(1)} %get-tuple-element.6), channel_id=1, source_target_pairs={{1,0},{2,1},{3,2},{4,3},{5,4},{6,5},{7,6},{9,8},{10,9},{11,10},{12... | collective-permute-start | bytes 110600 | tf_op jit(solution)/shard_map/ppermute | solution.py:17
  30.9 0.1 broadcast_and_fusion
  31.0 0.0 collective-permute-done.3
  31.0 3.6 %collective-permute-done.4 = bf16[4,12,2,192]{3,1,2,0:T(8,128)(2,1)S(1)} collective-permute-done((bf16[4,12,2,192]{3,1,2,0:T(8,128)(2,1)S(1)}, bf16[4,12,2,192]{3,1,2,0:T(8,128)(2,1)S(1)}, u32[]{:S(2)}, u32[]{:S(2)}) %collective-permute-start.4) | collective-permute-done | bytes 36896 | tf_op jit(solution)/shard_map/ppermute | solution.py:17
  34.6 0.7 %maximum_bitcast_fusion = bf16[4,12,1,36,192]{4,1,3,0,2:T(8,128)(2,1)S(1)} fusion(bf16[4,12,2,192]{3,1,2,0:T(8,128)(2,1)S(1)} %collective-permute-done.4, bf16[4,2,32,192]{3,1,2,0:T(2,128)(2,1)S(1)} %collective-permute-done.2, bf16[2,8,32,192]{3,1,2,0:T(8,128)(2,1)S(1)} %fusion.30, bf16[2,8,32,192]{3,1,2,0:T(8,128)(2,1)S(1)} %collective-permute-done, ...), kind=kLoop, calls=%fused_computation.12 | loop fusion | flops 3981312 | bytes 1327104 | tf_op jit(solution)/shard_map/broadcast_in_dim | solution.py:42
  35.3 0.7 %copy.24 = bf16[4,12,1,36,192]{4,0,3,1,2:T(4,128)(2,1)S(1)} copy(bf16[4,12,1,36,192]{4,1,3,0,2:T(8,128)(2,1)S(1)} %maximum_bitcast_fusion) | data formatting | bytes 1327104
  35.9 0.0 copy-start.2
  36.0 0.0 copy-start.7
  36.0 0.5 pad.clone
  36.4 0.1 copy.11
  36.6 0.1 slice.21
  36.7 0.0 copy-done
  36.7 0.0 copy-done.2
  36.7 0.0 copy-done.7
  36.7 2.5 %convert_multiply_fusion = (f32[2,10,8,5,192]{4,2,3,1,0:T(8,128)S(1)}, f32[2,10,8,5,192]{4,2,3,1,0:T(8,128)S(1)}) fusion(f32[192]{0:T(256)S(1)} %copy-done.2, bf16[3,3,3,192,192]{4,3,2,1,0:T(8,128)(2,1)S(1)} %copy-done, bf16[4,12,1,7,2,192]{5,3,4,1,0,2:T(8,128)(2,1)S(1)} %slice.21, bf16[4,12,1,8,5,192]{5,3,4,1,0,2:T(8,128)(2,1)S(1)} %copy.11, ...), kind=kOutput, calls=%fused_computation.20 | convolution fusion | flops 1596389376 | bytes 4215592 | tf_op jit(solution)/shard_map/conv_general_dilated | solution.py:41
  39.2 0.6 %copy.13 = f32[2,10,8,5,192]{4,0,3,2,1:T(2,128)S(1)} copy(f32[2,10,8,5,192]{4,2,3,1,0:T(8,128)S(1)} %get-tuple-element.9) | data formatting | bytes 1228800 | tf_op jit(solution)/shard_map/mul | solution.py:32
  39.8 0.0 copy-start.3
  39.8 0.2 slice_bitcast_fusion
  40.1 1.4 %fusion.18 = f32[1,2,10,34]{3,0,2,1:T(1,128)S(1)} fusion(f32[2,10,34,192]{3,0,2,1:T(2,128)S(1)} %slice_bitcast_fusion), kind=kOutput, calls=%fused_computation.18 | convolution fusion | flops 1566720 | bytes 524960 | tf_op jit(solution)/shard_map/dot_general | solution.py:32
  41.5 0.9 %copy.23 = f32[1,2,10,34]{1,3,2,0:T(8,128)} copy(f32[1,2,10,34]{3,0,2,1:T(1,128)S(1)} %fusion.18) | data formatting | bytes 5440 | tf_op jit(solution)/shard_map/dot_general | solution.py:32
  42.4 1.0 %fusion.36 = f32[2,10,34]{0,2,1:T(8,128)S(1)} fusion(f32[1,2,10,34]{1,3,2,0:T(8,128)} %copy.23), kind=kLoop, calls=%fused_computation.47 | loop fusion | flops 1360 | bytes 5440 | tf_op jit(solution)/shard_map/rsqrt | solution.py:33
  43.4 0.6 %copy.12 = f32[2,10,8,5,192]{4,0,3,2,1:T(2,128)S(1)} copy(f32[2,10,8,5,192]{4,2,3,1,0:T(8,128)S(1)} %get-tuple-element.10) | data formatting | bytes 1228800 | tf_op jit(solution)/shard_map/conv_general_dilated | solution.py:41
  44.0 0.0 copy-done.3
  44.0 1.4 %select_convert_fusion = bf16[2,10,34,192]{3,0,2,1:T(2,128)(2,1)S(1)} fusion(pred[10,34]{1,0:T(8,128)(4,1)S(1)} %broadcast_and_fusion, f32[2,10,1,40,192]{4,0,3,1,2:T(2,128)S(1)} %bitcast.51, f32[192]{0:T(256)S(1)} %copy-done.3, f32[2,10,34]{0,2,1:T(8,128)S(1)} %fusion.36, f32[192]{0:T(256)S(1)} %copy-done.2), kind=kLoop, calls=%fused_computation.30 | loop fusion | flops 1436160 | bytes 787956 | tf_op jit(solution)/shard_map/convert_element_type | solution.py:69
  45.4 0.0 copy-start.5
  45.4 0.0 copy-start.6
  45.5 2.4 %collective-permute-start.5 = (bf16[2,10,34,192]{3,0,2,1:T(2,128)(2,1)S(1)}, bf16[2,10,34,192]{3,0,2,1:T(2,128)(2,1)S(1)}, u32[]{:S(2)}, u32[]{:S(2)}) collective-permute-start(bf16[2,10,34,192]{3,0,2,1:T(2,128)(2,1)S(1)} %select_convert_fusion), channel_id=1, source_target_pairs={{0,32},{32,64},{64,96},{96,128},{128,160},{160,192},{192,224},{224... | collective-permute-start | bytes 783368 | tf_op jit(solution)/shard_map/ppermute | solution.py:27
  47.8 10.4 %collective-permute-done.5 = bf16[2,10,34,192]{3,0,2,1:T(2,128)(2,1)S(1)} collective-permute-done((bf16[2,10,34,192]{3,0,2,1:T(2,128)(2,1)S(1)}, bf16[2,10,34,192]{3,0,2,1:T(2,128)(2,1)S(1)}, u32[]{:S(2)}, u32[]{:S(2)}) %collective-permute-start.5) | collective-permute-done | bytes 261152 | tf_op jit(solution)/shard_map/ppermute | solution.py:27
  58.2 0.8 %maximum_bitcast_fusion.1 = bf16[4,10,1,34,192]{4,0,3,1,2:T(4,128)(2,1)S(1)} fusion(bf16[2,10,34,192]{3,0,2,1:T(2,128)(2,1)S(1)} %select_convert_fusion, bf16[2,10,34,192]{3,0,2,1:T(2,128)(2,1)S(1)} %collective-permute-done.5), kind=kLoop, calls=%fused_computation.29 | loop fusion | flops 1044480 | bytes 1044480 | tf_op jit(solution)/shard_map/broadcast_in_dim | solution.py:42
  59.0 0.4 pad.2
  59.4 0.1 copy.15
  59.5 0.1 slice.24
  59.6 0.0 copy-done.5
  59.6 0.0 copy-done.6
  59.6 0.0 copy-start.1
  59.7 0.0 copy-start.4
  59.7 2.0 %convolution_select_fusion = f32[2,8,8,5,192]{4,2,3,1,0:T(8,128)S(1)} fusion(bf16[3,3,3,192,192]{4,3,2,1,0:T(8,128)(2,1)S(1)} %copy-done.5, bf16[4,10,1,7,2,192]{5,3,4,1,0,2:T(8,128)(2,1)S(1)} %slice.24, bf16[4,10,1,8,5,192]{5,3,4,1,0,2:T(8,128)(2,1)S(1)} %copy.15, pred[8,5]{0,1:T(8,128)(4,1)S(1)} %copy-done.6), kind=kOutput, calls=%fused_computation.11 | convolution fusion | flops 1276723200 | bytes 3311656 | tf_op jit(solution)/shard_map/conv_general_dilated | solution.py:41
  61.7 0.2 copy.16
  61.9 0.0 copy-done.1
  61.9 0.0 copy-done.4
  61.9 0.2 fusion.32
  62.1 0.8 %copy.17 = bf16[2,8,32,192]{3,2,1,0:T(8,128)(2,1)} copy(bf16[2,8,32,192]{3,1,2,0:T(8,128)(2,1)S(1)} %fusion.32) | data formatting | bytes 393216 | tf_op jit(solution)/shard_map/convert_element_type | solution.py:73
  (3 shorter events, 0.0 us)
Async XLA Ops:
  0.0 36.7 %copy-start = (bf16[3,3,3,192,192]{4,3,2,1,0:T(8,128)(2,1)S(1)}, bf16[3,3,3,192,192]{4,3,2,1,0:T(8,128)(2,1)}, u32[]{:S(2)}) copy-start(bf16[3,3,3,192,192]{4,3,2,1,0:T(8,128)(2,1)} %param.9) | copy-start | bytes 5971972
  3.8 10.3 %collective-permute-start = (bf16[2,8,32,192]{3,1,2,0:T(8,128)(2,1)S(1)}, bf16[2,8,32,192]{3,1,2,0:T(8,128)(2,1)S(1)}, u32[]{:S(2)}, u32[]{:S(2)}) collective-permute-start(bf16[2,8,32,192]{3,1,2,0:T(8,128)(2,1)S(1)} %fusion.30), channel_id=1, source_target_pairs={{0,32},{32,64},{64,96},{96,128},{128,160},{160,192},{192,224},{224... | collective-permute-start | bytes 589832 | tf_op jit(solution)/shard_map/ppermute | solution.py:27
  14.3 5.1 %collective-permute-start.1 = (bf16[4,2,32,192]{3,1,2,0:T(2,128)(2,1)S(1)}, bf16[4,2,32,192]{3,1,2,0:T(2,128)(2,1)S(1)}, u32[]{:S(2)}, u32[]{:S(2)}) collective-permute-start(bf16[4,2,32,192]{3,1,2,0:T(2,128)(2,1)S(1)} %get-tuple-element.7), channel_id=1, source_target_pairs={{0,8},{8,16},{16,24},{1,9},{9,17},{17,25},{2,10},{10,18},{18,26},{... | collective-permute-start | bytes 294920 | tf_op jit(solution)/shard_map/ppermute | solution.py:15
  17.4 5.7 %collective-permute-start.2 = (bf16[4,2,32,192]{3,1,2,0:T(2,128)(2,1)S(1)}, bf16[4,2,32,192]{3,1,2,0:T(2,128)(2,1)S(1)}, u32[]{:S(2)}, u32[]{:S(2)}) collective-permute-start(bf16[4,2,32,192]{3,1,2,0:T(2,128)(2,1)S(1)} %get-tuple-element.8), channel_id=1, source_target_pairs={{8,0},{16,8},{24,16},{9,1},{17,9},{25,17},{10,2},{18,10},{26,18},{... | collective-permute-start | bytes 294920 | tf_op jit(solution)/shard_map/ppermute | solution.py:17
  23.2 7.8 %collective-permute-start.3 = (bf16[4,12,2,192]{3,1,2,0:T(8,128)(2,1)S(1)}, bf16[4,12,2,192]{3,1,2,0:T(8,128)(2,1)S(1)}, u32[]{:S(2)}, u32[]{:S(2)}) collective-permute-start(bf16[4,12,2,192]{3,1,2,0:T(8,128)(2,1)S(1)} %get-tuple-element.5), channel_id=1, source_target_pairs={{0,1},{1,2},{2,3},{3,4},{4,5},{5,6},{6,7},{8,9},{9,10},{10,11},{11... | collective-permute-start | bytes 110600 | tf_op jit(solution)/shard_map/ppermute | solution.py:15
  29.0 5.6 %collective-permute-start.4 = (bf16[4,12,2,192]{3,1,2,0:T(8,128)(2,1)S(1)}, bf16[4,12,2,192]{3,1,2,0:T(8,128)(2,1)S(1)}, u32[]{:S(2)}, u32[]{:S(2)}) collective-permute-start(bf16[4,12,2,192]{3,1,2,0:T(8,128)(2,1)S(1)} %get-tuple-element.6), channel_id=1, source_target_pairs={{1,0},{2,1},{3,2},{4,3},{5,4},{6,5},{7,6},{9,8},{10,9},{11,10},{12... | collective-permute-start | bytes 110600 | tf_op jit(solution)/shard_map/ppermute | solution.py:17
  35.9 0.7 %copy-start.2 = (f32[192]{0:T(256)S(1)}, f32[192]{0:T(256)}, u32[]{:S(2)}) copy-start(f32[192]{0:T(256)} %param.10) | copy-start | bytes 2308
  36.0 0.7 %copy-start.7 = (pred[8,5]{0,1:T(8,128)(4,1)S(1)}, pred[8,5]{0,1:T(8,128)(4,1)}, u32[]{:S(2)}) copy-start(pred[8,5]{0,1:T(8,128)(4,1)} %constant.47) | copy-start | bytes 124
  39.8 4.2 %copy-start.3 = (f32[192]{0:T(256)S(1)}, f32[192]{0:T(256)}, u32[]{:S(2)}) copy-start(f32[192]{0:T(256)} %param.11) | copy-start | bytes 2308
  45.4 14.2 %copy-start.5 = (bf16[3,3,3,192,192]{4,3,2,1,0:T(8,128)(2,1)S(1)}, bf16[3,3,3,192,192]{4,3,2,1,0:T(8,128)(2,1)}, u32[]{:S(2)}) copy-start(bf16[3,3,3,192,192]{4,3,2,1,0:T(8,128)(2,1)} %param.12) | copy-start | bytes 5971972
  45.4 14.2 %copy-start.6 = (pred[8,5]{0,1:T(8,128)(4,1)S(1)}, pred[8,5]{0,1:T(8,128)(4,1)}, u32[]{:S(2)}) copy-start(pred[8,5]{0,1:T(8,128)(4,1)} %constant.46) | copy-start | bytes 124
  45.5 12.8 %collective-permute-start.5 = (bf16[2,10,34,192]{3,0,2,1:T(2,128)(2,1)S(1)}, bf16[2,10,34,192]{3,0,2,1:T(2,128)(2,1)S(1)}, u32[]{:S(2)}, u32[]{:S(2)}) collective-permute-start(bf16[2,10,34,192]{3,0,2,1:T(2,128)(2,1)S(1)} %select_convert_fusion), channel_id=1, source_target_pairs={{0,32},{32,64},{64,96},{96,128},{128,160},{160,192},{192,224},{224... | collective-permute-start | bytes 783368 | tf_op jit(solution)/shard_map/ppermute | solution.py:27
  59.6 2.2 %copy-start.1 = (bf16[2,8,32,192]{3,2,1,0:T(8,128)(2,1)S(1)}, bf16[2,8,32,192]{3,2,1,0:T(8,128)(2,1)}, u32[]{:S(2)}) copy-start(bf16[2,8,32,192]{3,2,1,0:T(8,128)(2,1)} %param.7) | copy-start | bytes 589828
  59.7 2.2 %copy-start.4 = (f32[192]{0:T(256)S(1)}, f32[192]{0:T(256)}, u32[]{:S(2)}) copy-start(f32[192]{0:T(256)} %param.13) | copy-start | bytes 2308

commit v8 on v3

--- a/solution.py
+++ b/solution.py
@@ -31,12 +31,12 @@
     return values * lax.rsqrt(jnp.mean(values * values, axis=-1, keepdims=True) + 1e-06) * gain
 
 
-def conv_valid(stack, kernel):
+def conv_valid(stack, kernel, frame_pad=(0, 0)):
     out = lax.conv_general_dilated(
         stack[None],
         kernel,
         window_strides=(1, 1, 1),
-        padding="VALID",
+        padding=(frame_pad, (0, 0), (0, 0)),
         dimension_numbers=("NDHWC", "DHWIO", "NDHWC"),
         preferred_element_type=jnp.float32,
     )
@@ -61,9 +61,10 @@
     second_act = jax.nn.silu(rms_norm(hidden.astype(jnp.float32), second_gain))
     keep = inside("row", rows, 1)[:, None] & inside("col", cols, 1)[None, :]
     second_act = jnp.where(keep[None, :, :, None], second_act, 0.0).astype(jnp.bfloat16)
-    second_cache = shifted(second_act, "tm", 1)
-    second_conv = conv_valid(jnp.concatenate([second_cache, second_act], axis=0), second_weight)
-    decoded = values + second_conv + second_bias
+    ahead = conv_valid(second_act, second_weight[0:2], (0, 1)).astype(jnp.bfloat16)
+    behind = shifted(ahead, "tm", 1)
+    own = conv_valid(second_act, second_weight[1:3], (1, 0))
+    decoded = values + own + behind.astype(jnp.float32) + second_bias
     return decoded.astype(jnp.bfloat16)
 
 

time: 57.6 us -> 54.8 us (0.951)
  the two profiles are of different devices: /device:TPU:273 before, /device:TPU:401 now
where the time goes in v8:
time: 54.8 us; the launch traced here: 54.5 us
  waiting for transfers between devices  22.7 us (41%)
  starting transfers between devices  16.8 us (31%)
  other arithmetic  5.7 us (10%)
  matrix products  5.29 us (10%)
  local copies, waits for them, and re-layouts  3.69 us (7%)
    ppermute x2, waiting for transfers between devices, shifted(): lax.ppermute(value, axis, [(source, source + steps) for source in range(i...  14.7 us
    ppermute x2, starting transfers between devices, with_halo(): lax.ppermute(tail, axis, [(i, i + 1) for i in range(ends)])  8.88 us
    ppermute x2, waiting for transfers between devices, with_halo(): lax.ppermute(head, axis, [(i + 1, i) for i in range(ends)])  7.37 us
    conv_general_dilated x3, matrix products, conv_valid(): lax.conv_general_dilated(stack[None], kernel, window_strides=(1, 1, 1), p...  5.29 us
    ppermute x2, starting transfers between devices, shifted(): lax.ppermute(value, axis, [(source, source + steps) for source in range(i...  4.7 us
    ppermute x2, starting transfers between devices, with_halo(): lax.ppermute(head, axis, [(i + 1, i) for i in range(ends)])  3.21 us
    reduce_sum x2, other arithmetic, rms_norm(): jnp.mean(values * values, axis=-1, keepdims=True) + 1e-06  1.81 us
    conv_general_dilated x6, local copies, waits for them, and re-layouts, conv_valid(): lax.conv_general_dilated(stack[None], kernel, window_strides=(1, 1, 1), p...  1.37 us
  transfers between devices with their start and end apart: 6, of which 5 were waited for; matrix products, arithmetic and copies ran while one was open for 3% of the time, Pallas kernels for 0%

profile of v8, /device:TPU:401, one launch (start us, length us, event | category | flops | bytes accessed | tf_op | source)
XLA Modules:
  0.0 54.5 jit_solution(15239058298833725735)
XLA Ops:
  0.0 0.0 copy-start
  0.0 1.3 %fusion.32 = f32[2,8,32]{1,2,0:T(8,128)S(1)} fusion(bf16[2,8,32,192]{3,2,1,0:T(8,128)(2,1)} %param.7), kind=kLoop, calls=%fused_computation.35 | loop fusion | flops 294400 | bytes 198656 | tf_op jit(solution)/shard_map/reduce_sum | solution.py:31
  1.4 1.2 %fusion.39 = bf16[2,8,32,192]{3,1,2,0:T(8,128)(2,1)S(1)} fusion(f32[192]{0:T(256)} %param.8, f32[2,8,32]{1,2,0:T(8,128)S(1)} %add_rsqrt_fusion.1, bf16[2,8,32,192]{3,2,1,0:T(8,128)(2,1)} %param.7), kind=kLoop, calls=%fused_computation.42 | loop fusion | flops 786432 | bytes 396032 | tf_op jit(solution)/shard_map/convert_element_type | solution.py:56
  2.6 2.6 %collective-permute-start = (bf16[2,8,32,192]{3,1,2,0:T(8,128)(2,1)S(1)}, bf16[2,8,32,192]{3,1,2,0:T(8,128)(2,1)S(1)}, u32[]{:S(2)}, u32[]{:S(2)}) collective-permute-start(bf16[2,8,32,192]{3,1,2,0:T(8,128)(2,1)S(1)} %fusion.39), channel_id=1, source_target_pairs={{0,32},{32,64},{64,96},{96,128},{128,160},{160,192},{192,224},{224... | collective-permute-start | bytes 589832 | tf_op jit(solution)/shard_map/ppermute | solution.py:27
  5.3 7.6 %collective-permute-done = bf16[2,8,32,192]{3,1,2,0:T(8,128)(2,1)S(1)} collective-permute-done((bf16[2,8,32,192]{3,1,2,0:T(8,128)(2,1)S(1)}, bf16[2,8,32,192]{3,1,2,0:T(8,128)(2,1)S(1)}, u32[]{:S(2)}, u32[]{:S(2)}) %collective-permute-start) | collective-permute-done | bytes 196640 | tf_op jit(solution)/shard_map/ppermute | solution.py:27
  12.9 0.2 pad_maximum_fusion.1
  13.1 3.1 %collective-permute-start.1 = (bf16[4,2,32,192]{3,1,2,0:T(2,128)(2,1)S(1)}, bf16[4,2,32,192]{3,1,2,0:T(2,128)(2,1)S(1)}, u32[]{:S(2)}, u32[]{:S(2)}) collective-permute-start(bf16[4,2,32,192]{3,1,2,0:T(2,128)(2,1)S(1)} %get-tuple-element.7), channel_id=1, source_target_pairs={{0,8},{8,16},{16,24},{1,9},{9,17},{17,25},{2,10},{10,18},{18,26},{... | collective-permute-start | bytes 294920 | tf_op jit(solution)/shard_map/ppermute | solution.py:15
  16.2 1.3 %collective-permute-start.2 = (bf16[4,2,32,192]{3,1,2,0:T(2,128)(2,1)S(1)}, bf16[4,2,32,192]{3,1,2,0:T(2,128)(2,1)S(1)}, u32[]{:S(2)}, u32[]{:S(2)}) collective-permute-start(bf16[4,2,32,192]{3,1,2,0:T(2,128)(2,1)S(1)} %get-tuple-element.8), channel_id=1, source_target_pairs={{8,0},{16,8},{24,16},{9,1},{17,9},{25,17},{10,2},{18,10},{26,18},{... | collective-permute-start | bytes 294920 | tf_op jit(solution)/shard_map/ppermute | solution.py:17
  17.5 0.6 %collective-permute-done.1 = bf16[4,2,32,192]{3,1,2,0:T(2,128)(2,1)S(1)} collective-permute-done((bf16[4,2,32,192]{3,1,2,0:T(2,128)(2,1)S(1)}, bf16[4,2,32,192]{3,1,2,0:T(2,128)(2,1)S(1)}, u32[]{:S(2)}, u32[]{:S(2)}) %collective-permute-start.1) | collective-permute-done | bytes 98336 | tf_op jit(solution)/shard_map/ppermute | solution.py:15
  18.1 3.8 %collective-permute-done.2 = bf16[4,2,32,192]{3,1,2,0:T(2,128)(2,1)S(1)} collective-permute-done((bf16[4,2,32,192]{3,1,2,0:T(2,128)(2,1)S(1)}, bf16[4,2,32,192]{3,1,2,0:T(2,128)(2,1)S(1)}, u32[]{:S(2)}, u32[]{:S(2)}) %collective-permute-start.2) | collective-permute-done | bytes 98336 | tf_op jit(solution)/shard_map/ppermute | solution.py:17
  21.9 0.1 pad_maximum_fusion.5
  22.0 5.8 %collective-permute-start.3 = (bf16[4,12,2,192]{3,1,2,0:T(8,128)(2,1)S(1)}, bf16[4,12,2,192]{3,1,2,0:T(8,128)(2,1)S(1)}, u32[]{:S(2)}, u32[]{:S(2)}) collective-permute-start(bf16[4,12,2,192]{3,1,2,0:T(8,128)(2,1)S(1)} %get-tuple-element.5), channel_id=1, source_target_pairs={{0,1},{1,2},{2,3},{3,4},{4,5},{5,6},{6,7},{8,9},{9,10},{10,11},{11... | collective-permute-start | bytes 110600 | tf_op jit(solution)/shard_map/ppermute | solution.py:15
  27.8 1.9 %collective-permute-start.4 = (bf16[4,12,2,192]{3,1,2,0:T(8,128)(2,1)S(1)}, bf16[4,12,2,192]{3,1,2,0:T(8,128)(2,1)S(1)}, u32[]{:S(2)}, u32[]{:S(2)}) collective-permute-start(bf16[4,12,2,192]{3,1,2,0:T(8,128)(2,1)S(1)} %get-tuple-element.6), channel_id=1, source_target_pairs={{1,0},{2,1},{3,2},{4,3},{5,4},{6,5},{7,6},{9,8},{10,9},{11,10},{12... | collective-permute-start | bytes 110600 | tf_op jit(solution)/shard_map/ppermute | solution.py:17
  29.7 0.1 broadcast_and_fusion
  29.8 0.0 collective-permute-done.3
  29.8 3.6 %collective-permute-done.4 = bf16[4,12,2,192]{3,1,2,0:T(8,128)(2,1)S(1)} collective-permute-done((bf16[4,12,2,192]{3,1,2,0:T(8,128)(2,1)S(1)}, bf16[4,12,2,192]{3,1,2,0:T(8,128)(2,1)S(1)}, u32[]{:S(2)}, u32[]{:S(2)}) %collective-permute-start.4) | collective-permute-done | bytes 36896 | tf_op jit(solution)/shard_map/ppermute | solution.py:17
  33.4 0.7 %maximum_bitcast_fusion = bf16[4,12,1,36,192]{4,1,3,0,2:T(8,128)(2,1)S(1)} fusion(bf16[4,12,2,192]{3,1,2,0:T(8,128)(2,1)S(1)} %collective-permute-done.4, bf16[4,2,32,192]{3,1,2,0:T(2,128)(2,1)S(1)} %collective-permute-done.2, bf16[2,8,32,192]{3,1,2,0:T(8,128)(2,1)S(1)} %fusion.39, bf16[2,8,32,192]{3,1,2,0:T(8,128)(2,1)S(1)} %collective-permute-done, ...), kind=kLoop, calls=%fused_computation.16 | loop fusion | flops 3981312 | bytes 1327104 | tf_op jit(solution)/shard_map/broadcast_in_dim | solution.py:36
  34.0 0.3 pad
  34.3 0.0 copy-start.2
  34.3 0.0 copy-start.7
  34.3 0.4 copy.11
  34.7 0.1 slice.31
  34.8 0.0 copy-done
  34.8 0.2 copy-done.2
  35.0 0.0 copy-done.7
  35.0 2.5 %fusion.43 = (f32[2,10,8,5,192]{4,2,3,1,0:T(8,128)S(1)}, f32[2,10,8,5,192]{4,2,3,1,0:T(8,128)S(1)}) fusion(f32[192]{0:T(256)S(1)} %copy-done.2, bf16[3,3,3,192,192]{4,3,2,1,0:T(8,128)(2,1)S(1)} %copy-done, bf16[4,12,1,7,2,192]{5,3,4,1,0,2:T(8,128)(2,1)S(1)} %slice.31, bf16[4,12,1,8,5,192]{5,3,4,1,0,2:T(8,128)(2,1)S(1)} %copy.11, pred[8,5]{0,1:T(8,128)(4,1)S(1)} %copy-done.7), kind=kOutput, calls=%fused_computation.47 | convolution fusion | flops 1596235776 | bytes 4215592 | tf_op jit(solution)/shard_map/conv_general_dilated | solution.py:35
  37.5 0.6 %copy.13 = f32[2,10,8,5,192]{4,0,3,2,1:T(2,128)S(1)} copy(f32[2,10,8,5,192]{4,2,3,1,0:T(8,128)S(1)} %get-tuple-element.10) | data formatting | bytes 1228800 | tf_op jit(solution)/shard_map/conv_general_dilated | solution.py:35
  38.1 0.0 copy-start.3
  38.1 0.5 multiply_reduce_fusion
  38.7 0.6 %copy.12 = f32[2,10,8,5,192]{4,0,3,2,1:T(2,128)S(1)} copy(f32[2,10,8,5,192]{4,2,3,1,0:T(8,128)S(1)} %get-tuple-element.9) | data formatting | bytes 1228800 | tf_op jit(solution)/shard_map/convert_element_type | solution.py:61
  39.3 0.0 copy-start.5
  39.3 0.0 copy-start.6
  39.3 0.0 copy-done.3
  39.3 1.3 %fusion.44 = bf16[2,10,1,34,192]{4,0,3,1,2:T(2,128)(2,1)S(1)} fusion(f32[192]{0:T(256)S(1)} %copy-done.3, f32[2,10,34]{0,2,1:T(8,128)S(1)} %add_rsqrt_fusion, f32[2,10,1,40,192]{4,0,3,1,2:T(2,128)S(1)} %bitcast.47, pred[10,34]{1,0:T(8,128)(4,1)S(1)} %broadcast_and_fusion), kind=kLoop, calls=%fused_computation.48 | loop fusion | flops 1044480 | bytes 787188 | tf_op jit(solution)/shard_map/convert_element_type | solution.py:63
  40.7 0.3 pad.2
  41.1 0.0 copy-done.5
  41.1 0.0 copy-done.6
  41.2 1.4 %fusion.21 = bf16[2,8,8,5,192]{4,2,3,1,0:T(8,128)(2,1)S(1)} fusion(bf16[3,3,3,192,192]{4,3,2,1,0:T(8,128)(2,1)S(1)} %copy-done.5, pred[8,5]{0,1:T(8,128)(4,1)S(1)} %copy-done.6, bf16[2,10,1,7,2,192]{5,3,4,1,0,2:T(8,128)(2,1)S(1)} %slice.34, bf16[2,10,1,8,5,192]{5,3,4,1,0,2:T(8,128)(2,1)S(1)} %copy.15), kind=kOutput, calls=%fused_computation.15 | convolution fusion | flops 638545920 | bytes 2589696 | tf_op jit(solution)/shard_map/conv_general_dilated | solution.py:35
  42.6 0.1 copy.17
  42.7 0.0 copy-start.1
  42.7 0.0 copy-start.4
  42.7 2.1 %collective-permute-start.5 = (bf16[2,8,32,192]{3,1,2,0:T(8,128)(2,1)S(1)}, bf16[2,8,32,192]{3,1,2,0:T(8,128)(2,1)S(1)}, u32[]{:S(2)}, u32[]{:S(2)}) collective-permute-start(bf16[2,8,32,192]{3,1,2,0:T(8,128)(2,1)S(1)} %slice_bitcast_fusion.2), channel_id=1, source_target_pairs={{0,32},{32,64},{64,96},{96,128},{128,160},{160,192},{192,224},{224... | collective-permute-start | bytes 589832 | tf_op jit(solution)/shard_map/ppermute | solution.py:27
  44.8 1.4 %fusion.15 = f32[2,8,8,5,192]{4,2,3,1,0:T(8,128)S(1)} fusion(bf16[3,3,3,192,192]{4,3,2,1,0:T(8,128)(2,1)S(1)} %copy-done.5, pred[8,5]{0,1:T(8,128)(4,1)S(1)} %copy-done.6, bf16[2,10,1,7,2,192]{5,3,4,1,0,2:T(8,128)(2,1)S(1)} %slice.34, bf16[2,10,1,8,5,192]{5,3,4,1,0,2:T(8,128)(2,1)S(1)} %copy.15), kind=kOutput, calls=%fused_computation.13 | convolution fusion | flops 638423040 | bytes 2835456 | tf_op jit(solution)/shard_map/conv_general_dilated | solution.py:35
  46.2 0.2 copy.16
  46.4 7.1 %collective-permute-done.5 = bf16[2,8,32,192]{3,1,2,0:T(8,128)(2,1)S(1)} collective-permute-done((bf16[2,8,32,192]{3,1,2,0:T(8,128)(2,1)S(1)}, bf16[2,8,32,192]{3,1,2,0:T(8,128)(2,1)S(1)}, u32[]{:S(2)}, u32[]{:S(2)}) %collective-permute-start.5) | collective-permute-done | bytes 196640 | tf_op jit(solution)/shard_map/ppermute | solution.py:27
  53.5 0.0 copy-done.1
  53.5 0.0 copy-done.4
  53.5 0.2 fusion.42
  53.7 0.8 %copy.18 = bf16[2,8,32,192]{3,2,1,0:T(8,128)(2,1)} copy(bf16[2,8,32,192]{3,1,2,0:T(8,128)(2,1)S(1)} %fusion.42) | data formatting | bytes 393216 | tf_op jit(solution)/shard_map/convert_element_type | solution.py:68
  (7 shorter events, 0.2 us)
Async XLA Ops:
  0.0 34.8 %copy-start = (bf16[3,3,3,192,192]{4,3,2,1,0:T(8,128)(2,1)S(1)}, bf16[3,3,3,192,192]{4,3,2,1,0:T(8,128)(2,1)}, u32[]{:S(2)}) copy-start(bf16[3,3,3,192,192]{4,3,2,1,0:T(8,128)(2,1)} %param.9) | copy-start | bytes 5971972
  2.6 10.3 %collective-permute-start = (bf16[2,8,32,192]{3,1,2,0:T(8,128)(2,1)S(1)}, bf16[2,8,32,192]{3,1,2,0:T(8,128)(2,1)S(1)}, u32[]{:S(2)}, u32[]{:S(2)}) collective-permute-start(bf16[2,8,32,192]{3,1,2,0:T(8,128)(2,1)S(1)} %fusion.39), channel_id=1, source_target_pairs={{0,32},{32,64},{64,96},{96,128},{128,160},{160,192},{192,224},{224... | collective-permute-start | bytes 589832 | tf_op jit(solution)/shard_map/ppermute | solution.py:27
  13.1 5.1 %collective-permute-start.1 = (bf16[4,2,32,192]{3,1,2,0:T(2,128)(2,1)S(1)}, bf16[4,2,32,192]{3,1,2,0:T(2,128)(2,1)S(1)}, u32[]{:S(2)}, u32[]{:S(2)}) collective-permute-start(bf16[4,2,32,192]{3,1,2,0:T(2,128)(2,1)S(1)} %get-tuple-element.7), channel_id=1, source_target_pairs={{0,8},{8,16},{16,24},{1,9},{9,17},{17,25},{2,10},{10,18},{18,26},{... | collective-permute-start | bytes 294920 | tf_op jit(solution)/shard_map/ppermute | solution.py:15
  16.2 5.7 %collective-permute-start.2 = (bf16[4,2,32,192]{3,1,2,0:T(2,128)(2,1)S(1)}, bf16[4,2,32,192]{3,1,2,0:T(2,128)(2,1)S(1)}, u32[]{:S(2)}, u32[]{:S(2)}) collective-permute-start(bf16[4,2,32,192]{3,1,2,0:T(2,128)(2,1)S(1)} %get-tuple-element.8), channel_id=1, source_target_pairs={{8,0},{16,8},{24,16},{9,1},{17,9},{25,17},{10,2},{18,10},{26,18},{... | collective-permute-start | bytes 294920 | tf_op jit(solution)/shard_map/ppermute | solution.py:17
  22.0 7.8 %collective-permute-start.3 = (bf16[4,12,2,192]{3,1,2,0:T(8,128)(2,1)S(1)}, bf16[4,12,2,192]{3,1,2,0:T(8,128)(2,1)S(1)}, u32[]{:S(2)}, u32[]{:S(2)}) collective-permute-start(bf16[4,12,2,192]{3,1,2,0:T(8,128)(2,1)S(1)} %get-tuple-element.5), channel_id=1, source_target_pairs={{0,1},{1,2},{2,3},{3,4},{4,5},{5,6},{6,7},{8,9},{9,10},{10,11},{11... | collective-permute-start | bytes 110600 | tf_op jit(solution)/shard_map/ppermute | solution.py:15
  27.8 5.6 %collective-permute-start.4 = (bf16[4,12,2,192]{3,1,2,0:T(8,128)(2,1)S(1)}, bf16[4,12,2,192]{3,1,2,0:T(8,128)(2,1)S(1)}, u32[]{:S(2)}, u32[]{:S(2)}) collective-permute-start(bf16[4,12,2,192]{3,1,2,0:T(8,128)(2,1)S(1)} %get-tuple-element.6), channel_id=1, source_target_pairs={{1,0},{2,1},{3,2},{4,3},{5,4},{6,5},{7,6},{9,8},{10,9},{11,10},{12... | collective-permute-start | bytes 110600 | tf_op jit(solution)/shard_map/ppermute | solution.py:17
  34.3 0.7 %copy-start.2 = (f32[192]{0:T(256)S(1)}, f32[192]{0:T(256)}, u32[]{:S(2)}) copy-start(f32[192]{0:T(256)} %param.10) | copy-start | bytes 2308
  34.3 0.7 %copy-start.7 = (pred[8,5]{0,1:T(8,128)(4,1)S(1)}, pred[8,5]{0,1:T(8,128)(4,1)}, u32[]{:S(2)}) copy-start(pred[8,5]{0,1:T(8,128)(4,1)} %constant.51) | copy-start | bytes 124
  38.1 1.2 %copy-start.3 = (f32[192]{0:T(256)S(1)}, f32[192]{0:T(256)}, u32[]{:S(2)}) copy-start(f32[192]{0:T(256)} %param.11) | copy-start | bytes 2308
  39.3 1.8 %copy-start.5 = (bf16[3,3,3,192,192]{4,3,2,1,0:T(8,128)(2,1)S(1)}, bf16[3,3,3,192,192]{4,3,2,1,0:T(8,128)(2,1)}, u32[]{:S(2)}) copy-start(bf16[3,3,3,192,192]{4,3,2,1,0:T(8,128)(2,1)} %param.12) | copy-start | bytes 5971972
  39.3 1.8 %copy-start.6 = (pred[8,5]{0,1:T(8,128)(4,1)S(1)}, pred[8,5]{0,1:T(8,128)(4,1)}, u32[]{:S(2)}) copy-start(pred[8,5]{0,1:T(8,128)(4,1)} %constant.50) | copy-start | bytes 124
  42.7 10.8 %copy-start.1 = (bf16[2,8,32,192]{3,2,1,0:T(8,128)(2,1)S(1)}, bf16[2,8,32,192]{3,2,1,0:T(8,128)(2,1)}, u32[]{:S(2)}) copy-start(bf16[2,8,32,192]{3,2,1,0:T(8,128)(2,1)} %param.7) | copy-start | bytes 589828
  42.7 10.8 %copy-start.4 = (f32[192]{0:T(256)S(1)}, f32[192]{0:T(256)}, u32[]{:S(2)}) copy-start(f32[192]{0:T(256)} %param.13) | copy-start | bytes 2308
  42.7 10.8 %collective-permute-start.5 = (bf16[2,8,32,192]{3,1,2,0:T(8,128)(2,1)S(1)}, bf16[2,8,32,192]{3,1,2,0:T(8,128)(2,1)S(1)}, u32[]{:S(2)}, u32[]{:S(2)}) collective-permute-start(bf16[2,8,32,192]{3,1,2,0:T(8,128)(2,1)S(1)} %slice_bitcast_fusion.2), channel_id=1, source_target_pairs={{0,32},{32,64},{64,96},{96,128},{128,160},{160,192},{192,224},{224... | collective-permute-start | bytes 589832 | tf_op jit(solution)/shard_map/ppermute | solution.py:27

commit v9 on v8

--- a/solution.py
+++ b/solution.py
@@ -7,14 +7,18 @@
 def with_halo(cells, sides, width):
     for axis, dim in sides:
         count = lax.axis_size(axis)
-        ends = count - 1
+        even = lax.axis_index(axis) % 2 == 0
         head = lax.slice_in_dim(cells, 0, width, axis=dim)
         tail = lax.slice_in_dim(cells, cells.shape[dim] - width, cells.shape[dim], axis=dim)
+        first = [(i, i ^ 1) for i in range(count - count % 2)]
+        second = [(i, i + 1 if i % 2 else i - 1) for i in range(1, count - 1)]
+        got_first = lax.ppermute(jnp.where(even, tail, head), axis, first)
+        got_second = lax.ppermute(jnp.where(even, head, tail), axis, second)
         cells = jnp.concatenate(
             [
-                lax.ppermute(tail, axis, [(i, i + 1) for i in range(ends)]),
+                jnp.where(even, got_second, got_first),
                 cells,
-                lax.ppermute(head, axis, [(i + 1, i) for i in range(ends)]),
+                jnp.where(even, got_first, got_second),
             ],
             axis=dim,
         )
@@ -43,6 +47,23 @@
     return out[0]
 
 
+def conv_folded(stack, kernel):
+    taps = kernel.shape[0]
+    count = stack.shape[0] - taps + 1
+    wide = jnp.concatenate([stack[p : p + count] for p in range(taps)], axis=-1)
+    folded = jnp.transpose(kernel, (1, 2, 0, 3, 4)).reshape(
+        kernel.shape[1], kernel.shape[2], taps * kernel.shape[3], kernel.shape[4]
+    )
+    return lax.conv_general_dilated(
+        wide,
+        folded,
+        window_strides=(1, 1),
+        padding="VALID",
+        dimension_numbers=("NHWC", "HWIO", "NHWC"),
+        preferred_element_type=jnp.float32,
+    )
+
+
 def inside(axis, size, width):
     total = size * lax.axis_size(axis)
     start = lax.axis_index(axis) * size - width
@@ -56,7 +77,7 @@
     first_act = jax.nn.silu(rms_norm(values, first_gain)).astype(jnp.bfloat16)
     stack = jnp.concatenate([shifted(first_act, "tm", 1), first_act], axis=0)
     first_ext = with_halo(stack, (("row", 1), ("col", 2)), 2)
-    first_conv = conv_valid(first_ext, first_weight)
+    first_conv = conv_folded(first_ext, first_weight)
     hidden = (first_conv + first_bias).astype(jnp.bfloat16)
     second_act = jax.nn.silu(rms_norm(hidden.astype(jnp.float32), second_gain))
     keep = inside("row", rows, 1)[:, None] & inside("col", cols, 1)[None, :]

time: 54.8 us -> 57.5 us (1.049)
  the two profiles are of different devices: /device:TPU:401 before, /device:TPU:404 now
where the time goes in v9:
time: 57.5 us; the launch traced here: 57.1 us
  waiting for transfers between devices  24.1 us (42%)
  starting transfers between devices  14.4 us (25%)
  other arithmetic  6.55 us (11%)
  local copies, waits for them, and re-layouts  6.35 us (11%)
  matrix products  5.31 us (9%)
    ppermute x2, waiting for transfers between devices, shifted(): lax.ppermute(value, axis, [(source, source + steps) for source in range(i...  16.4 us
    ppermute x2, waiting for transfers between devices, with_halo(): got_second = lax.ppermute(jnp.where(even, head, tail), axis, second)  5.88 us
    ppermute x2, starting transfers between devices, with_halo(): got_first = lax.ppermute(jnp.where(even, tail, head), axis, first)  5.03 us
    ppermute x2, starting transfers between devices, shifted(): lax.ppermute(value, axis, [(source, source + steps) for source in range(i...  4.98 us
    ppermute x2, starting transfers between devices, with_halo(): got_second = lax.ppermute(jnp.where(even, head, tail), axis, second)  4.38 us
    conv_general_dilated x2, matrix products, conv_valid(): lax.conv_general_dilated(stack[None], kernel, window_strides=(1, 1, 1), p...  2.82 us
    conv_general_dilated x1, matrix products, conv_folded(): lax.conv_general_dilated(wide, folded, window_strides=(1, 1), padding='VA...  2.49 us
    unnamed x18, local copies, waits for them, and re-layouts  2.4 us
  transfers between devices with their start and end apart: 6, of which 5 were waited for; matrix products, arithmetic and copies ran while one was open for 3% of the time, Pallas kernels for 0%

profile of v9, /device:TPU:404, one launch (start us, length us, event | category | flops | bytes accessed | tf_op | source)
XLA Modules:
  0.0 57.1 jit_solution(15532436764986370734)
XLA Ops:
  0.0 1.2 %fusion.34 = f32[2,8,32]{1,2,0:T(8,128)S(1)} fusion(bf16[2,8,32,192]{3,2,1,0:T(8,128)(2,1)} %param.7), kind=kLoop, calls=%fused_computation.30 | loop fusion | flops 294400 | bytes 198656 | tf_op jit(solution)/shard_map/reduce_sum | solution.py:35
  1.2 0.0 copy-start
  1.2 1.4 %fusion.41 = bf16[2,8,32,192]{3,1,2,0:T(8,128)(2,1)S(1)} fusion(f32[192]{0:T(256)} %param.8, f32[2,8,32]{1,2,0:T(8,128)S(1)} %add_rsqrt_fusion.1, bf16[2,8,32,192]{3,2,1,0:T(8,128)(2,1)} %param.7), kind=kLoop, calls=%fused_computation.37 | loop fusion | flops 786432 | bytes 396032 | tf_op jit(solution)/shard_map/convert_element_type | solution.py:77
  2.6 2.9 %collective-permute-start = (bf16[2,8,32,192]{3,1,2,0:T(8,128)(2,1)S(1)}, bf16[2,8,32,192]{3,1,2,0:T(8,128)(2,1)S(1)}, u32[]{:S(2)}, u32[]{:S(2)}) collective-permute-start(bf16[2,8,32,192]{3,1,2,0:T(8,128)(2,1)S(1)} %fusion.41), channel_id=1, source_target_pairs={{0,32},{32,64},{64,96},{96,128},{128,160},{160,192},{192,224},{224... | collective-permute-start | bytes 589832 | tf_op jit(solution)/shard_map/ppermute | solution.py:31
  5.6 8.2 %collective-permute-done = bf16[2,8,32,192]{3,1,2,0:T(8,128)(2,1)S(1)} collective-permute-done((bf16[2,8,32,192]{3,1,2,0:T(8,128)(2,1)S(1)}, bf16[2,8,32,192]{3,1,2,0:T(8,128)(2,1)S(1)}, u32[]{:S(2)}, u32[]{:S(2)}) %collective-permute-start) | collective-permute-done | bytes 196640 | tf_op jit(solution)/shard_map/ppermute | solution.py:31
  13.8 0.3 broadcast_select_fusion.3
  14.1 3.1 %collective-permute-start.2 = (bf16[4,2,32,192]{3,1,2,0:T(2,128)(2,1)S(1)}, bf16[4,2,32,192]{3,1,2,0:T(2,128)(2,1)S(1)}, u32[]{:S(2)}, u32[]{:S(2)}) collective-permute-start(bf16[4,2,32,192]{3,1,2,0:T(2,128)(2,1)S(1)} %bitcast.68), channel_id=1, source_target_pairs={{0,8},{8,0},{16,24},{24,16},{1,9},{9,1},{17,25},{25,17},{2,10},{10... | collective-permute-start | bytes 294920 | tf_op jit(solution)/shard_map/ppermute | solution.py:15
  17.2 1.9 %collective-permute-start.1 = (bf16[4,2,32,192]{3,1,2,0:T(2,128)(2,1)S(1)}, bf16[4,2,32,192]{3,1,2,0:T(2,128)(2,1)S(1)}, u32[]{:S(2)}, u32[]{:S(2)}) collective-permute-start(bf16[4,2,32,192]{3,1,2,0:T(2,128)(2,1)S(1)} %get-tuple-element.8), channel_id=1, source_target_pairs={{8,16},{16,8},{9,17},{17,9},{10,18},{18,10},{11,19},{19,11},{12,20... | collective-permute-start | bytes 294920 | tf_op jit(solution)/shard_map/ppermute | solution.py:16
  19.1 1.8 %collective-permute-done.2 = bf16[4,2,32,192]{3,1,2,0:T(2,128)(2,1)S(1)} collective-permute-done((bf16[4,2,32,192]{3,1,2,0:T(2,128)(2,1)S(1)}, bf16[4,2,32,192]{3,1,2,0:T(2,128)(2,1)S(1)}, u32[]{:S(2)}, u32[]{:S(2)}) %collective-permute-start.2) | collective-permute-done | bytes 98336 | tf_op jit(solution)/shard_map/ppermute | solution.py:15
  21.0 3.1 %collective-permute-done.1 = bf16[4,2,32,192]{3,1,2,0:T(2,128)(2,1)S(1)} collective-permute-done((bf16[4,2,32,192]{3,1,2,0:T(2,128)(2,1)S(1)}, bf16[4,2,32,192]{3,1,2,0:T(2,128)(2,1)S(1)}, u32[]{:S(2)}, u32[]{:S(2)}) %collective-permute-start.1) | collective-permute-done | bytes 98336 | tf_op jit(solution)/shard_map/ppermute | solution.py:16
  24.1 0.1 broadcast_select_fusion.7
  24.2 1.9 %collective-permute-start.4 = (bf16[4,12,2,192]{3,1,2,0:T(8,128)(2,1)S(1)}, bf16[4,12,2,192]{3,1,2,0:T(8,128)(2,1)S(1)}, u32[]{:S(2)}, u32[]{:S(2)}) collective-permute-start(bf16[4,12,2,192]{3,1,2,0:T(8,128)(2,1)S(1)} %broadcast_select_fusion.6), channel_id=1, source_target_pairs={{0,1},{1,0},{2,3},{3,2},{4,5},{5,4},{6,7},{7,6},{8,9},{9,8},{10,11... | collective-permute-start | bytes 110600 | tf_op jit(solution)/shard_map/ppermute | solution.py:15
  26.1 2.5 %collective-permute-start.3 = (bf16[4,12,2,192]{3,1,2,0:T(8,128)(2,1)S(1)}, bf16[4,12,2,192]{3,1,2,0:T(8,128)(2,1)S(1)}, u32[]{:S(2)}, u32[]{:S(2)}) collective-permute-start(bf16[4,12,2,192]{3,1,2,0:T(8,128)(2,1)S(1)} %get-tuple-element.5), channel_id=1, source_target_pairs={{1,2},{2,1},{3,4},{4,3},{5,6},{6,5},{9,10},{10,9},{11,12},{12,11},... | collective-permute-start | bytes 110600 | tf_op jit(solution)/shard_map/ppermute | solution.py:16
  28.6 0.1 broadcast_and_fusion
  28.7 0.0 copy-done
  28.7 0.3 copy.24
  28.9 0.0 collective-permute-done.4
  29.0 2.8 %collective-permute-done.3 = bf16[4,12,2,192]{3,1,2,0:T(8,128)(2,1)S(1)} collective-permute-done((bf16[4,12,2,192]{3,1,2,0:T(8,128)(2,1)S(1)}, bf16[4,12,2,192]{3,1,2,0:T(8,128)(2,1)S(1)}, u32[]{:S(2)}, u32[]{:S(2)}) %collective-permute-start.3) | collective-permute-done | bytes 36896 | tf_op jit(solution)/shard_map/ppermute | solution.py:16
  31.7 0.7 %pad_maximum_fusion = bf16[4,12,36,192]{3,1,2,0:T(8,128)(2,1)S(1)} fusion(bf16[4,12,2,192]{3,1,2,0:T(8,128)(2,1)S(1)} %get-tuple-element.17, bf16[4,2,32,192]{3,1,2,0:T(2,128)(2,1)S(1)} %bitcast.62, bf16[2,8,32,192]{3,1,2,0:T(8,128)(2,1)S(1)} %fusion.41, bf16[2,8,32,192]{3,1,2,0:T(8,128)(2,1)S(1)} %collective-permute-done, ...), kind=kLoop, calls=%fused_computation.17 | loop fusion | flops 3981312 | bytes 1327104 | tf_op jit(solution)/shard_map/concatenate | solution.py:17
  32.4 0.1 fusion.54
  32.5 0.6 maximum_bitcast_fusion
  33.1 1.1 %copy.33 = bf16[12,2,36,576]{3,1,2,0:T(2,128)(2,1)S(1)} copy(bf16[12,2,36,576]{3,0,2,1:T(8,128)(2,1)S(1)} %maximum_bitcast_fusion) | data formatting | bytes 1990656
  34.3 1.0 %pad.clone = bf16[12,2,40,576]{3,1,2,0:T(2,128)(2,1)S(1)} pad(bf16[12,2,36,576]{3,1,2,0:T(2,128)(2,1)S(1)} %copy.33, bf16[]{:T(256)} %constant.55), padding=0_0x0_0x0_4x0_0 | pad | bytes 2101250 | tf_op jit(solution)/shard_map/concatenate | solution.py:53
  35.2 0.3 slice.46
  35.5 0.0 copy-start.5
  35.5 0.0 copy-start.7
  35.6 1.6 %fusion.4 = bf16[12,2,8,7,576]{4,1,3,2,0:T(2,128)(2,1)S(1)} fusion(bf16[12,2,7,2,576]{4,1,3,2,0:T(2,128)(2,1)S(1)} %slice.46, bf16[12,2,8,5,576]{4,1,3,2,0:T(2,128)(2,1)S(1)} %bitcast.54), kind=kLoop, calls=%fused_computation.5 | loop fusion | flops 4644864 | bytes 3041280 | tf_op jit(solution)/shard_map/conv_general_dilated | solution.py:57
  37.2 0.0 copy-done.5
  37.2 0.0 copy-done.7
  37.2 2.5 %multiply_reduce_fusion = (f32[10,16,5]{1,2,0:T(8,128)S(1)}, f32[10,16,5,192]{3,1,2,0:T(8,128)S(1)}) fusion(f32[192]{0:T(256)S(1)} %copy-done.5, bf16[3,3,576,192]{3,2,1,0:T(8,128)(2,1)S(1)} %bitcast.56, bf16[12,2,8,7,576]{4,1,3,2,0:T(2,128)(2,1)S(1)} %fusion.4, pred[16,5]{0,1:T(8,128)(4,1)S(1)} %copy-done.7), kind=kOutput, calls=%fused_computation.23 | convolution fusion | flops 1593445632 | bytes 4157392 | tf_op jit(solution)/shard_map/conv_general_dilated | solution.py:57
  39.7 0.5 copy.25
  40.2 0.0 copy-start.2
  40.2 0.1 reshape.76
  40.4 0.1 copy.26
  40.5 0.1 reshape.78
  40.7 0.2 copy-done.2
  40.9 0.0 copy-start.4
  40.9 0.0 copy-start.6
  40.9 0.3 fusion.45
  41.2 0.3 copy.34
  41.5 0.3 pad.2.clone
  41.9 0.7 %copy-done.4 = bf16[3,3,3,192,192]{4,3,2,1,0:T(8,128)(2,1)S(1)} copy-done((bf16[3,3,3,192,192]{4,3,2,1,0:T(8,128)(2,1)S(1)}, bf16[3,3,3,192,192]{4,3,2,1,0:T(8,128)(2,1)}, u32[]{:S(2)}) %copy-start.4) | copy-done | bytes 1990680
  42.6 0.0 copy-done.6
  42.6 1.4 %fusion.26 = bf16[2,8,8,5,192]{4,2,3,1,0:T(8,128)(2,1)S(1)} fusion(bf16[3,3,3,192,192]{4,3,2,1,0:T(8,128)(2,1)S(1)} %copy-done.4, pred[8,5]{0,1:T(8,128)(4,1)S(1)} %copy-done.6, bf16[2,10,1,7,2,192]{5,3,4,1,0,2:T(8,128)(2,1)S(1)} %slice.49, bf16[2,10,1,8,5,192]{5,3,4,1,0,2:T(8,128)(2,1)S(1)} %copy.29), kind=kOutput, calls=%fused_computation.16 | convolution fusion | flops 638545920 | bytes 2589696 | tf_op jit(solution)/shard_map/conv_general_dilated | solution.py:39
  44.1 0.1 copy.31
  44.2 0.0 copy-start.1
  44.2 0.0 copy-start.3
  44.2 2.1 %collective-permute-start.5 = (bf16[2,8,32,192]{3,1,2,0:T(8,128)(2,1)S(1)}, bf16[2,8,32,192]{3,1,2,0:T(8,128)(2,1)S(1)}, u32[]{:S(2)}, u32[]{:S(2)}) collective-permute-start(bf16[2,8,32,192]{3,1,2,0:T(8,128)(2,1)S(1)} %slice_bitcast_fusion.2), channel_id=1, source_target_pairs={{0,32},{32,64},{64,96},{96,128},{128,160},{160,192},{192,224},{224... | collective-permute-start | bytes 589832 | tf_op jit(solution)/shard_map/ppermute | solution.py:31
  46.2 1.4 %fusion.20 = f32[2,8,8,5,192]{4,2,3,1,0:T(8,128)S(1)} fusion(bf16[3,3,3,192,192]{4,3,2,1,0:T(8,128)(2,1)S(1)} %copy-done.4, pred[8,5]{0,1:T(8,128)(4,1)S(1)} %copy-done.6, bf16[2,10,1,7,2,192]{5,3,4,1,0,2:T(8,128)(2,1)S(1)} %slice.49, bf16[2,10,1,8,5,192]{5,3,4,1,0,2:T(8,128)(2,1)S(1)} %copy.29), kind=kOutput, calls=%fused_computation.14 | convolution fusion | flops 638423040 | bytes 2835456 | tf_op jit(solution)/shard_map/conv_general_dilated | solution.py:39
  47.7 0.2 copy.30
  47.9 8.3 %collective-permute-done.5 = bf16[2,8,32,192]{3,1,2,0:T(8,128)(2,1)S(1)} collective-permute-done((bf16[2,8,32,192]{3,1,2,0:T(8,128)(2,1)S(1)}, bf16[2,8,32,192]{3,1,2,0:T(8,128)(2,1)S(1)}, u32[]{:S(2)}, u32[]{:S(2)}) %collective-permute-start.5) | collective-permute-done | bytes 196640 | tf_op jit(solution)/shard_map/ppermute | solution.py:31
  56.1 0.0 copy-done.1
  56.1 0.0 copy-done.3
  56.1 0.2 fusion.44
  56.4 0.8 %copy.32 = bf16[2,8,32,192]{3,2,1,0:T(8,128)(2,1)} copy(bf16[2,8,32,192]{3,1,2,0:T(8,128)(2,1)S(1)} %fusion.44) | data formatting | bytes 393216 | tf_op jit(solution)/shard_map/convert_element_type | solution.py:89
  (12 shorter events, 0.2 us)
Async XLA Ops:
  1.2 27.5 %copy-start = (bf16[3,3,3,192,192]{4,3,2,1,0:T(8,128)(2,1)S(1)}, bf16[3,3,3,192,192]{4,3,2,1,0:T(8,128)(2,1)}, u32[]{:S(2)}) copy-start(bf16[3,3,3,192,192]{4,3,2,1,0:T(8,128)(2,1)} %param.9) | copy-start | bytes 5971972
  2.6 11.2 %collective-permute-start = (bf16[2,8,32,192]{3,1,2,0:T(8,128)(2,1)S(1)}, bf16[2,8,32,192]{3,1,2,0:T(8,128)(2,1)S(1)}, u32[]{:S(2)}, u32[]{:S(2)}) collective-permute-start(bf16[2,8,32,192]{3,1,2,0:T(8,128)(2,1)S(1)} %fusion.41), channel_id=1, source_target_pairs={{0,32},{32,64},{64,96},{96,128},{128,160},{160,192},{192,224},{224... | collective-permute-start | bytes 589832 | tf_op jit(solution)/shard_map/ppermute | solution.py:31
  14.1 6.9 %collective-permute-start.2 = (bf16[4,2,32,192]{3,1,2,0:T(2,128)(2,1)S(1)}, bf16[4,2,32,192]{3,1,2,0:T(2,128)(2,1)S(1)}, u32[]{:S(2)}, u32[]{:S(2)}) collective-permute-start(bf16[4,2,32,192]{3,1,2,0:T(2,128)(2,1)S(1)} %bitcast.68), channel_id=1, source_target_pairs={{0,8},{8,0},{16,24},{24,16},{1,9},{9,1},{17,25},{25,17},{2,10},{10... | collective-permute-start | bytes 294920 | tf_op jit(solution)/shard_map/ppermute | solution.py:15
  17.2 6.9 %collective-permute-start.1 = (bf16[4,2,32,192]{3,1,2,0:T(2,128)(2,1)S(1)}, bf16[4,2,32,192]{3,1,2,0:T(2,128)(2,1)S(1)}, u32[]{:S(2)}, u32[]{:S(2)}) collective-permute-start(bf16[4,2,32,192]{3,1,2,0:T(2,128)(2,1)S(1)} %get-tuple-element.8), channel_id=1, source_target_pairs={{8,16},{16,8},{9,17},{17,9},{10,18},{18,10},{11,19},{19,11},{12,20... | collective-permute-start | bytes 294920 | tf_op jit(solution)/shard_map/ppermute | solution.py:16
  24.2 4.7 %collective-permute-start.4 = (bf16[4,12,2,192]{3,1,2,0:T(8,128)(2,1)S(1)}, bf16[4,12,2,192]{3,1,2,0:T(8,128)(2,1)S(1)}, u32[]{:S(2)}, u32[]{:S(2)}) collective-permute-start(bf16[4,12,2,192]{3,1,2,0:T(8,128)(2,1)S(1)} %broadcast_select_fusion.6), channel_id=1, source_target_pairs={{0,1},{1,0},{2,3},{3,2},{4,5},{5,4},{6,7},{7,6},{8,9},{9,8},{10,11... | collective-permute-start | bytes 110600 | tf_op jit(solution)/shard_map/ppermute | solution.py:15
  26.1 5.6 %collective-permute-start.3 = (bf16[4,12,2,192]{3,1,2,0:T(8,128)(2,1)S(1)}, bf16[4,12,2,192]{3,1,2,0:T(8,128)(2,1)S(1)}, u32[]{:S(2)}, u32[]{:S(2)}) collective-permute-start(bf16[4,12,2,192]{3,1,2,0:T(8,128)(2,1)S(1)} %get-tuple-element.5), channel_id=1, source_target_pairs={{1,2},{2,1},{3,4},{4,3},{5,6},{6,5},{9,10},{10,9},{11,12},{12,11},... | collective-permute-start | bytes 110600 | tf_op jit(solution)/shard_map/ppermute | solution.py:16
  35.5 1.7 %copy-start.5 = (f32[192]{0:T(256)S(1)}, f32[192]{0:T(256)}, u32[]{:S(2)}) copy-start(f32[192]{0:T(256)} %param.10) | copy-start | bytes 2308
  35.5 1.7 %copy-start.7 = (pred[16,5]{0,1:T(8,128)(4,1)S(1)}, pred[16,5]{0,1:T(8,128)(4,1)}, u32[]{:S(2)}) copy-start(pred[16,5]{0,1:T(8,128)(4,1)} %constant.68) | copy-start | bytes 244
  40.2 0.7 %copy-start.2 = (f32[192]{0:T(256)S(1)}, f32[192]{0:T(256)}, u32[]{:S(2)}) copy-start(f32[192]{0:T(256)} %param.11) | copy-start | bytes 2308
  40.9 1.7 %copy-start.4 = (bf16[3,3,3,192,192]{4,3,2,1,0:T(8,128)(2,1)S(1)}, bf16[3,3,3,192,192]{4,3,2,1,0:T(8,128)(2,1)}, u32[]{:S(2)}) copy-start(bf16[3,3,3,192,192]{4,3,2,1,0:T(8,128)(2,1)} %param.12) | copy-start | bytes 5971972
  40.9 1.8 %copy-start.6 = (pred[8,5]{0,1:T(8,128)(4,1)S(1)}, pred[8,5]{0,1:T(8,128)(4,1)}, u32[]{:S(2)}) copy-start(pred[8,5]{0,1:T(8,128)(4,1)} %constant.67) | copy-start | bytes 124
  44.2 12.0 %copy-start.1 = (bf16[2,8,32,192]{3,2,1,0:T(8,128)(2,1)S(1)}, bf16[2,8,32,192]{3,2,1,0:T(8,128)(2,1)}, u32[]{:S(2)}) copy-start(bf16[2,8,32,192]{3,2,1,0:T(8,128)(2,1)} %param.7) | copy-start | bytes 589828
  44.2 12.0 %copy-start.3 = (f32[192]{0:T(256)S(1)}, f32[192]{0:T(256)}, u32[]{:S(2)}) copy-start(f32[192]{0:T(256)} %param.13) | copy-start | bytes 2308
  44.2 11.9 %collective-permute-start.5 = (bf16[2,8,32,192]{3,1,2,0:T(8,128)(2,1)S(1)}, bf16[2,8,32,192]{3,1,2,0:T(8,128)(2,1)S(1)}, u32[]{:S(2)}, u32[]{:S(2)}) collective-permute-start(bf16[2,8,32,192]{3,1,2,0:T(8,128)(2,1)S(1)} %slice_bitcast_fusion.2), channel_id=1, source_target_pairs={{0,32},{32,64},{64,96},{96,128},{128,160},{160,192},{192,224},{224... | collective-permute-start | bytes 589832 | tf_op jit(solution)/shard_map/ppermute | solution.py:31

commit v10 on v8

--- a/solution.py
+++ b/solution.py
@@ -7,14 +7,16 @@
 def with_halo(cells, sides, width):
     for axis, dim in sides:
         count = lax.axis_size(axis)
-        ends = count - 1
+        here = lax.axis_index(axis)
         head = lax.slice_in_dim(cells, 0, width, axis=dim)
         tail = lax.slice_in_dim(cells, cells.shape[dim] - width, cells.shape[dim], axis=dim)
+        before = lax.ppermute(tail, axis, [(i, (i + 1) % count) for i in range(count)])
+        after = lax.ppermute(head, axis, [((i + 1) % count, i) for i in range(count)])
         cells = jnp.concatenate(
             [
-                lax.ppermute(tail, axis, [(i, i + 1) for i in range(ends)]),
+                jnp.where(here > 0, before, jnp.zeros_like(before)),
                 cells,
-                lax.ppermute(head, axis, [(i + 1, i) for i in range(ends)]),
+                jnp.where(here < count - 1, after, jnp.zeros_like(after)),
             ],
             axis=dim,
         )
@@ -23,8 +25,8 @@
 
 def shifted(value, axis, steps):
     count = lax.axis_size(axis)
-    initial, last = (max(0, -steps), min(count, count - steps))
-    return lax.ppermute(value, axis, [(source, source + steps) for source in range(initial, last)])
+    moved = lax.ppermute(value, axis, [(i, (i + 1) % count) for i in range(count)])
+    return jnp.where(lax.axis_index(axis) > 0, moved, jnp.zeros_like(moved))
 
 
 def rms_norm(values, gain):

time: 54.8 us -> 59.5 us (1.086)
  the two profiles are of different devices: /device:TPU:401 before, /device:TPU:1 now
where the time goes in v10:
time: 59.5 us; the launch traced here: 59.2 us
  waiting for transfers between devices  25.8 us (43%)
  starting transfers between devices  16.7 us (28%)
  other arithmetic  7.43 us (12%)
  matrix products  5.28 us (9%)
  local copies, waits for them, and re-layouts  3.69 us (6%)
    ppermute x2, waiting for transfers between devices, shifted(): lax.ppermute(value, axis, [(i, (i + 1) % count) for i in range(count)])  20.7 us
    ppermute x2, starting transfers between devices, with_halo(): lax.ppermute(tail, axis, [(i, (i + 1) % count) for i in range(count)])  6.91 us
    ppermute x2, starting transfers between devices, shifted(): lax.ppermute(value, axis, [(i, (i + 1) % count) for i in range(count)])  6.42 us
    conv_general_dilated x3, matrix products, conv_valid(): lax.conv_general_dilated(stack[None], kernel, window_strides=(1, 1, 1), p...  5.28 us
    ppermute x2, starting transfers between devices, with_halo(): lax.ppermute(head, axis, [((i + 1) % count, i) for i in range(count)])  3.38 us
    ppermute x2, waiting for transfers between devices, with_halo(): lax.ppermute(head, axis, [((i + 1) % count, i) for i in range(count)])  3.16 us
    ppermute x2, waiting for transfers between devices, with_halo(): lax.ppermute(tail, axis, [(i, (i + 1) % count) for i in range(count)])  1.97 us
    reduce_sum x2, other arithmetic, rms_norm(): jnp.mean(values * values, axis=-1, keepdims=True) + 1e-06  1.81 us
  transfers between devices with their start and end apart: 6, of which 6 were waited for; matrix products, arithmetic and copies ran while one was open for 4% of the time, Pallas kernels for 0%

profile of v10, /device:TPU:1, one launch (start us, length us, event | category | flops | bytes accessed | tf_op | source)
XLA Modules:
  0.0 59.2 jit_solution(17608778056405596445)
XLA Ops:
  0.0 0.0 copy-start
  0.0 1.3 %fusion.32 = f32[2,8,32]{1,2,0:T(8,128)S(1)} fusion(bf16[2,8,32,192]{3,2,1,0:T(8,128)(2,1)} %param.7), kind=kLoop, calls=%fused_computation.35 | loop fusion | flops 294400 | bytes 198656 | tf_op jit(solution)/shard_map/reduce_sum | solution.py:33
  1.4 1.2 %fusion.39 = bf16[2,8,32,192]{3,1,2,0:T(8,128)(2,1)S(1)} fusion(f32[192]{0:T(256)} %param.8, f32[2,8,32]{1,2,0:T(8,128)S(1)} %add_rsqrt_fusion.1, bf16[2,8,32,192]{3,2,1,0:T(8,128)(2,1)} %param.7), kind=kLoop, calls=%fused_computation.42 | loop fusion | flops 786432 | bytes 396032 | tf_op jit(solution)/shard_map/convert_element_type | solution.py:58
  2.6 4.4 %collective-permute-start = (bf16[2,8,32,192]{3,1,2,0:T(8,128)(2,1)S(1)}, bf16[2,8,32,192]{3,1,2,0:T(8,128)(2,1)S(1)}, u32[]{:S(2)}, u32[]{:S(2)}) collective-permute-start(bf16[2,8,32,192]{3,1,2,0:T(8,128)(2,1)S(1)} %fusion.39), channel_id=1, source_target_pairs={{0,32},{32,64},{64,96},{96,128},{128,160},{160,192},{192,224},{224... | collective-permute-start | bytes 589832 | tf_op jit(solution)/shard_map/ppermute | solution.py:28
  7.0 13.5 %collective-permute-done = bf16[2,8,32,192]{3,1,2,0:T(8,128)(2,1)S(1)} collective-permute-done((bf16[2,8,32,192]{3,1,2,0:T(8,128)(2,1)S(1)}, bf16[2,8,32,192]{3,1,2,0:T(8,128)(2,1)S(1)}, u32[]{:S(2)}, u32[]{:S(2)}) %collective-permute-start) | collective-permute-done | bytes 196640 | tf_op jit(solution)/shard_map/ppermute | solution.py:28
  20.6 0.2 pad_maximum_fusion.1
  20.8 3.1 %collective-permute-start.1 = (bf16[4,2,32,192]{3,1,2,0:T(2,128)(2,1)S(1)}, bf16[4,2,32,192]{3,1,2,0:T(2,128)(2,1)S(1)}, u32[]{:S(2)}, u32[]{:S(2)}) collective-permute-start(bf16[4,2,32,192]{3,1,2,0:T(2,128)(2,1)S(1)} %get-tuple-element.7), channel_id=1, source_target_pairs={{0,8},{8,16},{16,24},{24,0},{1,9},{9,17},{17,25},{25,1},{2,10},{10... | collective-permute-start | bytes 294920 | tf_op jit(solution)/shard_map/ppermute | solution.py:13
  23.9 3.4 %collective-permute-start.2 = (bf16[4,2,32,192]{3,1,2,0:T(2,128)(2,1)S(1)}, bf16[4,2,32,192]{3,1,2,0:T(2,128)(2,1)S(1)}, u32[]{:S(2)}, u32[]{:S(2)}) collective-permute-start(bf16[4,2,32,192]{3,1,2,0:T(2,128)(2,1)S(1)} %get-tuple-element.8), channel_id=1, source_target_pairs={{8,0},{16,8},{24,16},{0,24},{9,1},{17,9},{25,17},{1,25},{10,2},{18... | collective-permute-start | bytes 294920 | tf_op jit(solution)/shard_map/ppermute | solution.py:14
  27.3 0.4 collective-permute-done.1
  27.7 0.1 broadcast_select_fusion.2
  27.8 1.9 %collective-permute-done.2 = bf16[4,2,32,192]{3,1,2,0:T(2,128)(2,1)S(1)} collective-permute-done((bf16[4,2,32,192]{3,1,2,0:T(2,128)(2,1)S(1)}, bf16[4,2,32,192]{3,1,2,0:T(2,128)(2,1)S(1)}, u32[]{:S(2)}, u32[]{:S(2)}) %collective-permute-start.2) | collective-permute-done | bytes 98336 | tf_op jit(solution)/shard_map/ppermute | solution.py:14
  29.7 0.1 broadcast_select_fusion
  29.8 0.7 %pad_maximum_fusion.5 = (bf16[4,12,2,192]{3,1,2,0:T(8,128)(2,1)}, bf16[4,12,2,192]{3,1,2,0:T(8,128)(2,1)S(1)}) fusion(bf16[4,2,32,192]{3,1,2,0:T(2,128)(2,1)S(1)} %broadcast_select_fusion, bf16[4,2,32,192]{3,1,2,0:T(2,128)(2,1)S(1)} %broadcast_select_fusion.2, bf16[2,8,32,192]{3,1,2,0:T(8,128)(2,1)S(1)} %fusion.39, ...), kind=kLoop, calls=%fused_computation.59 | loop fusion | flops 294912 | bytes 663552 | tf_op jit(solution)/shard_map/slice | solution.py:12
  30.5 3.8 %collective-permute-start.3 = (bf16[4,12,2,192]{3,1,2,0:T(8,128)(2,1)}, bf16[4,12,2,192]{3,1,2,0:T(8,128)(2,1)}, u32[]{:S(2)}, u32[]{:S(2)}) collective-permute-start(bf16[4,12,2,192]{3,1,2,0:T(8,128)(2,1)} %get-tuple-element.5), channel_id=1, source_target_pairs={{0,1},{1,2},{2,3},{3,4},{4,5},{5,6},{6,7},{7,0},{8,9},{9,10},{10,1... | collective-permute-start | bytes 110600 | tf_op jit(solution)/shard_map/ppermute | solution.py:13
  34.3 0.1 broadcast_and_fusion
  34.4 0.0 collective-permute-start.4
  34.4 1.6 %collective-permute-done.3 = bf16[4,12,2,192]{3,1,2,0:T(8,128)(2,1)} collective-permute-done((bf16[4,12,2,192]{3,1,2,0:T(8,128)(2,1)}, bf16[4,12,2,192]{3,1,2,0:T(8,128)(2,1)}, u32[]{:S(2)}, u32[]{:S(2)}) %collective-permute-start.3) | collective-permute-done | bytes 36896 | tf_op jit(solution)/shard_map/ppermute | solution.py:13
  35.9 0.8 %broadcast_select_fusion.4 = bf16[4,12,2,192]{3,1,2,0:T(8,128)(2,1)S(1)} fusion(bf16[4,12,2,192]{3,1,2,0:T(8,128)(2,1)} %collective-permute-done.3, pred[]{:T(512)S(6)} %gt.10), kind=kLoop, calls=%fused_computation.61 | loop fusion | flops 18432 | bytes 73729 | tf_op jit(solution)/shard_map/jit(_where)/select_n | solution.py:17
  36.8 1.3 %collective-permute-done.4 = bf16[4,12,2,192]{3,1,2,0:T(8,128)(2,1)S(1)} collective-permute-done((bf16[4,12,2,192]{3,1,2,0:T(8,128)(2,1)S(1)}, bf16[4,12,2,192]{3,1,2,0:T(8,128)(2,1)S(1)}, u32[]{:S(2)}, u32[]{:S(2)}) %collective-permute-start.4) | collective-permute-done | bytes 36896 | tf_op jit(solution)/shard_map/ppermute | solution.py:14
  38.1 0.7 %maximum_bitcast_fusion = bf16[4,12,1,36,192]{4,1,3,0,2:T(8,128)(2,1)S(1)} fusion(bf16[4,12,2,192]{3,1,2,0:T(8,128)(2,1)S(1)} %broadcast_select_fusion.3, bf16[4,2,32,192]{3,1,2,0:T(2,128)(2,1)S(1)} %broadcast_select_fusion, bf16[2,8,32,192]{3,1,2,0:T(8,128)(2,1)S(1)} %fusion.39, bf16[2,8,32,192]{3,1,2,0:T(8,128)(2,1)S(1)} %broadcast_select_fusion.1, ...), kind=kLoop, calls=%fused_computation.16 | loop fusion | flops 3981312 | bytes 1327104 | tf_op jit(solution)/shard_map/broadcast_in_dim | solution.py:38
  38.8 0.3 pad
  39.0 0.0 copy-start.2
  39.0 0.0 copy-start.7
  39.1 0.4 copy.11
  39.4 0.1 slice.31
  39.5 0.0 copy-done
  39.5 0.2 copy-done.2
  39.7 0.0 copy-done.7
  39.7 2.5 %fusion.43 = (f32[2,10,8,5,192]{4,2,3,1,0:T(8,128)S(1)}, f32[2,10,8,5,192]{4,2,3,1,0:T(8,128)S(1)}) fusion(f32[192]{0:T(256)S(1)} %copy-done.2, bf16[3,3,3,192,192]{4,3,2,1,0:T(8,128)(2,1)S(1)} %copy-done, bf16[4,12,1,7,2,192]{5,3,4,1,0,2:T(8,128)(2,1)S(1)} %slice.31, bf16[4,12,1,8,5,192]{5,3,4,1,0,2:T(8,128)(2,1)S(1)} %copy.11, pred[8,5]{0,1:T(8,128)(4,1)S(1)} %copy-done.7), kind=kOutput, calls=%fused_computation.47 | convolution fusion | flops 1596235776 | bytes 4215592 | tf_op jit(solution)/shard_map/conv_general_dilated | solution.py:37
  42.2 0.6 %copy.13 = f32[2,10,8,5,192]{4,0,3,2,1:T(2,128)S(1)} copy(f32[2,10,8,5,192]{4,2,3,1,0:T(8,128)S(1)} %get-tuple-element.10) | data formatting | bytes 1228800 | tf_op jit(solution)/shard_map/conv_general_dilated | solution.py:37
  42.8 0.0 copy-start.3
  42.9 0.5 multiply_reduce_fusion
  43.4 0.6 %copy.12 = f32[2,10,8,5,192]{4,0,3,2,1:T(2,128)S(1)} copy(f32[2,10,8,5,192]{4,2,3,1,0:T(8,128)S(1)} %get-tuple-element.9) | data formatting | bytes 1228800 | tf_op jit(solution)/shard_map/convert_element_type | solution.py:63
  44.0 0.0 copy-start.5
  44.0 0.0 copy-start.6
  44.1 0.0 copy-done.3
  44.1 1.3 %fusion.44 = bf16[2,10,1,34,192]{4,0,3,1,2:T(2,128)(2,1)S(1)} fusion(f32[192]{0:T(256)S(1)} %copy-done.3, f32[2,10,34]{0,2,1:T(8,128)S(1)} %add_rsqrt_fusion, f32[2,10,1,40,192]{4,0,3,1,2:T(2,128)S(1)} %bitcast.47, pred[10,34]{1,0:T(8,128)(4,1)S(1)} %broadcast_and_fusion), kind=kLoop, calls=%fused_computation.48 | loop fusion | flops 1044480 | bytes 787188 | tf_op jit(solution)/shard_map/convert_element_type | solution.py:65
  45.4 0.3 pad.2
  45.8 0.0 copy-done.5
  45.9 0.0 copy-done.6
  45.9 1.4 %fusion.21 = bf16[2,8,8,5,192]{4,2,3,1,0:T(8,128)(2,1)S(1)} fusion(bf16[3,3,3,192,192]{4,3,2,1,0:T(8,128)(2,1)S(1)} %copy-done.5, pred[8,5]{0,1:T(8,128)(4,1)S(1)} %copy-done.6, bf16[2,10,1,7,2,192]{5,3,4,1,0,2:T(8,128)(2,1)S(1)} %slice.34, bf16[2,10,1,8,5,192]{5,3,4,1,0,2:T(8,128)(2,1)S(1)} %copy.15), kind=kOutput, calls=%fused_computation.15 | convolution fusion | flops 638545920 | bytes 2589696 | tf_op jit(solution)/shard_map/conv_general_dilated | solution.py:37
  47.3 0.1 copy.17
  47.4 0.0 copy-start.1
  47.4 0.0 copy-start.4
  47.4 2.1 %collective-permute-start.5 = (bf16[2,8,32,192]{3,1,2,0:T(8,128)(2,1)S(1)}, bf16[2,8,32,192]{3,1,2,0:T(8,128)(2,1)S(1)}, u32[]{:S(2)}, u32[]{:S(2)}) collective-permute-start(bf16[2,8,32,192]{3,1,2,0:T(8,128)(2,1)S(1)} %slice_bitcast_fusion.2), channel_id=1, source_target_pairs={{0,32},{32,64},{64,96},{96,128},{128,160},{160,192},{192,224},{224... | collective-permute-start | bytes 589832 | tf_op jit(solution)/shard_map/ppermute | solution.py:28
  49.5 1.4 %fusion.15 = f32[2,8,8,5,192]{4,2,3,1,0:T(8,128)S(1)} fusion(bf16[3,3,3,192,192]{4,3,2,1,0:T(8,128)(2,1)S(1)} %copy-done.5, pred[8,5]{0,1:T(8,128)(4,1)S(1)} %copy-done.6, bf16[2,10,1,7,2,192]{5,3,4,1,0,2:T(8,128)(2,1)S(1)} %slice.34, bf16[2,10,1,8,5,192]{5,3,4,1,0,2:T(8,128)(2,1)S(1)} %copy.15), kind=kOutput, calls=%fused_computation.13 | convolution fusion | flops 638423040 | bytes 2835456 | tf_op jit(solution)/shard_map/conv_general_dilated | solution.py:37
  50.9 0.2 copy.16
  51.1 7.1 %collective-permute-done.5 = bf16[2,8,32,192]{3,1,2,0:T(8,128)(2,1)S(1)} collective-permute-done((bf16[2,8,32,192]{3,1,2,0:T(8,128)(2,1)S(1)}, bf16[2,8,32,192]{3,1,2,0:T(8,128)(2,1)S(1)}, u32[]{:S(2)}, u32[]{:S(2)}) %collective-permute-start.5) | collective-permute-done | bytes 196640 | tf_op jit(solution)/shard_map/ppermute | solution.py:28
  58.2 0.0 copy-done.1
  58.2 0.0 copy-done.4
  58.2 0.2 fusion.42
  58.4 0.8 %copy.18 = bf16[2,8,32,192]{3,2,1,0:T(8,128)(2,1)} copy(bf16[2,8,32,192]{3,1,2,0:T(8,128)(2,1)S(1)} %fusion.42) | data formatting | bytes 393216 | tf_op jit(solution)/shard_map/convert_element_type | solution.py:70
  (9 shorter events, 0.2 us)
Async XLA Ops:
  0.0 39.5 %copy-start = (bf16[3,3,3,192,192]{4,3,2,1,0:T(8,128)(2,1)S(1)}, bf16[3,3,3,192,192]{4,3,2,1,0:T(8,128)(2,1)}, u32[]{:S(2)}) copy-start(bf16[3,3,3,192,192]{4,3,2,1,0:T(8,128)(2,1)} %param.9) | copy-start | bytes 5971972
  2.6 17.9 %collective-permute-start = (bf16[2,8,32,192]{3,1,2,0:T(8,128)(2,1)S(1)}, bf16[2,8,32,192]{3,1,2,0:T(8,128)(2,1)S(1)}, u32[]{:S(2)}, u32[]{:S(2)}) collective-permute-start(bf16[2,8,32,192]{3,1,2,0:T(8,128)(2,1)S(1)} %fusion.39), channel_id=1, source_target_pairs={{0,32},{32,64},{64,96},{96,128},{128,160},{160,192},{192,224},{224... | collective-permute-start | bytes 589832 | tf_op jit(solution)/shard_map/ppermute | solution.py:28
  20.8 6.9 %collective-permute-start.1 = (bf16[4,2,32,192]{3,1,2,0:T(2,128)(2,1)S(1)}, bf16[4,2,32,192]{3,1,2,0:T(2,128)(2,1)S(1)}, u32[]{:S(2)}, u32[]{:S(2)}) collective-permute-start(bf16[4,2,32,192]{3,1,2,0:T(2,128)(2,1)S(1)} %get-tuple-element.7), channel_id=1, source_target_pairs={{0,8},{8,16},{16,24},{24,0},{1,9},{9,17},{17,25},{25,1},{2,10},{10... | collective-permute-start | bytes 294920 | tf_op jit(solution)/shard_map/ppermute | solution.py:13
  23.9 5.8 %collective-permute-start.2 = (bf16[4,2,32,192]{3,1,2,0:T(2,128)(2,1)S(1)}, bf16[4,2,32,192]{3,1,2,0:T(2,128)(2,1)S(1)}, u32[]{:S(2)}, u32[]{:S(2)}) collective-permute-start(bf16[4,2,32,192]{3,1,2,0:T(2,128)(2,1)S(1)} %get-tuple-element.8), channel_id=1, source_target_pairs={{8,0},{16,8},{24,16},{0,24},{9,1},{17,9},{25,17},{1,25},{10,2},{18... | collective-permute-start | bytes 294920 | tf_op jit(solution)/shard_map/ppermute | solution.py:14
  30.5 5.4 %collective-permute-start.3 = (bf16[4,12,2,192]{3,1,2,0:T(8,128)(2,1)}, bf16[4,12,2,192]{3,1,2,0:T(8,128)(2,1)}, u32[]{:S(2)}, u32[]{:S(2)}) collective-permute-start(bf16[4,12,2,192]{3,1,2,0:T(8,128)(2,1)} %get-tuple-element.5), channel_id=1, source_target_pairs={{0,1},{1,2},{2,3},{3,4},{4,5},{5,6},{6,7},{7,0},{8,9},{9,10},{10,1... | collective-permute-start | bytes 110600 | tf_op jit(solution)/shard_map/ppermute | solution.py:13
  34.4 3.7 %collective-permute-start.4 = (bf16[4,12,2,192]{3,1,2,0:T(8,128)(2,1)S(1)}, bf16[4,12,2,192]{3,1,2,0:T(8,128)(2,1)S(1)}, u32[]{:S(2)}, u32[]{:S(2)}) collective-permute-start(bf16[4,12,2,192]{3,1,2,0:T(8,128)(2,1)S(1)} %get-tuple-element.6), channel_id=1, source_target_pairs={{1,0},{2,1},{3,2},{4,3},{5,4},{6,5},{7,6},{0,7},{9,8},{10,9},{11,1... | collective-permute-start | bytes 110600 | tf_op jit(solution)/shard_map/ppermute | solution.py:14
  39.0 0.7 %copy-start.2 = (f32[192]{0:T(256)S(1)}, f32[192]{0:T(256)}, u32[]{:S(2)}) copy-start(f32[192]{0:T(256)} %param.10) | copy-start | bytes 2308
  39.0 0.7 %copy-start.7 = (pred[8,5]{0,1:T(8,128)(4,1)S(1)}, pred[8,5]{0,1:T(8,128)(4,1)}, u32[]{:S(2)}) copy-start(pred[8,5]{0,1:T(8,128)(4,1)} %constant.66) | copy-start | bytes 124
  42.8 1.2 %copy-start.3 = (f32[192]{0:T(256)S(1)}, f32[192]{0:T(256)}, u32[]{:S(2)}) copy-start(f32[192]{0:T(256)} %param.11) | copy-start | bytes 2308
  44.0 1.8 %copy-start.5 = (bf16[3,3,3,192,192]{4,3,2,1,0:T(8,128)(2,1)S(1)}, bf16[3,3,3,192,192]{4,3,2,1,0:T(8,128)(2,1)}, u32[]{:S(2)}) copy-start(bf16[3,3,3,192,192]{4,3,2,1,0:T(8,128)(2,1)} %param.12) | copy-start | bytes 5971972
  44.0 1.8 %copy-start.6 = (pred[8,5]{0,1:T(8,128)(4,1)S(1)}, pred[8,5]{0,1:T(8,128)(4,1)}, u32[]{:S(2)}) copy-start(pred[8,5]{0,1:T(8,128)(4,1)} %constant.65) | copy-start | bytes 124
  47.4 10.8 %copy-start.1 = (bf16[2,8,32,192]{3,2,1,0:T(8,128)(2,1)S(1)}, bf16[2,8,32,192]{3,2,1,0:T(8,128)(2,1)}, u32[]{:S(2)}) copy-start(bf16[2,8,32,192]{3,2,1,0:T(8,128)(2,1)} %param.7) | copy-start | bytes 589828
  47.4 10.8 %copy-start.4 = (f32[192]{0:T(256)S(1)}, f32[192]{0:T(256)}, u32[]{:S(2)}) copy-start(f32[192]{0:T(256)} %param.13) | copy-start | bytes 2308
  47.4 10.8 %collective-permute-start.5 = (bf16[2,8,32,192]{3,1,2,0:T(8,128)(2,1)S(1)}, bf16[2,8,32,192]{3,1,2,0:T(8,128)(2,1)S(1)}, u32[]{:S(2)}, u32[]{:S(2)}) collective-permute-start(bf16[2,8,32,192]{3,1,2,0:T(8,128)(2,1)S(1)} %slice_bitcast_fusion.2), channel_id=1, source_target_pairs={{0,32},{32,64},{64,96},{96,128},{128,160},{160,192},{192,224},{224... | collective-permute-start | bytes 589832 | tf_op jit(solution)/shard_map/ppermute | solution.py:28

commit v11 on v8

--- a/solution.py
+++ b/solution.py
@@ -55,7 +55,7 @@
     values = latents.astype(jnp.float32)
     first_act = jax.nn.silu(rms_norm(values, first_gain)).astype(jnp.bfloat16)
     stack = jnp.concatenate([shifted(first_act, "tm", 1), first_act], axis=0)
-    first_ext = with_halo(stack, (("row", 1), ("col", 2)), 2)
+    first_ext = with_halo(stack, (("col", 2), ("row", 1)), 2)
     first_conv = conv_valid(first_ext, first_weight)
     hidden = (first_conv + first_bias).astype(jnp.bfloat16)
     second_act = jax.nn.silu(rms_norm(hidden.astype(jnp.float32), second_gain))

time: 54.8 us -> 55.2 us (level)
  the two profiles are of different devices: /device:TPU:401 before, /device:TPU:144 now
where the time goes in v11:
time: 55.2 us; the launch traced here: 54.9 us
  waiting for transfers between devices  23.1 us (42%)
  starting transfers between devices  16.8 us (30%)
  other arithmetic  5.7 us (10%)
  matrix products  5.29 us (10%)
  local copies, waits for them, and re-layouts  3.69 us (7%)
    ppermute x2, waiting for transfers between devices, shifted(): lax.ppermute(value, axis, [(source, source + steps) for source in range(i...  14.5 us
    ppermute x2, starting transfers between devices, shifted(): lax.ppermute(value, axis, [(source, source + steps) for source in range(i...  6.57 us
    ppermute x2, waiting for transfers between devices, with_halo(): lax.ppermute(head, axis, [(i + 1, i) for i in range(ends)])  6.23 us
    ppermute x2, starting transfers between devices, with_halo(): lax.ppermute(tail, axis, [(i, i + 1) for i in range(ends)])  5.32 us
    conv_general_dilated x3, matrix products, conv_valid(): lax.conv_general_dilated(stack[None], kernel, window_strides=(1, 1, 1), p...  5.29 us
    ppermute x2, starting transfers between devices, with_halo(): lax.ppermute(head, axis, [(i + 1, i) for i in range(ends)])  4.93 us
    ppermute x2, waiting for transfers between devices, with_halo(): lax.ppermute(tail, axis, [(i, i + 1) for i in range(ends)])  2.41 us
    reduce_sum x2, other arithmetic, rms_norm(): jnp.mean(values * values, axis=-1, keepdims=True) + 1e-06  1.81 us
  transfers between devices with their start and end apart: 6, of which 5 were waited for; matrix products, arithmetic and copies ran while one was open for 3% of the time, Pallas kernels for 0%

profile of v11, /device:TPU:144, one launch (start us, length us, event | category | flops | bytes accessed | tf_op | source)
XLA Modules:
  0.0 54.9 jit_solution(1835258681823703290)
XLA Ops:
  0.0 0.0 copy-start
  0.0 1.3 %fusion.32 = f32[2,8,32]{1,2,0:T(8,128)S(1)} fusion(bf16[2,8,32,192]{3,2,1,0:T(8,128)(2,1)} %param.7), kind=kLoop, calls=%fused_computation.35 | loop fusion | flops 294400 | bytes 198656 | tf_op jit(solution)/shard_map/reduce_sum | solution.py:31
  1.4 1.2 %fusion.39 = bf16[2,8,32,192]{3,1,2,0:T(8,128)(2,1)S(1)} fusion(f32[192]{0:T(256)} %param.8, f32[2,8,32]{1,2,0:T(8,128)S(1)} %add_rsqrt_fusion.1, bf16[2,8,32,192]{3,2,1,0:T(8,128)(2,1)} %param.7), kind=kLoop, calls=%fused_computation.42 | loop fusion | flops 786432 | bytes 396032 | tf_op jit(solution)/shard_map/convert_element_type | solution.py:56
  2.6 3.8 %collective-permute-start = (bf16[2,8,32,192]{3,1,2,0:T(8,128)(2,1)S(1)}, bf16[2,8,32,192]{3,1,2,0:T(8,128)(2,1)S(1)}, u32[]{:S(2)}, u32[]{:S(2)}) collective-permute-start(bf16[2,8,32,192]{3,1,2,0:T(8,128)(2,1)S(1)} %fusion.39), channel_id=1, source_target_pairs={{0,32},{32,64},{64,96},{96,128},{128,160},{160,192},{192,224},{224... | collective-permute-start | bytes 589832 | tf_op jit(solution)/shard_map/ppermute | solution.py:27
  6.4 7.3 %collective-permute-done = bf16[2,8,32,192]{3,1,2,0:T(8,128)(2,1)S(1)} collective-permute-done((bf16[2,8,32,192]{3,1,2,0:T(8,128)(2,1)S(1)}, bf16[2,8,32,192]{3,1,2,0:T(8,128)(2,1)S(1)}, u32[]{:S(2)}, u32[]{:S(2)}) %collective-permute-start) | collective-permute-done | bytes 196640 | tf_op jit(solution)/shard_map/ppermute | solution.py:27
  13.8 1.9 %collective-permute-start.1 = (bf16[4,8,2,192]{3,1,2,0:T(8,128)(2,1)S(1)}, bf16[4,8,2,192]{3,1,2,0:T(8,128)(2,1)S(1)}, u32[]{:S(2)}, u32[]{:S(2)}) collective-permute-start(bf16[4,8,2,192]{3,1,2,0:T(8,128)(2,1)S(1)} %get-tuple-element.7), channel_id=1, source_target_pairs={{0,1},{1,2},{2,3},{3,4},{4,5},{5,6},{6,7},{8,9},{9,10},{10,11},{11... | collective-permute-start | bytes 73736 | tf_op jit(solution)/shard_map/ppermute | solution.py:15
  15.7 3.6 %collective-permute-start.2 = (bf16[4,8,2,192]{3,1,2,0:T(8,128)(2,1)S(1)}, bf16[4,8,2,192]{3,1,2,0:T(8,128)(2,1)S(1)}, u32[]{:S(2)}, u32[]{:S(2)}) collective-permute-start(bf16[4,8,2,192]{3,1,2,0:T(8,128)(2,1)S(1)} %get-tuple-element.8), channel_id=1, source_target_pairs={{1,0},{2,1},{3,2},{4,3},{5,4},{6,5},{7,6},{9,8},{10,9},{11,10},{12... | collective-permute-start | bytes 73736 | tf_op jit(solution)/shard_map/ppermute | solution.py:17
  19.4 0.0 collective-permute-done.1
  19.4 1.6 %collective-permute-done.2 = bf16[4,8,2,192]{3,1,2,0:T(8,128)(2,1)S(1)} collective-permute-done((bf16[4,8,2,192]{3,1,2,0:T(8,128)(2,1)S(1)}, bf16[4,8,2,192]{3,1,2,0:T(8,128)(2,1)S(1)}, u32[]{:S(2)}, u32[]{:S(2)}) %collective-permute-start.2) | collective-permute-done | bytes 24608 | tf_op jit(solution)/shard_map/ppermute | solution.py:17
  20.9 0.2 pad_maximum_fusion.3
  21.1 3.4 %collective-permute-start.3 = (bf16[4,2,36,192]{3,1,2,0:T(2,128)(2,1)S(1)}, bf16[4,2,36,192]{3,1,2,0:T(2,128)(2,1)S(1)}, u32[]{:S(2)}, u32[]{:S(2)}) collective-permute-start(bf16[4,2,36,192]{3,1,2,0:T(2,128)(2,1)S(1)} %get-tuple-element.5), channel_id=1, source_target_pairs={{0,8},{8,16},{16,24},{1,9},{9,17},{17,25},{2,10},{10,18},{18,26},{... | collective-permute-start | bytes 331784 | tf_op jit(solution)/shard_map/ppermute | solution.py:15
  24.5 1.3 %collective-permute-start.4 = (bf16[4,2,36,192]{3,1,2,0:T(2,128)(2,1)S(1)}, bf16[4,2,36,192]{3,1,2,0:T(2,128)(2,1)S(1)}, u32[]{:S(2)}, u32[]{:S(2)}) collective-permute-start(bf16[4,2,36,192]{3,1,2,0:T(2,128)(2,1)S(1)} %get-tuple-element.6), channel_id=1, source_target_pairs={{8,0},{16,8},{24,16},{9,1},{17,9},{25,17},{10,2},{18,10},{26,18},{... | collective-permute-start | bytes 331784 | tf_op jit(solution)/shard_map/ppermute | solution.py:17
  25.8 0.1 broadcast_and_fusion
  25.9 2.4 %collective-permute-done.3 = bf16[4,2,36,192]{3,1,2,0:T(2,128)(2,1)S(1)} collective-permute-done((bf16[4,2,36,192]{3,1,2,0:T(2,128)(2,1)S(1)}, bf16[4,2,36,192]{3,1,2,0:T(2,128)(2,1)S(1)}, u32[]{:S(2)}, u32[]{:S(2)}) %collective-permute-start.3) | collective-permute-done | bytes 110624 | tf_op jit(solution)/shard_map/ppermute | solution.py:15
  28.3 4.7 %collective-permute-done.4 = bf16[4,2,36,192]{3,1,2,0:T(2,128)(2,1)S(1)} collective-permute-done((bf16[4,2,36,192]{3,1,2,0:T(2,128)(2,1)S(1)}, bf16[4,2,36,192]{3,1,2,0:T(2,128)(2,1)S(1)}, u32[]{:S(2)}, u32[]{:S(2)}) %collective-permute-start.4) | collective-permute-done | bytes 110624 | tf_op jit(solution)/shard_map/ppermute | solution.py:17
  33.0 0.7 %maximum_bitcast_fusion = bf16[4,12,1,36,192]{4,1,3,0,2:T(8,128)(2,1)S(1)} fusion(bf16[4,2,36,192]{3,1,2,0:T(2,128)(2,1)S(1)} %collective-permute-done.4, bf16[4,8,2,192]{3,1,2,0:T(8,128)(2,1)S(1)} %collective-permute-done.2, bf16[2,8,32,192]{3,1,2,0:T(8,128)(2,1)S(1)} %fusion.39, bf16[2,8,32,192]{3,1,2,0:T(8,128)(2,1)S(1)} %collective-permute-done, ...), kind=kLoop, calls=%fused_computation.16 | loop fusion | flops 3981312 | bytes 1327104 | tf_op jit(solution)/shard_map/broadcast_in_dim | solution.py:36
  33.7 0.3 pad
  34.0 0.0 copy-start.2
  34.0 0.0 copy-start.7
  34.0 0.4 copy.11
  34.4 0.1 slice.31
  34.5 0.0 copy-done
  34.5 0.2 copy-done.2
  34.7 0.0 copy-done.7
  34.7 2.5 %fusion.43 = (f32[2,10,8,5,192]{4,2,3,1,0:T(8,128)S(1)}, f32[2,10,8,5,192]{4,2,3,1,0:T(8,128)S(1)}) fusion(f32[192]{0:T(256)S(1)} %copy-done.2, bf16[3,3,3,192,192]{4,3,2,1,0:T(8,128)(2,1)S(1)} %copy-done, bf16[4,12,1,7,2,192]{5,3,4,1,0,2:T(8,128)(2,1)S(1)} %slice.31, bf16[4,12,1,8,5,192]{5,3,4,1,0,2:T(8,128)(2,1)S(1)} %copy.11, pred[8,5]{0,1:T(8,128)(4,1)S(1)} %copy-done.7), kind=kOutput, calls=%fused_computation.47 | convolution fusion | flops 1596235776 | bytes 4215592 | tf_op jit(solution)/shard_map/conv_general_dilated | solution.py:35
  37.2 0.6 %copy.13 = f32[2,10,8,5,192]{4,0,3,2,1:T(2,128)S(1)} copy(f32[2,10,8,5,192]{4,2,3,1,0:T(8,128)S(1)} %get-tuple-element.10) | data formatting | bytes 1228800 | tf_op jit(solution)/shard_map/conv_general_dilated | solution.py:35
  37.8 0.0 copy-start.3
  37.8 0.5 multiply_reduce_fusion
  38.4 0.6 %copy.12 = f32[2,10,8,5,192]{4,0,3,2,1:T(2,128)S(1)} copy(f32[2,10,8,5,192]{4,2,3,1,0:T(8,128)S(1)} %get-tuple-element.9) | data formatting | bytes 1228800 | tf_op jit(solution)/shard_map/convert_element_type | solution.py:61
  39.0 0.0 copy-start.5
  39.0 0.0 copy-start.6
  39.0 0.0 copy-done.3
  39.0 1.3 %fusion.44 = bf16[2,10,1,34,192]{4,0,3,1,2:T(2,128)(2,1)S(1)} fusion(f32[192]{0:T(256)S(1)} %copy-done.3, f32[2,10,34]{0,2,1:T(8,128)S(1)} %add_rsqrt_fusion, f32[2,10,1,40,192]{4,0,3,1,2:T(2,128)S(1)} %bitcast.47, pred[10,34]{1,0:T(8,128)(4,1)S(1)} %broadcast_and_fusion), kind=kLoop, calls=%fused_computation.48 | loop fusion | flops 1044480 | bytes 787188 | tf_op jit(solution)/shard_map/convert_element_type | solution.py:63
  40.4 0.3 pad.2
  40.8 0.0 copy-done.5
  40.8 0.0 copy-done.6
  40.9 1.4 %fusion.21 = bf16[2,8,8,5,192]{4,2,3,1,0:T(8,128)(2,1)S(1)} fusion(bf16[3,3,3,192,192]{4,3,2,1,0:T(8,128)(2,1)S(1)} %copy-done.5, pred[8,5]{0,1:T(8,128)(4,1)S(1)} %copy-done.6, bf16[2,10,1,7,2,192]{5,3,4,1,0,2:T(8,128)(2,1)S(1)} %slice.34, bf16[2,10,1,8,5,192]{5,3,4,1,0,2:T(8,128)(2,1)S(1)} %copy.15), kind=kOutput, calls=%fused_computation.15 | convolution fusion | flops 638545920 | bytes 2589696 | tf_op jit(solution)/shard_map/conv_general_dilated | solution.py:35
  42.3 0.1 copy.17
  42.4 0.0 copy-start.1
  42.4 0.0 copy-start.4
  42.4 2.7 %collective-permute-start.5 = (bf16[2,8,32,192]{3,1,2,0:T(8,128)(2,1)S(1)}, bf16[2,8,32,192]{3,1,2,0:T(8,128)(2,1)S(1)}, u32[]{:S(2)}, u32[]{:S(2)}) collective-permute-start(bf16[2,8,32,192]{3,1,2,0:T(8,128)(2,1)S(1)} %slice_bitcast_fusion.2), channel_id=1, source_target_pairs={{0,32},{32,64},{64,96},{96,128},{128,160},{160,192},{192,224},{224... | collective-permute-start | bytes 589832 | tf_op jit(solution)/shard_map/ppermute | solution.py:27
  45.1 1.4 %fusion.15 = f32[2,8,8,5,192]{4,2,3,1,0:T(8,128)S(1)} fusion(bf16[3,3,3,192,192]{4,3,2,1,0:T(8,128)(2,1)S(1)} %copy-done.5, pred[8,5]{0,1:T(8,128)(4,1)S(1)} %copy-done.6, bf16[2,10,1,7,2,192]{5,3,4,1,0,2:T(8,128)(2,1)S(1)} %slice.34, bf16[2,10,1,8,5,192]{5,3,4,1,0,2:T(8,128)(2,1)S(1)} %copy.15), kind=kOutput, calls=%fused_computation.13 | convolution fusion | flops 638423040 | bytes 2835456 | tf_op jit(solution)/shard_map/conv_general_dilated | solution.py:35
  46.6 0.2 copy.16
  46.8 7.2 %collective-permute-done.5 = bf16[2,8,32,192]{3,1,2,0:T(8,128)(2,1)S(1)} collective-permute-done((bf16[2,8,32,192]{3,1,2,0:T(8,128)(2,1)S(1)}, bf16[2,8,32,192]{3,1,2,0:T(8,128)(2,1)S(1)}, u32[]{:S(2)}, u32[]{:S(2)}) %collective-permute-start.5) | collective-permute-done | bytes 196640 | tf_op jit(solution)/shard_map/ppermute | solution.py:27
  54.0 0.0 copy-done.1
  54.0 0.0 copy-done.4
  54.0 0.2 fusion.42
  54.2 0.8 %copy.18 = bf16[2,8,32,192]{3,2,1,0:T(8,128)(2,1)} copy(bf16[2,8,32,192]{3,1,2,0:T(8,128)(2,1)S(1)} %fusion.42) | data formatting | bytes 393216 | tf_op jit(solution)/shard_map/convert_element_type | solution.py:68
  (8 shorter events, 0.2 us)
Async XLA Ops:
  0.0 34.5 %copy-start = (bf16[3,3,3,192,192]{4,3,2,1,0:T(8,128)(2,1)S(1)}, bf16[3,3,3,192,192]{4,3,2,1,0:T(8,128)(2,1)}, u32[]{:S(2)}) copy-start(bf16[3,3,3,192,192]{4,3,2,1,0:T(8,128)(2,1)} %param.9) | copy-start | bytes 5971972
  2.6 11.2 %collective-permute-start = (bf16[2,8,32,192]{3,1,2,0:T(8,128)(2,1)S(1)}, bf16[2,8,32,192]{3,1,2,0:T(8,128)(2,1)S(1)}, u32[]{:S(2)}, u32[]{:S(2)}) collective-permute-start(bf16[2,8,32,192]{3,1,2,0:T(8,128)(2,1)S(1)} %fusion.39), channel_id=1, source_target_pairs={{0,32},{32,64},{64,96},{96,128},{128,160},{160,192},{192,224},{224... | collective-permute-start | bytes 589832 | tf_op jit(solution)/shard_map/ppermute | solution.py:27
  13.8 5.6 %collective-permute-start.1 = (bf16[4,8,2,192]{3,1,2,0:T(8,128)(2,1)S(1)}, bf16[4,8,2,192]{3,1,2,0:T(8,128)(2,1)S(1)}, u32[]{:S(2)}, u32[]{:S(2)}) collective-permute-start(bf16[4,8,2,192]{3,1,2,0:T(8,128)(2,1)S(1)} %get-tuple-element.7), channel_id=1, source_target_pairs={{0,1},{1,2},{2,3},{3,4},{4,5},{5,6},{6,7},{8,9},{9,10},{10,11},{11... | collective-permute-start | bytes 73736 | tf_op jit(solution)/shard_map/ppermute | solution.py:15
  15.7 5.2 %collective-permute-start.2 = (bf16[4,8,2,192]{3,1,2,0:T(8,128)(2,1)S(1)}, bf16[4,8,2,192]{3,1,2,0:T(8,128)(2,1)S(1)}, u32[]{:S(2)}, u32[]{:S(2)}) collective-permute-start(bf16[4,8,2,192]{3,1,2,0:T(8,128)(2,1)S(1)} %get-tuple-element.8), channel_id=1, source_target_pairs={{1,0},{2,1},{3,2},{4,3},{5,4},{6,5},{7,6},{9,8},{10,9},{11,10},{12... | collective-permute-start | bytes 73736 | tf_op jit(solution)/shard_map/ppermute | solution.py:17
  21.1 7.2 %collective-permute-start.3 = (bf16[4,2,36,192]{3,1,2,0:T(2,128)(2,1)S(1)}, bf16[4,2,36,192]{3,1,2,0:T(2,128)(2,1)S(1)}, u32[]{:S(2)}, u32[]{:S(2)}) collective-permute-start(bf16[4,2,36,192]{3,1,2,0:T(2,128)(2,1)S(1)} %get-tuple-element.5), channel_id=1, source_target_pairs={{0,8},{8,16},{16,24},{1,9},{9,17},{17,25},{2,10},{10,18},{18,26},{... | collective-permute-start | bytes 331784 | tf_op jit(solution)/shard_map/ppermute | solution.py:15
  24.5 8.5 %collective-permute-start.4 = (bf16[4,2,36,192]{3,1,2,0:T(2,128)(2,1)S(1)}, bf16[4,2,36,192]{3,1,2,0:T(2,128)(2,1)S(1)}, u32[]{:S(2)}, u32[]{:S(2)}) collective-permute-start(bf16[4,2,36,192]{3,1,2,0:T(2,128)(2,1)S(1)} %get-tuple-element.6), channel_id=1, source_target_pairs={{8,0},{16,8},{24,16},{9,1},{17,9},{25,17},{10,2},{18,10},{26,18},{... | collective-permute-start | bytes 331784 | tf_op jit(solution)/shard_map/ppermute | solution.py:17
  34.0 0.7 %copy-start.2 = (f32[192]{0:T(256)S(1)}, f32[192]{0:T(256)}, u32[]{:S(2)}) copy-start(f32[192]{0:T(256)} %param.10) | copy-start | bytes 2308
  34.0 0.7 %copy-start.7 = (pred[8,5]{0,1:T(8,128)(4,1)S(1)}, pred[8,5]{0,1:T(8,128)(4,1)}, u32[]{:S(2)}) copy-start(pred[8,5]{0,1:T(8,128)(4,1)} %constant.51) | copy-start | bytes 124
  37.8 1.2 %copy-start.3 = (f32[192]{0:T(256)S(1)}, f32[192]{0:T(256)}, u32[]{:S(2)}) copy-start(f32[192]{0:T(256)} %param.11) | copy-start | bytes 2308
  39.0 1.8 %copy-start.5 = (bf16[3,3,3,192,192]{4,3,2,1,0:T(8,128)(2,1)S(1)}, bf16[3,3,3,192,192]{4,3,2,1,0:T(8,128)(2,1)}, u32[]{:S(2)}) copy-start(bf16[3,3,3,192,192]{4,3,2,1,0:T(8,128)(2,1)} %param.12) | copy-start | bytes 5971972
  39.0 1.8 %copy-start.6 = (pred[8,5]{0,1:T(8,128)(4,1)S(1)}, pred[8,5]{0,1:T(8,128)(4,1)}, u32[]{:S(2)}) copy-start(pred[8,5]{0,1:T(8,128)(4,1)} %constant.50) | copy-start | bytes 124
  42.4 11.6 %copy-start.1 = (bf16[2,8,32,192]{3,2,1,0:T(8,128)(2,1)S(1)}, bf16[2,8,32,192]{3,2,1,0:T(8,128)(2,1)}, u32[]{:S(2)}) copy-start(bf16[2,8,32,192]{3,2,1,0:T(8,128)(2,1)} %param.7) | copy-start | bytes 589828
  42.4 11.6 %copy-start.4 = (f32[192]{0:T(256)S(1)}, f32[192]{0:T(256)}, u32[]{:S(2)}) copy-start(f32[192]{0:T(256)} %param.13) | copy-start | bytes 2308
  42.4 11.6 %collective-permute-start.5 = (bf16[2,8,32,192]{3,1,2,0:T(8,128)(2,1)S(1)}, bf16[2,8,32,192]{3,1,2,0:T(8,128)(2,1)S(1)}, u32[]{:S(2)}, u32[]{:S(2)}) collective-permute-start(bf16[2,8,32,192]{3,1,2,0:T(8,128)(2,1)S(1)} %slice_bitcast_fusion.2), channel_id=1, source_target_pairs={{0,32},{32,64},{64,96},{96,128},{128,160},{160,192},{192,224},{224... | collective-permute-start | bytes 589832 | tf_op jit(solution)/shard_map/ppermute | solution.py:27

commit v12 on v11

--- a/solution.py
+++ b/solution.py
@@ -55,8 +55,13 @@
     values = latents.astype(jnp.float32)
     first_act = jax.nn.silu(rms_norm(values, first_gain)).astype(jnp.bfloat16)
     stack = jnp.concatenate([shifted(first_act, "tm", 1), first_act], axis=0)
-    first_ext = with_halo(stack, (("col", 2), ("row", 1)), 2)
-    first_conv = conv_valid(first_ext, first_weight)
+    wide = with_halo(stack, (("col", 2),), 2)
+    middle = conv_valid(wide, first_weight)
+    first_ext = with_halo(wide, (("row", 1),), 2)
+    edge = 2 * 2
+    top = conv_valid(first_ext[:, :edge], first_weight)
+    bottom = conv_valid(first_ext[:, first_ext.shape[1] - edge :], first_weight)
+    first_conv = jnp.concatenate([top, middle, bottom], axis=1)
     hidden = (first_conv + first_bias).astype(jnp.bfloat16)
     second_act = jax.nn.silu(rms_norm(hidden.astype(jnp.float32), second_gain))
     keep = inside("row", rows, 1)[:, None] & inside("col", cols, 1)[None, :]

time: 55.2 us -> 53.8 us (0.975)
  the two profiles are of different devices: /device:TPU:144 before, /device:TPU:274 now
where the time goes in v12:
time: 53.8 us; the launch traced here: 53.6 us
  waiting for transfers between devices  21.1 us (39%)
  starting transfers between devices  16.4 us (30%)
  other arithmetic  6.49 us (12%)
  matrix products  5.68 us (11%)
  local copies, waits for them, and re-layouts  3.49 us (6%)
    ppermute x2, waiting for transfers between devices, shifted(): lax.ppermute(value, axis, [(source, source + steps) for source in range(i...  16.1 us
    ppermute x2, starting transfers between devices, with_halo(): lax.ppermute(head, axis, [(i + 1, i) for i in range(ends)])  6.09 us
    conv_general_dilated x5, matrix products, conv_valid(): lax.conv_general_dilated(stack[None], kernel, window_strides=(1, 1, 1), p...  5.68 us
    ppermute x2, starting transfers between devices, with_halo(): lax.ppermute(tail, axis, [(i, i + 1) for i in range(ends)])  5.32 us
    ppermute x2, waiting for transfers between devices, with_halo(): lax.ppermute(head, axis, [(i + 1, i) for i in range(ends)])  4.98 us
    ppermute x2, starting transfers between devices, shifted(): lax.ppermute(value, axis, [(source, source + steps) for source in range(i...  4.98 us
    convert_element_type x1, other arithmetic, local(): jnp.where(keep[None, :, :, None], second_act, 0.0).astype(jnp.bfloat16)  2.17 us
    reduce_sum x2, other arithmetic, rms_norm(): jnp.mean(values * values, axis=-1, keepdims=True) + 1e-06  1.95 us
  transfers between devices with their start and end apart: 6, of which 4 were waited for; matrix products, arithmetic and copies ran while one was open for 8% of the time, Pallas kernels for 0%

profile of v12, /device:TPU:274, one launch (start us, length us, event | category | flops | bytes accessed | tf_op | source)
XLA Modules:
  0.0 53.6 jit_solution(7130440128698200044)
XLA Ops:
  0.0 0.0 copy-start
  0.0 1.3 %fusion.27 = f32[2,8,32]{1,2,0:T(8,128)S(1)} fusion(bf16[2,8,32,192]{3,2,1,0:T(8,128)(2,1)} %param.7), kind=kLoop, calls=%fused_computation.35 | loop fusion | flops 294400 | bytes 198656 | tf_op jit(solution)/shard_map/reduce_sum | solution.py:31
  1.4 1.2 %fusion.34 = bf16[2,8,32,192]{3,1,2,0:T(8,128)(2,1)S(1)} fusion(f32[192]{0:T(256)} %param.8, f32[2,8,32]{1,2,0:T(8,128)S(1)} %add_rsqrt_fusion.1, bf16[2,8,32,192]{3,2,1,0:T(8,128)(2,1)} %param.7), kind=kLoop, calls=%fused_computation.42 | loop fusion | flops 786432 | bytes 396032 | tf_op jit(solution)/shard_map/convert_element_type | solution.py:56
  2.6 2.9 %collective-permute-start = (bf16[2,8,32,192]{3,1,2,0:T(8,128)(2,1)S(1)}, bf16[2,8,32,192]{3,1,2,0:T(8,128)(2,1)S(1)}, u32[]{:S(2)}, u32[]{:S(2)}) collective-permute-start(bf16[2,8,32,192]{3,1,2,0:T(8,128)(2,1)S(1)} %fusion.34), channel_id=1, source_target_pairs={{0,32},{32,64},{64,96},{96,128},{128,160},{160,192},{192,224},{224... | collective-permute-start | bytes 589832 | tf_op jit(solution)/shard_map/ppermute | solution.py:27
  5.6 8.2 %collective-permute-done = bf16[2,8,32,192]{3,1,2,0:T(8,128)(2,1)S(1)} collective-permute-done((bf16[2,8,32,192]{3,1,2,0:T(8,128)(2,1)S(1)}, bf16[2,8,32,192]{3,1,2,0:T(8,128)(2,1)S(1)}, u32[]{:S(2)}, u32[]{:S(2)}) %collective-permute-start) | collective-permute-done | bytes 196640 | tf_op jit(solution)/shard_map/ppermute | solution.py:27
  13.8 1.9 %collective-permute-start.1 = (bf16[4,8,2,192]{3,1,2,0:T(8,128)(2,1)S(1)}, bf16[4,8,2,192]{3,1,2,0:T(8,128)(2,1)S(1)}, u32[]{:S(2)}, u32[]{:S(2)}) collective-permute-start(bf16[4,8,2,192]{3,1,2,0:T(8,128)(2,1)S(1)} %get-tuple-element.11), channel_id=1, source_target_pairs={{0,1},{1,2},{2,3},{3,4},{4,5},{5,6},{6,7},{8,9},{9,10},{10,11},{11... | collective-permute-start | bytes 73736 | tf_op jit(solution)/shard_map/ppermute | solution.py:15
  15.7 3.6 %collective-permute-start.2 = (bf16[4,8,2,192]{3,1,2,0:T(8,128)(2,1)S(1)}, bf16[4,8,2,192]{3,1,2,0:T(8,128)(2,1)S(1)}, u32[]{:S(2)}, u32[]{:S(2)}) collective-permute-start(bf16[4,8,2,192]{3,1,2,0:T(8,128)(2,1)S(1)} %get-tuple-element.12), channel_id=1, source_target_pairs={{1,0},{2,1},{3,2},{4,3},{5,4},{6,5},{7,6},{9,8},{10,9},{11,10},{12... | collective-permute-start | bytes 73736 | tf_op jit(solution)/shard_map/ppermute | solution.py:17
  19.3 0.1 broadcast_and_fusion
  19.4 0.0 collective-permute-done.1
  19.4 1.5 %collective-permute-done.2 = bf16[4,8,2,192]{3,1,2,0:T(8,128)(2,1)S(1)} collective-permute-done((bf16[4,8,2,192]{3,1,2,0:T(8,128)(2,1)S(1)}, bf16[4,8,2,192]{3,1,2,0:T(8,128)(2,1)S(1)}, u32[]{:S(2)}, u32[]{:S(2)}) %collective-permute-start.2) | collective-permute-done | bytes 24608 | tf_op jit(solution)/shard_map/ppermute | solution.py:17
  20.9 0.1 fusion.73
  21.1 0.0 copy-start.7
  21.1 0.2 fusion.74
  21.3 3.4 %collective-permute-start.3 = (bf16[4,2,36,192]{3,1,2,0:T(2,128)(2,1)S(1)}, bf16[4,2,36,192]{3,1,2,0:T(2,128)(2,1)S(1)}, u32[]{:S(2)}, u32[]{:S(2)}) collective-permute-start(bf16[4,2,36,192]{3,1,2,0:T(2,128)(2,1)S(1)} %get-tuple-element.7), channel_id=1, source_target_pairs={{0,8},{8,16},{16,24},{1,9},{9,17},{17,25},{2,10},{10,18},{18,26},{... | collective-permute-start | bytes 331784 | tf_op jit(solution)/shard_map/ppermute | solution.py:15
  24.7 2.4 %collective-permute-start.4 = (bf16[4,2,36,192]{3,1,2,0:T(2,128)(2,1)S(1)}, bf16[4,2,36,192]{3,1,2,0:T(2,128)(2,1)S(1)}, u32[]{:S(2)}, u32[]{:S(2)}) collective-permute-start(bf16[4,2,36,192]{3,1,2,0:T(2,128)(2,1)S(1)} %get-tuple-element.8), channel_id=1, source_target_pairs={{8,0},{16,8},{24,16},{9,1},{17,9},{25,17},{10,2},{18,10},{26,18},{... | collective-permute-start | bytes 331784 | tf_op jit(solution)/shard_map/ppermute | solution.py:17
  27.1 0.1 pad.2
  27.2 0.1 copy.13
  27.4 0.1 slice.47
  27.4 0.0 copy-done
  27.5 0.0 copy-done.7
  27.5 1.6 %convolution_select_fusion = f32[2,6,8,5,192]{4,2,3,1,0:T(8,128)S(1)} fusion(bf16[3,3,3,192,192]{4,3,2,1,0:T(8,128)(2,1)S(1)} %copy-done, bf16[4,8,1,7,2,192]{5,3,4,1,0,2:T(8,128)(2,1)S(1)} %slice.47, bf16[4,8,1,8,5,192]{5,3,4,1,0,2:T(8,128)(2,1)S(1)} %copy.13, pred[8,5]{0,1:T(8,128)(4,1)S(1)} %copy-done.7), kind=kOutput, calls=%fused_computation.9 | convolution fusion | flops 957671424 | bytes 3022888 | tf_op jit(solution)/shard_map/conv_general_dilated | solution.py:35
  29.0 0.4 copy.14
  29.4 0.2 slice_bitcast_fusion.2
  29.6 0.0 collective-permute-done.3
  29.7 3.5 %collective-permute-done.4 = bf16[4,2,36,192]{3,1,2,0:T(2,128)(2,1)S(1)} collective-permute-done((bf16[4,2,36,192]{3,1,2,0:T(2,128)(2,1)S(1)}, bf16[4,2,36,192]{3,1,2,0:T(2,128)(2,1)S(1)}, u32[]{:S(2)}, u32[]{:S(2)}) %collective-permute-start.4) | collective-permute-done | bytes 110624 | tf_op jit(solution)/shard_map/ppermute | solution.py:17
  33.1 0.6 %fusion.53 = (bf16[4,4,1,36,192]{4,1,3,0,2:T(4,128)(2,1)S(1)}, bf16[4,4,1,36,192]{4,1,3,0,2:T(4,128)(2,1)S(1)}) fusion(bf16[4,2,36,192]{3,1,2,0:T(2,128)(2,1)S(1)} %collective-permute-done.3, bf16[4,8,2,192]{3,1,2,0:T(8,128)(2,1)S(1)} %collective-permute-done.2, bf16[4,8,2,192]{3,1,2,0:T(8,128)(2,1)S(1)} %collective-permute-done.1, ...), kind=kLoop, calls=%fused_computation.67 | loop fusion | flops 2211840 | bytes 1105920 | tf_op jit(solution)/shard_map/broadcast_in_dim | solution.py:36
  33.8 0.1 pad
  34.0 0.7 %convolution_select_fusion.2 = f32[2,2,8,5,192]{4,2,3,1,0:T(8,128)S(1)} fusion(bf16[3,3,3,192,192]{4,3,2,1,0:T(8,128)(2,1)S(1)} %copy-done, bf16[4,4,1,7,2,192]{5,3,4,1,0,2:T(8,128)(2,1)S(1)} %slice.45, bf16[4,4,1,8,5,192]{5,3,4,1,0,2:T(8,128)(2,1)S(1)} %copy.10, pred[8,5]{0,1:T(8,128)(4,1)S(1)} %copy-done.7), kind=kOutput, calls=%fused_computation.13 | convolution fusion | flops 319567872 | bytes 2445352 | tf_op jit(solution)/shard_map/conv_general_dilated | solution.py:35
  34.7 0.1 copy.11
  34.8 0.1 slice_bitcast_fusion.5
  34.9 0.1 copy.20
  34.9 0.1 pad.4
  35.2 0.0 copy-start.2
  35.2 0.7 %convolution_select_fusion.1 = f32[2,2,8,5,192]{4,2,3,1,0:T(8,128)S(1)} fusion(bf16[3,3,3,192,192]{4,3,2,1,0:T(8,128)(2,1)S(1)} %copy-done, bf16[4,4,1,7,2,192]{5,3,4,1,0,2:T(8,128)(2,1)S(1)} %slice.50, bf16[4,4,1,8,5,192]{5,3,4,1,0,2:T(8,128)(2,1)S(1)} %copy.16, pred[8,5]{0,1:T(8,128)(4,1)S(1)} %copy-done.7), kind=kOutput, calls=%fused_computation.12 | convolution fusion | flops 319567872 | bytes 2445352 | tf_op jit(solution)/shard_map/conv_general_dilated | solution.py:35
  35.8 0.0 copy-start.3
  35.9 0.1 copy.17
  36.0 0.1 copy.32
  36.0 0.0 copy-done.2
  36.1 0.6 %multiply_reduce_fusion = f32[2,10,34]{0,2,1:T(8,128)S(1)} fusion(f32[2,2,34,192]{3,0,2,1:T(2,128)S(1)} %bitcast.58, f32[2,6,34,192]{3,0,2,1:T(2,128)S(1)} %get-tuple-element.14, f32[2,2,34,192]{3,0,2,1:T(2,128)S(1)} %copy.20, f32[192]{0:T(256)S(1)} %copy-done.2), kind=kLoop, calls=%fused_computation.31 | loop fusion | flops 913240 | bytes 525728 | tf_op jit(solution)/shard_map/reduce_sum | solution.py:31
  36.7 0.0 copy-start.5
  36.7 0.0 copy-start.6
  36.7 0.1 copy.19
  36.8 0.0 copy-done.3
  36.8 2.2 %fusion.51 = bf16[2,10,1,34,192]{4,0,3,1,2:T(2,128)(2,1)S(1)} fusion(f32[192]{0:T(256)S(1)} %copy-done.3, f32[2,10,34]{0,2,1:T(8,128)S(1)} %add_rsqrt_fusion, f32[192]{0:T(256)S(1)} %copy-done.2, f32[1,2,2,34,192]{4,1,3,2,0:T(2,128)S(1)} %bitcast.59, f32[1,2,6,34,192]{4,1,3,2,0:T(2,128)S(1)} %get-tuple-element.13, f32[1,2,2,34,192]{4,1,3,2,0:T(2,128)S(1)} %copy.19, ...), kind=kLoop, calls=%fused_computation.58 | loop fusion | flops 1697280 | bytes 787956 | tf_op jit(solution)/shard_map/convert_element_type | solution.py:68
  39.0 0.3 pad.6
  39.4 0.0 copy-done.5
  39.5 0.0 copy-done.6
  39.5 1.4 %fusion.11 = bf16[2,8,8,5,192]{4,2,3,1,0:T(8,128)(2,1)S(1)} fusion(bf16[3,3,3,192,192]{4,3,2,1,0:T(8,128)(2,1)S(1)} %copy-done.5, pred[8,5]{0,1:T(8,128)(4,1)S(1)} %copy-done.6, bf16[2,10,1,7,2,192]{5,3,4,1,0,2:T(8,128)(2,1)S(1)} %slice.52, bf16[2,10,1,8,5,192]{5,3,4,1,0,2:T(8,128)(2,1)S(1)} %copy.22), kind=kOutput, calls=%fused_computation.8 | convolution fusion | flops 638545920 | bytes 2589696 | tf_op jit(solution)/shard_map/conv_general_dilated | solution.py:35
  40.9 0.1 copy.24
  41.0 0.0 copy-start.1
  41.0 0.0 copy-start.4
  41.0 2.1 %collective-permute-start.5 = (bf16[2,8,32,192]{3,1,2,0:T(8,128)(2,1)S(1)}, bf16[2,8,32,192]{3,1,2,0:T(8,128)(2,1)S(1)}, u32[]{:S(2)}, u32[]{:S(2)}) collective-permute-start(bf16[2,8,32,192]{3,1,2,0:T(8,128)(2,1)S(1)} %slice_bitcast_fusion.3), channel_id=1, source_target_pairs={{0,32},{32,64},{64,96},{96,128},{128,160},{160,192},{192,224},{224... | collective-permute-start | bytes 589832 | tf_op jit(solution)/shard_map/ppermute | solution.py:27
  43.1 1.4 %fusion.5 = f32[2,8,8,5,192]{4,2,3,1,0:T(8,128)S(1)} fusion(bf16[3,3,3,192,192]{4,3,2,1,0:T(8,128)(2,1)S(1)} %copy-done.5, pred[8,5]{0,1:T(8,128)(4,1)S(1)} %copy-done.6, bf16[2,10,1,7,2,192]{5,3,4,1,0,2:T(8,128)(2,1)S(1)} %slice.52, bf16[2,10,1,8,5,192]{5,3,4,1,0,2:T(8,128)(2,1)S(1)} %copy.22), kind=kOutput, calls=%fused_computation.6 | convolution fusion | flops 638423040 | bytes 2835456 | tf_op jit(solution)/shard_map/conv_general_dilated | solution.py:35
  44.5 0.2 copy.23
  44.7 7.9 %collective-permute-done.5 = bf16[2,8,32,192]{3,1,2,0:T(8,128)(2,1)S(1)} collective-permute-done((bf16[2,8,32,192]{3,1,2,0:T(8,128)(2,1)S(1)}, bf16[2,8,32,192]{3,1,2,0:T(8,128)(2,1)S(1)}, u32[]{:S(2)}, u32[]{:S(2)}) %collective-permute-start.5) | collective-permute-done | bytes 196640 | tf_op jit(solution)/shard_map/ppermute | solution.py:27
  52.6 0.0 copy-done.1
  52.6 0.0 copy-done.4
  52.6 0.2 fusion.37
  52.8 0.8 %copy.25 = bf16[2,8,32,192]{3,2,1,0:T(8,128)(2,1)} copy(bf16[2,8,32,192]{3,1,2,0:T(8,128)(2,1)S(1)} %fusion.37) | data formatting | bytes 393216 | tf_op jit(solution)/shard_map/convert_element_type | solution.py:73
  (13 shorter events, 0.3 us)
Async XLA Ops:
  0.0 27.4 %copy-start = (bf16[3,3,3,192,192]{4,3,2,1,0:T(8,128)(2,1)S(1)}, bf16[3,3,3,192,192]{4,3,2,1,0:T(8,128)(2,1)}, u32[]{:S(2)}) copy-start(bf16[3,3,3,192,192]{4,3,2,1,0:T(8,128)(2,1)} %param.9) | copy-start | bytes 5971972
  2.6 11.2 %collective-permute-start = (bf16[2,8,32,192]{3,1,2,0:T(8,128)(2,1)S(1)}, bf16[2,8,32,192]{3,1,2,0:T(8,128)(2,1)S(1)}, u32[]{:S(2)}, u32[]{:S(2)}) collective-permute-start(bf16[2,8,32,192]{3,1,2,0:T(8,128)(2,1)S(1)} %fusion.34), channel_id=1, source_target_pairs={{0,32},{32,64},{64,96},{96,128},{128,160},{160,192},{192,224},{224... | collective-permute-start | bytes 589832 | tf_op jit(solution)/shard_map/ppermute | solution.py:27
  13.8 5.7 %collective-permute-start.1 = (bf16[4,8,2,192]{3,1,2,0:T(8,128)(2,1)S(1)}, bf16[4,8,2,192]{3,1,2,0:T(8,128)(2,1)S(1)}, u32[]{:S(2)}, u32[]{:S(2)}) collective-permute-start(bf16[4,8,2,192]{3,1,2,0:T(8,128)(2,1)S(1)} %get-tuple-element.11), channel_id=1, source_target_pairs={{0,1},{1,2},{2,3},{3,4},{4,5},{5,6},{6,7},{8,9},{9,10},{10,11},{11... | collective-permute-start | bytes 73736 | tf_op jit(solution)/shard_map/ppermute | solution.py:15
  15.7 5.2 %collective-permute-start.2 = (bf16[4,8,2,192]{3,1,2,0:T(8,128)(2,1)S(1)}, bf16[4,8,2,192]{3,1,2,0:T(8,128)(2,1)S(1)}, u32[]{:S(2)}, u32[]{:S(2)}) collective-permute-start(bf16[4,8,2,192]{3,1,2,0:T(8,128)(2,1)S(1)} %get-tuple-element.12), channel_id=1, source_target_pairs={{1,0},{2,1},{3,2},{4,3},{5,4},{6,5},{7,6},{9,8},{10,9},{11,10},{12... | collective-permute-start | bytes 73736 | tf_op jit(solution)/shard_map/ppermute | solution.py:17
  21.1 6.4 %copy-start.7 = (pred[8,5]{0,1:T(8,128)(4,1)S(1)}, pred[8,5]{0,1:T(8,128)(4,1)}, u32[]{:S(2)}) copy-start(pred[8,5]{0,1:T(8,128)(4,1)} %constant.59) | copy-start | bytes 124
  21.3 8.4 %collective-permute-start.3 = (bf16[4,2,36,192]{3,1,2,0:T(2,128)(2,1)S(1)}, bf16[4,2,36,192]{3,1,2,0:T(2,128)(2,1)S(1)}, u32[]{:S(2)}, u32[]{:S(2)}) collective-permute-start(bf16[4,2,36,192]{3,1,2,0:T(2,128)(2,1)S(1)} %get-tuple-element.7), channel_id=1, source_target_pairs={{0,8},{8,16},{16,24},{1,9},{9,17},{17,25},{2,10},{10,18},{18,26},{... | collective-permute-start | bytes 331784 | tf_op jit(solution)/shard_map/ppermute | solution.py:15
  24.7 8.5 %collective-permute-start.4 = (bf16[4,2,36,192]{3,1,2,0:T(2,128)(2,1)S(1)}, bf16[4,2,36,192]{3,1,2,0:T(2,128)(2,1)S(1)}, u32[]{:S(2)}, u32[]{:S(2)}) collective-permute-start(bf16[4,2,36,192]{3,1,2,0:T(2,128)(2,1)S(1)} %get-tuple-element.8), channel_id=1, source_target_pairs={{8,0},{16,8},{24,16},{9,1},{17,9},{25,17},{10,2},{18,10},{26,18},{... | collective-permute-start | bytes 331784 | tf_op jit(solution)/shard_map/ppermute | solution.py:17
  35.2 0.9 %copy-start.2 = (f32[192]{0:T(256)S(1)}, f32[192]{0:T(256)}, u32[]{:S(2)}) copy-start(f32[192]{0:T(256)} %param.10) | copy-start | bytes 2308
  35.8 1.0 %copy-start.3 = (f32[192]{0:T(256)S(1)}, f32[192]{0:T(256)}, u32[]{:S(2)}) copy-start(f32[192]{0:T(256)} %param.11) | copy-start | bytes 2308
  36.7 2.8 %copy-start.5 = (bf16[3,3,3,192,192]{4,3,2,1,0:T(8,128)(2,1)S(1)}, bf16[3,3,3,192,192]{4,3,2,1,0:T(8,128)(2,1)}, u32[]{:S(2)}) copy-start(bf16[3,3,3,192,192]{4,3,2,1,0:T(8,128)(2,1)} %param.12) | copy-start | bytes 5971972
  36.7 2.8 %copy-start.6 = (pred[8,5]{0,1:T(8,128)(4,1)S(1)}, pred[8,5]{0,1:T(8,128)(4,1)}, u32[]{:S(2)}) copy-start(pred[8,5]{0,1:T(8,128)(4,1)} %constant.58) | copy-start | bytes 124
  41.0 11.6 %copy-start.1 = (bf16[2,8,32,192]{3,2,1,0:T(8,128)(2,1)S(1)}, bf16[2,8,32,192]{3,2,1,0:T(8,128)(2,1)}, u32[]{:S(2)}) copy-start(bf16[2,8,32,192]{3,2,1,0:T(8,128)(2,1)} %param.7) | copy-start | bytes 589828
  41.0 11.6 %copy-start.4 = (f32[192]{0:T(256)S(1)}, f32[192]{0:T(256)}, u32[]{:S(2)}) copy-start(f32[192]{0:T(256)} %param.13) | copy-start | bytes 2308
  41.0 11.6 %collective-permute-start.5 = (bf16[2,8,32,192]{3,1,2,0:T(8,128)(2,1)S(1)}, bf16[2,8,32,192]{3,1,2,0:T(8,128)(2,1)S(1)}, u32[]{:S(2)}, u32[]{:S(2)}) collective-permute-start(bf16[2,8,32,192]{3,1,2,0:T(8,128)(2,1)S(1)} %slice_bitcast_fusion.3), channel_id=1, source_target_pairs={{0,32},{32,64},{64,96},{96,128},{128,160},{160,192},{192,224},{224... | collective-permute-start | bytes 589832 | tf_op jit(solution)/shard_map/ppermute | solution.py:27

commit v13 on v12

--- a/solution.py
+++ b/solution.py
@@ -61,8 +61,9 @@
     edge = 2 * 2
     top = conv_valid(first_ext[:, :edge], first_weight)
     bottom = conv_valid(first_ext[:, first_ext.shape[1] - edge :], first_weight)
-    first_conv = jnp.concatenate([top, middle, bottom], axis=1)
-    hidden = (first_conv + first_bias).astype(jnp.bfloat16)
+    hidden = jnp.concatenate(
+        [(piece + first_bias).astype(jnp.bfloat16) for piece in (top, middle, bottom)], axis=1
+    )
     second_act = jax.nn.silu(rms_norm(hidden.astype(jnp.float32), second_gain))
     keep = inside("row", rows, 1)[:, None] & inside("col", cols, 1)[None, :]
     second_act = jnp.where(keep[None, :, :, None], second_act, 0.0).astype(jnp.bfloat16)

time: 53.8 us -> 54.3 us (level)
  the two profiles are of different devices: /device:TPU:274 before, /device:TPU:401 now
where the time goes in v13:
time: 54.3 us; the launch traced here: 53.4 us
  waiting for transfers between devices  21.2 us (39%)
  starting transfers between devices  15.4 us (28%)
  other arithmetic  6.86 us (13%)
  matrix products  5.76 us (11%)
  local copies, waits for them, and re-layouts  3.75 us (7%)
    ppermute x2, waiting for transfers between devices, shifted(): lax.ppermute(value, axis, [(source, source + steps) for source in range(i...  14.6 us
    ppermute x2, starting transfers between devices, with_halo(): lax.ppermute(tail, axis, [(i, i + 1) for i in range(ends)])  7.45 us
    ppermute x2, waiting for transfers between devices, with_halo(): lax.ppermute(head, axis, [(i + 1, i) for i in range(ends)])  6.58 us
    conv_general_dilated x5, matrix products, conv_valid(): lax.conv_general_dilated(stack[None], kernel, window_strides=(1, 1, 1), p...  5.76 us
    ppermute x2, starting transfers between devices, shifted(): lax.ppermute(value, axis, [(source, source + steps) for source in range(i...  4.7 us
    ppermute x2, starting transfers between devices, with_halo(): lax.ppermute(head, axis, [(i + 1, i) for i in range(ends)])  3.21 us
    convert_element_type x1, other arithmetic, local(): jnp.where(keep[None, :, :, None], second_act, 0.0).astype(jnp.bfloat16)  2.28 us
    reduce_sum x2, other arithmetic, rms_norm(): jnp.mean(values * values, axis=-1, keepdims=True) + 1e-06  1.95 us
  transfers between devices with their start and end apart: 6, of which 4 were waited for; matrix products, arithmetic and copies ran while one was open for 8% of the time, Pallas kernels for 0%

profile of v13, /device:TPU:401, one launch (start us, length us, event | category | flops | bytes accessed | tf_op | source)
XLA Modules:
  0.0 53.4 jit_solution(1808428652508605916)
XLA Ops:
  0.0 0.0 copy-start
  0.0 1.3 %fusion.25 = f32[2,8,32]{1,2,0:T(8,128)S(1)} fusion(bf16[2,8,32,192]{3,2,1,0:T(8,128)(2,1)} %param.7), kind=kLoop, calls=%fused_computation.31 | loop fusion | flops 294400 | bytes 198656 | tf_op jit(solution)/shard_map/reduce_sum | solution.py:31
  1.4 1.2 %fusion.32 = bf16[2,8,32,192]{3,1,2,0:T(8,128)(2,1)S(1)} fusion(f32[192]{0:T(256)} %param.8, f32[2,8,32]{1,2,0:T(8,128)S(1)} %add_rsqrt_fusion.1, bf16[2,8,32,192]{3,2,1,0:T(8,128)(2,1)} %param.7), kind=kLoop, calls=%fused_computation.38 | loop fusion | flops 786432 | bytes 396032 | tf_op jit(solution)/shard_map/convert_element_type | solution.py:56
  2.6 2.6 %collective-permute-start = (bf16[2,8,32,192]{3,1,2,0:T(8,128)(2,1)S(1)}, bf16[2,8,32,192]{3,1,2,0:T(8,128)(2,1)S(1)}, u32[]{:S(2)}, u32[]{:S(2)}) collective-permute-start(bf16[2,8,32,192]{3,1,2,0:T(8,128)(2,1)S(1)} %fusion.32), channel_id=1, source_target_pairs={{0,32},{32,64},{64,96},{96,128},{128,160},{160,192},{192,224},{224... | collective-permute-start | bytes 589832 | tf_op jit(solution)/shard_map/ppermute | solution.py:27
  5.3 7.6 %collective-permute-done = bf16[2,8,32,192]{3,1,2,0:T(8,128)(2,1)S(1)} collective-permute-done((bf16[2,8,32,192]{3,1,2,0:T(8,128)(2,1)S(1)}, bf16[2,8,32,192]{3,1,2,0:T(8,128)(2,1)S(1)}, u32[]{:S(2)}, u32[]{:S(2)}) %collective-permute-start) | collective-permute-done | bytes 196640 | tf_op jit(solution)/shard_map/ppermute | solution.py:27
  12.9 4.3 %collective-permute-start.1 = (bf16[4,8,2,192]{3,1,2,0:T(8,128)(2,1)S(1)}, bf16[4,8,2,192]{3,1,2,0:T(8,128)(2,1)S(1)}, u32[]{:S(2)}, u32[]{:S(2)}) collective-permute-start(bf16[4,8,2,192]{3,1,2,0:T(8,128)(2,1)S(1)} %get-tuple-element.11), channel_id=1, source_target_pairs={{0,1},{1,2},{2,3},{3,4},{4,5},{5,6},{6,7},{8,9},{9,10},{10,11},{11... | collective-permute-start | bytes 73736 | tf_op jit(solution)/shard_map/ppermute | solution.py:15
  17.2 1.9 %collective-permute-start.2 = (bf16[4,8,2,192]{3,1,2,0:T(8,128)(2,1)S(1)}, bf16[4,8,2,192]{3,1,2,0:T(8,128)(2,1)S(1)}, u32[]{:S(2)}, u32[]{:S(2)}) collective-permute-start(bf16[4,8,2,192]{3,1,2,0:T(8,128)(2,1)S(1)} %get-tuple-element.12), channel_id=1, source_target_pairs={{1,0},{2,1},{3,2},{4,3},{5,4},{6,5},{7,6},{9,8},{10,9},{11,10},{12... | collective-permute-start | bytes 73736 | tf_op jit(solution)/shard_map/ppermute | solution.py:17
  19.2 0.1 broadcast_and_fusion
  19.2 0.0 collective-permute-done.1
  19.2 3.2 %collective-permute-done.2 = bf16[4,8,2,192]{3,1,2,0:T(8,128)(2,1)S(1)} collective-permute-done((bf16[4,8,2,192]{3,1,2,0:T(8,128)(2,1)S(1)}, bf16[4,8,2,192]{3,1,2,0:T(8,128)(2,1)S(1)}, u32[]{:S(2)}, u32[]{:S(2)}) %collective-permute-start.2) | collective-permute-done | bytes 24608 | tf_op jit(solution)/shard_map/ppermute | solution.py:17
  22.5 0.1 fusion.77
  22.6 0.0 copy-start.2
  22.6 0.0 copy-start.7
  22.6 0.2 fusion.78
  22.8 3.1 %collective-permute-start.3 = (bf16[4,2,36,192]{3,1,2,0:T(2,128)(2,1)S(1)}, bf16[4,2,36,192]{3,1,2,0:T(2,128)(2,1)S(1)}, u32[]{:S(2)}, u32[]{:S(2)}) collective-permute-start(bf16[4,2,36,192]{3,1,2,0:T(2,128)(2,1)S(1)} %get-tuple-element.7), channel_id=1, source_target_pairs={{0,8},{8,16},{16,24},{1,9},{9,17},{17,25},{2,10},{10,18},{18,26},{... | collective-permute-start | bytes 331784 | tf_op jit(solution)/shard_map/ppermute | solution.py:15
  26.0 1.3 %collective-permute-start.4 = (bf16[4,2,36,192]{3,1,2,0:T(2,128)(2,1)S(1)}, bf16[4,2,36,192]{3,1,2,0:T(2,128)(2,1)S(1)}, u32[]{:S(2)}, u32[]{:S(2)}) collective-permute-start(bf16[4,2,36,192]{3,1,2,0:T(2,128)(2,1)S(1)} %get-tuple-element.8), channel_id=1, source_target_pairs={{8,0},{16,8},{24,16},{9,1},{17,9},{25,17},{10,2},{18,10},{26,18},{... | collective-permute-start | bytes 331784 | tf_op jit(solution)/shard_map/ppermute | solution.py:17
  27.3 0.1 pad.2
  27.4 0.1 copy.13
  27.5 0.1 slice.50
  27.6 0.0 copy-done
  27.6 0.0 copy-done.2
  27.6 0.0 copy-done.7
  27.6 1.6 %add_convert_fusion = (bf16[2,6,8,5,192]{4,2,3,1,0:T(8,128)(2,1)S(1)}, f32[2,6,8,5,192]{4,2,3,1,0:T(8,128)S(1)}) fusion(f32[192]{0:T(256)S(1)} %copy-done.2, bf16[3,3,3,192,192]{4,3,2,1,0:T(8,128)(2,1)S(1)} %copy-done, bf16[4,8,1,7,2,192]{5,3,4,1,0,2:T(8,128)(2,1)S(1)} %slice.50, bf16[4,8,1,8,5,192]{5,3,4,1,0,2:T(8,128)(2,1)S(1)} %copy.13, ...), kind=kOutput, calls=%fused_computation.43 | convolution fusion | flops 957855744 | bytes 3207976 | tf_op jit(solution)/shard_map/conv_general_dilated | solution.py:35
  29.2 0.4 copy.21
  29.6 0.1 fusion.50
  29.7 0.2 copy.14
  29.9 0.1 slice_bitcast_fusion.3
  30.1 0.0 collective-permute-done.3
  30.1 3.4 %collective-permute-done.4 = bf16[4,2,36,192]{3,1,2,0:T(2,128)(2,1)S(1)} collective-permute-done((bf16[4,2,36,192]{3,1,2,0:T(2,128)(2,1)S(1)}, bf16[4,2,36,192]{3,1,2,0:T(2,128)(2,1)S(1)}, u32[]{:S(2)}, u32[]{:S(2)}) %collective-permute-start.4) | collective-permute-done | bytes 110624 | tf_op jit(solution)/shard_map/ppermute | solution.py:17
  33.4 0.6 %fusion.53 = (bf16[4,4,1,36,192]{4,1,3,0,2:T(4,128)(2,1)S(1)}, bf16[4,4,1,36,192]{4,1,3,0,2:T(4,128)(2,1)S(1)}) fusion(bf16[4,2,36,192]{3,1,2,0:T(2,128)(2,1)S(1)} %collective-permute-done.3, bf16[4,8,2,192]{3,1,2,0:T(8,128)(2,1)S(1)} %collective-permute-done.2, bf16[4,8,2,192]{3,1,2,0:T(8,128)(2,1)S(1)} %collective-permute-done.1, ...), kind=kLoop, calls=%fused_computation.65 | loop fusion | flops 2211840 | bytes 1105920 | tf_op jit(solution)/shard_map/broadcast_in_dim | solution.py:36
  34.1 0.1 pad.4
  34.3 0.7 %convolution_select_fusion.1 = f32[2,2,8,5,192]{4,2,3,1,0:T(8,128)S(1)} fusion(bf16[3,3,3,192,192]{4,3,2,1,0:T(8,128)(2,1)S(1)} %copy-done, bf16[4,4,1,7,2,192]{5,3,4,1,0,2:T(8,128)(2,1)S(1)} %slice.53, bf16[4,4,1,8,5,192]{5,3,4,1,0,2:T(8,128)(2,1)S(1)} %copy.16, pred[8,5]{0,1:T(8,128)(4,1)S(1)} %copy-done.7), kind=kOutput, calls=%fused_computation.12 | convolution fusion | flops 319567872 | bytes 2445352 | tf_op jit(solution)/shard_map/conv_general_dilated | solution.py:35
  35.0 0.1 pad
  35.2 0.1 copy.22
  35.3 0.7 %add_convert_fusion.2 = (bf16[2,2,8,5,192]{4,2,3,1,0:T(8,128)(2,1)S(1)}, bf16[2,2,8,5,192]{4,2,3,1,0:T(8,128)(2,1)S(1)}, f32[2,2,8,5,192]{4,2,3,1,0:T(8,128)S(1)}) fusion(f32[192]{0:T(256)S(1)} %copy-done.2, f32[2,2,8,5,192]{4,2,3,1,0:T(8,128)S(1)} %convolution_select_fusion.1, bf16[3,3,3,192,192]{4,3,2,1,0:T(8,128)(2,1)S(1)} %copy-done, ...), kind=kOutput, calls=%fused_computation.75 | convolution fusion | flops 319690752 | bytes 2691880 | tf_op jit(solution)/shard_map/conv_general_dilated | solution.py:35
  36.0 0.0 copy-start.3
  36.0 0.1 copy.20
  36.1 0.1 fusion.61
  36.2 0.1 copy.23
  36.3 0.1 copy.24
  36.3 0.6 %multiply_reduce_fusion = f32[2,10,34]{0,2,1:T(8,128)S(1)} fusion(bf16[2,2,34,192]{3,0,2,1:T(2,128)(2,1)S(1)} %copy.24, bf16[2,6,34,192]{3,0,2,1:T(2,128)(2,1)S(1)} %fusion.50, bf16[2,2,34,192]{3,0,2,1:T(2,128)(2,1)S(1)} %copy.23), kind=kLoop, calls=%fused_computation.27 | loop fusion | flops 652120 | bytes 263840 | tf_op jit(solution)/shard_map/reduce_sum | solution.py:31
  37.0 0.0 copy-start.5
  37.0 0.0 copy-start.6
  37.0 0.1 copy.17
  37.1 0.1 slice.54
  37.1 0.1 copy.35
  37.2 0.1 copy.11
  37.3 0.1 slice_bitcast_fusion.6
  37.3 0.1 copy.19
  37.4 0.0 copy-done.3
  37.4 2.3 %fusion.51 = bf16[2,10,1,34,192]{4,0,3,1,2:T(2,128)(2,1)S(1)} fusion(f32[192]{0:T(256)S(1)} %copy-done.3, f32[2,10,34]{0,2,1:T(8,128)S(1)} %add_rsqrt_fusion, bf16[1,2,2,34,192]{4,1,3,2,0:T(2,128)(2,1)S(1)} %bitcast.83, bf16[1,2,6,34,192]{4,1,3,2,0:T(2,128)(2,1)S(1)} %slice_bitcast_fusion.3, bf16[1,2,2,34,192]{4,1,3,2,0:T(2,128)(2,1)S(1)} %copy.19, ...), kind=kLoop, calls=%fused_computation.58 | loop fusion | flops 1436160 | bytes 526068 | tf_op jit(solution)/shard_map/convert_element_type | solution.py:69
  39.7 0.3 pad.6
  40.1 0.0 copy-done.5
  40.1 0.0 copy-done.6
  40.1 1.5 %fusion.11 = bf16[2,8,8,5,192]{4,2,3,1,0:T(8,128)(2,1)S(1)} fusion(bf16[3,3,3,192,192]{4,3,2,1,0:T(8,128)(2,1)S(1)} %copy-done.5, pred[8,5]{0,1:T(8,128)(4,1)S(1)} %copy-done.6, bf16[2,10,1,7,2,192]{5,3,4,1,0,2:T(8,128)(2,1)S(1)} %slice.58, bf16[2,10,1,8,5,192]{5,3,4,1,0,2:T(8,128)(2,1)S(1)} %copy.26), kind=kOutput, calls=%fused_computation.8 | convolution fusion | flops 638545920 | bytes 2589696 | tf_op jit(solution)/shard_map/conv_general_dilated | solution.py:35
  41.6 0.1 copy.28
  41.7 0.0 copy-start.1
  41.7 0.0 copy-start.4
  41.7 2.1 %collective-permute-start.5 = (bf16[2,8,32,192]{3,1,2,0:T(8,128)(2,1)S(1)}, bf16[2,8,32,192]{3,1,2,0:T(8,128)(2,1)S(1)}, u32[]{:S(2)}, u32[]{:S(2)}) collective-permute-start(bf16[2,8,32,192]{3,1,2,0:T(8,128)(2,1)S(1)} %slice_bitcast_fusion.2), channel_id=1, source_target_pairs={{0,32},{32,64},{64,96},{96,128},{128,160},{160,192},{192,224},{224... | collective-permute-start | bytes 589832 | tf_op jit(solution)/shard_map/ppermute | solution.py:27
  43.8 1.4 %fusion.5 = f32[2,8,8,5,192]{4,2,3,1,0:T(8,128)S(1)} fusion(bf16[3,3,3,192,192]{4,3,2,1,0:T(8,128)(2,1)S(1)} %copy-done.5, pred[8,5]{0,1:T(8,128)(4,1)S(1)} %copy-done.6, bf16[2,10,1,7,2,192]{5,3,4,1,0,2:T(8,128)(2,1)S(1)} %slice.58, bf16[2,10,1,8,5,192]{5,3,4,1,0,2:T(8,128)(2,1)S(1)} %copy.26), kind=kOutput, calls=%fused_computation.6 | convolution fusion | flops 638423040 | bytes 2835456 | tf_op jit(solution)/shard_map/conv_general_dilated | solution.py:35
  45.2 0.2 copy.27
  45.4 7.0 %collective-permute-done.5 = bf16[2,8,32,192]{3,1,2,0:T(8,128)(2,1)S(1)} collective-permute-done((bf16[2,8,32,192]{3,1,2,0:T(8,128)(2,1)S(1)}, bf16[2,8,32,192]{3,1,2,0:T(8,128)(2,1)S(1)}, u32[]{:S(2)}, u32[]{:S(2)}) %collective-permute-start.5) | collective-permute-done | bytes 196640 | tf_op jit(solution)/shard_map/ppermute | solution.py:27
  52.4 0.2 fusion.35
  52.7 0.8 %copy.29 = bf16[2,8,32,192]{3,2,1,0:T(8,128)(2,1)} copy(bf16[2,8,32,192]{3,1,2,0:T(8,128)(2,1)S(1)} %fusion.35) | data formatting | bytes 393216 | tf_op jit(solution)/shard_map/convert_element_type | solution.py:74
  (14 shorter events, 0.3 us)
Async XLA Ops:
  0.0 27.6 %copy-start = (bf16[3,3,3,192,192]{4,3,2,1,0:T(8,128)(2,1)S(1)}, bf16[3,3,3,192,192]{4,3,2,1,0:T(8,128)(2,1)}, u32[]{:S(2)}) copy-start(bf16[3,3,3,192,192]{4,3,2,1,0:T(8,128)(2,1)} %param.9) | copy-start | bytes 5971972
  2.6 10.3 %collective-permute-start = (bf16[2,8,32,192]{3,1,2,0:T(8,128)(2,1)S(1)}, bf16[2,8,32,192]{3,1,2,0:T(8,128)(2,1)S(1)}, u32[]{:S(2)}, u32[]{:S(2)}) collective-permute-start(bf16[2,8,32,192]{3,1,2,0:T(8,128)(2,1)S(1)} %fusion.32), channel_id=1, source_target_pairs={{0,32},{32,64},{64,96},{96,128},{128,160},{160,192},{192,224},{224... | collective-permute-start | bytes 589832 | tf_op jit(solution)/shard_map/ppermute | solution.py:27
  12.9 6.3 %collective-permute-start.1 = (bf16[4,8,2,192]{3,1,2,0:T(8,128)(2,1)S(1)}, bf16[4,8,2,192]{3,1,2,0:T(8,128)(2,1)S(1)}, u32[]{:S(2)}, u32[]{:S(2)}) collective-permute-start(bf16[4,8,2,192]{3,1,2,0:T(8,128)(2,1)S(1)} %get-tuple-element.11), channel_id=1, source_target_pairs={{0,1},{1,2},{2,3},{3,4},{4,5},{5,6},{6,7},{8,9},{9,10},{10,11},{11... | collective-permute-start | bytes 73736 | tf_op jit(solution)/shard_map/ppermute | solution.py:15
  17.2 5.2 %collective-permute-start.2 = (bf16[4,8,2,192]{3,1,2,0:T(8,128)(2,1)S(1)}, bf16[4,8,2,192]{3,1,2,0:T(8,128)(2,1)S(1)}, u32[]{:S(2)}, u32[]{:S(2)}) collective-permute-start(bf16[4,8,2,192]{3,1,2,0:T(8,128)(2,1)S(1)} %get-tuple-element.12), channel_id=1, source_target_pairs={{1,0},{2,1},{3,2},{4,3},{5,4},{6,5},{7,6},{9,8},{10,9},{11,10},{12... | collective-permute-start | bytes 73736 | tf_op jit(solution)/shard_map/ppermute | solution.py:17
  22.6 5.0 %copy-start.2 = (f32[192]{0:T(256)S(1)}, f32[192]{0:T(256)}, u32[]{:S(2)}) copy-start(f32[192]{0:T(256)} %param.10) | copy-start | bytes 2308
  22.6 5.0 %copy-start.7 = (pred[8,5]{0,1:T(8,128)(4,1)S(1)}, pred[8,5]{0,1:T(8,128)(4,1)}, u32[]{:S(2)}) copy-start(pred[8,5]{0,1:T(8,128)(4,1)} %constant.59) | copy-start | bytes 124
  22.8 7.2 %collective-permute-start.3 = (bf16[4,2,36,192]{3,1,2,0:T(2,128)(2,1)S(1)}, bf16[4,2,36,192]{3,1,2,0:T(2,128)(2,1)S(1)}, u32[]{:S(2)}, u32[]{:S(2)}) collective-permute-start(bf16[4,2,36,192]{3,1,2,0:T(2,128)(2,1)S(1)} %get-tuple-element.7), channel_id=1, source_target_pairs={{0,8},{8,16},{16,24},{1,9},{9,17},{17,25},{2,10},{10,18},{18,26},{... | collective-permute-start | bytes 331784 | tf_op jit(solution)/shard_map/ppermute | solution.py:15
  26.0 7.5 %collective-permute-start.4 = (bf16[4,2,36,192]{3,1,2,0:T(2,128)(2,1)S(1)}, bf16[4,2,36,192]{3,1,2,0:T(2,128)(2,1)S(1)}, u32[]{:S(2)}, u32[]{:S(2)}) collective-permute-start(bf16[4,2,36,192]{3,1,2,0:T(2,128)(2,1)S(1)} %get-tuple-element.8), channel_id=1, source_target_pairs={{8,0},{16,8},{24,16},{9,1},{17,9},{25,17},{10,2},{18,10},{26,18},{... | collective-permute-start | bytes 331784 | tf_op jit(solution)/shard_map/ppermute | solution.py:17
  36.0 1.4 %copy-start.3 = (f32[192]{0:T(256)S(1)}, f32[192]{0:T(256)}, u32[]{:S(2)}) copy-start(f32[192]{0:T(256)} %param.11) | copy-start | bytes 2308
  37.0 3.2 %copy-start.5 = (bf16[3,3,3,192,192]{4,3,2,1,0:T(8,128)(2,1)S(1)}, bf16[3,3,3,192,192]{4,3,2,1,0:T(8,128)(2,1)}, u32[]{:S(2)}) copy-start(bf16[3,3,3,192,192]{4,3,2,1,0:T(8,128)(2,1)} %param.12) | copy-start | bytes 5971972
  37.0 3.2 %copy-start.6 = (pred[8,5]{0,1:T(8,128)(4,1)S(1)}, pred[8,5]{0,1:T(8,128)(4,1)}, u32[]{:S(2)}) copy-start(pred[8,5]{0,1:T(8,128)(4,1)} %constant.58) | copy-start | bytes 124
  41.7 10.7 %copy-start.1 = (bf16[2,8,32,192]{3,2,1,0:T(8,128)(2,1)S(1)}, bf16[2,8,32,192]{3,2,1,0:T(8,128)(2,1)}, u32[]{:S(2)}) copy-start(bf16[2,8,32,192]{3,2,1,0:T(8,128)(2,1)} %param.7) | copy-start | bytes 589828
  41.7 10.7 %copy-start.4 = (f32[192]{0:T(256)S(1)}, f32[192]{0:T(256)}, u32[]{:S(2)}) copy-start(f32[192]{0:T(256)} %param.13) | copy-start | bytes 2308
  41.7 10.7 %collective-permute-start.5 = (bf16[2,8,32,192]{3,1,2,0:T(8,128)(2,1)S(1)}, bf16[2,8,32,192]{3,1,2,0:T(8,128)(2,1)S(1)}, u32[]{:S(2)}, u32[]{:S(2)}) collective-permute-start(bf16[2,8,32,192]{3,1,2,0:T(8,128)(2,1)S(1)} %slice_bitcast_fusion.2), channel_id=1, source_target_pairs={{0,32},{32,64},{64,96},{96,128},{128,160},{160,192},{192,224},{224... | collective-permute-start | bytes 589832 | tf_op jit(solution)/shard_map/ppermute | solution.py:27

commit v14 on v12

--- a/solution.py
+++ b/solution.py
@@ -61,11 +61,15 @@
     edge = 2 * 2
     top = conv_valid(first_ext[:, :edge], first_weight)
     bottom = conv_valid(first_ext[:, first_ext.shape[1] - edge :], first_weight)
-    first_conv = jnp.concatenate([top, middle, bottom], axis=1)
-    hidden = (first_conv + first_bias).astype(jnp.bfloat16)
-    second_act = jax.nn.silu(rms_norm(hidden.astype(jnp.float32), second_gain))
     keep = inside("row", rows, 1)[:, None] & inside("col", cols, 1)[None, :]
-    second_act = jnp.where(keep[None, :, :, None], second_act, 0.0).astype(jnp.bfloat16)
+    limits = (0, top.shape[1], top.shape[1] + middle.shape[1], keep.shape[0])
+    pieces = []
+    for index, piece in enumerate((top, middle, bottom)):
+        hidden = (piece + first_bias).astype(jnp.bfloat16).astype(jnp.float32)
+        act = jax.nn.silu(rms_norm(hidden, second_gain))
+        mask = keep[limits[index] : limits[index + 1]]
+        pieces.append(jnp.where(mask[None, :, :, None], act, 0.0).astype(jnp.bfloat16))
+    second_act = jnp.concatenate(pieces, axis=1)
     ahead = conv_valid(second_act, second_weight[0:2], (0, 1)).astype(jnp.bfloat16)
     behind = shifted(ahead, "tm", 1)
     own = conv_valid(second_act, second_weight[1:3], (1, 0))

time: 53.8 us -> 49.6 us (0.922)
  the two profiles are of different devices: /device:TPU:274 before, /device:TPU:262 now
where the time goes in v14:
time: 49.6 us; the launch traced here: 49.3 us
  waiting for transfers between devices  20.3 us (41%)
  starting transfers between devices  13.3 us (27%)
  other arithmetic  6.01 us (12%)
  matrix products  5.75 us (12%)
  local copies, waits for them, and re-layouts  3.47 us (7%)
    ppermute x2, waiting for transfers between devices, shifted(): lax.ppermute(value, axis, [(source, source + steps) for source in range(i...  16 us
    conv_general_dilated x5, matrix products, conv_valid(): lax.conv_general_dilated(stack[None], kernel, window_strides=(1, 1, 1), p...  5.75 us
    ppermute x2, starting transfers between devices, shifted(): lax.ppermute(value, axis, [(source, source + steps) for source in range(i...  4.98 us
    ppermute x2, waiting for transfers between devices, with_halo(): lax.ppermute(tail, axis, [(i, i + 1) for i in range(ends)])  4.33 us
    ppermute x2, starting transfers between devices, with_halo(): lax.ppermute(tail, axis, [(i, i + 1) for i in range(ends)])  4.32 us
    ppermute x2, starting transfers between devices, with_halo(): lax.ppermute(head, axis, [(i + 1, i) for i in range(ends)])  4.03 us
    reduce_sum x3, other arithmetic, rms_norm(): jnp.mean(values * values, axis=-1, keepdims=True) + 1e-06  1.88 us
    broadcast_in_dim x3, other arithmetic, conv_valid(): stack[None]  1.31 us
  transfers between devices with their start and end apart: 6, of which 4 were waited for; matrix products, arithmetic and copies ran while one was open for 11% of the time, Pallas kernels for 0%

profile of v14, /device:TPU:262, one launch (start us, length us, event | category | flops | bytes accessed | tf_op | source)
XLA Modules:
  0.0 49.3 jit_solution(3327879978843806618)
XLA Ops:
  0.0 0.0 copy-start
  0.0 1.3 %fusion.25 = f32[2,8,32]{1,2,0:T(8,128)S(1)} fusion(bf16[2,8,32,192]{3,2,1,0:T(8,128)(2,1)} %param.7), kind=kLoop, calls=%fused_computation.28 | loop fusion | flops 294400 | bytes 198656 | tf_op jit(solution)/shard_map/reduce_sum | solution.py:31
  1.4 1.2 %fusion.32 = bf16[2,8,32,192]{3,1,2,0:T(8,128)(2,1)S(1)} fusion(f32[192]{0:T(256)} %param.8, f32[2,8,32]{1,2,0:T(8,128)S(1)} %add_rsqrt_fusion.3, bf16[2,8,32,192]{3,2,1,0:T(8,128)(2,1)} %param.7), kind=kLoop, calls=%fused_computation.35 | loop fusion | flops 786432 | bytes 396032 | tf_op jit(solution)/shard_map/convert_element_type | solution.py:56
  2.6 2.9 %collective-permute-start = (bf16[2,8,32,192]{3,1,2,0:T(8,128)(2,1)S(1)}, bf16[2,8,32,192]{3,1,2,0:T(8,128)(2,1)S(1)}, u32[]{:S(2)}, u32[]{:S(2)}) collective-permute-start(bf16[2,8,32,192]{3,1,2,0:T(8,128)(2,1)S(1)} %fusion.32), channel_id=1, source_target_pairs={{0,32},{32,64},{64,96},{96,128},{128,160},{160,192},{192,224},{224... | collective-permute-start | bytes 589832 | tf_op jit(solution)/shard_map/ppermute | solution.py:27
  5.6 0.1 broadcast_and_fusion
  5.6 8.1 %collective-permute-done = bf16[2,8,32,192]{3,1,2,0:T(8,128)(2,1)S(1)} collective-permute-done((bf16[2,8,32,192]{3,1,2,0:T(8,128)(2,1)S(1)}, bf16[2,8,32,192]{3,1,2,0:T(8,128)(2,1)S(1)}, u32[]{:S(2)}, u32[]{:S(2)}) %collective-permute-start) | collective-permute-done | bytes 196640 | tf_op jit(solution)/shard_map/ppermute | solution.py:27
  13.8 1.3 %collective-permute-start.2 = (bf16[4,8,2,192]{3,1,2,0:T(8,128)(2,1)S(1)}, bf16[4,8,2,192]{3,1,2,0:T(8,128)(2,1)S(1)}, u32[]{:S(2)}, u32[]{:S(2)}) collective-permute-start(bf16[4,8,2,192]{3,1,2,0:T(8,128)(2,1)S(1)} %get-tuple-element.14), channel_id=1, source_target_pairs={{1,0},{2,1},{3,2},{4,3},{5,4},{6,5},{7,6},{9,8},{10,9},{11,10},{12... | collective-permute-start | bytes 73736 | tf_op jit(solution)/shard_map/ppermute | solution.py:17
  15.1 3.0 %collective-permute-start.1 = (bf16[4,8,2,192]{3,1,2,0:T(8,128)(2,1)S(1)}, bf16[4,8,2,192]{3,1,2,0:T(8,128)(2,1)S(1)}, u32[]{:S(2)}, u32[]{:S(2)}) collective-permute-start(bf16[4,8,2,192]{3,1,2,0:T(8,128)(2,1)S(1)} %get-tuple-element.13), channel_id=1, source_target_pairs={{0,1},{1,2},{2,3},{3,4},{4,5},{5,6},{6,7},{8,9},{9,10},{10,11},{11... | collective-permute-start | bytes 73736 | tf_op jit(solution)/shard_map/ppermute | solution.py:15
  18.1 0.1 fusion.84
  18.2 0.1 slice.60
  18.3 0.1 copy.12
  18.4 0.0 collective-permute-done.2
  18.4 0.6 %collective-permute-done.1 = bf16[4,8,2,192]{3,1,2,0:T(8,128)(2,1)S(1)} collective-permute-done((bf16[4,8,2,192]{3,1,2,0:T(8,128)(2,1)S(1)}, bf16[4,8,2,192]{3,1,2,0:T(8,128)(2,1)S(1)}, u32[]{:S(2)}, u32[]{:S(2)}) %collective-permute-start.1) | collective-permute-done | bytes 24608 | tf_op jit(solution)/shard_map/ppermute | solution.py:15
  18.9 0.1 fusion.82
  19.1 0.0 copy-start.7
  19.1 0.2 fusion.83
  19.3 2.7 %collective-permute-start.4 = (bf16[4,2,36,192]{3,1,2,0:T(2,128)(2,1)S(1)}, bf16[4,2,36,192]{3,1,2,0:T(2,128)(2,1)S(1)}, u32[]{:S(2)}, u32[]{:S(2)}) collective-permute-start(bf16[4,2,36,192]{3,1,2,0:T(2,128)(2,1)S(1)} %get-tuple-element.11), channel_id=1, source_target_pairs={{8,0},{16,8},{24,16},{9,1},{17,9},{25,17},{10,2},{18,10},{26,18},{... | collective-permute-start | bytes 331784 | tf_op jit(solution)/shard_map/ppermute | solution.py:17
  22.0 1.3 %collective-permute-start.3 = (bf16[4,2,36,192]{3,1,2,0:T(2,128)(2,1)S(1)}, bf16[4,2,36,192]{3,1,2,0:T(2,128)(2,1)S(1)}, u32[]{:S(2)}, u32[]{:S(2)}) collective-permute-start(bf16[4,2,36,192]{3,1,2,0:T(2,128)(2,1)S(1)} %get-tuple-element.12), channel_id=1, source_target_pairs={{0,8},{8,16},{16,24},{1,9},{9,17},{17,25},{2,10},{10,18},{18,26},{... | collective-permute-start | bytes 331784 | tf_op jit(solution)/shard_map/ppermute | solution.py:15
  23.3 0.1 pad.2
  23.5 0.1 copy.14
  23.6 0.1 slice.61
  23.7 0.0 copy-done
  23.7 0.0 copy-done.7
  23.7 0.0 copy-start.2
  23.7 0.0 copy-start.3
  23.7 1.6 %convolution_select_fusion = f32[2,6,8,5,192]{4,2,3,1,0:T(8,128)S(1)} fusion(bf16[3,3,3,192,192]{4,3,2,1,0:T(8,128)(2,1)S(1)} %copy-done, bf16[4,8,1,7,2,192]{5,3,4,1,0,2:T(8,128)(2,1)S(1)} %slice.61, bf16[4,8,1,8,5,192]{5,3,4,1,0,2:T(8,128)(2,1)S(1)} %copy.14, pred[8,5]{0,1:T(8,128)(4,1)S(1)} %copy-done.7), kind=kOutput, calls=%fused_computation.9 | convolution fusion | flops 957671424 | bytes 3022888 | tf_op jit(solution)/shard_map/conv_general_dilated | solution.py:35
  25.3 0.4 copy.15
  25.7 0.0 copy-done.2
  25.7 0.3 fusion.49
  26.0 0.0 copy-done.3
  26.0 0.8 %select_convert_fusion = bf16[2,6,34,192]{3,0,2,1:T(2,128)(2,1)S(1)} fusion(pred[6,34]{1,0:T(8,128)(4,1)S(1)} %copy.12, f32[192]{0:T(256)S(1)} %copy-done.3, f32[2,6,34]{0,2,1:T(8,128)S(1)} %add_rsqrt_fusion, f32[192]{0:T(256)S(1)} %copy-done.2, f32[2,6,1,40,192]{4,0,3,1,2:T(2,128)S(1)} %bitcast.70), kind=kLoop, calls=%fused_computation.59 | loop fusion | flops 861696 | bytes 473388 | tf_op jit(solution)/shard_map/convert_element_type | solution.py:71
  26.8 0.0 collective-permute-done.4
  26.8 3.8 %collective-permute-done.3 = bf16[4,2,36,192]{3,1,2,0:T(2,128)(2,1)S(1)} collective-permute-done((bf16[4,2,36,192]{3,1,2,0:T(2,128)(2,1)S(1)}, bf16[4,2,36,192]{3,1,2,0:T(2,128)(2,1)S(1)}, u32[]{:S(2)}, u32[]{:S(2)}) %collective-permute-start.3) | collective-permute-done | bytes 110624 | tf_op jit(solution)/shard_map/ppermute | solution.py:15
  30.6 0.6 %fusion.53 = (bf16[4,4,1,36,192]{4,1,3,0,2:T(4,128)(2,1)S(1)}, bf16[4,4,1,36,192]{4,1,3,0,2:T(4,128)(2,1)S(1)}) fusion(bf16[4,2,36,192]{3,1,2,0:T(2,128)(2,1)S(1)} %collective-permute-done.4, bf16[4,8,2,192]{3,1,2,0:T(8,128)(2,1)S(1)} %collective-permute-done.2, bf16[4,8,2,192]{3,1,2,0:T(8,128)(2,1)S(1)} %collective-permute-done.1, ...), kind=kLoop, calls=%fused_computation.62 | loop fusion | flops 2211840 | bytes 1105920 | tf_op jit(solution)/shard_map/broadcast_in_dim | solution.py:36
  31.2 0.1 pad
  31.4 0.7 %convolution_select_fusion.2 = f32[2,2,8,5,192]{4,2,3,1,0:T(8,128)S(1)} fusion(bf16[3,3,3,192,192]{4,3,2,1,0:T(8,128)(2,1)S(1)} %copy-done, bf16[4,4,1,7,2,192]{5,3,4,1,0,2:T(8,128)(2,1)S(1)} %slice.58, bf16[4,4,1,8,5,192]{5,3,4,1,0,2:T(8,128)(2,1)S(1)} %copy.10, pred[8,5]{0,1:T(8,128)(4,1)S(1)} %copy-done.7), kind=kOutput, calls=%fused_computation.13 | convolution fusion | flops 319567872 | bytes 2445352 | tf_op jit(solution)/shard_map/conv_general_dilated | solution.py:35
  32.1 0.1 copy.11
  32.2 0.1 pad.4
  32.4 0.7 %convolution_select_fusion.1 = f32[2,2,8,5,192]{4,2,3,1,0:T(8,128)S(1)} fusion(bf16[3,3,3,192,192]{4,3,2,1,0:T(8,128)(2,1)S(1)} %copy-done, bf16[4,4,1,7,2,192]{5,3,4,1,0,2:T(8,128)(2,1)S(1)} %slice.65, bf16[4,4,1,8,5,192]{5,3,4,1,0,2:T(8,128)(2,1)S(1)} %copy.17, pred[8,5]{0,1:T(8,128)(4,1)S(1)} %copy-done.7), kind=kOutput, calls=%fused_computation.12 | convolution fusion | flops 319567872 | bytes 2445352 | tf_op jit(solution)/shard_map/conv_general_dilated | solution.py:35
  33.1 0.1 copy.18
  33.2 0.2 fusion.59
  33.4 0.0 copy-start.5
  33.4 0.0 copy-start.6
  33.5 0.4 select_convert_fusion.2
  33.9 0.1 copy.20
  34.0 0.1 copy.19
  34.0 0.5 %maximum_bitcast_fusion = bf16[2,10,1,34,192]{4,0,3,1,2:T(2,128)(2,1)S(1)} fusion(bf16[2,2,34,192]{3,0,2,1:T(2,128)(2,1)S(1)} %copy.20, bf16[2,6,34,192]{3,0,2,1:T(2,128)(2,1)S(1)} %select_convert_fusion, bf16[2,2,34,192]{3,0,2,1:T(2,128)(2,1)S(1)} %copy.19), kind=kLoop, calls=%fused_computation.60 | loop fusion | flops 261120 | bytes 522240 | tf_op jit(solution)/shard_map/broadcast_in_dim | solution.py:36
  34.6 0.3 pad.6
  35.0 0.1 copy-done.5
  35.2 0.0 copy-done.6
  35.2 1.5 %fusion.11 = bf16[2,8,8,5,192]{4,2,3,1,0:T(8,128)(2,1)S(1)} fusion(bf16[3,3,3,192,192]{4,3,2,1,0:T(8,128)(2,1)S(1)} %copy-done.5, pred[8,5]{0,1:T(8,128)(4,1)S(1)} %copy-done.6, bf16[2,10,1,7,2,192]{5,3,4,1,0,2:T(8,128)(2,1)S(1)} %slice.67, bf16[2,10,1,8,5,192]{5,3,4,1,0,2:T(8,128)(2,1)S(1)} %copy.22), kind=kOutput, calls=%fused_computation.8 | convolution fusion | flops 638545920 | bytes 2589696 | tf_op jit(solution)/shard_map/conv_general_dilated | solution.py:35
  36.6 0.1 copy.24
  36.7 0.0 copy-start.1
  36.7 0.0 copy-start.4
  36.7 2.1 %collective-permute-start.5 = (bf16[2,8,32,192]{3,1,2,0:T(8,128)(2,1)S(1)}, bf16[2,8,32,192]{3,1,2,0:T(8,128)(2,1)S(1)}, u32[]{:S(2)}, u32[]{:S(2)}) collective-permute-start(bf16[2,8,32,192]{3,1,2,0:T(8,128)(2,1)S(1)} %slice_bitcast_fusion.2), channel_id=1, source_target_pairs={{0,32},{32,64},{64,96},{96,128},{128,160},{160,192},{192,224},{224... | collective-permute-start | bytes 589832 | tf_op jit(solution)/shard_map/ppermute | solution.py:27
  38.8 1.4 %fusion.5 = f32[2,8,8,5,192]{4,2,3,1,0:T(8,128)S(1)} fusion(bf16[3,3,3,192,192]{4,3,2,1,0:T(8,128)(2,1)S(1)} %copy-done.5, pred[8,5]{0,1:T(8,128)(4,1)S(1)} %copy-done.6, bf16[2,10,1,7,2,192]{5,3,4,1,0,2:T(8,128)(2,1)S(1)} %slice.67, bf16[2,10,1,8,5,192]{5,3,4,1,0,2:T(8,128)(2,1)S(1)} %copy.22), kind=kOutput, calls=%fused_computation.6 | convolution fusion | flops 638423040 | bytes 2835456 | tf_op jit(solution)/shard_map/conv_general_dilated | solution.py:35
  40.2 0.2 copy.23
  40.5 7.9 %collective-permute-done.5 = bf16[2,8,32,192]{3,1,2,0:T(8,128)(2,1)S(1)} collective-permute-done((bf16[2,8,32,192]{3,1,2,0:T(8,128)(2,1)S(1)}, bf16[2,8,32,192]{3,1,2,0:T(8,128)(2,1)S(1)}, u32[]{:S(2)}, u32[]{:S(2)}) %collective-permute-start.5) | collective-permute-done | bytes 196640 | tf_op jit(solution)/shard_map/ppermute | solution.py:27
  48.3 0.0 copy-done.1
  48.3 0.0 copy-done.4
  48.3 0.2 fusion.35
  48.5 0.8 %copy.25 = bf16[2,8,32,192]{3,2,1,0:T(8,128)(2,1)} copy(bf16[2,8,32,192]{3,1,2,0:T(8,128)(2,1)S(1)} %fusion.35) | data formatting | bytes 393216 | tf_op jit(solution)/shard_map/convert_element_type | solution.py:77
  (13 shorter events, 0.3 us)
Async XLA Ops:
  0.0 23.7 %copy-start = (bf16[3,3,3,192,192]{4,3,2,1,0:T(8,128)(2,1)S(1)}, bf16[3,3,3,192,192]{4,3,2,1,0:T(8,128)(2,1)}, u32[]{:S(2)}) copy-start(bf16[3,3,3,192,192]{4,3,2,1,0:T(8,128)(2,1)} %param.9) | copy-start | bytes 5971972
  2.6 11.2 %collective-permute-start = (bf16[2,8,32,192]{3,1,2,0:T(8,128)(2,1)S(1)}, bf16[2,8,32,192]{3,1,2,0:T(8,128)(2,1)S(1)}, u32[]{:S(2)}, u32[]{:S(2)}) collective-permute-start(bf16[2,8,32,192]{3,1,2,0:T(8,128)(2,1)S(1)} %fusion.32), channel_id=1, source_target_pairs={{0,32},{32,64},{64,96},{96,128},{128,160},{160,192},{192,224},{224... | collective-permute-start | bytes 589832 | tf_op jit(solution)/shard_map/ppermute | solution.py:27
  13.8 4.6 %collective-permute-start.2 = (bf16[4,8,2,192]{3,1,2,0:T(8,128)(2,1)S(1)}, bf16[4,8,2,192]{3,1,2,0:T(8,128)(2,1)S(1)}, u32[]{:S(2)}, u32[]{:S(2)}) collective-permute-start(bf16[4,8,2,192]{3,1,2,0:T(8,128)(2,1)S(1)} %get-tuple-element.14), channel_id=1, source_target_pairs={{1,0},{2,1},{3,2},{4,3},{5,4},{6,5},{7,6},{9,8},{10,9},{11,10},{12... | collective-permute-start | bytes 73736 | tf_op jit(solution)/shard_map/ppermute | solution.py:17
  15.1 3.9 %collective-permute-start.1 = (bf16[4,8,2,192]{3,1,2,0:T(8,128)(2,1)S(1)}, bf16[4,8,2,192]{3,1,2,0:T(8,128)(2,1)S(1)}, u32[]{:S(2)}, u32[]{:S(2)}) collective-permute-start(bf16[4,8,2,192]{3,1,2,0:T(8,128)(2,1)S(1)} %get-tuple-element.13), channel_id=1, source_target_pairs={{0,1},{1,2},{2,3},{3,4},{4,5},{5,6},{6,7},{8,9},{9,10},{10,11},{11... | collective-permute-start | bytes 73736 | tf_op jit(solution)/shard_map/ppermute | solution.py:15
  19.1 4.6 %copy-start.7 = (pred[8,5]{0,1:T(8,128)(4,1)S(1)}, pred[8,5]{0,1:T(8,128)(4,1)}, u32[]{:S(2)}) copy-start(pred[8,5]{0,1:T(8,128)(4,1)} %constant.66) | copy-start | bytes 124
  19.3 7.5 %collective-permute-start.4 = (bf16[4,2,36,192]{3,1,2,0:T(2,128)(2,1)S(1)}, bf16[4,2,36,192]{3,1,2,0:T(2,128)(2,1)S(1)}, u32[]{:S(2)}, u32[]{:S(2)}) collective-permute-start(bf16[4,2,36,192]{3,1,2,0:T(2,128)(2,1)S(1)} %get-tuple-element.11), channel_id=1, source_target_pairs={{8,0},{16,8},{24,16},{9,1},{17,9},{25,17},{10,2},{18,10},{26,18},{... | collective-permute-start | bytes 331784 | tf_op jit(solution)/shard_map/ppermute | solution.py:17
  22.0 8.5 %collective-permute-start.3 = (bf16[4,2,36,192]{3,1,2,0:T(2,128)(2,1)S(1)}, bf16[4,2,36,192]{3,1,2,0:T(2,128)(2,1)S(1)}, u32[]{:S(2)}, u32[]{:S(2)}) collective-permute-start(bf16[4,2,36,192]{3,1,2,0:T(2,128)(2,1)S(1)} %get-tuple-element.12), channel_id=1, source_target_pairs={{0,8},{8,16},{16,24},{1,9},{9,17},{17,25},{2,10},{10,18},{18,26},{... | collective-permute-start | bytes 331784 | tf_op jit(solution)/shard_map/ppermute | solution.py:15
  23.7 2.0 %copy-start.2 = (f32[192]{0:T(256)S(1)}, f32[192]{0:T(256)}, u32[]{:S(2)}) copy-start(f32[192]{0:T(256)} %param.10) | copy-start | bytes 2308
  23.7 2.3 %copy-start.3 = (f32[192]{0:T(256)S(1)}, f32[192]{0:T(256)}, u32[]{:S(2)}) copy-start(f32[192]{0:T(256)} %param.11) | copy-start | bytes 2308
  33.4 1.8 %copy-start.5 = (bf16[3,3,3,192,192]{4,3,2,1,0:T(8,128)(2,1)S(1)}, bf16[3,3,3,192,192]{4,3,2,1,0:T(8,128)(2,1)}, u32[]{:S(2)}) copy-start(bf16[3,3,3,192,192]{4,3,2,1,0:T(8,128)(2,1)} %param.12) | copy-start | bytes 5971972
  33.4 1.7 %copy-start.6 = (pred[8,5]{0,1:T(8,128)(4,1)S(1)}, pred[8,5]{0,1:T(8,128)(4,1)}, u32[]{:S(2)}) copy-start(pred[8,5]{0,1:T(8,128)(4,1)} %constant.65) | copy-start | bytes 124
  36.7 11.6 %copy-start.1 = (bf16[2,8,32,192]{3,2,1,0:T(8,128)(2,1)S(1)}, bf16[2,8,32,192]{3,2,1,0:T(8,128)(2,1)}, u32[]{:S(2)}) copy-start(bf16[2,8,32,192]{3,2,1,0:T(8,128)(2,1)} %param.7) | copy-start | bytes 589828
  36.7 11.6 %copy-start.4 = (f32[192]{0:T(256)S(1)}, f32[192]{0:T(256)}, u32[]{:S(2)}) copy-start(f32[192]{0:T(256)} %param.13) | copy-start | bytes 2308
  36.7 11.6 %collective-permute-start.5 = (bf16[2,8,32,192]{3,1,2,0:T(8,128)(2,1)S(1)}, bf16[2,8,32,192]{3,1,2,0:T(8,128)(2,1)S(1)}, u32[]{:S(2)}, u32[]{:S(2)}) collective-permute-start(bf16[2,8,32,192]{3,1,2,0:T(8,128)(2,1)S(1)} %slice_bitcast_fusion.2), channel_id=1, source_target_pairs={{0,32},{32,64},{64,96},{96,128},{128,160},{160,192},{192,224},{224... | collective-permute-start | bytes 589832 | tf_op jit(solution)/shard_map/ppermute | solution.py:27

commit v15 on v14

--- a/solution.py
+++ b/solution.py
@@ -70,7 +70,16 @@
         mask = keep[limits[index] : limits[index + 1]]
         pieces.append(jnp.where(mask[None, :, :, None], act, 0.0).astype(jnp.bfloat16))
     second_act = jnp.concatenate(pieces, axis=1)
-    ahead = conv_valid(second_act, second_weight[0:2], (0, 1)).astype(jnp.bfloat16)
+    top_act, middle_act, bottom_act = pieces
+    reach = middle_act.shape[1]
+    parts = (
+        jnp.concatenate([top_act, middle_act[:, :2]], axis=1),
+        middle_act,
+        jnp.concatenate([middle_act[:, reach - 2 :], bottom_act], axis=1),
+    )
+    ahead = jnp.concatenate(
+        [conv_valid(part, second_weight[0:2], (0, 1)).astype(jnp.bfloat16) for part in parts], axis=1
+    )
     behind = shifted(ahead, "tm", 1)
     own = conv_valid(second_act, second_weight[1:3], (1, 0))
     decoded = values + own + behind.astype(jnp.float32) + second_bias

time: 49.6 us -> 58.3 us (1.18)
  the two profiles are of different devices: /device:TPU:262 before, /device:TPU:399 now
where the time goes in v15:
time: 58.3 us; the launch traced here: 58 us
  waiting for transfers between devices  17.2 us (30%)
  starting transfers between devices  17 us (29%)
  other arithmetic  8.98 us (15%)
  local copies, waits for them, and re-layouts  7.13 us (12%)
  matrix products  6.93 us (12%)
  between operations  0.63 us (1%)
    ppermute x2, waiting for transfers between devices, shifted(): lax.ppermute(value, axis, [(source, source + steps) for source in range(i...  14.8 us
    conv_general_dilated x7, matrix products, conv_valid(): lax.conv_general_dilated(stack[None], kernel, window_strides=(1, 1, 1), p...  6.93 us
    ppermute x2, starting transfers between devices, with_halo(): lax.ppermute(head, axis, [(i + 1, i) for i in range(ends)])  6.58 us
    ppermute x2, starting transfers between devices, with_halo(): lax.ppermute(tail, axis, [(i, i + 1) for i in range(ends)])  5.9 us
    ppermute x2, starting transfers between devices, shifted(): lax.ppermute(value, axis, [(source, source + steps) for source in range(i...  4.57 us
    convert_element_type x3, other arithmetic, local(): jnp.where(mask[None, :, :, None], act, 0.0).astype(jnp.bfloat16)  2.98 us
    ppermute x2, waiting for transfers between devices, with_halo(): lax.ppermute(head, axis, [(i + 1, i) for i in range(ends)])  2.48 us
    broadcast_in_dim x5, other arithmetic, conv_valid(): stack[None]  2.38 us
  transfers between devices with their start and end apart: 6, of which 3 were waited for; matrix products, arithmetic and copies ran while one was open for 20% of the time, Pallas kernels for 0%

profile of v15, /device:TPU:399, one launch (start us, length us, event | category | flops | bytes accessed | tf_op | source)
XLA Modules:
  0.0 58.0 jit_solution(8160874421439931003)
XLA Ops:
  0.0 1.3 %fusion.57 = f32[2,8,32]{1,2,0:T(8,128)S(1)} fusion(bf16[2,8,32,192]{3,2,1,0:T(8,128)(2,1)} %param.7), kind=kLoop, calls=%fused_computation.56 | loop fusion | flops 294400 | bytes 198656 | tf_op jit(solution)/shard_map/reduce_sum | solution.py:31
  1.4 1.2 %fusion.64 = bf16[2,8,32,192]{3,1,2,0:T(8,128)(2,1)S(1)} fusion(f32[192]{0:T(256)} %param.8, f32[2,8,32]{1,2,0:T(8,128)S(1)} %add_rsqrt_fusion.3, bf16[2,8,32,192]{3,2,1,0:T(8,128)(2,1)} %param.7), kind=kLoop, calls=%fused_computation.63 | loop fusion | flops 786432 | bytes 396032 | tf_op jit(solution)/shard_map/convert_element_type | solution.py:56
  2.6 2.6 %collective-permute-start = (bf16[2,8,32,192]{3,1,2,0:T(8,128)(2,1)S(1)}, bf16[2,8,32,192]{3,1,2,0:T(8,128)(2,1)S(1)}, u32[]{:S(2)}, u32[]{:S(2)}) collective-permute-start(bf16[2,8,32,192]{3,1,2,0:T(8,128)(2,1)S(1)} %fusion.64), channel_id=1, source_target_pairs={{0,32},{32,64},{64,96},{96,128},{128,160},{160,192},{192,224},{224... | collective-permute-start | bytes 589832 | tf_op jit(solution)/shard_map/ppermute | solution.py:27
  5.3 0.1 broadcast_and_fusion
  5.4 7.5 %collective-permute-done = bf16[2,8,32,192]{3,1,2,0:T(8,128)(2,1)S(1)} collective-permute-done((bf16[2,8,32,192]{3,1,2,0:T(8,128)(2,1)S(1)}, bf16[2,8,32,192]{3,1,2,0:T(8,128)(2,1)S(1)}, u32[]{:S(2)}, u32[]{:S(2)}) %collective-permute-start) | collective-permute-done | bytes 196640 | tf_op jit(solution)/shard_map/ppermute | solution.py:27
  12.9 4.6 %collective-permute-start.1 = (bf16[4,8,2,192]{3,1,2,0:T(8,128)(2,1)S(1)}, bf16[4,8,2,192]{3,1,2,0:T(8,128)(2,1)S(1)}, u32[]{:S(2)}, u32[]{:S(2)}) collective-permute-start(bf16[4,8,2,192]{3,1,2,0:T(8,128)(2,1)S(1)} %get-tuple-element.13), channel_id=1, source_target_pairs={{0,1},{1,2},{2,3},{3,4},{4,5},{5,6},{6,7},{8,9},{9,10},{10,11},{11... | collective-permute-start | bytes 73736 | tf_op jit(solution)/shard_map/ppermute | solution.py:15
  17.5 1.9 %collective-permute-start.2 = (bf16[4,8,2,192]{3,1,2,0:T(8,128)(2,1)S(1)}, bf16[4,8,2,192]{3,1,2,0:T(8,128)(2,1)S(1)}, u32[]{:S(2)}, u32[]{:S(2)}) collective-permute-start(bf16[4,8,2,192]{3,1,2,0:T(8,128)(2,1)S(1)} %get-tuple-element.14), channel_id=1, source_target_pairs={{1,0},{2,1},{3,2},{4,3},{5,4},{6,5},{7,6},{9,8},{10,9},{11,10},{12... | collective-permute-start | bytes 73736 | tf_op jit(solution)/shard_map/ppermute | solution.py:17
  19.5 0.1 fusion.145
  19.5 0.1 slice.75
  19.6 0.7 %copy.26 = pred[6,34]{1,0:T(8,128)(4,1)} copy(pred[6,34]{0,1:T(8,128)(4,1)S(1)} %slice.75) | data formatting | bytes 408 | tf_op jit(solution)/shard_map/slice | solution.py:70
  20.3 2.5 %collective-permute-done.2 = bf16[4,8,2,192]{3,1,2,0:T(8,128)(2,1)S(1)} collective-permute-done((bf16[4,8,2,192]{3,1,2,0:T(8,128)(2,1)S(1)}, bf16[4,8,2,192]{3,1,2,0:T(8,128)(2,1)S(1)}, u32[]{:S(2)}, u32[]{:S(2)}) %collective-permute-start.2) | collective-permute-done | bytes 24608 | tf_op jit(solution)/shard_map/ppermute | solution.py:17
  22.8 0.1 fusion.142
  22.9 0.0 copy-start.6
  22.9 0.0 copy-start.12
  22.9 0.9 %fusion.143 = (bf16[4,2,36,192]{3,1,2,0:T(2,128)(2,1)}, bf16[4,2,36,192]{3,1,2,0:T(2,128)(2,1)}) fusion(bf16[4,8,36,192]{3,1,2,0:T(8,128)(2,1)S(1)} %get-tuple-element.8), kind=kLoop, calls=%fused_computation.176 | loop fusion | bytes 442368 | tf_op jit(solution)/shard_map/slice | solution.py:11
  23.8 1.3 %collective-permute-start.3 = (bf16[4,2,36,192]{3,1,2,0:T(2,128)(2,1)}, bf16[4,2,36,192]{3,1,2,0:T(2,128)(2,1)}, u32[]{:S(2)}, u32[]{:S(2)}) collective-permute-start(bf16[4,2,36,192]{3,1,2,0:T(2,128)(2,1)} %get-tuple-element.12), channel_id=1, source_target_pairs={{0,8},{8,16},{16,24},{1,9},{9,17},{17,25},{2,10},{10,18},{18,26},{... | collective-permute-start | bytes 331784 | tf_op jit(solution)/shard_map/ppermute | solution.py:15
  25.1 4.7 %collective-permute-start.4 = (bf16[4,2,36,192]{3,1,2,0:T(2,128)(2,1)}, bf16[4,2,36,192]{3,1,2,0:T(2,128)(2,1)}, u32[]{:S(2)}, u32[]{:S(2)}) collective-permute-start(bf16[4,2,36,192]{3,1,2,0:T(2,128)(2,1)} %get-tuple-element.11), channel_id=1, source_target_pairs={{8,0},{16,8},{24,16},{9,1},{17,9},{25,17},{10,2},{18,10},{26,18},{... | collective-permute-start | bytes 331784 | tf_op jit(solution)/shard_map/ppermute | solution.py:17
  29.8 0.1 pad.2
  29.9 0.1 copy.13
  30.0 0.1 slice.76
  30.1 2.3 %fusion.94 = (f32[2,6,8,5,192]{4,2,3,1,0:T(8,128)}, f32[2,6,8,5,192]{4,2,3,1,0:T(8,128)S(1)}) fusion(f32[192]{0:T(256)S(1)} %copy-done.6, bf16[3,3,3,192,192]{4,3,2,1,0:T(8,128)(2,1)S(1)} %copy-done, bf16[4,8,1,7,2,192]{5,3,4,1,0,2:T(8,128)(2,1)S(1)} %slice.76, bf16[4,8,1,8,5,192]{5,3,4,1,0,2:T(8,128)(2,1)S(1)} %copy.13, pred[8,5]{0,1:T(8,128)(4,1)S(1)} %copy-done.12), kind=kOutput, calls=%fused_computation.105 | convolution fusion | flops 957947904 | bytes 3392296 | tf_op jit(solution)/shard_map/conv_general_dilated | solution.py:35
  32.5 0.4 copy.14
  32.9 0.1 slice.77
  33.0 0.2 fusion.46
  33.3 0.4 copy.28
  33.6 1.1 %fusion.54 = bf16[2,6,34,192]{3,1,2,0:T(8,128)(2,1)S(1)} fusion(f32[192]{0:T(256)} %param.11, f32[2,6,34]{1,2,0:T(8,128)S(1)} %add_rsqrt_fusion.1, pred[6,34]{0,1:T(8,128)(4,1)S(1)} %slice.75, f32[192]{0:T(256)} %param.10, f32[2,6,1,34,192]{4,0,3,1,2:T(2,128)S(1)} %slice.77), kind=kLoop, calls=%fused_computation.51 | loop fusion | flops 861696 | bytes 473388 | tf_op jit(solution)/shard_map/convert_element_type | solution.py:71
  34.7 0.1 fusion.144
  34.9 1.4 %copy.27 = f32[2,6,8,5,192]{4,0,3,2,1:T(2,128)S(1)} copy(f32[2,6,8,5,192]{4,2,3,1,0:T(8,128)} %get-tuple-element.21) | data formatting | bytes 737280 | tf_op jit(solution)/shard_map/convert_element_type | solution.py:68
  36.3 1.4 %fusion.109 = bf16[2,6,1,34,192]{4,0,3,1,2:T(2,128)(2,1)S(1)} fusion(f32[192]{0:T(256)} %param.11, f32[2,6,34]{0,2,1:T(8,128)S(1)} %copy.28, f32[2,6,1,40,192]{4,0,3,1,2:T(2,128)S(1)} %bitcast.108, pred[6,34]{1,0:T(8,128)(4,1)} %copy.26), kind=kLoop, calls=%fused_computation.118 | loop fusion | flops 626688 | bytes 472620 | tf_op jit(solution)/shard_map/convert_element_type | solution.py:71
  37.7 0.2 pad.10
  38.0 0.0 copy-start.2
  38.0 0.8 %fusion.15 = bf16[2,4,8,5,192]{4,2,3,1,0:T(8,128)(2,1)S(1)} fusion(bf16[3,3,3,192,192]{4,3,2,1,0:T(8,128)(2,1)S(1)} %copy-done.10, bf16[2,6,1,7,2,192]{5,3,4,1,0,2:T(8,128)(2,1)S(1)} %slice.88, bf16[2,6,1,8,5,192]{5,3,4,1,0,2:T(8,128)(2,1)S(1)} %copy.30, pred[8,5]{0,1:T(8,128)(4,1)S(1)} %copy-done.11), kind=kOutput, calls=%fused_computation.13 | convolution fusion | flops 319401984 | bytes 2237440 | tf_op jit(solution)/shard_map/conv_general_dilated | solution.py:35
  38.9 0.0 copy-start.13
  38.9 0.1 copy.31
  39.0 1.6 %fusion.91 = (bf16[4,4,1,36,192]{4,1,3,0,2:T(4,128)(2,1)S(1)}, bf16[4,4,1,36,192]{4,1,3,0,2:T(4,128)(2,1)S(1)}) fusion(bf16[4,2,36,192]{3,1,2,0:T(2,128)(2,1)} %collective-permute-done.4, bf16[4,8,2,192]{3,1,2,0:T(8,128)(2,1)S(1)} %copy-done.5, bf16[4,8,2,192]{3,1,2,0:T(8,128)(2,1)S(1)} %collective-permute-done.1, bf16[2,8,32,192]{3,1,2,0:T(8,128)(2,1)S(1)} %fusion.64, ...), kind=kLoop, calls=%fused_computation.94 | loop fusion | flops 2211840 | bytes 1105920 | tf_op jit(solution)/shard_map/broadcast_in_dim | solution.py:36
  40.7 0.1 pad.4
  40.9 0.7 %convolution_select_fusion.1 = f32[2,2,8,5,192]{4,2,3,1,0:T(8,128)S(1)} fusion(bf16[3,3,3,192,192]{4,3,2,1,0:T(8,128)(2,1)S(1)} %copy-done, bf16[4,4,1,7,2,192]{5,3,4,1,0,2:T(8,128)(2,1)S(1)} %slice.80, bf16[4,4,1,8,5,192]{5,3,4,1,0,2:T(8,128)(2,1)S(1)} %copy.17, pred[8,5]{0,1:T(8,128)(4,1)S(1)} %copy-done.13), kind=kOutput, calls=%fused_computation.18 | convolution fusion | flops 319567872 | bytes 2445352 | tf_op jit(solution)/shard_map/conv_general_dilated | solution.py:35
  41.6 0.1 copy.18
  41.7 0.1 pad
  41.9 0.0 copy-start.7
  41.9 0.0 copy-start.8
  41.9 0.7 %convolution_select_fusion.2 = f32[2,2,8,5,192]{4,2,3,1,0:T(8,128)S(1)} fusion(bf16[3,3,3,192,192]{4,3,2,1,0:T(8,128)(2,1)S(1)} %copy-done, bf16[4,4,1,7,2,192]{5,3,4,1,0,2:T(8,128)(2,1)S(1)} %slice.73, bf16[4,4,1,8,5,192]{5,3,4,1,0,2:T(8,128)(2,1)S(1)} %copy.10, pred[8,5]{0,1:T(8,128)(4,1)S(1)} %copy-done.13), kind=kOutput, calls=%fused_computation.19 | convolution fusion | flops 319567872 | bytes 2445352 | tf_op jit(solution)/shard_map/conv_general_dilated | solution.py:35
  42.6 0.1 copy.11
  42.7 0.2 fusion.111
  43.0 0.4 select_convert_fusion.2
  43.4 0.2 maximum_bitcast_fusion.1
  43.6 0.1 pad.8
  43.7 0.5 fusion.28
  44.2 0.1 copy.25
  44.4 0.3 maximum_bitcast_fusion
  44.7 0.2 maximum_bitcast_fusion.2
  44.8 0.1 pad.12
  45.0 0.5 fusion.25
  45.5 0.1 copy.34
  45.6 0.2 pad_maximum_fusion.9
  45.9 1.9 %collective-permute-start.5 = (bf16[2,8,32,192]{3,1,2,0:T(8,128)(2,1)S(1)}, bf16[2,8,32,192]{3,1,2,0:T(8,128)(2,1)S(1)}, u32[]{:S(2)}, u32[]{:S(2)}) collective-permute-start(bf16[2,8,32,192]{3,1,2,0:T(8,128)(2,1)S(1)} %pad_maximum_fusion.9), channel_id=1, source_target_pairs={{0,32},{32,64},{64,96},{96,128},{128,160},{160,192},{192,224},{224... | collective-permute-start | bytes 589832 | tf_op jit(solution)/shard_map/ppermute | solution.py:27
  47.8 0.1 pad.6
  47.9 0.1 copy.21
  48.1 0.0 copy-start.9
  48.1 1.4 %fusion.9 = f32[2,8,8,5,192]{4,2,3,1,0:T(8,128)S(1)} fusion(bf16[3,3,3,192,192]{4,3,2,1,0:T(8,128)(2,1)S(1)} %copy-done.10, bf16[2,10,1,7,2,192]{5,3,4,1,0,2:T(8,128)(2,1)S(1)} %slice.82, bf16[2,10,1,8,5,192]{5,3,4,1,0,2:T(8,128)(2,1)S(1)} %copy.21, pred[8,5]{0,1:T(8,128)(4,1)S(1)} %copy-done.11), kind=kOutput, calls=%fused_computation.10 | convolution fusion | flops 638423040 | bytes 2835456 | tf_op jit(solution)/shard_map/conv_general_dilated | solution.py:35
  49.5 0.2 copy.22
  49.7 7.2 %collective-permute-done.5 = bf16[2,8,32,192]{3,1,2,0:T(8,128)(2,1)S(1)} collective-permute-done((bf16[2,8,32,192]{3,1,2,0:T(8,128)(2,1)S(1)}, bf16[2,8,32,192]{3,1,2,0:T(8,128)(2,1)S(1)}, u32[]{:S(2)}, u32[]{:S(2)}) %collective-permute-start.5) | collective-permute-done | bytes 196640 | tf_op jit(solution)/shard_map/ppermute | solution.py:27
  57.0 0.2 fusion.67
  57.2 0.8 %copy.35 = bf16[2,8,32,192]{3,2,1,0:T(8,128)(2,1)} copy(bf16[2,8,32,192]{3,1,2,0:T(8,128)(2,1)S(1)} %fusion.67) | data formatting | bytes 393216 | tf_op jit(solution)/shard_map/convert_element_type | solution.py:86
  (44 shorter events, 0.6 us)
Async XLA Ops:
  0.0 30.1 %copy-start = (bf16[3,3,3,192,192]{4,3,2,1,0:T(8,128)(2,1)S(1)}, bf16[3,3,3,192,192]{4,3,2,1,0:T(8,128)(2,1)}, u32[]{:S(2)}) copy-start(bf16[3,3,3,192,192]{4,3,2,1,0:T(8,128)(2,1)} %param.9) | copy-start | bytes 5971972
  2.6 10.3 %collective-permute-start = (bf16[2,8,32,192]{3,1,2,0:T(8,128)(2,1)S(1)}, bf16[2,8,32,192]{3,1,2,0:T(8,128)(2,1)S(1)}, u32[]{:S(2)}, u32[]{:S(2)}) collective-permute-start(bf16[2,8,32,192]{3,1,2,0:T(8,128)(2,1)S(1)} %fusion.64), channel_id=1, source_target_pairs={{0,32},{32,64},{64,96},{96,128},{128,160},{160,192},{192,224},{224... | collective-permute-start | bytes 589832 | tf_op jit(solution)/shard_map/ppermute | solution.py:27
  12.9 17.0 %copy-start.1 = (bf16[2,8,32,192]{3,1,2,0:T(8,128)(2,1)}, bf16[2,8,32,192]{3,1,2,0:T(8,128)(2,1)S(1)}, u32[]{:S(2)}) copy-start(bf16[2,8,32,192]{3,1,2,0:T(8,128)(2,1)S(1)} %collective-permute-done) | copy-start | bytes 589828
  12.9 7.4 %collective-permute-start.1 = (bf16[4,8,2,192]{3,1,2,0:T(8,128)(2,1)S(1)}, bf16[4,8,2,192]{3,1,2,0:T(8,128)(2,1)S(1)}, u32[]{:S(2)}, u32[]{:S(2)}) collective-permute-start(bf16[4,8,2,192]{3,1,2,0:T(8,128)(2,1)S(1)} %get-tuple-element.13), channel_id=1, source_target_pairs={{0,1},{1,2},{2,3},{3,4},{4,5},{5,6},{6,7},{8,9},{9,10},{10,11},{11... | collective-permute-start | bytes 73736 | tf_op jit(solution)/shard_map/ppermute | solution.py:15
  17.5 5.2 %collective-permute-start.2 = (bf16[4,8,2,192]{3,1,2,0:T(8,128)(2,1)S(1)}, bf16[4,8,2,192]{3,1,2,0:T(8,128)(2,1)S(1)}, u32[]{:S(2)}, u32[]{:S(2)}) collective-permute-start(bf16[4,8,2,192]{3,1,2,0:T(8,128)(2,1)S(1)} %get-tuple-element.14), channel_id=1, source_target_pairs={{1,0},{2,1},{3,2},{4,3},{5,4},{6,5},{7,6},{9,8},{10,9},{11,10},{12... | collective-permute-start | bytes 73736 | tf_op jit(solution)/shard_map/ppermute | solution.py:17
  22.8 7.3 %copy-start.4 = (bf16[4,8,2,192]{3,1,2,0:T(8,128)(2,1)}, bf16[4,8,2,192]{3,1,2,0:T(8,128)(2,1)S(1)}, u32[]{:S(2)}) copy-start(bf16[4,8,2,192]{3,1,2,0:T(8,128)(2,1)S(1)} %collective-permute-done.2) | copy-start | bytes 73732
  22.9 7.2 %copy-start.6 = (f32[192]{0:T(256)S(1)}, f32[192]{0:T(256)}, u32[]{:S(2)}) copy-start(f32[192]{0:T(256)} %param.10) | copy-start | bytes 2308
  22.9 7.2 %copy-start.12 = (pred[8,5]{0,1:T(8,128)(4,1)S(1)}, pred[8,5]{0,1:T(8,128)(4,1)}, u32[]{:S(2)}) copy-start(pred[8,5]{0,1:T(8,128)(4,1)} %constant.74) | copy-start | bytes 124
  23.8 15.2 %collective-permute-start.3 = (bf16[4,2,36,192]{3,1,2,0:T(2,128)(2,1)}, bf16[4,2,36,192]{3,1,2,0:T(2,128)(2,1)}, u32[]{:S(2)}, u32[]{:S(2)}) collective-permute-start(bf16[4,2,36,192]{3,1,2,0:T(2,128)(2,1)} %get-tuple-element.12), channel_id=1, source_target_pairs={{0,8},{8,16},{16,24},{1,9},{9,17},{17,25},{2,10},{10,18},{18,26},{... | collective-permute-start | bytes 331784 | tf_op jit(solution)/shard_map/ppermute | solution.py:15
  25.1 13.9 %collective-permute-start.4 = (bf16[4,2,36,192]{3,1,2,0:T(2,128)(2,1)}, bf16[4,2,36,192]{3,1,2,0:T(2,128)(2,1)}, u32[]{:S(2)}, u32[]{:S(2)}) collective-permute-start(bf16[4,2,36,192]{3,1,2,0:T(2,128)(2,1)} %get-tuple-element.11), channel_id=1, source_target_pairs={{8,0},{16,8},{24,16},{9,1},{17,9},{25,17},{10,2},{18,10},{26,18},{... | collective-permute-start | bytes 331784 | tf_op jit(solution)/shard_map/ppermute | solution.py:17
  33.6 4.4 %copy-start.10 = (bf16[3,3,3,192,192]{4,3,2,1,0:T(8,128)(2,1)S(1)}, bf16[3,3,3,192,192]{4,3,2,1,0:T(8,128)(2,1)}, u32[]{:S(2)}) copy-start(bf16[3,3,3,192,192]{4,3,2,1,0:T(8,128)(2,1)} %param.12) | copy-start | bytes 5971972
  33.6 4.4 %copy-start.11 = (pred[8,5]{0,1:T(8,128)(4,1)S(1)}, pred[8,5]{0,1:T(8,128)(4,1)}, u32[]{:S(2)}) copy-start(pred[8,5]{0,1:T(8,128)(4,1)} %constant.73) | copy-start | bytes 124
  38.0 1.0 %copy-start.2 = (bf16[2,8,32,192]{3,1,2,0:T(8,128)(2,1)S(1)}, bf16[2,8,32,192]{3,1,2,0:T(8,128)(2,1)}, u32[]{:S(2)}) copy-start(bf16[2,8,32,192]{3,1,2,0:T(8,128)(2,1)} %copy-done.1) | copy-start | bytes 589828
  38.0 1.0 %copy-start.5 = (bf16[4,8,2,192]{3,1,2,0:T(8,128)(2,1)S(1)}, bf16[4,8,2,192]{3,1,2,0:T(8,128)(2,1)}, u32[]{:S(2)}) copy-start(bf16[4,8,2,192]{3,1,2,0:T(8,128)(2,1)} %copy-done.4) | copy-start | bytes 73732
  38.9 2.0 %copy-start.13 = (pred[8,5]{0,1:T(8,128)(4,1)S(1)}, pred[8,5]{0,1:T(8,128)(4,1)}, u32[]{:S(2)}) copy-start(pred[8,5]{0,1:T(8,128)(4,1)} %constant.74) | copy-start | bytes 124
  41.9 0.8 %copy-start.7 = (f32[192]{0:T(256)S(1)}, f32[192]{0:T(256)}, u32[]{:S(2)}) copy-start(f32[192]{0:T(256)} %param.10) | copy-start | bytes 2308
  41.9 1.0 %copy-start.8 = (f32[192]{0:T(256)S(1)}, f32[192]{0:T(256)}, u32[]{:S(2)}) copy-start(f32[192]{0:T(256)} %param.11) | copy-start | bytes 2308
  45.9 11.1 %collective-permute-start.5 = (bf16[2,8,32,192]{3,1,2,0:T(8,128)(2,1)S(1)}, bf16[2,8,32,192]{3,1,2,0:T(8,128)(2,1)S(1)}, u32[]{:S(2)}, u32[]{:S(2)}) collective-permute-start(bf16[2,8,32,192]{3,1,2,0:T(8,128)(2,1)S(1)} %pad_maximum_fusion.9), channel_id=1, source_target_pairs={{0,32},{32,64},{64,96},{96,128},{128,160},{160,192},{192,224},{224... | collective-permute-start | bytes 589832 | tf_op jit(solution)/shard_map/ppermute | solution.py:27
  48.1 8.9 %copy-start.3 = (bf16[2,8,32,192]{3,2,1,0:T(8,128)(2,1)S(1)}, bf16[2,8,32,192]{3,2,1,0:T(8,128)(2,1)}, u32[]{:S(2)}) copy-start(bf16[2,8,32,192]{3,2,1,0:T(8,128)(2,1)} %param.7) | copy-start | bytes 589828
  48.1 8.9 %copy-start.9 = (f32[192]{0:T(256)S(1)}, f32[192]{0:T(256)}, u32[]{:S(2)}) copy-start(f32[192]{0:T(256)} %param.13) | copy-start | bytes 2308

commit v16 on v14

--- a/solution.py
+++ b/solution.py
@@ -59,16 +59,21 @@
     middle = conv_valid(wide, first_weight)
     first_ext = with_halo(wide, (("row", 1),), 2)
     edge = 2 * 2
-    top = conv_valid(first_ext[:, :edge], first_weight)
-    bottom = conv_valid(first_ext[:, first_ext.shape[1] - edge :], first_weight)
+    ends = jnp.concatenate([first_ext[:, :edge], first_ext[:, first_ext.shape[1] - edge :]], axis=1)
+    joined = conv_valid(ends, first_weight)
     keep = inside("row", rows, 1)[:, None] & inside("col", cols, 1)[None, :]
-    limits = (0, top.shape[1], top.shape[1] + middle.shape[1], keep.shape[0])
-    pieces = []
-    for index, piece in enumerate((top, middle, bottom)):
+    span = middle.shape[1]
+
+    def activated(piece, mask):
         hidden = (piece + first_bias).astype(jnp.bfloat16).astype(jnp.float32)
         act = jax.nn.silu(rms_norm(hidden, second_gain))
-        mask = keep[limits[index] : limits[index + 1]]
-        pieces.append(jnp.where(mask[None, :, :, None], act, 0.0).astype(jnp.bfloat16))
+        return jnp.where(mask[None, :, :, None], act, 0.0).astype(jnp.bfloat16)
+
+    middle_act = activated(middle, keep[2 : 2 + span])
+    edge_keep = jnp.concatenate([keep[:2], keep[:2], keep[2 + span :]], axis=0)
+    edge_act = activated(joined, edge_keep)
+    top_act, bottom_act = edge_act[:, :2], edge_act[:, 4:]
+    pieces = (top_act, middle_act, bottom_act)
     second_act = jnp.concatenate(pieces, axis=1)
     ahead = conv_valid(second_act, second_weight[0:2], (0, 1)).astype(jnp.bfloat16)
     behind = shifted(ahead, "tm", 1)

time: 49.6 us -> 56.5 us (1.14)
  the two profiles are of different devices: /device:TPU:262 before, /device:TPU:401 now
where the time goes in v16:
time: 56.5 us; the launch traced here: 55.6 us
  waiting for transfers between devices  23.9 us (42%)
  starting transfers between devices  15.2 us (27%)
  other arithmetic  6.51 us (12%)
  matrix products  5.94 us (11%)
  local copies, waits for them, and re-layouts  3.61 us (6%)
    ppermute x2, waiting for transfers between devices, shifted(): lax.ppermute(value, axis, [(source, source + steps) for source in range(i...  14.5 us
    ppermute x2, waiting for transfers between devices, with_halo(): lax.ppermute(head, axis, [(i + 1, i) for i in range(ends)])  7.52 us
    ppermute x2, starting transfers between devices, with_halo(): lax.ppermute(tail, axis, [(i, i + 1) for i in range(ends)])  7.45 us
    conv_general_dilated x4, matrix products, conv_valid(): lax.conv_general_dilated(stack[None], kernel, window_strides=(1, 1, 1), p...  5.94 us
    ppermute x2, starting transfers between devices, shifted(): lax.ppermute(value, axis, [(source, source + steps) for source in range(i...  4.57 us
    ppermute x2, starting transfers between devices, with_halo(): lax.ppermute(head, axis, [(i + 1, i) for i in range(ends)])  3.21 us
    ppermute x2, waiting for transfers between devices, with_halo(): lax.ppermute(tail, axis, [(i, i + 1) for i in range(ends)])  1.9 us
    reduce_sum x2, other arithmetic, rms_norm(): jnp.mean(values * values, axis=-1, keepdims=True) + 1e-06  1.89 us
  transfers between devices with their start and end apart: 6, of which 5 were waited for; matrix products, arithmetic and copies ran while one was open for 3% of the time, Pallas kernels for 0%

profile of v16, /device:TPU:401, one launch (start us, length us, event | category | flops | bytes accessed | tf_op | source)
XLA Modules:
  0.0 55.6 jit_solution(2283413412515986957)
XLA Ops:
  0.0 0.0 copy-start
  0.0 1.3 %fusion.48 = f32[2,8,32]{1,2,0:T(8,128)S(1)} fusion(bf16[2,8,32,192]{3,2,1,0:T(8,128)(2,1)} %param.7), kind=kLoop, calls=%fused_computation.50 | loop fusion | flops 294400 | bytes 198656 | tf_op jit(solution)/shard_map/reduce_sum | solution.py:31
  1.4 1.2 %fusion.55 = bf16[2,8,32,192]{3,1,2,0:T(8,128)(2,1)S(1)} fusion(f32[192]{0:T(256)} %param.8, f32[2,8,32]{1,2,0:T(8,128)S(1)} %add_rsqrt_fusion.2, bf16[2,8,32,192]{3,2,1,0:T(8,128)(2,1)} %param.7), kind=kLoop, calls=%fused_computation.57 | loop fusion | flops 786432 | bytes 396032 | tf_op jit(solution)/shard_map/convert_element_type | solution.py:56
  2.6 2.6 %collective-permute-start = (bf16[2,8,32,192]{3,1,2,0:T(8,128)(2,1)S(1)}, bf16[2,8,32,192]{3,1,2,0:T(8,128)(2,1)S(1)}, u32[]{:S(2)}, u32[]{:S(2)}) collective-permute-start(bf16[2,8,32,192]{3,1,2,0:T(8,128)(2,1)S(1)} %fusion.55), channel_id=1, source_target_pairs={{0,32},{32,64},{64,96},{96,128},{128,160},{160,192},{192,224},{224... | collective-permute-start | bytes 589832 | tf_op jit(solution)/shard_map/ppermute | solution.py:27
  5.3 0.1 broadcast_and_fusion
  5.4 7.5 %collective-permute-done = bf16[2,8,32,192]{3,1,2,0:T(8,128)(2,1)S(1)} collective-permute-done((bf16[2,8,32,192]{3,1,2,0:T(8,128)(2,1)S(1)}, bf16[2,8,32,192]{3,1,2,0:T(8,128)(2,1)S(1)}, u32[]{:S(2)}, u32[]{:S(2)}) %collective-permute-start) | collective-permute-done | bytes 196640 | tf_op jit(solution)/shard_map/ppermute | solution.py:27
  12.9 4.3 %collective-permute-start.1 = (bf16[4,8,2,192]{3,1,2,0:T(8,128)(2,1)S(1)}, bf16[4,8,2,192]{3,1,2,0:T(8,128)(2,1)S(1)}, u32[]{:S(2)}, u32[]{:S(2)}) collective-permute-start(bf16[4,8,2,192]{3,1,2,0:T(8,128)(2,1)S(1)} %get-tuple-element.11), channel_id=1, source_target_pairs={{0,1},{1,2},{2,3},{3,4},{4,5},{5,6},{6,7},{8,9},{9,10},{10,11},{11... | collective-permute-start | bytes 73736 | tf_op jit(solution)/shard_map/ppermute | solution.py:15
  17.2 1.9 %collective-permute-start.2 = (bf16[4,8,2,192]{3,1,2,0:T(8,128)(2,1)S(1)}, bf16[4,8,2,192]{3,1,2,0:T(8,128)(2,1)S(1)}, u32[]{:S(2)}, u32[]{:S(2)}) collective-permute-start(bf16[4,8,2,192]{3,1,2,0:T(8,128)(2,1)S(1)} %get-tuple-element.12), channel_id=1, source_target_pairs={{1,0},{2,1},{3,2},{4,3},{5,4},{6,5},{7,6},{9,8},{10,9},{11,10},{12... | collective-permute-start | bytes 73736 | tf_op jit(solution)/shard_map/ppermute | solution.py:17
  19.2 0.0 collective-permute-done.1
  19.2 3.3 %collective-permute-done.2 = bf16[4,8,2,192]{3,1,2,0:T(8,128)(2,1)S(1)} collective-permute-done((bf16[4,8,2,192]{3,1,2,0:T(8,128)(2,1)S(1)}, bf16[4,8,2,192]{3,1,2,0:T(8,128)(2,1)S(1)}, u32[]{:S(2)}, u32[]{:S(2)}) %collective-permute-start.2) | collective-permute-done | bytes 24608 | tf_op jit(solution)/shard_map/ppermute | solution.py:17
  22.5 0.1 pad_maximum_fusion
  22.6 0.2 fusion.84
  22.8 3.1 %collective-permute-start.3 = (bf16[4,2,36,192]{3,1,2,0:T(2,128)(2,1)S(1)}, bf16[4,2,36,192]{3,1,2,0:T(2,128)(2,1)S(1)}, u32[]{:S(2)}, u32[]{:S(2)}) collective-permute-start(bf16[4,2,36,192]{3,1,2,0:T(2,128)(2,1)S(1)} %get-tuple-element.9), channel_id=1, source_target_pairs={{0,8},{8,16},{16,24},{1,9},{9,17},{17,25},{2,10},{10,18},{18,26},{... | collective-permute-start | bytes 331784 | tf_op jit(solution)/shard_map/ppermute | solution.py:15
  25.9 1.3 %collective-permute-start.4 = (bf16[4,2,36,192]{3,1,2,0:T(2,128)(2,1)S(1)}, bf16[4,2,36,192]{3,1,2,0:T(2,128)(2,1)S(1)}, u32[]{:S(2)}, u32[]{:S(2)}) collective-permute-start(bf16[4,2,36,192]{3,1,2,0:T(2,128)(2,1)S(1)} %get-tuple-element.10), channel_id=1, source_target_pairs={{8,0},{16,8},{24,16},{9,1},{17,9},{25,17},{10,2},{18,10},{26,18},{... | collective-permute-start | bytes 331784 | tf_op jit(solution)/shard_map/ppermute | solution.py:17
  27.3 1.9 %collective-permute-done.3 = bf16[4,2,36,192]{3,1,2,0:T(2,128)(2,1)S(1)} collective-permute-done((bf16[4,2,36,192]{3,1,2,0:T(2,128)(2,1)S(1)}, bf16[4,2,36,192]{3,1,2,0:T(2,128)(2,1)S(1)}, u32[]{:S(2)}, u32[]{:S(2)}) %collective-permute-start.3) | collective-permute-done | bytes 110624 | tf_op jit(solution)/shard_map/ppermute | solution.py:15
  29.2 4.3 %collective-permute-done.4 = bf16[4,2,36,192]{3,1,2,0:T(2,128)(2,1)S(1)} collective-permute-done((bf16[4,2,36,192]{3,1,2,0:T(2,128)(2,1)S(1)}, bf16[4,2,36,192]{3,1,2,0:T(2,128)(2,1)S(1)}, u32[]{:S(2)}, u32[]{:S(2)}) %collective-permute-start.4) | collective-permute-done | bytes 110624 | tf_op jit(solution)/shard_map/ppermute | solution.py:17
  33.4 0.7 %fusion.40 = (bf16[4,8,1,36,192]{4,1,3,0,2:T(8,128)(2,1)S(1)}, bf16[4,8,1,36,192]{4,1,3,0,2:T(8,128)(2,1)S(1)}) fusion(bf16[4,2,36,192]{3,1,2,0:T(2,128)(2,1)S(1)} %collective-permute-done.4, bf16[4,8,2,192]{3,1,2,0:T(8,128)(2,1)S(1)} %collective-permute-done.2, bf16[4,8,2,192]{3,1,2,0:T(8,128)(2,1)S(1)} %collective-permute-done.1, ...), kind=kLoop, calls=%fused_computation.41 | loop fusion | flops 8404992 | bytes 1548288 | tf_op jit(solution)/shard_map/broadcast_in_dim | solution.py:36
  34.1 0.1 pad
  34.3 0.0 copy-start.7
  34.3 0.1 copy.10
  34.4 0.1 slice.67
  34.5 0.0 copy-done
  34.5 0.5 copy-done.7
  34.9 1.6 %convolution_select_fusion.1 = f32[2,6,8,5,192]{4,2,3,1,0:T(8,128)S(1)} fusion(bf16[3,3,3,192,192]{4,3,2,1,0:T(8,128)(2,1)S(1)} %copy-done, bf16[4,8,1,7,2,192]{5,3,4,1,0,2:T(8,128)(2,1)S(1)} %slice.67, bf16[4,8,1,8,5,192]{5,3,4,1,0,2:T(8,128)(2,1)S(1)} %copy.10, pred[8,5]{0,1:T(8,128)(4,1)S(1)} %copy-done.7), kind=kOutput, calls=%fused_computation.11 | convolution fusion | flops 957671424 | bytes 3022888 | tf_op jit(solution)/shard_map/conv_general_dilated | solution.py:35
  36.5 0.4 copy.11
  36.9 0.1 pad.2
  37.0 0.1 copy.13
  37.1 0.1 slice.71
  37.2 0.0 copy-start.2
  37.2 1.6 %convolution_select_fusion = f32[2,6,8,5,192]{4,2,3,1,0:T(8,128)S(1)} fusion(bf16[3,3,3,192,192]{4,3,2,1,0:T(8,128)(2,1)S(1)} %copy-done, bf16[4,8,1,7,2,192]{5,3,4,1,0,2:T(8,128)(2,1)S(1)} %slice.71, bf16[4,8,1,8,5,192]{5,3,4,1,0,2:T(8,128)(2,1)S(1)} %copy.13, pred[8,5]{0,1:T(8,128)(4,1)S(1)} %copy-done.7), kind=kOutput, calls=%fused_computation.10 | convolution fusion | flops 957671424 | bytes 3022888 | tf_op jit(solution)/shard_map/conv_general_dilated | solution.py:35
  38.8 0.0 copy-start.3
  38.8 0.4 copy.14
  39.2 0.0 copy-done.2
  39.2 0.6 %fusion.63 = (f32[2,6,34]{0,2,1:T(8,128)S(1)}, f32[2,6,34]{0,2,1:T(8,128)S(1)}) fusion(f32[192]{0:T(256)S(1)} %copy-done.2, f32[2,6,1,40,192]{4,0,3,1,2:T(2,128)S(1)} %bitcast.53, f32[2,6,1,40,192]{4,0,3,1,2:T(2,128)S(1)} %bitcast.51), kind=kLoop, calls=%fused_computation.72 | loop fusion | flops 782544 | bytes 630720 | tf_op jit(solution)/shard_map/reduce_sum | solution.py:31
  39.8 0.0 copy-done.3
  39.8 0.0 copy-start.5
  39.8 1.6 %select_convert_fusion = (bf16[2,6,34,192]{3,0,2,1:T(2,128)(2,1)S(1)}, bf16[2,6,34,192]{3,0,2,1:T(2,128)(2,1)S(1)}) fusion(pred[6,34]{1,0:T(8,128)(4,1)S(1)} %slice.70, f32[2,6,34]{0,2,1:T(8,128)S(1)} %get-tuple-element.19, f32[192]{0:T(256)S(1)} %copy-done.3, f32[192]{0:T(256)S(1)} %copy-done.2, f32[2,6,1,40,192]{4,0,3,1,2:T(2,128)S(1)} %bitcast.54, ...), kind=kLoop, calls=%fused_computation.80 | loop fusion | flops 1723392 | bytes 945240 | tf_op jit(solution)/shard_map/convert_element_type | solution.py:70
  41.4 0.1 fusion.85
  41.5 0.0 copy-start.6
  41.5 0.5 maximum_bitcast_fusion
  42.1 0.3 pad.4
  42.5 0.0 copy-done.5
  42.5 0.0 copy-done.6
  42.5 1.4 %fusion.12 = bf16[2,8,8,5,192]{4,2,3,1,0:T(8,128)(2,1)S(1)} fusion(bf16[3,3,3,192,192]{4,3,2,1,0:T(8,128)(2,1)S(1)} %copy-done.5, pred[8,5]{0,1:T(8,128)(4,1)S(1)} %copy-done.6, bf16[2,10,1,7,2,192]{5,3,4,1,0,2:T(8,128)(2,1)S(1)} %slice.74, bf16[2,10,1,8,5,192]{5,3,4,1,0,2:T(8,128)(2,1)S(1)} %copy.16), kind=kOutput, calls=%fused_computation.9 | convolution fusion | flops 638545920 | bytes 2589696 | tf_op jit(solution)/shard_map/conv_general_dilated | solution.py:35
  44.0 0.1 copy.18
  44.1 1.9 %collective-permute-start.5 = (bf16[2,8,32,192]{3,1,2,0:T(8,128)(2,1)S(1)}, bf16[2,8,32,192]{3,1,2,0:T(8,128)(2,1)S(1)}, u32[]{:S(2)}, u32[]{:S(2)}) collective-permute-start(bf16[2,8,32,192]{3,1,2,0:T(8,128)(2,1)S(1)} %slice_bitcast_fusion.3), channel_id=1, source_target_pairs={{0,32},{32,64},{64,96},{96,128},{128,160},{160,192},{192,224},{224... | collective-permute-start | bytes 589832 | tf_op jit(solution)/shard_map/ppermute | solution.py:27
  46.0 1.4 %fusion.6 = f32[2,8,8,5,192]{4,2,3,1,0:T(8,128)S(1)} fusion(bf16[3,3,3,192,192]{4,3,2,1,0:T(8,128)(2,1)S(1)} %copy-done.5, pred[8,5]{0,1:T(8,128)(4,1)S(1)} %copy-done.6, bf16[2,10,1,7,2,192]{5,3,4,1,0,2:T(8,128)(2,1)S(1)} %slice.74, bf16[2,10,1,8,5,192]{5,3,4,1,0,2:T(8,128)(2,1)S(1)} %copy.16), kind=kOutput, calls=%fused_computation.7 | convolution fusion | flops 638423040 | bytes 2835456 | tf_op jit(solution)/shard_map/conv_general_dilated | solution.py:35
  47.4 0.0 copy-start.1
  47.4 0.0 copy-start.4
  47.4 0.2 copy.17
  47.6 7.0 %collective-permute-done.5 = bf16[2,8,32,192]{3,1,2,0:T(8,128)(2,1)S(1)} collective-permute-done((bf16[2,8,32,192]{3,1,2,0:T(8,128)(2,1)S(1)}, bf16[2,8,32,192]{3,1,2,0:T(8,128)(2,1)S(1)}, u32[]{:S(2)}, u32[]{:S(2)}) %collective-permute-start.5) | collective-permute-done | bytes 196640 | tf_op jit(solution)/shard_map/ppermute | solution.py:27
  54.6 0.0 copy-done.1
  54.6 0.0 copy-done.4
  54.6 0.2 fusion.58
  54.9 0.8 %copy.19 = bf16[2,8,32,192]{3,2,1,0:T(8,128)(2,1)} copy(bf16[2,8,32,192]{3,1,2,0:T(8,128)(2,1)S(1)} %fusion.58) | data formatting | bytes 393216 | tf_op jit(solution)/shard_map/convert_element_type | solution.py:82
  (11 shorter events, 0.2 us)
Async XLA Ops:
  0.0 34.5 %copy-start = (bf16[3,3,3,192,192]{4,3,2,1,0:T(8,128)(2,1)S(1)}, bf16[3,3,3,192,192]{4,3,2,1,0:T(8,128)(2,1)}, u32[]{:S(2)}) copy-start(bf16[3,3,3,192,192]{4,3,2,1,0:T(8,128)(2,1)} %param.9) | copy-start | bytes 5971972
  2.6 10.3 %collective-permute-start = (bf16[2,8,32,192]{3,1,2,0:T(8,128)(2,1)S(1)}, bf16[2,8,32,192]{3,1,2,0:T(8,128)(2,1)S(1)}, u32[]{:S(2)}, u32[]{:S(2)}) collective-permute-start(bf16[2,8,32,192]{3,1,2,0:T(8,128)(2,1)S(1)} %fusion.55), channel_id=1, source_target_pairs={{0,32},{32,64},{64,96},{96,128},{128,160},{160,192},{192,224},{224... | collective-permute-start | bytes 589832 | tf_op jit(solution)/shard_map/ppermute | solution.py:27
  12.9 6.3 %collective-permute-start.1 = (bf16[4,8,2,192]{3,1,2,0:T(8,128)(2,1)S(1)}, bf16[4,8,2,192]{3,1,2,0:T(8,128)(2,1)S(1)}, u32[]{:S(2)}, u32[]{:S(2)}) collective-permute-start(bf16[4,8,2,192]{3,1,2,0:T(8,128)(2,1)S(1)} %get-tuple-element.11), channel_id=1, source_target_pairs={{0,1},{1,2},{2,3},{3,4},{4,5},{5,6},{6,7},{8,9},{9,10},{10,11},{11... | collective-permute-start | bytes 73736 | tf_op jit(solution)/shard_map/ppermute | solution.py:15
  17.2 5.2 %collective-permute-start.2 = (bf16[4,8,2,192]{3,1,2,0:T(8,128)(2,1)S(1)}, bf16[4,8,2,192]{3,1,2,0:T(8,128)(2,1)S(1)}, u32[]{:S(2)}, u32[]{:S(2)}) collective-permute-start(bf16[4,8,2,192]{3,1,2,0:T(8,128)(2,1)S(1)} %get-tuple-element.12), channel_id=1, source_target_pairs={{1,0},{2,1},{3,2},{4,3},{5,4},{6,5},{7,6},{9,8},{10,9},{11,10},{12... | collective-permute-start | bytes 73736 | tf_op jit(solution)/shard_map/ppermute | solution.py:17
  22.8 6.3 %collective-permute-start.3 = (bf16[4,2,36,192]{3,1,2,0:T(2,128)(2,1)S(1)}, bf16[4,2,36,192]{3,1,2,0:T(2,128)(2,1)S(1)}, u32[]{:S(2)}, u32[]{:S(2)}) collective-permute-start(bf16[4,2,36,192]{3,1,2,0:T(2,128)(2,1)S(1)} %get-tuple-element.9), channel_id=1, source_target_pairs={{0,8},{8,16},{16,24},{1,9},{9,17},{17,25},{2,10},{10,18},{18,26},{... | collective-permute-start | bytes 331784 | tf_op jit(solution)/shard_map/ppermute | solution.py:15
  25.9 7.5 %collective-permute-start.4 = (bf16[4,2,36,192]{3,1,2,0:T(2,128)(2,1)S(1)}, bf16[4,2,36,192]{3,1,2,0:T(2,128)(2,1)S(1)}, u32[]{:S(2)}, u32[]{:S(2)}) collective-permute-start(bf16[4,2,36,192]{3,1,2,0:T(2,128)(2,1)S(1)} %get-tuple-element.10), channel_id=1, source_target_pairs={{8,0},{16,8},{24,16},{9,1},{17,9},{25,17},{10,2},{18,10},{26,18},{... | collective-permute-start | bytes 331784 | tf_op jit(solution)/shard_map/ppermute | solution.py:17
  34.3 0.7 %copy-start.7 = (pred[8,5]{0,1:T(8,128)(4,1)S(1)}, pred[8,5]{0,1:T(8,128)(4,1)}, u32[]{:S(2)}) copy-start(pred[8,5]{0,1:T(8,128)(4,1)} %constant.57) | copy-start | bytes 124
  37.2 2.0 %copy-start.2 = (f32[192]{0:T(256)S(1)}, f32[192]{0:T(256)}, u32[]{:S(2)}) copy-start(f32[192]{0:T(256)} %param.10) | copy-start | bytes 2308
  38.8 1.0 %copy-start.3 = (f32[192]{0:T(256)S(1)}, f32[192]{0:T(256)}, u32[]{:S(2)}) copy-start(f32[192]{0:T(256)} %param.11) | copy-start | bytes 2308
  39.8 2.7 %copy-start.5 = (bf16[3,3,3,192,192]{4,3,2,1,0:T(8,128)(2,1)S(1)}, bf16[3,3,3,192,192]{4,3,2,1,0:T(8,128)(2,1)}, u32[]{:S(2)}) copy-start(bf16[3,3,3,192,192]{4,3,2,1,0:T(8,128)(2,1)} %param.12) | copy-start | bytes 5971972
  41.5 1.0 %copy-start.6 = (pred[8,5]{0,1:T(8,128)(4,1)S(1)}, pred[8,5]{0,1:T(8,128)(4,1)}, u32[]{:S(2)}) copy-start(pred[8,5]{0,1:T(8,128)(4,1)} %constant.56) | copy-start | bytes 124
  44.1 10.6 %collective-permute-start.5 = (bf16[2,8,32,192]{3,1,2,0:T(8,128)(2,1)S(1)}, bf16[2,8,32,192]{3,1,2,0:T(8,128)(2,1)S(1)}, u32[]{:S(2)}, u32[]{:S(2)}) collective-permute-start(bf16[2,8,32,192]{3,1,2,0:T(8,128)(2,1)S(1)} %slice_bitcast_fusion.3), channel_id=1, source_target_pairs={{0,32},{32,64},{64,96},{96,128},{128,160},{160,192},{192,224},{224... | collective-permute-start | bytes 589832 | tf_op jit(solution)/shard_map/ppermute | solution.py:27
  47.4 7.2 %copy-start.1 = (bf16[2,8,32,192]{3,2,1,0:T(8,128)(2,1)S(1)}, bf16[2,8,32,192]{3,2,1,0:T(8,128)(2,1)}, u32[]{:S(2)}) copy-start(bf16[2,8,32,192]{3,2,1,0:T(8,128)(2,1)} %param.7) | copy-start | bytes 589828
  47.4 7.2 %copy-start.4 = (f32[192]{0:T(256)S(1)}, f32[192]{0:T(256)}, u32[]{:S(2)}) copy-start(f32[192]{0:T(256)} %param.13) | copy-start | bytes 2308
